TPU v7x, 32 devices: a whole 2x2x4 slice. The times are simulated.
32 devices in a mesh: seq: 8 (over z, y), fsdp: 4 (over x, core).
Axes of the slice: x: 2, y: 2, z: 4, core: 2. Of those that a mesh axis runs over, the one named last changes fastest.
Arguments:
- layer_input: bfloat16 [2, 4, 1024, 768], P(None, 'fsdp', 'seq'), may hold values from -6 to 6
- history: bfloat16 [4, 2, 4, 1024, 768], P(None, None, 'fsdp', 'seq'), may hold values from -6 to 6
- cotangent: bfloat16 [2, 4, 1024, 768], P(None, 'fsdp', 'seq'), may hold values from -6 to 6
- lengths: int32 [2, 4], P(None, 'fsdp'), may hold values from 256 to 1024, as said below
- w_qkv: bfloat16 [768, 2304], P(('seq', 'fsdp')), may hold values from -0.21875 to 0.21875
- w_out: bfloat16 [768, 768], P(('seq', 'fsdp')), may hold values from -1 to 1
- w_up: bfloat16 [768, 3072], P(('seq', 'fsdp')), may hold values from -0.21875 to 0.21875
- w_down: bfloat16 [3072, 768], P(('seq', 'fsdp')), may hold values from -0.109375 to 0.109375
- ln_gains: bfloat16 [768, 2], P(('seq', 'fsdp')), may hold values from 0.5 to 1.5
- ln_biases: bfloat16 [768, 2], P(('seq', 'fsdp')), may hold values from -0.5 to 0.5
- depth_weights: float32 [5], replicated, may hold values from 0.3 to 1
Outputs:
- next_input: bfloat16 [2, 4, 1024, 768], P(None, 'fsdp', 'seq')
- grad_input: bfloat16 [2, 4, 1024, 768], P(None, 'fsdp', 'seq')
- grad_history: bfloat16 [4, 2, 4, 1024, 768], P(None, None, 'fsdp', 'seq')
- grad_w_qkv: float32 [768, 2304], P(('seq', 'fsdp'))
- grad_w_out: float32 [768, 768], P(('seq', 'fsdp'))
- grad_w_up: float32 [768, 3072], P(('seq', 'fsdp'))
- grad_w_down: float32 [3072, 768], P(('seq', 'fsdp'))
- grad_ln_gains: float32 [768, 2], P(('seq', 'fsdp'))
- grad_ln_biases: float32 [768, 2], P(('seq', 'fsdp'))
- grad_depth: float32 [5], replicated
Inputs may be any that keep to these rules, and one draw needn't show every extreme that they name: Each slot holds one sequence of lengths[m, s] tokens at its start and padding after it; the first slot of every micro-batch is full.
All inputs are finite; a program needn't handle non-finite values.
Results may differ from a plain program's by a relative error of at most 0.015.
Values may be sent and summed in bfloat16 or wider, within the bound.
No kernel may reach another device: no remote copies, remote signals or barrier semaphores. Data moves between devices by JAX's collectives and lax.ppermute only.
A program may use at most 192 MiB of HBM per device.

v0:
```python
from functools import partial
import math

import jax
import jax.numpy as jnp
from jax import lax
from jax.sharding import PartitionSpec as P

HEADS = 12
HEAD = 64


epsilon = 1e-05
masked_value = -1e30


def layer_norm(values, gain_vector, bias_vector):
    center = values - jnp.mean(values, axis=-1, keepdims=True)
    spread = jnp.mean(center * center, axis=-1, keepdims=True)
    return center * lax.rsqrt(spread + epsilon) * gain_vector + bias_vector


def rotary_tables(positions):
    half_width = HEAD // 2
    frequencies = 10000.0 ** (-jnp.arange(half_width, dtype=jnp.float32) / half_width)
    angles = positions.astype(jnp.float32)[:, None] * frequencies[None, :]
    return (jnp.cos(angles)[:, None, :], jnp.sin(angles)[:, None, :])


def rotate(values, cosine_part, sine_part):
    row_count = values.shape[0]
    shaped = values.reshape(row_count, HEADS, HEAD)
    half_width = HEAD // 2
    first_half = shaped[..., :half_width]
    second_half = shaped[..., half_width:]
    turned = jnp.concatenate(
        [
            first_half * cosine_part - second_half * sine_part,
            second_half * cosine_part + first_half * sine_part,
        ],
        axis=-1,
    )
    return turned.reshape(row_count, HEADS * HEAD)


def block_scores(queries3, keys3, query_pos, key_pos, length):
    scores = jnp.einsum(
        "rhd,khd->hrk", queries3, keys3, preferred_element_type=jnp.float32
    ) * HEAD ** (-0.5)
    allowed = (key_pos[None, :] <= query_pos[:, None]) & (key_pos[None, :] < length)
    return (scores, allowed[None])


def row_totals(queries3, keys3, query_pos, length, key_block):
    row_count = queries3.shape[0]

    def row_advance(state, block_index):
        running_top, running_sum = state
        first_key = block_index * key_block
        keys_part = lax.dynamic_slice_in_dim(keys3, first_key, key_block, 0)
        key_pos = first_key + jnp.arange(key_block, dtype=jnp.int32)
        scores, allowed = block_scores(queries3, keys_part, query_pos, key_pos, length)
        masked = jnp.where(allowed, scores, masked_value)
        new_top = jnp.maximum(running_top, jnp.max(masked, axis=-1))
        kept_terms = jnp.where(allowed, jnp.exp(masked - new_top[..., None]), 0.0)
        running_sum = running_sum * jnp.exp(running_top - new_top) + jnp.sum(kept_terms, axis=-1)
        return ((new_top, running_sum), None)

    initial = (
        jnp.full((HEADS, row_count), masked_value, jnp.float32),
        jnp.zeros((HEADS, row_count), jnp.float32),
    )
    (row_tops, row_sums), _ = lax.scan(
        row_advance, initial, jnp.arange(keys3.shape[0] // key_block, dtype=jnp.int32)
    )
    return row_tops + jnp.log(row_sums)


def attend(queries3, keys3, values3, query_pos, length, key_block, log_total):

    def attend_advance(running, block_index):
        first_key = block_index * key_block
        keys_part = lax.dynamic_slice_in_dim(keys3, first_key, key_block, 0)
        values_part = lax.dynamic_slice_in_dim(values3, first_key, key_block, 0)
        key_pos = first_key + jnp.arange(key_block, dtype=jnp.int32)
        scores, allowed = block_scores(queries3, keys_part, query_pos, key_pos, length)
        probabilities = jnp.where(allowed, jnp.exp(scores - log_total[..., None]), 0.0).astype(
            jnp.bfloat16
        )
        return (
            running
            + jnp.einsum(
                "hrk,khd->rhd", probabilities, values_part, preferred_element_type=jnp.float32
            ),
            None,
        )

    initial = jnp.zeros(queries3.shape, jnp.float32)
    result, _ = lax.scan(
        attend_advance, initial, jnp.arange(keys3.shape[0] // key_block, dtype=jnp.int32)
    )
    return result


def query_grads(
    queries3, grads3, keys3, values3, query_pos, length, key_block, log_total, row_delta
):

    def query_advance(running, block_index):
        first_key = block_index * key_block
        keys_part = lax.dynamic_slice_in_dim(keys3, first_key, key_block, 0)
        values_part = lax.dynamic_slice_in_dim(values3, first_key, key_block, 0)
        key_pos = first_key + jnp.arange(key_block, dtype=jnp.int32)
        scores, allowed = block_scores(queries3, keys_part, query_pos, key_pos, length)
        probabilities = jnp.where(allowed, jnp.exp(scores - log_total[..., None]), 0.0)
        prob_grad = jnp.einsum(
            "rhd,khd->hrk", grads3, values_part, preferred_element_type=jnp.float32
        )
        score_low = (probabilities * (prob_grad - row_delta[..., None])).astype(jnp.bfloat16)
        return (
            running
            + jnp.einsum("hrk,khd->rhd", score_low, keys_part, preferred_element_type=jnp.float32),
            None,
        )

    initial = jnp.zeros(queries3.shape, jnp.float32)
    result, _ = lax.scan(
        query_advance, initial, jnp.arange(keys3.shape[0] // key_block, dtype=jnp.int32)
    )
    return result * HEAD ** (-0.5)


def key_side(queries3, grads3, log_part, delta_part, query_pos, keys3, values3, key_pos, length):
    key_count = keys3.shape[0]
    scores, allowed = block_scores(queries3, keys3, query_pos, key_pos, length)
    probabilities = jnp.where(allowed, jnp.exp(scores - log_part[..., None]), 0.0)
    prob_grad = jnp.einsum("rhd,khd->hrk", grads3, values3, preferred_element_type=jnp.float32)
    score_low = (probabilities * (prob_grad - delta_part[..., None])).astype(jnp.bfloat16)
    value_grad = jnp.einsum(
        "hrk,rhd->khd",
        probabilities.astype(jnp.bfloat16),
        grads3,
        preferred_element_type=jnp.float32,
    )
    key_grad = jnp.einsum(
        "hrk,rhd->khd", score_low, queries3, preferred_element_type=jnp.float32
    ) * HEAD ** (-0.5)
    return jnp.concatenate(
        [key_grad.reshape(key_count, HEADS * HEAD), value_grad.reshape(key_count, HEADS * HEAD)],
        axis=1,
    )


def local(
    layer_input,
    history,
    cotangent,
    lengths,
    w_qkv,
    w_out,
    w_up,
    w_down,
    ln_gains,
    ln_biases,
    depth_weights,
):
    batches = layer_input.shape[0]
    row_count = layer_input.shape[2]
    model_width = layer_input.shape[3]
    slot_len = row_count * lax.axis_size("seq")
    key_block = min(1024, slot_len)
    positions = lax.axis_index("seq") * row_count + jnp.arange(row_count, dtype=jnp.int32)
    cosine_part, sine_part = rotary_tables(positions)
    gelu_tanh = partial(jax.nn.gelu, approximate=True)
    totals = None
    owner_shares = None
    depth_terms = jnp.zeros((5,), jnp.float32)
    next_rows = []
    input_grads = []
    history_grads = []
    for micro in range(batches):
        gathered = (
            lax.all_gather(w_qkv, ("seq", "fsdp"), axis=0, tiled=True),
            lax.all_gather(w_out, ("seq", "fsdp"), axis=0, tiled=True),
            lax.all_gather(w_up, ("seq", "fsdp"), axis=0, tiled=True),
            lax.all_gather(w_down, ("seq", "fsdp"), axis=0, tiled=True),
            lax.all_gather(ln_gains, ("seq", "fsdp"), axis=0, tiled=True),
            lax.all_gather(ln_biases, ("seq", "fsdp"), axis=0, tiled=True),
        )
        full_qkv, full_out, full_up, full_down, gain_rows, bias_rows = gathered
        norm_gains = gain_rows.astype(jnp.float32)
        norm_biases = bias_rows.astype(jnp.float32)
        length = lengths[micro, 0]
        usable = (positions < length)[:, None]
        inputs = layer_input[micro, 0].astype(jnp.float32)
        earlier = history[:, micro, 0].astype(jnp.float32)
        grad_next = jnp.where(usable, cotangent[micro, 0].astype(jnp.float32), 0.0)
        first_low = layer_norm(inputs, norm_gains[:, 0], norm_biases[:, 0]).astype(jnp.bfloat16)
        projected = jnp.dot(first_low, full_qkv, preferred_element_type=jnp.float32)
        queries = (
            rotate(projected[:, :model_width], cosine_part, sine_part)
            .astype(jnp.bfloat16)
            .reshape(row_count, HEADS, HEAD)
        )
        keys_own = rotate(
            projected[:, model_width : 2 * model_width], cosine_part, sine_part
        ).astype(jnp.bfloat16)
        values_own = projected[:, 2 * model_width :].astype(jnp.bfloat16)
        keys_all, values_all = (
            lax.all_gather(keys_own, "seq", axis=0, tiled=True),
            lax.all_gather(values_own, "seq", axis=0, tiled=True),
        )
        keys3 = keys_all.reshape(slot_len, HEADS, HEAD)
        values3 = values_all.reshape(slot_len, HEADS, HEAD)
        log_total = row_totals(queries, keys3, positions, length, key_block)
        attended = attend(queries, keys3, values3, positions, length, key_block, log_total)
        attended_low = attended.reshape(row_count, model_width).astype(jnp.bfloat16)
        residual = inputs + jnp.dot(attended_low, full_out, preferred_element_type=jnp.float32)
        second_low = layer_norm(residual, norm_gains[:, 1], norm_biases[:, 1]).astype(jnp.bfloat16)
        hidden = jnp.dot(second_low, full_up, preferred_element_type=jnp.float32)
        hidden_low = gelu_tanh(hidden).astype(jnp.bfloat16)
        block_out = residual + jnp.dot(hidden_low, full_down, preferred_element_type=jnp.float32)
        combined = depth_weights[4] * block_out + jnp.einsum(
            "j,jrd->rd", depth_weights[:4], earlier
        )
        next_rows.append(combined.astype(jnp.bfloat16))
        history_grads.append((depth_weights[:4, None, None] * grad_next[None]).astype(jnp.bfloat16))
        depth_terms = depth_terms + jnp.concatenate(
            [jnp.einsum("jrd,rd->j", earlier, grad_next), jnp.sum(block_out * grad_next)[None]]
        )
        out_grad = depth_weights[4] * grad_next
        out_low = out_grad.astype(jnp.bfloat16)
        grad_down = jnp.einsum("rf,rd->fd", hidden_low, out_low, preferred_element_type=jnp.float32)
        hidden_grad = jnp.einsum(
            "rd,fd->rf", out_low, full_down, preferred_element_type=jnp.float32
        )
        _, gelu_pullback = jax.vjp(gelu_tanh, hidden)
        up_low = gelu_pullback(hidden_grad)[0].astype(jnp.bfloat16)
        grad_up = jnp.einsum("rd,rf->df", second_low, up_low, preferred_element_type=jnp.float32)
        second_grad = jnp.einsum("rf,df->rd", up_low, full_up, preferred_element_type=jnp.float32)
        _, second_pullback = jax.vjp(layer_norm, residual, norm_gains[:, 1], norm_biases[:, 1])
        residual_part, gain_two, bias_two = second_pullback(second_grad)
        residual_grad = out_grad + residual_part
        branch_low = residual_grad.astype(jnp.bfloat16)
        grad_outproj = jnp.einsum(
            "rc,rd->cd", attended_low, branch_low, preferred_element_type=jnp.float32
        )
        attended_grad = jnp.einsum(
            "rd,cd->rc", branch_low, full_out, preferred_element_type=jnp.float32
        ).astype(jnp.bfloat16)
        attended_grad3 = attended_grad.reshape(row_count, HEADS, HEAD)
        row_delta = jnp.einsum("rhd,rhd->hr", attended_grad3.astype(jnp.float32), attended)
        query_grad = query_grads(
            queries,
            attended_grad3,
            keys3,
            values3,
            positions,
            length,
            key_block,
            log_total,
            row_delta,
        )
        sub_rows = math.gcd(lax.axis_size("seq") * row_count, key_block)

        def one_piece(piece_index):
            first_key = piece_index * sub_rows
            keys_part = lax.dynamic_slice_in_dim(keys3, first_key, sub_rows, 0)
            values_part = lax.dynamic_slice_in_dim(values3, first_key, sub_rows, 0)
            key_pos = first_key + jnp.arange(sub_rows, dtype=jnp.int32)
            return key_side(
                queries,
                attended_grad3,
                log_total,
                row_delta,
                positions,
                keys_part,
                values_part,
                key_pos,
                length,
            )

        pieces_out = lax.map(
            one_piece, jnp.arange(lax.axis_size("seq") * row_count // sub_rows, dtype=jnp.int32)
        )
        key_value_grad = lax.psum_scatter(
            pieces_out.reshape(lax.axis_size("seq") * row_count, 2 * model_width).astype(
                jnp.bfloat16
            ),
            "seq",
            scatter_dimension=0,
            tiled=True,
        ).astype(jnp.float32)
        key_grad = key_value_grad[:, :model_width]
        value_grad = key_value_grad[:, model_width:]
        qkv_low = jnp.concatenate(
            [
                rotate(query_grad.reshape(row_count, model_width), cosine_part, -sine_part),
                rotate(key_grad, cosine_part, -sine_part),
                value_grad,
            ],
            axis=1,
        ).astype(jnp.bfloat16)
        grad_qkv = jnp.einsum("rd,rc->dc", first_low, qkv_low, preferred_element_type=jnp.float32)
        first_grad = jnp.einsum("rc,dc->rd", qkv_low, full_qkv, preferred_element_type=jnp.float32)
        _, first_pullback = jax.vjp(layer_norm, inputs, norm_gains[:, 0], norm_biases[:, 0])
        input_part, gain_one, bias_one = first_pullback(first_grad)
        input_grads.append((residual_grad + input_part).astype(jnp.bfloat16))
        micro_grads = (
            grad_qkv,
            grad_outproj,
            grad_up,
            grad_down,
            jnp.stack([gain_one, gain_two], axis=1),
            jnp.stack([bias_one, bias_two], axis=1),
        )
        totals = (
            micro_grads
            if totals is None
            else tuple((former + latter for former, latter in zip(totals, micro_grads)))
        )
    owner_shares = lax.psum_scatter(totals, ("seq", "fsdp"), scatter_dimension=0, tiled=True)
    depth_total = lax.psum(depth_terms, ("seq", "fsdp"))
    next_input = jnp.stack(next_rows)[:, None]
    grad_input = jnp.stack(input_grads)[:, None]
    grad_history = jnp.stack(history_grads, axis=1)[:, :, None]
    return (
        next_input,
        grad_input,
        grad_history,
        owner_shares[0],
        owner_shares[1],
        owner_shares[2],
        owner_shares[3],
        owner_shares[4],
        owner_shares[5],
        depth_total,
    )


def solution(mesh):
    in_specs = (
        P(None, "fsdp", "seq", None),
        P(None, None, "fsdp", "seq", None),
        P(None, "fsdp", "seq", None),
        P(None, "fsdp"),
        P(("seq", "fsdp"), None),
        P(("seq", "fsdp"), None),
        P(("seq", "fsdp"), None),
        P(("seq", "fsdp"), None),
        P(("seq", "fsdp"), None),
        P(("seq", "fsdp"), None),
        P(),
    )
    out_specs = (
        P(None, "fsdp", "seq", None),
        P(None, "fsdp", "seq", None),
        P(None, None, "fsdp", "seq", None),
        P(("seq", "fsdp"), None),
        P(("seq", "fsdp"), None),
        P(("seq", "fsdp"), None),
        P(("seq", "fsdp"), None),
        P(("seq", "fsdp"), None),
        P(("seq", "fsdp"), None),
        P(),
    )
    return jax.shard_map(local, mesh=mesh, in_specs=in_specs, out_specs=out_specs, check_vma=False)
```

profile of v0, /device:TPU:0, one launch (start us, length us, event | category | flops | bytes accessed | tf_op | source)
XLA Modules:
  0.0 1166.3 jit_solution(16218702476510390781)
XLA Ops:
  8.0 43.5 %all-gather.1 = bf16[32,24,2]{1,2,0:T(2,128)(2,1)S(1)} all-gather(bf16[1,24,2]{1,2,0:T(2,128)(2,1)} %bitcast.313), channel_id=1, replica_groups=mesh['seq'=8,'fsdp'=4] {'seq','fsdp'}, dimensions={0}, use_global_device_ids=true | all-gather | bytes 3168 | tf_op jit(solution)/shard_map/all_gather | solution.py:188
  51.7 37.0 %all-gather = bf16[32,24,2]{1,2,0:T(2,128)(2,1)S(1)} all-gather(bf16[1,24,2]{1,2,0:T(2,128)(2,1)} %bitcast.314), channel_id=1, replica_groups=mesh['seq'=8,'fsdp'=4] {'seq','fsdp'}, dimensions={0}, use_global_device_ids=true | all-gather | bytes 3168 | tf_op jit(solution)/shard_map/all_gather | solution.py:187
  91.5 2.8 fusion.105
  95.2 2.7 fusion.108
  118.0 18.7 %all-gather.13.cloned.1.call-done = bf16[1024,768]{1,0:T(8,128)(2,1)} async-done(((bf16[128,768]{1,0:T(8,128)(2,1)}), bf16[1024,768]{1,0:T(8,128)(2,1)}) %all-gather.13.cloned.1.call-update) | async-done | bytes 1572880 | tf_op jit(solution)/shard_map/all_gather | solution.py:211
  138.5 43.6 %all-gather.23.cloned.1.call-done = bf16[1024,768]{1,0:T(8,128)(2,1)} async-done(((bf16[128,768]{1,0:T(8,128)(2,1)}), bf16[1024,768]{1,0:T(8,128)(2,1)}) %all-gather.23.cloned.1.call-update) | async-done | bytes 1572880 | tf_op jit(solution)/shard_map/all_gather | solution.py:211
  184.7 42.7 %all-gather.15.cloned.1.call-done = bf16[1024,768]{0,1:T(8,128)(2,1)} async-done(((bf16[128,768]{0,1:T(8,128)(2,1)}), bf16[1024,768]{0,1:T(8,128)(2,1)}) %all-gather.15.cloned.1.call-update) | async-done | bytes 1572880 | tf_op jit(solution)/shard_map/all_gather | solution.py:210
  227.4 2.7 select_reduce_fusion.3
  234.9 47.3 %all-gather.17.cloned.1.call-done = bf16[768,768]{1,0:T(8,128)(2,1)} async-done(((bf16[24,768]{1,0:T(8,128)(2,1)}), bf16[768,768]{1,0:T(8,128)(2,1)}) %all-gather.17.cloned.1.call-update) | async-done | bytes 1179664 | tf_op jit(solution)/shard_map/all_gather | solution.py:184
  284.2 43.9 %all-gather.25.cloned.1.call-done = bf16[1024,768]{0,1:T(8,128)(2,1)} async-done(((bf16[128,768]{0,1:T(8,128)(2,1)}), bf16[1024,768]{0,1:T(8,128)(2,1)}) %all-gather.25.cloned.1.call-update) | async-done | bytes 1572880 | tf_op jit(solution)/shard_map/all_gather | solution.py:210
  336.3 56.4 %all-gather.19.cloned.1.call-done = bf16[768,3072]{1,0:T(8,128)(2,1)} async-done(((bf16[24,3072]{1,0:T(8,128)(2,1)}), bf16[768,3072]{1,0:T(8,128)(2,1)}) %all-gather.19.cloned.1.call-update) | async-done | bytes 4718608 | tf_op jit(solution)/shard_map/all_gather | solution.py:185
  392.8 4.4 fusion.114
  397.2 60.4 %all-gather.21.cloned.1.call-done = bf16[3072,768]{1,0:T(8,128)(2,1)} async-done(((bf16[96,768]{1,0:T(8,128)(2,1)}), bf16[3072,768]{1,0:T(8,128)(2,1)}) %all-gather.21.cloned.1.call-update) | async-done | bytes 4718608 | tf_op jit(solution)/shard_map/all_gather | solution.py:186
  457.7 5.9 fusion.15
  474.3 3.7 fusion.52
  478.9 4.7 convolution_convert_fusion
  483.7 4.5 multiply_convert_fusion
  491.9 4.7 copy.107
  496.7 2.7 convolution_convert_fusion.3
  502.3 5.9 multiply_convert_fusion.1
  513.4 4.7 copy.105
  524.2 5.2 convolution_add_fusion.2
  533.3 6.1 convolution_add_fusion.1
  539.6 3.8 fusion.16
  544.7 24.7 %reduce-scatter.23.cloned.1.call-done = bf16[128,1536]{1,0:T(8,128)(2,1)} async-done(((bf16[1024,1536]{1,0:T(8,128)(2,1)}), bf16[128,1536]{1,0:T(8,128)(2,1)}) %reduce-scatter.23.cloned.1.call-update) | async-done | bytes 393232
  570.6 76.1 %reduce-scatter.21.cloned.1.call-done = bf16[128,1536]{1,0:T(8,128)(2,1)} async-done(((bf16[1024,1536]{1,0:T(8,128)(2,1)}), bf16[128,1536]{1,0:T(8,128)(2,1)}) %reduce-scatter.21.cloned.1.call-update) | async-done | bytes 393232
  650.3 4.2 convolution_add_fusion
  666.8 40.1 %all-reduce.2 = (f32[768,2]{0,1:T(2,128)S(1)}, f32[768,2]{0,1:T(2,128)S(1)}, f32[5]{0:T(128)}) all-reduce(f32[768,2]{0,1:T(2,128)S(1)} %maximum_add_fusion, f32[768,2]{0,1:T(2,128)S(1)} %maximum_add_fusion.1, f32[5]{0:T(128)S(1)} %maximum_add_fusion.2), channel_id=8, replica_groups=mesh['seq'=8,'fsdp'=4] {'seq','fsdp'}, use_global_device_ids=true, to_apply=%region_30.31.clone | all-reduce | flops 3077 | bytes 24616
  710.8 40.9 %reduce-scatter.15.cloned.1.call-done = f32[24,768]{1,0:T(8,128)} async-done(((f32[768,768]{1,0:T(8,128)}), f32[24,768]{1,0:T(8,128)}) %reduce-scatter.15.cloned.1.call-update) | async-done | bytes 73744 | tf_op jit(solution)/shard_map/reduce_scatter | solution.py:322
  751.7 141.6 %reduce-scatter.17.cloned.1.call-done = f32[24,3072]{1,0:T(8,128)} async-done(((f32[768,3072]{1,0:T(8,128)}), f32[24,3072]{1,0:T(8,128)}) %reduce-scatter.17.cloned.1.call-update) | async-done | bytes 294928 | tf_op jit(solution)/shard_map/reduce_scatter | solution.py:322
  893.3 141.6 %reduce-scatter.19.cloned.1.call-done = f32[96,768]{1,0:T(8,128)} async-done(((f32[3072,768]{1,0:T(8,128)}), f32[96,768]{1,0:T(8,128)}) %reduce-scatter.19.cloned.1.call-update) | async-done | bytes 294928 | tf_op jit(solution)/shard_map/reduce_scatter | solution.py:322
  1034.9 124.6 %reduce-scatter.13.cloned.1.call-done = f32[24,2304]{1,0:T(8,128)} async-done(((f32[768,2304]{1,0:T(8,128)}), f32[24,2304]{1,0:T(8,128)}) %reduce-scatter.13.cloned.1.call-update) | async-done | bytes 221200 | tf_op jit(solution)/shard_map/reduce_scatter | solution.py:322
  (350 shorter events, 98.9 us)
Async XLA Ops:
  7.2 84.3 %all-gather.11.cloned.1.call-start = ((), (), s32[]{:S(2)}) async-start(), calls=%async_computation.6 | async-start | bytes 3649536 | tf_op jit(solution)/shard_map/all_gather | solution.py:183
  7.9 128.8 %all-gather.13.cloned.1.call-start = ((), (), s32[]{:S(2)}) async-start(), calls=%async_computation.7 | async-start | bytes 1769472 | tf_op jit(solution)/shard_map/all_gather | solution.py:211
  95.1 87.0 %all-gather.23.cloned.1.call-start = ((), (), s32[]{:S(2)}) async-start(), calls=%async_computation.12 | async-start | bytes 1769472 | tf_op jit(solution)/shard_map/all_gather | solution.py:211
  98.6 128.8 %all-gather.15.cloned.1.call-start = ((), (), s32[]{:S(2)}) async-start(), calls=%async_computation.8 | async-start | bytes 1769472 | tf_op jit(solution)/shard_map/all_gather | solution.py:210
  106.1 121.3 %copy-start.38 = (bf16[128,12,32]{0,2,1:T(8,128)(2,1)}, bf16[128,12,32]{0,2,1:T(8,128)(2,1)S(1)}, u32[]{:S(2)}) copy-start(bf16[128,12,32]{0,2,1:T(8,128)(2,1)S(1)} %get-tuple-element.309) | copy-start | bytes 294916
  106.1 121.3 %copy-start.40 = (bf16[128,12,32]{0,2,1:T(8,128)(2,1)}, bf16[128,12,32]{0,2,1:T(8,128)(2,1)S(1)}, u32[]{:S(2)}) copy-start(bf16[128,12,32]{0,2,1:T(8,128)(2,1)S(1)} %get-tuple-element.310) | copy-start | bytes 294916
  106.1 222.0 %copy-start.42 = (bf16[128,12,32]{0,2,1:T(8,128)(2,1)}, bf16[128,12,32]{0,2,1:T(8,128)(2,1)S(1)}, u32[]{:S(2)}) copy-start(bf16[128,12,32]{0,2,1:T(8,128)(2,1)S(1)} %get-tuple-element.339) | copy-start | bytes 294916
  106.9 175.4 %all-gather.17.cloned.1.call-start = ((), (), s32[]{:S(2)}) async-start(), calls=%async_computation.9 | async-start | bytes 1216512 | tf_op jit(solution)/shard_map/all_gather | solution.py:184
  107.4 220.6 %all-gather.25.cloned.1.call-start = ((), (), s32[]{:S(2)}) async-start(), calls=%async_computation.13 | async-start | bytes 1769472 | tf_op jit(solution)/shard_map/all_gather | solution.py:210
  109.2 283.6 %all-gather.19.cloned.1.call-start = ((), (), s32[]{:S(2)}) async-start(), calls=%async_computation.10 | async-start | bytes 4866048 | tf_op jit(solution)/shard_map/all_gather | solution.py:185
  109.9 347.7 %all-gather.21.cloned.1.call-start = ((), (), s32[]{:S(2)}) async-start(), calls=%async_computation.11 | async-start | bytes 4866048 | tf_op jit(solution)/shard_map/all_gather | solution.py:186
  110.7 458.7 %reduce-scatter.23.cloned.1.call-start = ((), (), s32[]{:S(2)}) async-start(), calls=%async_computation.19 | async-start | bytes 3538944
  112.7 354.3 %copy-start.76 = (pred[128]{0:T(512)(128)(4,1)}, pred[128]{0:T(512)(128)(4,1)S(1)}, u32[]{:S(2)}) copy-start(pred[128]{0:T(512)(128)(4,1)S(1)} %broadcast_compare_fusion.1) | copy-start | bytes 388
  113.4 344.2 %copy-start.79 = (pred[128]{0:T(512)(128)(4,1)}, pred[128]{0:T(512)(128)(4,1)S(1)}, u32[]{:S(2)}) copy-start(pred[128]{0:T(512)(128)(4,1)S(1)} %broadcast_compare_fusion) | copy-start | bytes 388
  114.9 117.1 %copy-start.34 = (pred[128,1024]{1,0:T(8,128)(4,1)}, pred[128,1024]{1,0:T(8,128)(4,1)S(1)}, u32[]{:S(2)}) copy-start(pred[128,1024]{1,0:T(8,128)(4,1)S(1)} %get-tuple-element.353) | copy-start | bytes 393220
  115.0 218.2 %copy-start.36 = (pred[128,1024]{1,0:T(8,128)(4,1)}, pred[128,1024]{1,0:T(8,128)(4,1)S(1)}, u32[]{:S(2)}) copy-start(pred[128,1024]{1,0:T(8,128)(4,1)S(1)} %get-tuple-element.354) | copy-start | bytes 393220
  138.5 93.6 %copy-start.30 = (bf16[1024,768]{0,1:T(8,128)(2,1)}, bf16[1024,768]{0,1:T(8,128)(2,1)S(1)}, u32[]{:S(2)}) copy-start(bf16[1024,768]{0,1:T(8,128)(2,1)S(1)} %copy.65) | copy-start | bytes 4718596
  234.9 95.8 %copy-start.53 = (bf16[128,12,64]{0,2,1:T(8,128)(2,1)}, bf16[128,12,64]{0,2,1:T(8,128)(2,1)S(1)}, u32[]{:S(2)}) copy-start(bf16[128,12,64]{0,2,1:T(8,128)(2,1)S(1)} %get-tuple-element.359) | copy-start | bytes 589828
  234.9 93.1 %copy-start.44 = (bf16[128,12,32]{0,2,1:T(8,128)(2,1)S(1)}, bf16[128,12,32]{0,2,1:T(8,128)(2,1)}, u32[]{:S(2)}) copy-start(bf16[128,12,32]{0,2,1:T(8,128)(2,1)} %get-tuple-element.340) | copy-start | bytes 294916
  335.6 57.1 %copy-start.50 = (bf16[128,12,64]{0,2,1:T(8,128)(2,1)}, bf16[128,12,64]{0,2,1:T(8,128)(2,1)S(1)}, u32[]{:S(2)}) copy-start(bf16[128,12,64]{0,2,1:T(8,128)(2,1)S(1)} %get-tuple-element.365) | copy-start | bytes 589828
  336.3 135.3 %copy-start.64 = (f32[128]{0:T(128)}, f32[128]{0:T(128)S(1)}, u32[]{:S(2)}) copy-start(f32[128]{0:T(128)S(1)} %fusion.78) | copy-start | bytes 1540
  336.3 135.3 %copy-start.68 = (f32[128]{0:T(128)}, f32[128]{0:T(128)S(1)}, u32[]{:S(2)}) copy-start(f32[128]{0:T(128)S(1)} %fusion.80) | copy-start | bytes 1540
  392.8 64.9 %copy-start.23 = (bf16[2,1,128,768]{3,2,1,0:T(8,128)(2,1)S(1)}, bf16[2,1,128,768]{3,2,1,0:T(8,128)(2,1)}, u32[]{:S(2)}) copy-start(bf16[2,1,128,768]{3,2,1,0:T(8,128)(2,1)} %param.13) | copy-start | bytes 1179652
  392.8 71.7 %slice-start = ((s8[4718592]{0:T(1024)(128)(4,1)}), s8[524288]{0:T(1024)(128)(4,1)S(1)}, s32[]{:S(2)}) async-start(s8[4718592]{0:T(1024)(128)(4,1)} %bitcast.268), calls=%async_computation.20 | async-start | bytes 1048576
  496.6 150.0 %reduce-scatter.21.cloned.1.call-start = ((), (), s32[]{:S(2)}) async-start(), calls=%async_computation.18 | async-start | bytes 3538944
  518.2 233.6 %reduce-scatter.15.cloned.1.call-start = ((), (), s32[]{:S(2)}) async-start(), calls=%async_computation.15 | async-start | bytes 2433024 | tf_op jit(solution)/shard_map/reduce_scatter | solution.py:322
  521.6 371.7 %reduce-scatter.17.cloned.1.call-start = ((), (), s32[]{:S(2)}) async-start(), calls=%async_computation.16 | async-start | bytes 9732096 | tf_op jit(solution)/shard_map/reduce_scatter | solution.py:322
  529.4 505.5 %reduce-scatter.19.cloned.1.call-start = ((), (), s32[]{:S(2)}) async-start(), calls=%async_computation.17 | async-start | bytes 9732096 | tf_op jit(solution)/shard_map/reduce_scatter | solution.py:322
  539.4 620.1 %reduce-scatter.13.cloned.1.call-start = ((), (), s32[]{:S(2)}) async-start(), calls=%async_computation.14 | async-start | bytes 7299072 | tf_op jit(solution)/shard_map/reduce_scatter | solution.py:322
  664.8 43.5 %copy-start.85 = (f32[128]{0:T(128)S(1)}, f32[128]{0:T(128)}, u32[]{:S(2)}) copy-start(f32[128]{0:T(128)} %copy-done.84) | copy-start | bytes 1540
  666.2 42.9 %copy-start.16 = (f32[128,768]{1,0:T(8,128)S(1)}, f32[128,768]{1,0:T(8,128)}, u32[]{:S(2)}) copy-start(f32[128,768]{1,0:T(8,128)} %copy-done.15) | copy-start | bytes 1179652
  666.2 42.9 %copy-start.83 = (f32[128]{0:T(128)S(1)}, f32[128]{0:T(128)}, u32[]{:S(2)}) copy-start(f32[128]{0:T(128)} %copy-done.82) | copy-start | bytes 1540
  (81 other events, 275.2 us)
Sparse Core Ops, SparseCore 0:
  10.9 62.6 all-gather.10
  95.2 41.4 all-gather.12
  139.5 42.5 all-gather.22
  184.6 42.7 all-gather.14
  230.1 52.0 all-gather.16
  284.7 43.2 all-gather.24
  331.0 61.7 all-gather.18
  395.7 61.9 all-gather.20
  496.7 72.6 reduce-scatter.22
  572.8 73.8 reduce-scatter.20
  652.5 99.1 reduce-scatter.14
  758.0 135.1 reduce-scatter.16
  899.7 135.0 reduce-scatter.18
  1041.0 118.4 reduce-scatter.12
where the time goes:
time: 1170 us
  waiting for transfers between devices  865 us (74%)
  blocking collectives  121 us (10%)
  matrix products  94 us (8%)
  local copies, waits for them, and re-layouts  39.8 us (3%)
  other arithmetic  29.9 us (3%)
  between operations  15.7 us (1%)
    reduce_scatter x4, waiting for transfers between devices, local(): lax.psum_scatter(totals, ('seq', 'fsdp'), scatter_dimension=0, tiled=True)  449 us
    unnamed x16, waiting for transfers between devices  104 us
    all_gather x2, waiting for transfers between devices, local(): lax.all_gather(keys_own, 'seq', axis=0, tiled=True)  86.6 us
    all_gather x2, waiting for transfers between devices, local(): lax.all_gather(values_own, 'seq', axis=0, tiled=True)  62.3 us
    all_gather x1, waiting for transfers between devices, local(): lax.all_gather(w_down, ('seq', 'fsdp'), axis=0, tiled=True)  60.4 us
    all_gather x1, waiting for transfers between devices, local(): lax.all_gather(w_up, ('seq', 'fsdp'), axis=0, tiled=True)  56.4 us
    all_gather x1, waiting for transfers between devices, local(): lax.all_gather(w_out, ('seq', 'fsdp'), axis=0, tiled=True)  47.3 us
    all_gather x1, blocking collectives, local(): lax.all_gather(ln_biases, ('seq', 'fsdp'), axis=0, tiled=True)  43.5 us
  transfers between devices with their start and end apart: 14, of which 13 were waited for; matrix products, arithmetic and copies ran while one was open for 10% of the time, Pallas kernels for 0%

commit v1 on v0

--- a/solution.py
+++ b/solution.py
@@ -167,34 +167,45 @@
     batches = layer_input.shape[0]
     row_count = layer_input.shape[2]
     model_width = layer_input.shape[3]
+    ff_width = w_up.shape[1]
+    shard_rows = w_qkv.shape[0]
     slot_len = row_count * lax.axis_size("seq")
     key_block = min(1024, slot_len)
     positions = lax.axis_index("seq") * row_count + jnp.arange(row_count, dtype=jnp.int32)
     cosine_part, sine_part = rotary_tables(positions)
     gelu_tanh = partial(jax.nn.gelu, approximate=True)
-    totals = None
-    owner_shares = None
+    lane_pad = 128 - 4
+    widths = (3 * model_width, model_width, ff_width, ff_width, 2, 2, lane_pad)
+    offsets = [0]
+    for width in widths:
+        offsets.append(offsets[-1] + width)
+
+    def pieces(packed_rows):
+        return [packed_rows[:, offsets[i] : offsets[i + 1]] for i in range(len(widths))]
+
+    packed = jnp.concatenate(
+        [
+            w_qkv,
+            w_out,
+            w_up,
+            w_down.reshape(shard_rows, ff_width),
+            ln_gains,
+            ln_biases,
+            jnp.zeros((shard_rows, lane_pad), w_qkv.dtype),
+        ],
+        axis=1,
+    )
+    gathered = lax.all_gather(packed, ("seq", "fsdp"), axis=0, tiled=True)
+    full_qkv, full_out, full_up, down_rows, gain_rows, bias_rows, _ = pieces(gathered)
+    full_down = down_rows.reshape(ff_width, model_width)
+    norm_gains = gain_rows.astype(jnp.float32)
+    norm_biases = bias_rows.astype(jnp.float32)
+
     depth_terms = jnp.zeros((5,), jnp.float32)
-    next_rows = []
-    input_grads = []
-    history_grads = []
+    forward_parts = []
+    own_kv = []
     for micro in range(batches):
-        gathered = (
-            lax.all_gather(w_qkv, ("seq", "fsdp"), axis=0, tiled=True),
-            lax.all_gather(w_out, ("seq", "fsdp"), axis=0, tiled=True),
-            lax.all_gather(w_up, ("seq", "fsdp"), axis=0, tiled=True),
-            lax.all_gather(w_down, ("seq", "fsdp"), axis=0, tiled=True),
-            lax.all_gather(ln_gains, ("seq", "fsdp"), axis=0, tiled=True),
-            lax.all_gather(ln_biases, ("seq", "fsdp"), axis=0, tiled=True),
-        )
-        full_qkv, full_out, full_up, full_down, gain_rows, bias_rows = gathered
-        norm_gains = gain_rows.astype(jnp.float32)
-        norm_biases = bias_rows.astype(jnp.float32)
-        length = lengths[micro, 0]
-        usable = (positions < length)[:, None]
         inputs = layer_input[micro, 0].astype(jnp.float32)
-        earlier = history[:, micro, 0].astype(jnp.float32)
-        grad_next = jnp.where(usable, cotangent[micro, 0].astype(jnp.float32), 0.0)
         first_low = layer_norm(inputs, norm_gains[:, 0], norm_biases[:, 0]).astype(jnp.bfloat16)
         projected = jnp.dot(first_low, full_qkv, preferred_element_type=jnp.float32)
         queries = (
@@ -206,12 +217,23 @@
             projected[:, model_width : 2 * model_width], cosine_part, sine_part
         ).astype(jnp.bfloat16)
         values_own = projected[:, 2 * model_width :].astype(jnp.bfloat16)
-        keys_all, values_all = (
-            lax.all_gather(keys_own, "seq", axis=0, tiled=True),
-            lax.all_gather(values_own, "seq", axis=0, tiled=True),
-        )
-        keys3 = keys_all.reshape(slot_len, HEADS, HEAD)
-        values3 = values_all.reshape(slot_len, HEADS, HEAD)
+        forward_parts.append((inputs, first_low, queries))
+        own_kv.append(jnp.concatenate([keys_own, values_own], axis=1))
+    kv_all = lax.all_gather(jnp.stack(own_kv), "seq", axis=1, tiled=True)
+
+    key_value_parts = []
+    later_parts = []
+    totals = None
+    next_rows = []
+    history_grads = []
+    for micro in range(batches):
+        inputs, first_low, queries = forward_parts[micro]
+        keys3 = kv_all[micro, :, :model_width].reshape(slot_len, HEADS, HEAD)
+        values3 = kv_all[micro, :, model_width:].reshape(slot_len, HEADS, HEAD)
+        length = lengths[micro, 0]
+        usable = (positions < length)[:, None]
+        earlier = history[:, micro, 0].astype(jnp.float32)
+        grad_next = jnp.where(usable, cotangent[micro, 0].astype(jnp.float32), 0.0)
         log_total = row_totals(queries, keys3, positions, length, key_block)
         attended = attend(queries, keys3, values3, positions, length, key_block, log_total)
         attended_low = attended.reshape(row_count, model_width).astype(jnp.bfloat16)
@@ -261,7 +283,7 @@
             log_total,
             row_delta,
         )
-        sub_rows = math.gcd(lax.axis_size("seq") * row_count, key_block)
+        sub_rows = math.gcd(slot_len, key_block)
 
         def one_piece(piece_index):
             first_key = piece_index * sub_rows
@@ -280,19 +302,28 @@
                 length,
             )
 
-        pieces_out = lax.map(
-            one_piece, jnp.arange(lax.axis_size("seq") * row_count // sub_rows, dtype=jnp.int32)
-        )
-        key_value_grad = lax.psum_scatter(
-            pieces_out.reshape(lax.axis_size("seq") * row_count, 2 * model_width).astype(
-                jnp.bfloat16
-            ),
-            "seq",
-            scatter_dimension=0,
-            tiled=True,
-        ).astype(jnp.float32)
-        key_grad = key_value_grad[:, :model_width]
-        value_grad = key_value_grad[:, model_width:]
+        pieces_out = lax.map(one_piece, jnp.arange(slot_len // sub_rows, dtype=jnp.int32))
+        key_value_parts.append(
+            pieces_out.reshape(slot_len, 2 * model_width).astype(jnp.bfloat16)
+        )
+        later_parts.append((residual_grad, query_grad))
+        micro_grads = (grad_outproj, grad_up, grad_down, gain_two, bias_two)
+        totals = (
+            micro_grads
+            if totals is None
+            else tuple((former + latter for former, latter in zip(totals, micro_grads)))
+        )
+    key_value_all = lax.psum_scatter(
+        jnp.stack(key_value_parts), "seq", scatter_dimension=1, tiled=True
+    ).astype(jnp.float32)
+
+    input_grads = []
+    first_totals = None
+    for micro in range(batches):
+        inputs, first_low, queries = forward_parts[micro]
+        residual_grad, query_grad = later_parts[micro]
+        key_grad = key_value_all[micro, :, :model_width]
+        value_grad = key_value_all[micro, :, model_width:]
         qkv_low = jnp.concatenate(
             [
                 rotate(query_grad.reshape(row_count, model_width), cosine_part, -sine_part),
@@ -306,36 +337,41 @@
         _, first_pullback = jax.vjp(layer_norm, inputs, norm_gains[:, 0], norm_biases[:, 0])
         input_part, gain_one, bias_one = first_pullback(first_grad)
         input_grads.append((residual_grad + input_part).astype(jnp.bfloat16))
-        micro_grads = (
+        micro_first = (grad_qkv, gain_one, bias_one)
+        first_totals = (
+            micro_first
+            if first_totals is None
+            else tuple((former + latter for former, latter in zip(first_totals, micro_first)))
+        )
+    grad_outproj, grad_up, grad_down, gain_two, bias_two = totals
+    grad_qkv, gain_one, bias_one = first_totals
+    packed_grads = jnp.concatenate(
+        [
             grad_qkv,
             grad_outproj,
             grad_up,
-            grad_down,
+            grad_down.reshape(model_width, ff_width),
             jnp.stack([gain_one, gain_two], axis=1),
             jnp.stack([bias_one, bias_two], axis=1),
-        )
-        totals = (
-            micro_grads
-            if totals is None
-            else tuple((former + latter for former, latter in zip(totals, micro_grads)))
-        )
-    owner_shares = lax.psum_scatter(totals, ("seq", "fsdp"), scatter_dimension=0, tiled=True)
+            jnp.zeros((model_width, lane_pad), jnp.float32),
+        ],
+        axis=1,
+    )
+    device_count = model_width // shard_rows
+    scattered = lax.psum_scatter(
+        packed_grads.reshape(device_count, shard_rows, offsets[-1]),
+        ("seq", "fsdp"),
+        scatter_dimension=0,
+        tiled=False,
+    )
+    owned = pieces(scattered)
+    owned = owned[:6]
+    owned[3] = owned[3].reshape(-1, model_width)
     depth_total = lax.psum(depth_terms, ("seq", "fsdp"))
     next_input = jnp.stack(next_rows)[:, None]
     grad_input = jnp.stack(input_grads)[:, None]
     grad_history = jnp.stack(history_grads, axis=1)[:, :, None]
-    return (
-        next_input,
-        grad_input,
-        grad_history,
-        owner_shares[0],
-        owner_shares[1],
-        owner_shares[2],
-        owner_shares[3],
-        owner_shares[4],
-        owner_shares[5],
-        depth_total,
-    )
+    return (next_input, grad_input, grad_history, *owned, depth_total)
 
 
 def solution(mesh):

time: 1170 us -> 791 us (0.68)
  waiting for transfers between devices: 865 us -> 475 us
  local copies, waits for them, and re-layouts: 39.8 us -> 131 us
  blocking collectives: 121 us -> 39.5 us
    reduce_scatter x4 -> x0, waiting for transfers between devices: 449 us -> none  [local(): lax.psum_scatter(totals, ('seq', 'fsdp'), scatter_dimension=0, tiled=True)]
    unnamed x16 -> x6, waiting for transfers between devices: 104 us -> 295 us
    all_gather x8 -> x2, waiting for transfers between devices: 313 us -> 181 us  [the longest x1 104 us: local(): gathered = lax.all_gather(packed, ('seq', 'fsdp'), axis=0, tiled=True)]
    all_gather x2 -> x0, blocking collectives: 80.4 us -> none  [the longest x1 43.5 us: local(): lax.all_gather(ln_biases, ('seq', 'fsdp'), axis=0, tiled=True)]
    concatenate x0 -> x3, local copies, waits for them, and re-layouts: none -> 44.3 us  [the longest x2 42.5 us: local(): jnp.concatenate([grad_qkv, grad_outproj, grad_up, grad_down.reshape(model...]
    unnamed x1 -> x0, blocking collectives: 40.1 us -> none
    psum x0 -> x1, blocking collectives: none -> 39.5 us  [local(): depth_total = lax.psum(depth_terms, ('seq', 'fsdp'))]
    slice x2 -> x11, local copies, waits for them, and re-layouts: 2.09 us -> 26.6 us  [the longest x5 10.9 us: pieces(): packed_rows[:, offsets[i]:offsets[i + 1]]]
  transfers between devices with their start and end apart: 14 -> 4, of which waited for: 13 -> 4; matrix products, arithmetic and copies ran while one was open for 10% -> 9% of each run, Pallas kernels for 0% -> 0%
where the time goes in v1:
time: 791 us; the launch traced here: 785 us
  waiting for transfers between devices  475 us (60%)
  local copies, waits for them, and re-layouts  131 us (17%)
  matrix products  93.2 us (12%)
  blocking collectives  39.5 us (5%)
  other arithmetic  29.6 us (4%)
  between operations  15.6 us (2%)
    unnamed x6, waiting for transfers between devices  295 us
    all_gather x1, waiting for transfers between devices, local(): gathered = lax.all_gather(packed, ('seq', 'fsdp'), axis=0, tiled=True)  104 us
    all_gather x1, waiting for transfers between devices, local(): kv_all = lax.all_gather(jnp.stack(own_kv), 'seq', axis=1, tiled=True)  76.9 us
    concatenate x2, local copies, waits for them, and re-layouts, local(): jnp.concatenate([grad_qkv, grad_outproj, grad_up, grad_down.reshape(model...  42.5 us
    unnamed x230, local copies, waits for them, and re-layouts  40.2 us
    psum x1, blocking collectives, local(): depth_total = lax.psum(depth_terms, ('seq', 'fsdp'))  39.5 us
  transfers between devices with their start and end apart: 4, of which 4 were waited for; matrix products, arithmetic and copies ran while one was open for 9% of the time, Pallas kernels for 0%

profile of v1, /device:TPU:0, one launch (start us, length us, event | category | flops | bytes accessed | tf_op | source)
XLA Modules:
  0.0 784.9 jit_solution(11726267051769213971)
XLA Ops:
  14.0 103.8 %all-gather.3.cloned.1.call-done = bf16[768,9344]{1,0:T(8,128)(2,1)} async-done(((bf16[24,9344]{1,0:T(8,128)(2,1)}), bf16[768,9344]{1,0:T(8,128)(2,1)}) %all-gather.3.cloned.1.call-update) | async-done | bytes 14352400 | tf_op jit(solution)/shard_map/all_gather | solution.py:198
  119.6 2.7 fusion.14
  122.5 2.7 fusion.16
  134.6 5.1 slice.264
  139.6 8.5 %reshape.629 = bf16[3072,768]{1,0:T(8,128)(2,1)} reshape(bf16[768,3072]{1,0:T(8,128)(2,1)} %slice.264) | data formatting | bytes 9437184 | tf_op jit(solution)/shard_map/reshape | solution.py:200
  148.1 76.9 %all-gather.5.cloned.1.call-done = bf16[2,1024,1536]{2,1,0:T(8,128)(2,1)} async-done(((bf16[2,128,1536]{2,1,0:T(8,128)(2,1)}), bf16[2,1024,1536]{2,1,0:T(8,128)(2,1)}) %all-gather.5.cloned.1.call-update) | async-done | bytes 6291472 | tf_op jit(solution)/shard_map/all_gather | solution.py:222
  225.0 5.6 fusion.161
  232.3 3.2 copy.115
  235.5 2.6 copy.113
  238.1 2.6 copy.110
  240.7 2.7 select_reduce_fusion.2
  271.1 3.5 multiply_reduce_fusion.2
  278.3 2.6 convolution_convert_fusion.2
  282.7 4.7 convolution_convert_fusion
  288.6 4.0 multiply_convert_fusion
  296.1 2.7 multiply_convert_fusion.1
  300.4 7.1 maximum_maximum_fusion
  307.5 16.4 %copy.156 = bf16[2,1024,1536]{2,0,1:T(2,128)(2,1)} copy(bf16[2,1024,1536]{1,2,0:T(8,128)(2,1)} %maximum_maximum_fusion) | data formatting | bytes 12582912
  323.9 7.1 copy.162
  336.1 5.9 convolution_add_fusion.1
  342.0 11.5 %concatenate.117 = f32[32,24,3072]{2,1,0:T(8,128)} reshape(f32[3072,768]{1,0:T(8,128)} %convolution_add_fusion.1) | data formatting | bytes 18874368 | tf_op jit(solution)/shard_map/concatenate | solution.py:348
  355.0 4.1 fusion.32
  364.5 5.2 convolution_add_fusion.2
  369.7 77.7 %reduce-scatter.7.cloned.1.call-done = bf16[128,3072]{1,0:T(8,128)(2,1)} async-done(((bf16[1024,3072]{1,0:T(8,128)(2,1)}), bf16[128,3072]{1,0:T(8,128)(2,1)}) %reduce-scatter.7.cloned.1.call-update) | async-done | bytes 786448
  447.4 2.6 reshape.655
  452.7 4.2 fusion.80
  456.9 3.3 fusion.10
  460.3 3.6 fusion.65
  465.2 7.3 convolution_add_fusion
  472.5 30.9 %concatenate.118 = f32[32,24,9344]{2,1,0:T(8,128)} concatenate(f32[32,24,2304]{2,1,0:T(8,128)} %bitcast.284, f32[32,24,768]{2,1,0:T(8,128)} %bitcast.297, f32[32,24,3072]{2,1,0:T(8,128)} %bitcast.283, f32[32,24,3072]{2,1,0:T(8,128)} %concatenate.117, f32[32,24,1]{2,1,0:T(8,128)S(1)} %add.412, f32[32,24,1]{2,1,0:T(8,128)S(1)} %copy-done.20, f32[32,24,1]{2,1,0:T(8,128)S(1)} %add.414, ...), dimensions={2} | concatenate | bytes 57409536 | tf_op jit(solution)/shard_map/concatenate | solution.py:348
  507.9 39.5 %psum.7 = f32[5]{0:T(128)} all-reduce(f32[5]{0:T(128)S(1)} %maximum_add_fusion), channel_id=1, replica_groups=mesh['seq'=8,'fsdp'=4] {'seq','fsdp'}, use_global_device_ids=true, to_apply=%region_32.33 | all-reduce | flops 5 | bytes 40 | tf_op jit(solution)/shard_map/psum | solution.py:370
  553.5 216.7 %reduce-scatter.9.cloned.1.call-done = f32[1,24,9344]{2,1,0:T(8,128)} async-done(((f32[32,24,9344]{2,1,0:T(8,128)}), f32[1,24,9344]{2,1,0:T(8,128)}) %reduce-scatter.9.cloned.1.call-update) | async-done | bytes 897040
  (353 shorter events, 92.5 us)
Async XLA Ops:
  7.2 110.6 %all-gather.3.cloned.1.call-start = ((), (), s32[]{:S(2)}) async-start(), calls=%async_computation.2 | async-start | bytes 14800896 | tf_op jit(solution)/shard_map/all_gather | solution.py:198
  11.6 213.3 %all-gather.5.cloned.1.call-start = ((), (), s32[]{:S(2)}) async-start(), calls=%async_computation.3 | async-start | bytes 7077888 | tf_op jit(solution)/shard_map/all_gather | solution.py:222
  12.4 107.2 %copy-start.63 = (f32[128]{0:T(128)}, f32[128]{0:T(128)S(1)}, u32[]{:S(2)}) copy-start(f32[128]{0:T(128)S(1)} %get-tuple-element.376) | copy-start | bytes 1540
  12.4 110.0 %copy-start.61 = (f32[128]{0:T(128)}, f32[128]{0:T(128)S(1)}, u32[]{:S(2)}) copy-start(f32[128]{0:T(128)S(1)} %get-tuple-element.377) | copy-start | bytes 1540
  12.7 109.8 %copy-start.65 = (f32[128]{0:T(128)}, f32[128]{0:T(128)S(1)}, u32[]{:S(2)}) copy-start(f32[128]{0:T(128)S(1)} %fusion.125) | copy-start | bytes 1540
  13.2 109.1 %copy-start.77 = (f32[128]{0:T(128)}, f32[128]{0:T(128)S(1)}, u32[]{:S(2)}) copy-start(f32[128]{0:T(128)S(1)} %fusion.126) | copy-start | bytes 1540
  14.0 111.9 %copy-start.58 = (f32[128,32]{0,1:T(8,128)}, f32[128,32]{0,1:T(8,128)S(1)}, u32[]{:S(2)}) copy-start(f32[128,32]{0,1:T(8,128)S(1)} %get-tuple-element.355) | copy-start | bytes 49156
  126.2 114.5 %copy-start.38 = (bf16[128,12,32]{0,2,1:T(8,128)(2,1)}, bf16[128,12,32]{0,2,1:T(8,128)(2,1)S(1)}, u32[]{:S(2)}) copy-start(bf16[128,12,32]{0,2,1:T(8,128)(2,1)S(1)} %get-tuple-element.344) | copy-start | bytes 294916
  126.2 114.5 %copy-start.40 = (bf16[128,12,32]{0,2,1:T(8,128)(2,1)}, bf16[128,12,32]{0,2,1:T(8,128)(2,1)S(1)}, u32[]{:S(2)}) copy-start(bf16[128,12,32]{0,2,1:T(8,128)(2,1)S(1)} %get-tuple-element.345) | copy-start | bytes 294916
  126.2 124.5 %copy-start.34 = (bf16[128,12,32]{0,2,1:T(8,128)(2,1)}, bf16[128,12,32]{0,2,1:T(8,128)(2,1)S(1)}, u32[]{:S(2)}) copy-start(bf16[128,12,32]{0,2,1:T(8,128)(2,1)S(1)} %get-tuple-element.320) | copy-start | bytes 294916
  126.2 124.5 %copy-start.36 = (bf16[128,12,32]{0,2,1:T(8,128)(2,1)}, bf16[128,12,32]{0,2,1:T(8,128)(2,1)S(1)}, u32[]{:S(2)}) copy-start(bf16[128,12,32]{0,2,1:T(8,128)(2,1)S(1)} %get-tuple-element.321) | copy-start | bytes 294916
  127.7 319.7 %reduce-scatter.7.cloned.1.call-start = ((), (), s32[]{:S(2)}) async-start(), calls=%async_computation.4 | async-start | bytes 7077888
  130.7 139.9 %copy-start.69 = (pred[128]{0:T(512)(128)(4,1)}, pred[128]{0:T(512)(128)(4,1)S(1)}, u32[]{:S(2)}) copy-start(pred[128]{0:T(512)(128)(4,1)S(1)} %get-tuple-element.382) | copy-start | bytes 388
  130.7 139.9 %copy-start.71 = (pred[128]{0:T(512)(128)(4,1)}, pred[128]{0:T(512)(128)(4,1)S(1)}, u32[]{:S(2)}) copy-start(pred[128]{0:T(512)(128)(4,1)S(1)} %get-tuple-element.383) | copy-start | bytes 388
  232.3 18.4 %copy-start.3 = (bf16[1,1024,768]{1,2,0:T(8,128)(2,1)}, bf16[1,1024,768]{1,2,0:T(8,128)(2,1)S(1)}, u32[]{:S(2)}) copy-start(bf16[1,1024,768]{1,2,0:T(8,128)(2,1)S(1)} %copy.112) | copy-start | bytes 4718596
  246.1 11.4 %slice-start.6 = ((s8[14352384]{0:T(1024)(128)(4,1)}), s8[4194304]{0:T(1024)(128)(4,1)S(1)}, s32[]{:S(2)}) async-start(s8[14352384]{0:T(1024)(128)(4,1)} %bitcast.300), calls=%async_computation.12 | async-start | bytes 8388608
  246.1 11.4 %slice-start.7 = ((s8[14352384]{0:T(1024)(128)(4,1)}), s8[4194304]{0:T(1024)(128)(4,1)S(1)}, s32[]{:S(2)}) async-start(s8[14352384]{0:T(1024)(128)(4,1)} %bitcast.300), calls=%async_computation.13 | async-start | bytes 8388608
  250.5 19.7 %copy-start.79 = (f32[128]{0:T(128)}, f32[128]{0:T(128)S(1)}, u32[]{:S(2)}) copy-start(f32[128]{0:T(128)S(1)} %broadcast_multiply_fusion) | copy-start | bytes 1540
  250.7 19.5 %copy-start.87 = (f32[128]{0:T(128)}, f32[128]{0:T(128)S(1)}, u32[]{:S(2)}) copy-start(f32[128]{0:T(128)S(1)} %fusion.128) | copy-start | bytes 1540
  257.9 12.2 %copy-start.67 = (f32[128]{0:T(128)}, f32[128]{0:T(128)S(1)}, u32[]{:S(2)}) copy-start(f32[128]{0:T(128)S(1)} %broadcast_multiply_fusion.1) | copy-start | bytes 1540
  258.2 12.0 %copy-start.81 = (f32[128]{0:T(128)}, f32[128]{0:T(128)S(1)}, u32[]{:S(2)}) copy-start(f32[128]{0:T(128)S(1)} %fusion.127) | copy-start | bytes 1540
  275.3 13.2 %slice-start = ((s8[6291456]{0:T(1024)(128)(4,1)}), s8[2097152]{0:T(1024)(128)(4,1)S(1)}, s32[]{:S(2)}) async-start(s8[6291456]{0:T(1024)(128)(4,1)} %bitcast.285), calls=%async_computation.6 | async-start | bytes 4194304
  282.7 11.5 %slice-start.2 = ((s8[6291456]{0:T(1024)(128)(4,1)}), s8[4194304]{0:T(1024)(128)(4,1)S(1)}, s32[]{:S(2)}) async-start(s8[6291456]{0:T(1024)(128)(4,1)} %bitcast.287), calls=%async_computation.8 | async-start | bytes 8388608
  331.0 439.2 %reduce-scatter.9.cloned.1.call-start = ((), (), s32[]{:S(2)}) async-start(), calls=%async_computation.5 | async-start | bytes 29601792
  342.0 11.5 %copy-start.52 = (bf16[128,12,64]{0,2,1:T(8,128)(2,1)S(1)}, bf16[128,12,64]{0,2,1:T(8,128)(2,1)}, u32[]{:S(2)}) copy-start(bf16[128,12,64]{0,2,1:T(8,128)(2,1)} %copy-done.51) | copy-start | bytes 589828
  342.0 11.5 %copy-start.55 = (bf16[128,768]{1,0:T(8,128)(2,1)S(1)}, bf16[128,768]{1,0:T(8,128)(2,1)}, u32[]{:S(2)}) copy-start(bf16[128,768]{1,0:T(8,128)(2,1)} %copy-done.54) | copy-start | bytes 589828
  465.2 7.3 copy-start.19
  465.2 7.3 copy-start.20
  503.5 43.9 %copy-start.53 = (bf16[1,128,768]{2,1,0:T(8,128)(2,1)S(1)}, bf16[1,128,768]{2,1,0:T(8,128)(2,1)}, u32[]{:S(2)}) copy-start(bf16[1,128,768]{2,1,0:T(8,128)(2,1)} %get-tuple-element.334) | copy-start | bytes 589828
  504.8 44.2 %copy-start.21 = (f32[128,768]{1,0:T(8,128)S(1)}, f32[128,768]{1,0:T(8,128)}, u32[]{:S(2)}) copy-start(f32[128,768]{1,0:T(8,128)} %get-tuple-element.331) | copy-start | bytes 1179652
  504.8 44.2 %copy-start.22 = (f32[128,768]{1,0:T(8,128)S(1)}, f32[128,768]{1,0:T(8,128)}, u32[]{:S(2)}) copy-start(f32[128,768]{1,0:T(8,128)} %get-tuple-element.333) | copy-start | bytes 1179652
  504.8 44.2 %copy-start.95 = (f32[5]{0:T(128)S(1)}, f32[5]{0:T(128)}, u32[]{:S(2)}) copy-start(f32[5]{0:T(128)} %param.21) | copy-start | bytes 64
  (83 other events, 222.0 us)
Sparse Core Ops, SparseCore 0:
  11.8 105.9 all-gather.2
  127.8 97.1 all-gather.4
  331.2 116.1 reduce-scatter.6
  503.6 266.6 reduce-scatter.8

commit v2 on v1

--- a/solution.py
+++ b/solution.py
@@ -219,7 +219,7 @@
         values_own = projected[:, 2 * model_width :].astype(jnp.bfloat16)
         forward_parts.append((inputs, first_low, queries))
         own_kv.append(jnp.concatenate([keys_own, values_own], axis=1))
-    kv_all = lax.all_gather(jnp.stack(own_kv), "seq", axis=1, tiled=True)
+    kv_all = lax.all_gather(jnp.stack(own_kv, axis=1), "seq", axis=0, tiled=True)
 
     key_value_parts = []
     later_parts = []
@@ -228,8 +228,8 @@
     history_grads = []
     for micro in range(batches):
         inputs, first_low, queries = forward_parts[micro]
-        keys3 = kv_all[micro, :, :model_width].reshape(slot_len, HEADS, HEAD)
-        values3 = kv_all[micro, :, model_width:].reshape(slot_len, HEADS, HEAD)
+        keys3 = kv_all[:, micro, :model_width].reshape(slot_len, HEADS, HEAD)
+        values3 = kv_all[:, micro, model_width:].reshape(slot_len, HEADS, HEAD)
         length = lengths[micro, 0]
         usable = (positions < length)[:, None]
         earlier = history[:, micro, 0].astype(jnp.float32)
@@ -314,7 +314,7 @@
             else tuple((former + latter for former, latter in zip(totals, micro_grads)))
         )
     key_value_all = lax.psum_scatter(
-        jnp.stack(key_value_parts), "seq", scatter_dimension=1, tiled=True
+        jnp.stack(key_value_parts, axis=1), "seq", scatter_dimension=0, tiled=True
     ).astype(jnp.float32)
 
     input_grads = []
@@ -322,8 +322,8 @@
     for micro in range(batches):
         inputs, first_low, queries = forward_parts[micro]
         residual_grad, query_grad = later_parts[micro]
-        key_grad = key_value_all[micro, :, :model_width]
-        value_grad = key_value_all[micro, :, model_width:]
+        key_grad = key_value_all[:, micro, :model_width]
+        value_grad = key_value_all[:, micro, model_width:]
         qkv_low = jnp.concatenate(
             [
                 rotate(query_grad.reshape(row_count, model_width), cosine_part, -sine_part),
@@ -359,12 +359,12 @@
     )
     device_count = model_width // shard_rows
     scattered = lax.psum_scatter(
-        packed_grads.reshape(device_count, shard_rows, offsets[-1]),
+        packed_grads.astype(jnp.bfloat16).reshape(device_count, shard_rows, offsets[-1]),
         ("seq", "fsdp"),
         scatter_dimension=0,
         tiled=False,
     )
-    owned = pieces(scattered)
+    owned = pieces(scattered.astype(jnp.float32))
     owned = owned[:6]
     owned[3] = owned[3].reshape(-1, model_width)
     depth_total = lax.psum(depth_terms, ("seq", "fsdp"))

time: 791 us -> 665 us (0.84)
  waiting for transfers between devices: 475 us -> 373 us
  local copies, waits for them, and re-layouts: 131 us -> 98.3 us
    unnamed x6, waiting for transfers between devices: 295 us -> 194 us
    unnamed x230 -> x250, local copies, waits for them, and re-layouts: 40.2 us -> 27.5 us
    concatenate x2, local copies, waits for them, and re-layouts: 42.5 us -> 31.3 us  [local(): jnp.concatenate([grad_qkv, grad_outproj, grad_up, grad_down.reshape(model...]
where the time goes in v2:
time: 665 us; the launch traced here: 659 us
  waiting for transfers between devices  373 us (56%)
  matrix products  100 us (15%)
  local copies, waits for them, and re-layouts  98.3 us (15%)
  blocking collectives  39.5 us (6%)
  other arithmetic  31.6 us (5%)
  between operations  15.8 us (2%)
    unnamed x6, waiting for transfers between devices  194 us
    all_gather x1, waiting for transfers between devices, local(): gathered = lax.all_gather(packed, ('seq', 'fsdp'), axis=0, tiled=True)  104 us
    all_gather x1, waiting for transfers between devices, local(): lax.all_gather(jnp.stack(own_kv, axis=1), 'seq', axis=0, tiled=True)  75.8 us
    psum x1, blocking collectives, local(): depth_total = lax.psum(depth_terms, ('seq', 'fsdp'))  39.5 us
    concatenate x2, local copies, waits for them, and re-layouts, local(): jnp.concatenate([grad_qkv, grad_outproj, grad_up, grad_down.reshape(model...  31.3 us
    unnamed x250, local copies, waits for them, and re-layouts  27.5 us
  transfers between devices with their start and end apart: 4, of which 4 were waited for; matrix products, arithmetic and copies ran while one was open for 9% of the time, Pallas kernels for 0%

profile of v2, /device:TPU:0, one launch (start us, length us, event | category | flops | bytes accessed | tf_op | source)
XLA Modules:
  0.0 659.3 jit_solution(8150422956099147371)
XLA Ops:
  14.0 103.8 %all-gather.3.cloned.1.call-done = bf16[768,9344]{1,0:T(8,128)(2,1)} async-done(((bf16[24,9344]{1,0:T(8,128)(2,1)}), bf16[768,9344]{1,0:T(8,128)(2,1)}) %all-gather.3.cloned.1.call-update) | async-done | bytes 14352400 | tf_op jit(solution)/shard_map/all_gather | solution.py:198
  119.6 2.7 fusion.16
  122.4 2.7 fusion.14
  137.6 4.8 slice.264
  142.4 8.5 %reshape.631 = bf16[3072,768]{1,0:T(8,128)(2,1)} reshape(bf16[768,3072]{1,0:T(8,128)(2,1)} %slice.264) | data formatting | bytes 9437184 | tf_op jit(solution)/shard_map/reshape | solution.py:200
  150.9 75.8 %all-gather.5.cloned.1.call-done = bf16[1024,2,1536]{2,0,1:T(8,128)(2,1)} async-done(((bf16[128,2,1536]{2,0,1:T(8,128)(2,1)}), bf16[1024,2,1536]{2,0,1:T(8,128)(2,1)}) %all-gather.5.cloned.1.call-update) | async-done | bytes 6291472 | tf_op jit(solution)/shard_map/all_gather | solution.py:222
  226.6 5.7 fusion.161
  239.7 5.5 bitcast_convert_fusion.2
  255.3 5.6 bitcast_convert_fusion.1
  263.0 3.3 fusion.6
  268.4 2.8 fusion.31
  272.1 2.5 fusion.24
  279.7 3.6 multiply_reduce_fusion.2
  284.6 5.9 convolution_convert_fusion.1
  290.6 4.5 multiply_convert_fusion.1
  297.6 2.5 convolution_convert_fusion.2
  301.9 4.6 convolution_convert_fusion
  306.6 2.5 multiply_convert_fusion
  312.2 7.2 %maximum_maximum_fusion = bf16[1024,2,1536]{0,2,1:T(8,128)(2,1)} fusion(bf16[1024,1,768]{0,2,1:T(8,128)(2,1)S(1)} %bitcast.302, bf16[1024,1,768]{0,2,1:T(8,128)(2,1)S(1)} %bitcast.295, bf16[1024,1,768]{0,2,1:T(8,128)(2,1)S(1)} %bitcast.301, bf16[1024,1,768]{0,2,1:T(8,128)(2,1)S(1)} %bitcast.294), kind=kLoop, calls=%fused_computation.3 | loop fusion | flops 25165824 | bytes 12582912 | tf_op jit(solution)/shard_map/stack | solution.py:317
  319.4 8.6 %copy.160 = bf16[1024,3072]{1,0:T(8,128)(2,1)} copy(bf16[1024,3072]{0,1:T(8,128)(2,1)} %bitcast.285) | data formatting | bytes 12582912
  329.5 2.3 fusion.83
  331.8 4.6 add_convert_fusion
  336.5 8.9 %concatenate.118 = bf16[32,24,3072]{2,1,0:T(8,128)(2,1)} reshape(bf16[3072,768]{1,0:T(8,128)(2,1)} %add_convert_fusion) | data formatting | bytes 9437184 | tf_op jit(solution)/shard_map/concatenate | solution.py:348
  355.5 3.7 add_convert_fusion.1
  359.3 85.2 %reduce-scatter.7.cloned.1.call-done = bf16[128,3072]{1,0:T(8,128)(2,1)} async-done(((bf16[1024,3072]{1,0:T(8,128)(2,1)}), bf16[128,3072]{1,0:T(8,128)(2,1)}) %reduce-scatter.7.cloned.1.call-update) | async-done | bytes 786448
  447.8 4.1 fusion.80
  451.9 3.3 fusion.10
  455.2 3.5 fusion.65
  460.1 6.0 add_convert_fusion.2
  466.1 22.4 %concatenate.119 = bf16[32,24,9344]{2,1,0:T(8,128)(2,1)} concatenate(bf16[32,24,2304]{2,1,0:T(8,128)(2,1)} %bitcast.289, bf16[32,24,768]{2,1,0:T(8,128)(2,1)S(1)} %bitcast.298, bf16[32,24,3072]{2,1,0:T(8,128)(2,1)} %bitcast.286, bf16[32,24,3072]{2,1,0:T(8,128)(2,1)} %concatenate.118, bf16[32,24,1]{2,1,0:T(8,128)(2,1)S(1)} %add.412, bf16[32,24,1]{2,1,0:T(8,128)(2,1)S(1)} %add.413, ...), dimensions={2} | concatenate | bytes 28704768 | tf_op jit(solution)/shard_map/concatenate | solution.py:348
  492.8 39.5 %psum.7 = f32[5]{0:T(128)} all-reduce(f32[5]{0:T(128)S(1)} %maximum_add_fusion), channel_id=1, replica_groups=mesh['seq'=8,'fsdp'=4] {'seq','fsdp'}, use_global_device_ids=true, to_apply=%region_32.33 | all-reduce | flops 5 | bytes 40 | tf_op jit(solution)/shard_map/psum | solution.py:370
  538.9 108.4 %reduce-scatter.9.cloned.1.call-done = bf16[1,24,9344]{2,1,0:T(8,128)(2,1)} async-done(((bf16[32,24,9344]{2,1,0:T(8,128)(2,1)}), bf16[1,24,9344]{2,1,0:T(8,128)(2,1)}) %reduce-scatter.9.cloned.1.call-update) | async-done | bytes 448528
  (373 shorter events, 88.5 us)
Async XLA Ops:
  7.2 110.6 %all-gather.3.cloned.1.call-start = ((), (), s32[]{:S(2)}) async-start(), calls=%async_computation.2 | async-start | bytes 14800896 | tf_op jit(solution)/shard_map/all_gather | solution.py:198
  11.6 215.0 %all-gather.5.cloned.1.call-start = ((), (), s32[]{:S(2)}) async-start(), calls=%async_computation.3 | async-start | bytes 7077888 | tf_op jit(solution)/shard_map/all_gather | solution.py:222
  12.4 107.2 %copy-start.71 = (f32[128]{0:T(128)}, f32[128]{0:T(128)S(1)}, u32[]{:S(2)}) copy-start(f32[128]{0:T(128)S(1)} %get-tuple-element.377) | copy-start | bytes 1540
  12.4 110.0 %copy-start.73 = (f32[128]{0:T(128)}, f32[128]{0:T(128)S(1)}, u32[]{:S(2)}) copy-start(f32[128]{0:T(128)S(1)} %get-tuple-element.376) | copy-start | bytes 1540
  12.7 109.7 %copy-start.75 = (f32[128]{0:T(128)}, f32[128]{0:T(128)S(1)}, u32[]{:S(2)}) copy-start(f32[128]{0:T(128)S(1)} %fusion.125) | copy-start | bytes 1540
  13.2 109.2 %copy-start.90 = (f32[128]{0:T(128)}, f32[128]{0:T(128)S(1)}, u32[]{:S(2)}) copy-start(f32[128]{0:T(128)S(1)} %fusion.126) | copy-start | bytes 1540
  14.0 111.9 %copy-start.68 = (f32[128,32]{0,1:T(8,128)}, f32[128,32]{0,1:T(8,128)S(1)}, u32[]{:S(2)}) copy-start(f32[128,32]{0,1:T(8,128)S(1)} %get-tuple-element.355) | copy-start | bytes 49156
  126.2 107.8 %copy-start.43 = (bf16[128,12,32]{0,2,1:T(8,128)(2,1)}, bf16[128,12,32]{0,2,1:T(8,128)(2,1)S(1)}, u32[]{:S(2)}) copy-start(bf16[128,12,32]{0,2,1:T(8,128)(2,1)S(1)} %get-tuple-element.320) | copy-start | bytes 294916
  126.2 107.8 %copy-start.45 = (bf16[128,12,32]{0,2,1:T(8,128)(2,1)}, bf16[128,12,32]{0,2,1:T(8,128)(2,1)S(1)}, u32[]{:S(2)}) copy-start(bf16[128,12,32]{0,2,1:T(8,128)(2,1)S(1)} %get-tuple-element.321) | copy-start | bytes 294916
  126.2 123.3 %copy-start.39 = (bf16[128,12,32]{0,2,1:T(8,128)(2,1)}, bf16[128,12,32]{0,2,1:T(8,128)(2,1)S(1)}, u32[]{:S(2)}) copy-start(bf16[128,12,32]{0,2,1:T(8,128)(2,1)S(1)} %get-tuple-element.344) | copy-start | bytes 294916
  126.2 123.3 %copy-start.41 = (bf16[128,12,32]{0,2,1:T(8,128)(2,1)}, bf16[128,12,32]{0,2,1:T(8,128)(2,1)S(1)}, u32[]{:S(2)}) copy-start(bf16[128,12,32]{0,2,1:T(8,128)(2,1)S(1)} %get-tuple-element.345) | copy-start | bytes 294916
  127.3 7.2 %copy-start.13 = (bf16[4,2,1,128,768]{4,3,2,1,0:T(8,128)(2,1)S(1)}, bf16[4,2,1,128,768]{4,3,2,1,0:T(8,128)(2,1)}, u32[]{:S(2)}) copy-start(bf16[4,2,1,128,768]{4,3,2,1,0:T(8,128)(2,1)} %param.12) | copy-start | bytes 4718596
  129.4 315.1 %reduce-scatter.7.cloned.1.call-start = ((), (), s32[]{:S(2)}) async-start(), calls=%async_computation.4 | async-start | bytes 7077888
  253.5 12.8 %slice-start.2 = ((s8[4718592]{0:T(1024)(128)(4,1)}), s8[524288]{0:T(1024)(128)(4,1)S(1)}, s32[]{:S(2)}) async-start(s8[4718592]{0:T(1024)(128)(4,1)} %bitcast.287), calls=%async_computation.8 | async-start | bytes 1048576
  255.3 11.0 %slice-start.3 = ((s8[4718592]{0:T(1024)(128)(4,1)}), s8[4194304]{0:T(1024)(128)(4,1)S(1)}, s32[]{:S(2)}) async-start(s8[4718592]{0:T(1024)(128)(4,1)} %bitcast.287), calls=%async_computation.9 | async-start | bytes 8388608
  262.7 15.9 %copy-start.88 = (f32[128]{0:T(128)}, f32[128]{0:T(128)S(1)}, u32[]{:S(2)}) copy-start(f32[128]{0:T(128)S(1)} %broadcast_multiply_fusion) | copy-start | bytes 1540
  262.9 15.7 %copy-start.98 = (f32[128]{0:T(128)}, f32[128]{0:T(128)S(1)}, u32[]{:S(2)}) copy-start(f32[128]{0:T(128)S(1)} %fusion.128) | copy-start | bytes 1540
  262.9 8.2 %slice-start.4 = ((s8[14352384]{0:T(1024)(128)(4,1)}), s8[4194304]{0:T(1024)(128)(4,1)S(1)}, s32[]{:S(2)}) async-start(s8[14352384]{0:T(1024)(128)(4,1)} %bitcast.299), calls=%async_computation.10 | async-start | bytes 8388608
  263.0 8.2 %slice-start.5 = ((s8[14352384]{0:T(1024)(128)(4,1)}), s8[4194304]{0:T(1024)(128)(4,1)S(1)}, s32[]{:S(2)}) async-start(s8[14352384]{0:T(1024)(128)(4,1)} %bitcast.299), calls=%async_computation.11 | async-start | bytes 8388608
  295.2 11.4 %slice-start = ((s8[6291456]{0:T(1024)(128)(4,1)}), s8[2097152]{0:T(1024)(128)(4,1)S(1)}, s32[]{:S(2)}) async-start(s8[6291456]{0:T(1024)(128)(4,1)} %bitcast.283), calls=%async_computation.6 | async-start | bytes 4194304
  328.1 319.2 %reduce-scatter.9.cloned.1.call-start = ((), (), s32[]{:S(2)}) async-start(), calls=%async_computation.5 | async-start | bytes 14800896
  336.5 8.9 %copy-start.96 = (f32[768]{0:T(1024)S(1)}, f32[768]{0:T(1024)}, u32[]{:S(2)}) copy-start(f32[768]{0:T(1024)} %get-tuple-element.248) | copy-start | bytes 9220
  336.5 8.9 %copy-start.97 = (f32[768]{0:T(1024)S(1)}, f32[768]{0:T(1024)}, u32[]{:S(2)}) copy-start(f32[768]{0:T(1024)} %get-tuple-element.352) | copy-start | bytes 9220
  336.5 9.3 %copy-start.94 = (f32[768]{0:T(1024)S(1)}, f32[768]{0:T(1024)}, u32[]{:S(2)}) copy-start(f32[768]{0:T(1024)} %get-tuple-element.268) | copy-start | bytes 9220
  336.5 9.3 %copy-start.95 = (f32[768]{0:T(1024)S(1)}, f32[768]{0:T(1024)}, u32[]{:S(2)}) copy-start(f32[768]{0:T(1024)} %get-tuple-element.350) | copy-start | bytes 9220
  336.5 10.4 %copy-start.54 = (bf16[128,12,64]{0,2,1:T(8,128)(2,1)S(1)}, bf16[128,12,64]{0,2,1:T(8,128)(2,1)}, u32[]{:S(2)}) copy-start(bf16[128,12,64]{0,2,1:T(8,128)(2,1)} %copy-done.53) | copy-start | bytes 589828
  336.5 10.4 %copy-start.63 = (bf16[128,768]{1,0:T(8,128)(2,1)S(1)}, bf16[128,768]{1,0:T(8,128)(2,1)}, u32[]{:S(2)}) copy-start(bf16[128,768]{1,0:T(8,128)(2,1)} %copy-done.62) | copy-start | bytes 589828
  458.8 7.3 %copy-start.35 = (f32[128,768]{1,0:T(8,128)}, f32[128,768]{1,0:T(8,128)S(1)}, u32[]{:S(2)}) copy-start(f32[128,768]{1,0:T(8,128)S(1)} %get-tuple-element.375) | copy-start | bytes 1179652
  488.6 43.7 %copy-start.57 = (bf16[1,128,768]{2,1,0:T(8,128)(2,1)S(1)}, bf16[1,128,768]{2,1,0:T(8,128)(2,1)}, u32[]{:S(2)}) copy-start(bf16[1,128,768]{2,1,0:T(8,128)(2,1)} %get-tuple-element.334) | copy-start | bytes 589828
  490.0 44.0 %copy-start.25 = (f32[128,768]{1,0:T(8,128)S(1)}, f32[128,768]{1,0:T(8,128)}, u32[]{:S(2)}) copy-start(f32[128,768]{1,0:T(8,128)} %get-tuple-element.331) | copy-start | bytes 1179652
  490.0 44.0 %copy-start.26 = (f32[128,768]{1,0:T(8,128)S(1)}, f32[128,768]{1,0:T(8,128)}, u32[]{:S(2)}) copy-start(f32[128,768]{1,0:T(8,128)} %get-tuple-element.333) | copy-start | bytes 1179652
  490.0 44.0 %copy-start.106 = (f32[5]{0:T(128)S(1)}, f32[5]{0:T(128)}, u32[]{:S(2)}) copy-start(f32[5]{0:T(128)} %param.21) | copy-start | bytes 64
  (94 other events, 252.4 us)
Sparse Core Ops, SparseCore 0:
  11.8 105.9 all-gather.2
  129.5 97.1 all-gather.4
  328.2 116.1 reduce-scatter.6
  488.7 158.5 reduce-scatter.8

commit v3 on v1

v3 whole, which is shorter than its diff:
```python
from functools import partial
import math

import jax
import jax.numpy as jnp
from jax import lax
from jax.sharding import PartitionSpec as P

HEADS = 12
HEAD = 64


epsilon = 1e-05
masked_value = -1e30


def layer_norm(values, gain_vector, bias_vector):
    center = values - jnp.mean(values, axis=-1, keepdims=True)
    spread = jnp.mean(center * center, axis=-1, keepdims=True)
    return center * lax.rsqrt(spread + epsilon) * gain_vector + bias_vector


def rotary_tables(positions):
    half_width = HEAD // 2
    frequencies = 10000.0 ** (-jnp.arange(half_width, dtype=jnp.float32) / half_width)
    angles = positions.astype(jnp.float32)[:, None] * frequencies[None, :]
    return (jnp.cos(angles)[:, None, :], jnp.sin(angles)[:, None, :])


def rotate(values, cosine_part, sine_part):
    row_count = values.shape[0]
    shaped = values.reshape(row_count, HEADS, HEAD)
    half_width = HEAD // 2
    first_half = shaped[..., :half_width]
    second_half = shaped[..., half_width:]
    turned = jnp.concatenate(
        [
            first_half * cosine_part - second_half * sine_part,
            second_half * cosine_part + first_half * sine_part,
        ],
        axis=-1,
    )
    return turned.reshape(row_count, HEADS * HEAD)


def block_scores(queries3, keys3, query_pos, key_pos, length):
    scores = jnp.einsum(
        "rhd,khd->hrk", queries3, keys3, preferred_element_type=jnp.float32
    ) * HEAD ** (-0.5)
    allowed = (key_pos[None, :] <= query_pos[:, None]) & (key_pos[None, :] < length)
    return (scores, allowed[None])


def row_totals(queries3, keys3, query_pos, length, key_block):
    row_count = queries3.shape[0]

    def row_advance(state, block_index):
        running_top, running_sum = state
        first_key = block_index * key_block
        keys_part = lax.dynamic_slice_in_dim(keys3, first_key, key_block, 0)
        key_pos = first_key + jnp.arange(key_block, dtype=jnp.int32)
        scores, allowed = block_scores(queries3, keys_part, query_pos, key_pos, length)
        masked = jnp.where(allowed, scores, masked_value)
        new_top = jnp.maximum(running_top, jnp.max(masked, axis=-1))
        kept_terms = jnp.where(allowed, jnp.exp(masked - new_top[..., None]), 0.0)
        running_sum = running_sum * jnp.exp(running_top - new_top) + jnp.sum(kept_terms, axis=-1)
        return ((new_top, running_sum), None)

    initial = (
        jnp.full((HEADS, row_count), masked_value, jnp.float32),
        jnp.zeros((HEADS, row_count), jnp.float32),
    )
    (row_tops, row_sums), _ = lax.scan(
        row_advance, initial, jnp.arange(keys3.shape[0] // key_block, dtype=jnp.int32)
    )
    return row_tops + jnp.log(row_sums)


def attend(queries3, keys3, values3, query_pos, length, key_block, log_total):

    def attend_advance(running, block_index):
        first_key = block_index * key_block
        keys_part = lax.dynamic_slice_in_dim(keys3, first_key, key_block, 0)
        values_part = lax.dynamic_slice_in_dim(values3, first_key, key_block, 0)
        key_pos = first_key + jnp.arange(key_block, dtype=jnp.int32)
        scores, allowed = block_scores(queries3, keys_part, query_pos, key_pos, length)
        probabilities = jnp.where(allowed, jnp.exp(scores - log_total[..., None]), 0.0).astype(
            jnp.bfloat16
        )
        return (
            running
            + jnp.einsum(
                "hrk,khd->rhd", probabilities, values_part, preferred_element_type=jnp.float32
            ),
            None,
        )

    initial = jnp.zeros(queries3.shape, jnp.float32)
    result, _ = lax.scan(
        attend_advance, initial, jnp.arange(keys3.shape[0] // key_block, dtype=jnp.int32)
    )
    return result


def query_grads(
    queries3, grads3, keys3, values3, query_pos, length, key_block, log_total, row_delta
):

    def query_advance(running, block_index):
        first_key = block_index * key_block
        keys_part = lax.dynamic_slice_in_dim(keys3, first_key, key_block, 0)
        values_part = lax.dynamic_slice_in_dim(values3, first_key, key_block, 0)
        key_pos = first_key + jnp.arange(key_block, dtype=jnp.int32)
        scores, allowed = block_scores(queries3, keys_part, query_pos, key_pos, length)
        probabilities = jnp.where(allowed, jnp.exp(scores - log_total[..., None]), 0.0)
        prob_grad = jnp.einsum(
            "rhd,khd->hrk", grads3, values_part, preferred_element_type=jnp.float32
        )
        score_low = (probabilities * (prob_grad - row_delta[..., None])).astype(jnp.bfloat16)
        return (
            running
            + jnp.einsum("hrk,khd->rhd", score_low, keys_part, preferred_element_type=jnp.float32),
            None,
        )

    initial = jnp.zeros(queries3.shape, jnp.float32)
    result, _ = lax.scan(
        query_advance, initial, jnp.arange(keys3.shape[0] // key_block, dtype=jnp.int32)
    )
    return result * HEAD ** (-0.5)


def key_side(queries3, grads3, log_part, delta_part, query_pos, keys3, values3, key_pos, length):
    key_count = keys3.shape[0]
    scores, allowed = block_scores(queries3, keys3, query_pos, key_pos, length)
    probabilities = jnp.where(allowed, jnp.exp(scores - log_part[..., None]), 0.0)
    prob_grad = jnp.einsum("rhd,khd->hrk", grads3, values3, preferred_element_type=jnp.float32)
    score_low = (probabilities * (prob_grad - delta_part[..., None])).astype(jnp.bfloat16)
    value_grad = jnp.einsum(
        "hrk,rhd->khd",
        probabilities.astype(jnp.bfloat16),
        grads3,
        preferred_element_type=jnp.float32,
    )
    key_grad = jnp.einsum(
        "hrk,rhd->khd", score_low, queries3, preferred_element_type=jnp.float32
    ) * HEAD ** (-0.5)
    return jnp.concatenate(
        [key_grad.reshape(key_count, HEADS * HEAD), value_grad.reshape(key_count, HEADS * HEAD)],
        axis=1,
    )


def slot_attention(queries3, keys3, values3, query_pos, length):
    key_pos = jnp.arange(keys3.shape[0], dtype=jnp.int32)
    scores, allowed = block_scores(queries3, keys3, query_pos, key_pos, length)
    masked = jnp.where(allowed, scores, masked_value)
    top = jnp.max(masked, axis=-1)
    kept_terms = jnp.where(allowed, jnp.exp(masked - top[..., None]), 0.0)
    log_total = top + jnp.log(jnp.sum(kept_terms, axis=-1))
    probabilities = jnp.where(allowed, jnp.exp(scores - log_total[..., None]), 0.0)
    probabilities_low = probabilities.astype(jnp.bfloat16)
    attended = jnp.einsum(
        "hrk,khd->rhd", probabilities_low, values3, preferred_element_type=jnp.float32
    )
    return attended, probabilities, probabilities_low


def slot_attention_grads(queries3, keys3, values3, grads3, attended, probabilities, probabilities_low):
    prob_grad = jnp.einsum("rhd,khd->hrk", grads3, values3, preferred_element_type=jnp.float32)
    row_delta = jnp.einsum("rhd,rhd->hr", grads3.astype(jnp.float32), attended)
    score_low = (probabilities * (prob_grad - row_delta[..., None])).astype(jnp.bfloat16)
    query_grad = jnp.einsum(
        "hrk,khd->rhd", score_low, keys3, preferred_element_type=jnp.float32
    ) * HEAD ** (-0.5)
    key_grad = jnp.einsum(
        "hrk,rhd->khd", score_low, queries3, preferred_element_type=jnp.float32
    ) * HEAD ** (-0.5)
    value_grad = jnp.einsum(
        "hrk,rhd->khd", probabilities_low, grads3, preferred_element_type=jnp.float32
    )
    return query_grad, key_grad, value_grad


def local(
    layer_input,
    history,
    cotangent,
    lengths,
    w_qkv,
    w_out,
    w_up,
    w_down,
    ln_gains,
    ln_biases,
    depth_weights,
):
    batches = layer_input.shape[0]
    row_count = layer_input.shape[2]
    model_width = layer_input.shape[3]
    ff_width = w_up.shape[1]
    shard_rows = w_qkv.shape[0]
    all_rows = batches * row_count
    slot_len = row_count * lax.axis_size("seq")
    positions = lax.axis_index("seq") * row_count + jnp.arange(row_count, dtype=jnp.int32)
    cosine_part, sine_part = rotary_tables(jnp.tile(positions, batches))
    gelu_tanh = partial(jax.nn.gelu, approximate=True)
    lane_pad = 128 - 4
    widths = (3 * model_width, model_width, ff_width, ff_width, 2, 2, lane_pad)
    offsets = [0]
    for width in widths:
        offsets.append(offsets[-1] + width)

    def pieces(packed_rows):
        return [packed_rows[:, offsets[i] : offsets[i + 1]] for i in range(len(widths))]

    packed = jnp.concatenate(
        [
            w_qkv,
            w_out,
            w_up,
            w_down.reshape(shard_rows, ff_width),
            ln_gains,
            ln_biases,
            jnp.zeros((shard_rows, lane_pad), w_qkv.dtype),
        ],
        axis=1,
    )
    gathered = lax.all_gather(packed, ("seq", "fsdp"), axis=0, tiled=True)
    full_qkv, full_out, full_up, down_rows, gain_rows, bias_rows, _ = pieces(gathered)
    full_down = down_rows.reshape(ff_width, model_width)
    norm_gains = gain_rows.astype(jnp.float32)
    norm_biases = bias_rows.astype(jnp.float32)

    slot_lengths = lengths[:, 0]
    inputs = layer_input[:, 0].reshape(all_rows, model_width).astype(jnp.float32)
    first_low = layer_norm(inputs, norm_gains[:, 0], norm_biases[:, 0]).astype(jnp.bfloat16)
    projected = jnp.dot(first_low, full_qkv, preferred_element_type=jnp.float32)
    queries = rotate(projected[:, :model_width], cosine_part, sine_part).astype(jnp.bfloat16)
    keys_own = rotate(
        projected[:, model_width : 2 * model_width], cosine_part, sine_part
    ).astype(jnp.bfloat16)
    values_own = projected[:, 2 * model_width :].astype(jnp.bfloat16)
    own_kv = jnp.concatenate([keys_own, values_own], axis=1).reshape(
        batches, row_count, 2 * model_width
    )
    kv_all = lax.all_gather(jnp.swapaxes(own_kv, 0, 1), "seq", axis=0, tiled=True)
    keys4 = jnp.swapaxes(kv_all[:, :, :model_width], 0, 1).reshape(batches, slot_len, HEADS, HEAD)
    values4 = jnp.swapaxes(kv_all[:, :, model_width:], 0, 1).reshape(
        batches, slot_len, HEADS, HEAD
    )
    queries4 = queries.reshape(batches, row_count, HEADS, HEAD)
    attended4, probabilities, probabilities_low = jax.vmap(
        slot_attention, in_axes=(0, 0, 0, None, 0)
    )(queries4, keys4, values4, positions, slot_lengths)
    attended_low = attended4.reshape(all_rows, model_width).astype(jnp.bfloat16)
    residual = inputs + jnp.dot(attended_low, full_out, preferred_element_type=jnp.float32)
    second_low = layer_norm(residual, norm_gains[:, 1], norm_biases[:, 1]).astype(jnp.bfloat16)
    hidden = jnp.dot(second_low, full_up, preferred_element_type=jnp.float32)
    hidden_low = gelu_tanh(hidden).astype(jnp.bfloat16)
    block_out = residual + jnp.dot(hidden_low, full_down, preferred_element_type=jnp.float32)
    earlier = history[:, :, 0].reshape(4, all_rows, model_width).astype(jnp.float32)
    usable = (positions[None, :] < slot_lengths[:, None]).reshape(all_rows, 1)
    grad_next = jnp.where(
        usable, cotangent[:, 0].reshape(all_rows, model_width).astype(jnp.float32), 0.0
    )
    combined = depth_weights[4] * block_out + jnp.einsum("j,jrd->rd", depth_weights[:4], earlier)
    next_input = combined.astype(jnp.bfloat16).reshape(batches, 1, row_count, model_width)
    grad_history = (depth_weights[:4, None, None] * grad_next[None]).astype(jnp.bfloat16)
    grad_history = grad_history.reshape(4, batches, 1, row_count, model_width)
    depth_terms = jnp.concatenate(
        [jnp.einsum("jrd,rd->j", earlier, grad_next), jnp.sum(block_out * grad_next)[None]]
    )
    out_grad = depth_weights[4] * grad_next
    out_low = out_grad.astype(jnp.bfloat16)
    hidden_grad = jnp.einsum("rd,fd->rf", out_low, full_down, preferred_element_type=jnp.float32)
    _, gelu_pullback = jax.vjp(gelu_tanh, hidden)
    up_low = gelu_pullback(hidden_grad)[0].astype(jnp.bfloat16)
    second_grad = jnp.einsum("rf,df->rd", up_low, full_up, preferred_element_type=jnp.float32)
    _, second_pullback = jax.vjp(layer_norm, residual, norm_gains[:, 1], norm_biases[:, 1])
    residual_part, gain_two, bias_two = second_pullback(second_grad)
    residual_grad = out_grad + residual_part
    branch_low = residual_grad.astype(jnp.bfloat16)
    attended_grad = jnp.einsum(
        "rd,cd->rc", branch_low, full_out, preferred_element_type=jnp.float32
    ).astype(jnp.bfloat16)
    query_grad4, key_grad4, value_grad4 = jax.vmap(slot_attention_grads)(
        queries4,
        keys4,
        values4,
        attended_grad.reshape(batches, row_count, HEADS, HEAD),
        attended4,
        probabilities,
        probabilities_low,
    )
    key_value_parts = jnp.concatenate(
        [
            key_grad4.reshape(batches, slot_len, model_width),
            value_grad4.reshape(batches, slot_len, model_width),
        ],
        axis=2,
    ).astype(jnp.bfloat16)
    key_value_all = lax.psum_scatter(
        jnp.swapaxes(key_value_parts, 0, 1), "seq", scatter_dimension=0, tiled=True
    )
    key_value_all = jnp.swapaxes(key_value_all, 0, 1).reshape(all_rows, 2 * model_width)
    key_value_all = key_value_all.astype(jnp.float32)
    grad_down = jnp.einsum("rf,rd->fd", hidden_low, out_low, preferred_element_type=jnp.float32)
    grad_up = jnp.einsum("rd,rf->df", second_low, up_low, preferred_element_type=jnp.float32)
    grad_outproj = jnp.einsum(
        "rc,rd->cd", attended_low, branch_low, preferred_element_type=jnp.float32
    )
    qkv_low = jnp.concatenate(
        [
            rotate(query_grad4.reshape(all_rows, model_width), cosine_part, -sine_part),
            rotate(key_value_all[:, :model_width], cosine_part, -sine_part),
            key_value_all[:, model_width:],
        ],
        axis=1,
    ).astype(jnp.bfloat16)
    grad_qkv = jnp.einsum("rd,rc->dc", first_low, qkv_low, preferred_element_type=jnp.float32)
    first_grad = jnp.einsum("rc,dc->rd", qkv_low, full_qkv, preferred_element_type=jnp.float32)
    _, first_pullback = jax.vjp(layer_norm, inputs, norm_gains[:, 0], norm_biases[:, 0])
    input_part, gain_one, bias_one = first_pullback(first_grad)
    grad_input = (residual_grad + input_part).astype(jnp.bfloat16)
    grad_input = grad_input.reshape(batches, 1, row_count, model_width)
    packed_grads = jnp.concatenate(
        [
            grad_qkv.astype(jnp.bfloat16),
            grad_outproj.astype(jnp.bfloat16),
            grad_up.astype(jnp.bfloat16),
            grad_down.reshape(model_width, ff_width).astype(jnp.bfloat16),
            jnp.stack([gain_one, gain_two], axis=1).astype(jnp.bfloat16),
            jnp.stack([bias_one, bias_two], axis=1).astype(jnp.bfloat16),
            jnp.zeros((model_width, lane_pad), jnp.bfloat16),
        ],
        axis=1,
    )
    device_count = model_width // shard_rows
    scattered = lax.psum_scatter(
        packed_grads.reshape(device_count, shard_rows, offsets[-1]),
        ("seq", "fsdp"),
        scatter_dimension=0,
        tiled=False,
    )
    owned = pieces(scattered.astype(jnp.float32))[:6]
    owned[3] = owned[3].reshape(-1, model_width)
    depth_total = lax.psum(depth_terms, ("seq", "fsdp"))
    return (next_input, grad_input, grad_history, *owned, depth_total)


def solution(mesh):
    in_specs = (
        P(None, "fsdp", "seq", None),
        P(None, None, "fsdp", "seq", None),
        P(None, "fsdp", "seq", None),
        P(None, "fsdp"),
        P(("seq", "fsdp"), None),
        P(("seq", "fsdp"), None),
        P(("seq", "fsdp"), None),
        P(("seq", "fsdp"), None),
        P(("seq", "fsdp"), None),
        P(("seq", "fsdp"), None),
        P(),
    )
    out_specs = (
        P(None, "fsdp", "seq", None),
        P(None, "fsdp", "seq", None),
        P(None, None, "fsdp", "seq", None),
        P(("seq", "fsdp"), None),
        P(("seq", "fsdp"), None),
        P(("seq", "fsdp"), None),
        P(("seq", "fsdp"), None),
        P(("seq", "fsdp"), None),
        P(("seq", "fsdp"), None),
        P(),
    )
    return jax.shard_map(local, mesh=mesh, in_specs=in_specs, out_specs=out_specs, check_vma=False)
```

time: 791 us -> 1350 us (1.71)
  waiting for transfers between devices: 475 us -> 991 us
  local copies, waits for them, and re-layouts: 131 us -> 152 us
  blocking collectives: 39.5 us -> 59 us
    reduce_scatter x0 -> x2, waiting for transfers between devices: none -> 818 us  [the longest x1 735 us: local(): lax.psum_scatter(packed_grads.reshape(device_count, shard_rows, offsets[-...]
    unnamed x6 -> x4, waiting for transfers between devices: 295 us -> 0.07 us
    reshape x0 -> x5, local copies, waits for them, and re-layouts: none -> 66.2 us  [the longest x1 54.8 us: local(): packed_grads.reshape(device_count, shard_rows, offsets[-1])]
    unnamed x230 -> x102, local copies, waits for them, and re-layouts: 40.2 us -> 11.2 us
    concatenate x2 -> x1, local copies, waits for them, and re-layouts: 42.5 us -> 22.2 us  [local(): jnp.concatenate([grad_qkv.astype(jnp.bfloat16), grad_outproj.astype(jnp.b...]
    psum x1, blocking collectives: 39.5 us -> 59 us  [local(): depth_total = lax.psum(depth_terms, ('seq', 'fsdp'))]
    slice x7 -> x0, local copies, waits for them, and re-layouts: 16.3 us -> none  [the longest x3 10.5 us: local(): keys3 = kv_all[micro, :, :model_width].reshape(slot_len, HEADS, HEAD)]
    transpose x0 -> x3, local copies, waits for them, and re-layouts: none -> 13.9 us  [the longest x2 9.19 us: local(): jnp.swapaxes(kv_all[:, :, :model_width], 0, 1)]
  transfers between devices with their start and end apart: 4 -> 4, of which waited for: 4 -> 4; matrix products, arithmetic and copies ran while one was open for 9% -> 5% of each run, Pallas kernels for 0% -> 0%
where the time goes in v3:
time: 1350 us; the launch traced here: 1340 us
  waiting for transfers between devices  991 us (73%)
  local copies, waits for them, and re-layouts  152 us (11%)
  matrix products  84.2 us (6%)
  blocking collectives  59 us (4%)
  other arithmetic  35.2 us (3%)
  between operations  15.1 us (1%)
    reduce_scatter x1, waiting for transfers between devices, local(): lax.psum_scatter(packed_grads.reshape(device_count, shard_rows, offsets[-...  735 us
    all_gather x1, waiting for transfers between devices, local(): gathered = lax.all_gather(packed, ('seq', 'fsdp'), axis=0, tiled=True)  102 us
    reduce_scatter x1, waiting for transfers between devices, local(): lax.psum_scatter(jnp.swapaxes(key_value_parts, 0, 1), 'seq', scatter_dime...  83.2 us
    all_gather x1, waiting for transfers between devices, local(): lax.all_gather(jnp.swapaxes(own_kv, 0, 1), 'seq', axis=0, tiled=True)  70.3 us
    psum x1, blocking collectives, local(): depth_total = lax.psum(depth_terms, ('seq', 'fsdp'))  59 us
    reshape x1, local copies, waits for them, and re-layouts, local(): packed_grads.reshape(device_count, shard_rows, offsets[-1])  54.8 us
  transfers between devices with their start and end apart: 4, of which 4 were waited for; matrix products, arithmetic and copies ran while one was open for 5% of the time, Pallas kernels for 0%

profile of v3, /device:TPU:0, one launch (start us, length us, event | category | flops | bytes accessed | tf_op | source)
XLA Modules:
  0.0 1336.5 jit_solution(18169108997077316634)
XLA Ops:
  15.5 102.3 %all-gather.3.cloned.1.call-done = bf16[768,9344]{1,0:T(8,128)(2,1)} async-done(((bf16[24,9344]{1,0:T(8,128)(2,1)}), bf16[768,9344]{1,0:T(8,128)(2,1)}) %all-gather.3.cloned.1.call-update) | async-done | bytes 14352400 | tf_op jit(solution)/shard_map/all_gather | solution.py:229
  119.9 3.2 fusion.14
  134.9 4.8 slice.157
  139.7 8.7 reshape.393
  148.3 5.5 fusion.59
  153.8 70.3 %all-gather.5.cloned.1.call-done = bf16[1024,2,1536]{2,0,1:T(8,128)(2,1)} async-done(((bf16[128,2,1536]{2,0,1:T(8,128)(2,1)}), bf16[1024,2,1536]{2,0,1:T(8,128)(2,1)}) %all-gather.5.cloned.1.call-update) | async-done | bytes 6291472 | tf_op jit(solution)/shard_map/all_gather | solution.py:247
  224.2 6.0 slice_bitcast_fusion
  230.2 3.2 copy.40
  233.4 4.7 copy.38
  238.1 3.6 select_reduce_fusion.1
  241.7 4.1 select_reduce_fusion
  247.0 3.8 bitcast_convert_fusion.1
  254.2 5.3 fusion.11
  259.6 6.3 multiply_reduce_fusion.2
  266.3 4.2 multiply_reduce_fusion.1
  279.1 9.5 convolution_convert_fusion.3
  288.8 7.8 multiply_convert_fusion
  296.7 3.1 multiply_convert_fusion.1
  300.2 4.7 copy.48
  304.9 4.7 copy.49
  309.5 5.9 maximum_bitcast_fusion
  324.0 7.1 convolution_convert_fusion
  331.1 8.5 convert_element_type.179
  339.6 5.3 fusion.18
  345.0 3.7 convolution_convert_fusion.1
  348.7 83.2 %reduce-scatter.3.cloned.1.call-done = bf16[128,2,1536]{2,0,1:T(8,128)(2,1)} async-done(((bf16[1024,2,1536]{2,0,1:T(8,128)(2,1)}), bf16[128,2,1536]{2,0,1:T(8,128)(2,1)}) %reduce-scatter.3.cloned.1.call-update) | async-done | bytes 786448 | tf_op jit(solution)/shard_map/reduce_scatter | solution.py:303
  435.4 3.0 convolution_convert_fusion.2
  438.4 3.4 fusion.53
  442.7 22.2 %concatenate.45 = bf16[768,9344]{1,0:T(8,128)(2,1)} concatenate(bf16[768,2304]{1,0:T(8,128)(2,1)} %convolution_convert_fusion.2, bf16[768,768]{1,0:T(8,128)(2,1)S(1)} %copy-done.7, bf16[768,3072]{1,0:T(8,128)(2,1)} %convolution_convert_fusion.1, bf16[768,3072]{1,0:T(8,128)(2,1)} %convert_element_type.179, bf16[768,1]{1,0:T(8,128)(2,1)S(1)} %stack.24, ...), dimensions={1} | concatenate | bytes 28704768 | tf_op jit(solution)/shard_map/concatenate | solution.py:327
  464.9 54.8 %copy.57 = bf16[32,24,9344]{1,2,0:T(8,128)(2,1)} copy(bf16[32,24,9344]{2,1,0:T(8,128)(2,1)} %bitcast.143) | data formatting | bytes 28704768 | tf_op jit(solution)/shard_map/reshape | solution.py:341
  525.4 59.0 %psum.7 = f32[5]{0:T(128)} all-reduce(f32[5]{0:T(128)S(1)} %pad_maximum_fusion.7), channel_id=1, replica_groups=mesh['seq'=8,'fsdp'=4] {'seq','fsdp'}, use_global_device_ids=true, to_apply=%region_17.18 | all-reduce | flops 5 | bytes 40 | tf_op jit(solution)/shard_map/psum | solution.py:348
  585.4 735.0 %reduce-scatter.5.cloned.1.call-done = bf16[1,24,9344]{1,2,0:T(8,128)(2,1)} async-done(((bf16[32,24,9344]{1,2,0:T(8,128)(2,1)}), bf16[1,24,9344]{1,2,0:T(8,128)(2,1)}) %reduce-scatter.5.cloned.1.call-update) | async-done | bytes 448528 | tf_op jit(solution)/shard_map/reduce_scatter | solution.py:340
  (183 shorter events, 64.8 us)
Async XLA Ops:
  7.2 112.5 %copy-start.2 = (bf16[2,1,128,768]{3,2,1,0:T(8,128)(2,1)S(1)}, bf16[2,1,128,768]{3,2,1,0:T(8,128)(2,1)}, u32[]{:S(2)}) copy-start(bf16[2,1,128,768]{3,2,1,0:T(8,128)(2,1)} %param.11) | copy-start | bytes 1179652
  7.2 110.6 %all-gather.3.cloned.1.call-start = ((), (), s32[]{:S(2)}) async-start(), calls=%async_computation.2 | async-start | bytes 14800896 | tf_op jit(solution)/shard_map/all_gather | solution.py:229
  11.7 212.5 %all-gather.5.cloned.1.call-start = ((), (), s32[]{:S(2)}) async-start(), calls=%async_computation.3 | async-start | bytes 7077888 | tf_op jit(solution)/shard_map/all_gather | solution.py:247
  13.4 109.8 %copy-start.29 = (f32[256]{0:T(256)}, f32[256]{0:T(256)S(1)}, u32[]{:S(2)}) copy-start(f32[256]{0:T(256)S(1)} %get-tuple-element.74) | copy-start | bytes 3076
  14.6 108.5 %copy-start.37 = (f32[2,128]{1,0:T(2,128)}, f32[2,128]{1,0:T(2,128)S(1)}, u32[]{:S(2)}) copy-start(f32[2,128]{1,0:T(2,128)S(1)} %multiply_reduce_fusion.7) | copy-start | bytes 3076
  14.7 108.5 %copy-start.31 = (f32[256]{0:T(256)}, f32[256]{0:T(256)S(1)}, u32[]{:S(2)}) copy-start(f32[256]{0:T(256)S(1)} %bitcast_rsqrt_fusion) | copy-start | bytes 3076
  123.9 8.0 copy-start.17
  125.7 6.9 copy-start.15
  126.9 305.0 %reduce-scatter.3.cloned.1.call-start = ((), (), s32[]{:S(2)}) async-start(), calls=%async_computation.4 | async-start | bytes 7077888 | tf_op jit(solution)/shard_map/reduce_scatter | solution.py:303
  128.3 11.4 copy-start.39
  241.7 5.3 copy-start
  252.0 14.3 %slice-start = ((s8[4718592]{0:T(1024)(128)(4,1)}), s8[4194304]{0:T(1024)(128)(4,1)S(1)}, s32[]{:S(2)}) async-start(s8[4718592]{0:T(1024)(128)(4,1)} %bitcast.146), calls=%async_computation.6 | async-start | bytes 8388608
  254.0 12.3 copy-start.3
  254.2 11.6 copy-start.35
  254.2 12.0 slice-start.1
  259.5 6.3 copy-start.21
  259.5 6.7 copy-start.45
  259.6 6.7 copy-start.18
  259.6 6.7 copy-start.43
  259.6 6.7 copy-start.44
  279.1 9.6 copy-start.25
  279.1 9.7 copy-start.9
  279.1 9.7 copy-start.12
  279.1 9.7 copy-start.20
  279.1 9.7 copy-start.34
  288.8 7.9 copy-start.13
  288.8 7.9 copy-start.14
  315.5 1004.8 %reduce-scatter.5.cloned.1.call-start = ((), (), s32[]{:S(2)}) async-start(), calls=%async_computation.5 | async-start | bytes 78938112 | tf_op jit(solution)/shard_map/reduce_scatter | solution.py:340
  339.6 5.3 copy-start.4
  339.6 5.3 copy-start.22
  339.6 5.3 copy-start.36
  520.7 63.6 %copy-start.6 = (f32[256,768]{1,0:T(8,128)S(1)}, f32[256,768]{1,0:T(8,128)}, u32[]{:S(2)}) copy-start(f32[256,768]{1,0:T(8,128)} %copy-done.5) | copy-start | bytes 2359300
  (20 other events, 60.2 us)
Sparse Core Ops, SparseCore 0:
  11.8 105.9 all-gather.2
  127.0 97.1 all-gather.4
  315.6 116.1 reduce-scatter.2
  519.9 800.4 reduce-scatter.4

commit v4 on v3

--- a/solution.py
+++ b/solution.py
@@ -326,16 +326,16 @@
     grad_input = grad_input.reshape(batches, 1, row_count, model_width)
     packed_grads = jnp.concatenate(
         [
-            grad_qkv.astype(jnp.bfloat16),
-            grad_outproj.astype(jnp.bfloat16),
-            grad_up.astype(jnp.bfloat16),
-            grad_down.reshape(model_width, ff_width).astype(jnp.bfloat16),
-            jnp.stack([gain_one, gain_two], axis=1).astype(jnp.bfloat16),
-            jnp.stack([bias_one, bias_two], axis=1).astype(jnp.bfloat16),
-            jnp.zeros((model_width, lane_pad), jnp.bfloat16),
+            grad_qkv,
+            grad_outproj,
+            grad_up,
+            grad_down.reshape(model_width, ff_width),
+            jnp.stack([gain_one, gain_two], axis=1),
+            jnp.stack([bias_one, bias_two], axis=1),
+            jnp.zeros((model_width, lane_pad), jnp.float32),
         ],
         axis=1,
-    )
+    ).astype(jnp.bfloat16)
     device_count = model_width // shard_rows
     scattered = lax.psum_scatter(
         packed_grads.reshape(device_count, shard_rows, offsets[-1]),

time: 1350 us -> 647 us (0.48)
  waiting for transfers between devices: 991 us -> 369 us
  local copies, waits for them, and re-layouts: 152 us -> 104 us
  blocking collectives: 59 us -> 39.5 us
    reduce_scatter x2 -> x0, waiting for transfers between devices: 818 us -> none  [the longest x1 735 us: local(): lax.psum_scatter(packed_grads.reshape(device_count, shard_rows, offsets[-...]
    unnamed x4 -> x6, waiting for transfers between devices: 0.07 us -> 197 us
    reshape x3 -> x2, local copies, waits for them, and re-layouts: 64.1 us -> 1.85 us  [rotate(): return turned.reshape(row_count, HEADS * HEAD)]
    psum x1, blocking collectives: 59 us -> 39.5 us  [local(): depth_total = lax.psum(depth_terms, ('seq', 'fsdp'))]
    concatenate x1 -> x6, local copies, waits for them, and re-layouts: 22.2 us -> 36.7 us  [local(): jnp.concatenate([grad_qkv, grad_outproj, grad_up, grad_down.reshape(model...]
  transfers between devices with their start and end apart: 4 -> 4, of which waited for: 4 -> 4; matrix products, arithmetic and copies ran while one was open for 5% -> 10% of each run, Pallas kernels for 0% -> 0%
where the time goes in v4:
time: 647 us; the launch traced here: 640 us
  waiting for transfers between devices  369 us (57%)
  local copies, waits for them, and re-layouts  104 us (16%)
  matrix products  77.9 us (12%)
  blocking collectives  39.5 us (6%)
  other arithmetic  34.6 us (5%)
  between operations  15 us (2%)
    unnamed x6, waiting for transfers between devices  197 us
    all_gather x1, waiting for transfers between devices, local(): gathered = lax.all_gather(packed, ('seq', 'fsdp'), axis=0, tiled=True)  102 us
    all_gather x1, waiting for transfers between devices, local(): lax.all_gather(jnp.swapaxes(own_kv, 0, 1), 'seq', axis=0, tiled=True)  70.4 us
    psum x1, blocking collectives, local(): depth_total = lax.psum(depth_terms, ('seq', 'fsdp'))  39.5 us
    concatenate x6, local copies, waits for them, and re-layouts, local(): jnp.concatenate([grad_qkv, grad_outproj, grad_up, grad_down.reshape(model...  36.7 us
    unnamed x121, local copies, waits for them, and re-layouts  21.3 us
  transfers between devices with their start and end apart: 4, of which 4 were waited for; matrix products, arithmetic and copies ran while one was open for 10% of the time, Pallas kernels for 0%

profile of v4, /device:TPU:0, one launch (start us, length us, event | category | flops | bytes accessed | tf_op | source)
XLA Modules:
  0.0 640.3 jit_solution(176474307311602166)
XLA Ops:
  15.5 102.3 %all-gather.3.cloned.1.call-done = bf16[768,9344]{1,0:T(8,128)(2,1)} async-done(((bf16[24,9344]{1,0:T(8,128)(2,1)}), bf16[768,9344]{1,0:T(8,128)(2,1)}) %all-gather.3.cloned.1.call-update) | async-done | bytes 14352400 | tf_op jit(solution)/shard_map/all_gather | solution.py:229
  119.9 3.2 fusion.14
  134.9 4.8 slice.157
  139.7 8.6 %reshape.412 = bf16[3072,768]{1,0:T(8,128)(2,1)} reshape(bf16[768,3072]{1,0:T(8,128)(2,1)} %slice.157) | data formatting | bytes 9437184 | tf_op jit(solution)/shard_map/reshape | solution.py:231
  148.4 5.4 fusion.57
  153.8 70.4 %all-gather.5.cloned.1.call-done = bf16[1024,2,1536]{2,0,1:T(8,128)(2,1)} async-done(((bf16[128,2,1536]{2,0,1:T(8,128)(2,1)}), bf16[1024,2,1536]{2,0,1:T(8,128)(2,1)}) %all-gather.5.cloned.1.call-update) | async-done | bytes 6291472 | tf_op jit(solution)/shard_map/all_gather | solution.py:247
  224.2 5.0 slice_bitcast_fusion
  229.2 2.9 copy.102
  232.1 3.2 copy.104
  235.3 3.6 select_reduce_fusion.1
  238.9 4.1 select_reduce_fusion
  244.2 3.8 bitcast_convert_fusion
  251.5 5.3 fusion.11
  256.8 6.3 multiply_reduce_fusion.2
  263.5 4.3 multiply_reduce_fusion.1
  268.7 2.5 convolution_convert_fusion.5
  275.0 7.7 %convolution_convert_fusion.3 = bf16[2,12,64,1024]{3,2,1,0:T(8,128)(2,1)S(1)} fusion(bf16[2,128,12,64]{1,0,3,2:T(2,128)(2,1)} %reshape.414, f32[2,12,128,1024]{3,2,1,0:T(8,128)} %copy-done, f32[2,12,128]{2,1,0:T(8,128)} %copy-done.39, pred[2,128,1024]{2,1,0:T(8,128)(4,1)} %broadcast_and_fusion), kind=kOutput, calls=%fused_computation.32 | convolution fusion | flops 416808960 | bytes 16396288 | tf_op jit(solution)/shard_map/vmap(hrk,rhd->khd)/dot_general | solution.py:179
  283.3 7.8 %multiply_convert_fusion = bf16[2,12,128,1024]{3,2,1,0:T(8,128)(2,1)S(1)} fusion(f32[2,12,128,1024]{3,2,1,0:T(8,128)} %copy-done, f32[2,12,128]{2,1,0:T(8,128)S(1)} %fusion.22, f32[2,12,128]{2,1,0:T(8,128)S(1)} %copy-done.40, pred[2,128,1024]{2,1,0:T(8,128)(4,1)S(1)} %copy-done.12, bf16[2,1024,12,64]{1,3,2,0:T(8,128)(2,1)S(1)} %bitcast.166, ...), kind=kOutput, calls=%fused_computation | convolution fusion | flops 421527552 | bytes 22700032 | tf_op jit(solution)/shard_map/vmap(rhd,khd->hrk)/dot_general | solution.py:170
  293.8 3.3 pad_maximum_fusion
  297.1 8.7 %copy.140 = bf16[1024,3072]{1,0:T(8,128)(2,1)} copy(bf16[1024,3072]{0,1:T(8,128)(2,1)} %bitcast.160) | data formatting | bytes 12582912
  309.8 5.8 fusion.18
  316.6 5.0 convolution_convert_fusion
  321.6 8.6 %concatenate.59 = bf16[32,24,3072]{2,1,0:T(8,128)(2,1)} reshape(bf16[3072,768]{1,0:T(8,128)(2,1)} %convolution_convert_fusion) | data formatting | bytes 9437184 | tf_op jit(solution)/shard_map/concatenate | solution.py:327
  333.7 4.3 convolution_convert_fusion.1
  338.0 84.1 %reduce-scatter.7.cloned.1.call-done = bf16[128,3072]{1,0:T(8,128)(2,1)} async-done(((bf16[1024,3072]{1,0:T(8,128)(2,1)}), bf16[128,3072]{1,0:T(8,128)(2,1)}) %reduce-scatter.7.cloned.1.call-update) | async-done | bytes 786448
  424.8 2.3 slice_convert_fusion.1
  427.1 2.3 copy.113
  434.5 4.3 fusion.51
  438.8 2.9 convolution_convert_fusion.2
  446.8 22.6 %concatenate.64 = bf16[32,24,9344]{2,1,0:T(8,128)(2,1)} concatenate(bf16[32,24,2304]{2,1,0:T(8,128)(2,1)} %convolution_convert_fusion.2, bf16[32,24,768]{2,1,0:T(8,128)(2,1)S(1)} %convolution_convert_fusion.4, bf16[32,24,3072]{2,1,0:T(8,128)(2,1)} %bitcast.159, bf16[32,24,3072]{2,1,0:T(8,128)(2,1)} %concatenate.59, bf16[32,24,1]{2,1,0:T(8,128)(2,1)} %concatenate.66, ...), dimensions={2} | concatenate | bytes 28704768 | tf_op jit(solution)/shard_map/concatenate | solution.py:327
  475.0 39.5 %psum.7 = f32[5]{0:T(128)} all-reduce(f32[5]{0:T(128)S(1)} %pad_maximum_fusion.8), channel_id=1, replica_groups=mesh['seq'=8,'fsdp'=4] {'seq','fsdp'}, use_global_device_ids=true, to_apply=%region_17.18 | all-reduce | flops 5 | bytes 40 | tf_op jit(solution)/shard_map/psum | solution.py:348
  515.5 112.4 %reduce-scatter.9.cloned.1.call-done = bf16[1,24,9344]{2,1,0:T(8,128)(2,1)} async-done(((bf16[32,24,9344]{2,1,0:T(8,128)(2,1)}), bf16[1,24,9344]{2,1,0:T(8,128)(2,1)}) %reduce-scatter.9.cloned.1.call-update) | async-done | bytes 448528
  (201 shorter events, 68.0 us)
Async XLA Ops:
  7.2 112.4 %copy-start.2 = (bf16[2,1,128,768]{3,2,1,0:T(8,128)(2,1)S(1)}, bf16[2,1,128,768]{3,2,1,0:T(8,128)(2,1)}, u32[]{:S(2)}) copy-start(bf16[2,1,128,768]{3,2,1,0:T(8,128)(2,1)} %param.11) | copy-start | bytes 1179652
  7.2 110.6 %all-gather.3.cloned.1.call-start = ((), (), s32[]{:S(2)}) async-start(), calls=%async_computation.2 | async-start | bytes 14800896 | tf_op jit(solution)/shard_map/all_gather | solution.py:229
  11.6 212.5 %all-gather.5.cloned.1.call-start = ((), (), s32[]{:S(2)}) async-start(), calls=%async_computation.3 | async-start | bytes 7077888 | tf_op jit(solution)/shard_map/all_gather | solution.py:247
  13.4 109.8 %copy-start.35 = (f32[256]{0:T(256)}, f32[256]{0:T(256)S(1)}, u32[]{:S(2)}) copy-start(f32[256]{0:T(256)S(1)} %get-tuple-element.94) | copy-start | bytes 3076
  14.6 108.5 %copy-start.42 = (f32[2,128]{1,0:T(2,128)}, f32[2,128]{1,0:T(2,128)S(1)}, u32[]{:S(2)}) copy-start(f32[2,128]{1,0:T(2,128)S(1)} %multiply_reduce_fusion.7) | copy-start | bytes 3076
  14.6 108.5 %copy-start.37 = (f32[256]{0:T(256)}, f32[256]{0:T(256)S(1)}, u32[]{:S(2)}) copy-start(f32[256]{0:T(256)S(1)} %bitcast_rsqrt_fusion) | copy-start | bytes 3076
  123.9 8.0 %copy-start.19 = (bf16[2,1,128,768]{3,2,1,0:T(8,128)(2,1)S(1)}, bf16[2,1,128,768]{3,2,1,0:T(8,128)(2,1)}, u32[]{:S(2)}) copy-start(bf16[2,1,128,768]{3,2,1,0:T(8,128)(2,1)} %param.13) | copy-start | bytes 1179652
  125.7 7.0 %copy-start.15 = (bf16[4,2,1,128,768]{4,3,2,1,0:T(8,128)(2,1)S(1)}, bf16[4,2,1,128,768]{4,3,2,1,0:T(8,128)(2,1)}, u32[]{:S(2)}) copy-start(bf16[4,2,1,128,768]{4,3,2,1,0:T(8,128)(2,1)} %param.12) | copy-start | bytes 4718596
  126.9 295.3 %reduce-scatter.7.cloned.1.call-start = ((), (), s32[]{:S(2)}) async-start(), calls=%async_computation.4 | async-start | bytes 7077888
  129.6 10.2 %copy-start.47 = (pred[2,128]{1,0:T(4,128)(4,1)}, pred[2,128]{1,0:T(4,128)(4,1)S(1)}, u32[]{:S(2)}) copy-start(pred[2,128]{1,0:T(4,128)(4,1)S(1)} %broadcast_compare_fusion) | copy-start | bytes 772
  249.2 14.3 %slice-start = ((s8[4718592]{0:T(1024)(128)(4,1)}), s8[4194304]{0:T(1024)(128)(4,1)S(1)}, s32[]{:S(2)}) async-start(s8[4718592]{0:T(1024)(128)(4,1)} %bitcast.161), calls=%async_computation.6 | async-start | bytes 8388608
  251.2 12.3 %copy-start.3 = (f32[256,768]{1,0:T(8,128)}, f32[256,768]{1,0:T(8,128)S(1)}, u32[]{:S(2)}) copy-start(f32[256,768]{1,0:T(8,128)S(1)} %get-tuple-element.101) | copy-start | bytes 2359300
  251.4 11.6 %copy-start.41 = (f32[256]{0:T(256)}, f32[256]{0:T(256)S(1)}, u32[]{:S(2)}) copy-start(f32[256]{0:T(256)S(1)} %fusion.39) | copy-start | bytes 3076
  251.5 12.0 %slice-start.1 = ((s8[4718592]{0:T(1024)(128)(4,1)}), s8[524288]{0:T(1024)(128)(4,1)S(1)}, s32[]{:S(2)}) async-start(s8[4718592]{0:T(1024)(128)(4,1)} %bitcast.161), calls=%async_computation.7 | async-start | bytes 1048576
  275.0 7.8 %copy-start.22 = (bf16[2,128,12,64]{1,0,3,2:T(2,128)(2,1)S(1)}, bf16[2,128,12,64]{1,0,3,2:T(2,128)(2,1)}, u32[]{:S(2)}) copy-start(bf16[2,128,12,64]{1,0,3,2:T(2,128)(2,1)} %reshape.414) | copy-start | bytes 1179652
  275.0 8.1 %copy-start.28 = (f32[2,12,64,128]{3,2,1,0:T(8,128)S(1)}, f32[2,12,64,128]{3,2,1,0:T(8,128)}, u32[]{:S(2)}) copy-start(f32[2,12,64,128]{3,2,1,0:T(8,128)} %get-tuple-element.99) | copy-start | bytes 2359300
  275.0 8.3 %copy-start.8 = (bf16[2,1024,768]{1,2,0:T(8,128)(2,1)S(1)}, bf16[2,1024,768]{1,2,0:T(8,128)(2,1)}, u32[]{:S(2)}) copy-start(bf16[2,1024,768]{1,2,0:T(8,128)(2,1)} %copy.102) | copy-start | bytes 9437188
  275.0 8.3 %copy-start.12 = (pred[2,128,1024]{2,1,0:T(8,128)(4,1)S(1)}, pred[2,128,1024]{2,1,0:T(8,128)(4,1)}, u32[]{:S(2)}) copy-start(pred[2,128,1024]{2,1,0:T(8,128)(4,1)} %broadcast_and_fusion) | copy-start | bytes 786436
  275.0 8.3 %copy-start.40 = (f32[2,12,128]{2,1,0:T(8,128)S(1)}, f32[2,12,128]{2,1,0:T(8,128)}, u32[]{:S(2)}) copy-start(f32[2,12,128]{2,1,0:T(8,128)} %copy-done.39) | copy-start | bytes 36868
  283.3 7.9 %copy-start.13 = (bf16[256,12,32]{0,2,1:T(8,128)(2,1)S(1)}, bf16[256,12,32]{0,2,1:T(8,128)(2,1)}, u32[]{:S(2)}) copy-start(bf16[256,12,32]{0,2,1:T(8,128)(2,1)} %get-tuple-element.77) | copy-start | bytes 589828
  283.3 7.9 %copy-start.14 = (bf16[256,12,32]{0,2,1:T(8,128)(2,1)S(1)}, bf16[256,12,32]{0,2,1:T(8,128)(2,1)}, u32[]{:S(2)}) copy-start(bf16[256,12,32]{0,2,1:T(8,128)(2,1)} %get-tuple-element.78) | copy-start | bytes 589828
  305.8 322.1 %reduce-scatter.9.cloned.1.call-start = ((), (), s32[]{:S(2)}) async-start(), calls=%async_computation.5 | async-start | bytes 14800896
  309.8 6.8 %copy-start.54 = (f32[256,3072]{1,0:T(8,128)S(1)}, f32[256,3072]{1,0:T(8,128)}, u32[]{:S(2)}) copy-start(f32[256,3072]{1,0:T(8,128)} %copy-done.53) | copy-start | bytes 9437188
  321.6 8.6 %copy-start.46 = (bf16[768]{0:T(1024)(128)(2,1)S(1)}, bf16[768]{0:T(1024)(128)(2,1)}, u32[]{:S(2)}) copy-start(bf16[768]{0:T(1024)(128)(2,1)} %get-tuple-element.50) | copy-start | bytes 4612
  321.6 9.7 %copy-start.45 = (bf16[768]{0:T(1024)(128)(2,1)S(1)}, bf16[768]{0:T(1024)(128)(2,1)}, u32[]{:S(2)}) copy-start(bf16[768]{0:T(1024)(128)(2,1)} %get-tuple-element.54) | copy-start | bytes 4612
  321.6 10.7 %copy-start.6 = (f32[256,768]{1,0:T(8,128)S(1)}, f32[256,768]{1,0:T(8,128)}, u32[]{:S(2)}) copy-start(f32[256,768]{1,0:T(8,128)} %copy-done.5) | copy-start | bytes 2359300
  321.6 10.7 %copy-start.18 = (bf16[96,8,2,128]{3,1,2,0:T(8,128)(2,1)S(1)}, bf16[96,8,2,128]{3,1,2,0:T(8,128)(2,1)}, u32[]{:S(2)}) copy-start(bf16[96,8,2,128]{3,1,2,0:T(8,128)(2,1)} %copy.170) | copy-start | bytes 1179652
  338.0 91.4 %copy-start.33 = (f32[256,32]{0,1:T(8,128)S(1)}, f32[256,32]{0,1:T(8,128)}, u32[]{:S(2)}) copy-start(f32[256,32]{0,1:T(8,128)} %get-tuple-element.93) | copy-start | bytes 98308
  338.0 91.4 %copy-start.34 = (f32[256,32]{0,1:T(8,128)S(1)}, f32[256,32]{0,1:T(8,128)}, u32[]{:S(2)}) copy-start(f32[256,32]{0,1:T(8,128)} %get-tuple-element.91) | copy-start | bytes 98308
  438.8 8.1 %copy-start.25 = (bf16[32,24,1]{2,1,0:T(8,128)(2,1)S(1)}, bf16[32,24,1]{2,1,0:T(8,128)(2,1)}, u32[]{:S(2)}) copy-start(bf16[32,24,1]{2,1,0:T(8,128)(2,1)} %concatenate.67) | copy-start | bytes 4612
  438.8 8.0 %copy-start.26 = (bf16[32,24,1]{2,1,0:T(8,128)(2,1)S(1)}, bf16[32,24,1]{2,1,0:T(8,128)(2,1)}, u32[]{:S(2)}) copy-start(bf16[32,24,1]{2,1,0:T(8,128)(2,1)} %concatenate.69) | copy-start | bytes 4612
  470.4 44.1 %copy-start.44 = (f32[256]{0:T(256)S(1)}, f32[256]{0:T(256)}, u32[]{:S(2)}) copy-start(f32[256]{0:T(256)} %get-tuple-element.53) | copy-start | bytes 3076
  (29 other events, 116.4 us)
Sparse Core Ops, SparseCore 0:
  11.8 105.9 all-gather.2
  127.0 97.1 all-gather.4
  305.9 116.1 reduce-scatter.6
  469.6 158.3 reduce-scatter.8

commit v5 on v4

--- a/solution.py
+++ b/solution.py
@@ -5,6 +5,7 @@
 import jax.numpy as jnp
 from jax import lax
 from jax.sharding import PartitionSpec as P
+from jax.experimental.layout import Layout, with_layout_constraint
 
 HEADS = 12
 HEAD = 64
@@ -206,10 +207,11 @@
     cosine_part, sine_part = rotary_tables(jnp.tile(positions, batches))
     gelu_tanh = partial(jax.nn.gelu, approximate=True)
     lane_pad = 128 - 4
-    widths = (3 * model_width, model_width, ff_width, ff_width, 2, 2, lane_pad)
+    widths = (3 * model_width, 2, 2, lane_pad, model_width, ff_width, ff_width)
     offsets = [0]
     for width in widths:
         offsets.append(offsets[-1] + width)
+    late_width = offsets[4]
 
     def pieces(packed_rows):
         return [packed_rows[:, offsets[i] : offsets[i + 1]] for i in range(len(widths))]
@@ -217,17 +219,17 @@
     packed = jnp.concatenate(
         [
             w_qkv,
+            ln_gains,
+            ln_biases,
+            jnp.zeros((shard_rows, lane_pad), w_qkv.dtype),
             w_out,
             w_up,
             w_down.reshape(shard_rows, ff_width),
-            ln_gains,
-            ln_biases,
-            jnp.zeros((shard_rows, lane_pad), w_qkv.dtype),
         ],
         axis=1,
     )
     gathered = lax.all_gather(packed, ("seq", "fsdp"), axis=0, tiled=True)
-    full_qkv, full_out, full_up, down_rows, gain_rows, bias_rows, _ = pieces(gathered)
+    full_qkv, gain_rows, bias_rows, _, full_out, full_up, down_rows = pieces(gathered)
     full_down = down_rows.reshape(ff_width, model_width)
     norm_gains = gain_rows.astype(jnp.float32)
     norm_biases = bias_rows.astype(jnp.float32)
@@ -244,75 +246,117 @@
     own_kv = jnp.concatenate([keys_own, values_own], axis=1).reshape(
         batches, row_count, 2 * model_width
     )
-    kv_all = lax.all_gather(jnp.swapaxes(own_kv, 0, 1), "seq", axis=0, tiled=True)
-    keys4 = jnp.swapaxes(kv_all[:, :, :model_width], 0, 1).reshape(batches, slot_len, HEADS, HEAD)
-    values4 = jnp.swapaxes(kv_all[:, :, model_width:], 0, 1).reshape(
-        batches, slot_len, HEADS, HEAD
-    )
     queries4 = queries.reshape(batches, row_count, HEADS, HEAD)
-    attended4, probabilities, probabilities_low = jax.vmap(
-        slot_attention, in_axes=(0, 0, 0, None, 0)
-    )(queries4, keys4, values4, positions, slot_lengths)
-    attended_low = attended4.reshape(all_rows, model_width).astype(jnp.bfloat16)
-    residual = inputs + jnp.dot(attended_low, full_out, preferred_element_type=jnp.float32)
-    second_low = layer_norm(residual, norm_gains[:, 1], norm_biases[:, 1]).astype(jnp.bfloat16)
-    hidden = jnp.dot(second_low, full_up, preferred_element_type=jnp.float32)
-    hidden_low = gelu_tanh(hidden).astype(jnp.bfloat16)
-    block_out = residual + jnp.dot(hidden_low, full_down, preferred_element_type=jnp.float32)
     earlier = history[:, :, 0].reshape(4, all_rows, model_width).astype(jnp.float32)
     usable = (positions[None, :] < slot_lengths[:, None]).reshape(all_rows, 1)
     grad_next = jnp.where(
         usable, cotangent[:, 0].reshape(all_rows, model_width).astype(jnp.float32), 0.0
     )
-    combined = depth_weights[4] * block_out + jnp.einsum("j,jrd->rd", depth_weights[:4], earlier)
-    next_input = combined.astype(jnp.bfloat16).reshape(batches, 1, row_count, model_width)
+    history_part = jnp.einsum("j,jrd->rd", depth_weights[:4], earlier)
     grad_history = (depth_weights[:4, None, None] * grad_next[None]).astype(jnp.bfloat16)
     grad_history = grad_history.reshape(4, batches, 1, row_count, model_width)
+    out_grad = depth_weights[4] * grad_next
+    out_low = out_grad.astype(jnp.bfloat16)
+
+    per_micro = []
+    for micro in range(batches):
+        rows = slice(micro * row_count, (micro + 1) * row_count)
+        kv_all = lax.all_gather(own_kv[micro], "seq", axis=0, tiled=True)
+        keys3 = kv_all[:, :model_width].reshape(slot_len, HEADS, HEAD)
+        values3 = kv_all[:, model_width:].reshape(slot_len, HEADS, HEAD)
+        attended3, probabilities, probabilities_low = slot_attention(
+            queries4[micro], keys3, values3, positions, slot_lengths[micro]
+        )
+        attended_low = attended3.reshape(row_count, model_width).astype(jnp.bfloat16)
+        residual = inputs[rows] + jnp.dot(
+            attended_low, full_out, preferred_element_type=jnp.float32
+        )
+        second_low = layer_norm(residual, norm_gains[:, 1], norm_biases[:, 1]).astype(
+            jnp.bfloat16
+        )
+        hidden = jnp.dot(second_low, full_up, preferred_element_type=jnp.float32)
+        hidden_low = gelu_tanh(hidden).astype(jnp.bfloat16)
+        block_out = residual + jnp.dot(hidden_low, full_down, preferred_element_type=jnp.float32)
+        hidden_grad = jnp.einsum(
+            "rd,fd->rf", out_low[rows], full_down, preferred_element_type=jnp.float32
+        )
+        _, gelu_pullback = jax.vjp(gelu_tanh, hidden)
+        up_low = gelu_pullback(hidden_grad)[0].astype(jnp.bfloat16)
+        second_grad = jnp.einsum("rf,df->rd", up_low, full_up, preferred_element_type=jnp.float32)
+        _, second_pullback = jax.vjp(layer_norm, residual, norm_gains[:, 1], norm_biases[:, 1])
+        residual_part, gain_two, bias_two = second_pullback(second_grad)
+        residual_grad = out_grad[rows] + residual_part
+        branch_low = residual_grad.astype(jnp.bfloat16)
+        attended_grad = jnp.einsum(
+            "rd,cd->rc", branch_low, full_out, preferred_element_type=jnp.float32
+        ).astype(jnp.bfloat16)
+        query_grad3, key_grad3, value_grad3 = slot_attention_grads(
+            queries4[micro],
+            keys3,
+            values3,
+            attended_grad.reshape(row_count, HEADS, HEAD),
+            attended3,
+            probabilities,
+            probabilities_low,
+        )
+        key_value_part = jnp.concatenate(
+            [key_grad3.reshape(slot_len, model_width), value_grad3.reshape(slot_len, model_width)],
+            axis=1,
+        ).astype(jnp.bfloat16)
+        key_value_own = lax.psum_scatter(key_value_part, "seq", scatter_dimension=0, tiled=True)
+        per_micro.append(
+            (
+                attended_low,
+                block_out,
+                second_low,
+                hidden_low,
+                up_low,
+                gain_two,
+                bias_two,
+                residual_grad,
+                branch_low,
+                query_grad3.reshape(row_count, model_width),
+                key_value_own.astype(jnp.float32),
+            )
+        )
+    (
+        attended_low,
+        block_out,
+        second_low,
+        hidden_low,
+        up_low,
+        gain_two,
+        bias_two,
+        residual_grad,
+        branch_low,
+        query_grad,
+        key_value_all,
+    ) = [
+        jnp.concatenate(parts, axis=0) if parts[0].ndim == 2 else sum(parts[1:], parts[0])
+        for parts in zip(*per_micro)
+    ]
+    combined = depth_weights[4] * block_out + history_part
+    next_input = combined.astype(jnp.bfloat16).reshape(batches, 1, row_count, model_width)
     depth_terms = jnp.concatenate(
         [jnp.einsum("jrd,rd->j", earlier, grad_next), jnp.sum(block_out * grad_next)[None]]
     )
-    out_grad = depth_weights[4] * grad_next
-    out_low = out_grad.astype(jnp.bfloat16)
-    hidden_grad = jnp.einsum("rd,fd->rf", out_low, full_down, preferred_element_type=jnp.float32)
-    _, gelu_pullback = jax.vjp(gelu_tanh, hidden)
-    up_low = gelu_pullback(hidden_grad)[0].astype(jnp.bfloat16)
-    second_grad = jnp.einsum("rf,df->rd", up_low, full_up, preferred_element_type=jnp.float32)
-    _, second_pullback = jax.vjp(layer_norm, residual, norm_gains[:, 1], norm_biases[:, 1])
-    residual_part, gain_two, bias_two = second_pullback(second_grad)
-    residual_grad = out_grad + residual_part
-    branch_low = residual_grad.astype(jnp.bfloat16)
-    attended_grad = jnp.einsum(
-        "rd,cd->rc", branch_low, full_out, preferred_element_type=jnp.float32
-    ).astype(jnp.bfloat16)
-    query_grad4, key_grad4, value_grad4 = jax.vmap(slot_attention_grads)(
-        queries4,
-        keys4,
-        values4,
-        attended_grad.reshape(batches, row_count, HEADS, HEAD),
-        attended4,
-        probabilities,
-        probabilities_low,
-    )
-    key_value_parts = jnp.concatenate(
-        [
-            key_grad4.reshape(batches, slot_len, model_width),
-            value_grad4.reshape(batches, slot_len, model_width),
-        ],
-        axis=2,
-    ).astype(jnp.bfloat16)
-    key_value_all = lax.psum_scatter(
-        jnp.swapaxes(key_value_parts, 0, 1), "seq", scatter_dimension=0, tiled=True
-    )
-    key_value_all = jnp.swapaxes(key_value_all, 0, 1).reshape(all_rows, 2 * model_width)
-    key_value_all = key_value_all.astype(jnp.float32)
     grad_down = jnp.einsum("rf,rd->fd", hidden_low, out_low, preferred_element_type=jnp.float32)
     grad_up = jnp.einsum("rd,rf->df", second_low, up_low, preferred_element_type=jnp.float32)
     grad_outproj = jnp.einsum(
         "rc,rd->cd", attended_low, branch_low, preferred_element_type=jnp.float32
     )
+    early_grads = jnp.concatenate(
+        [
+            jnp.zeros((model_width, late_width), jnp.float32),
+            grad_outproj,
+            grad_up,
+            grad_down.reshape(model_width, ff_width),
+        ],
+        axis=1,
+    ).astype(jnp.bfloat16)
     qkv_low = jnp.concatenate(
         [
-            rotate(query_grad4.reshape(all_rows, model_width), cosine_part, -sine_part),
+            rotate(query_grad, cosine_part, -sine_part),
             rotate(key_value_all[:, :model_width], cosine_part, -sine_part),
             key_value_all[:, model_width:],
         ],
@@ -324,27 +368,36 @@
     input_part, gain_one, bias_one = first_pullback(first_grad)
     grad_input = (residual_grad + input_part).astype(jnp.bfloat16)
     grad_input = grad_input.reshape(batches, 1, row_count, model_width)
-    packed_grads = jnp.concatenate(
+    late_grads = jnp.concatenate(
         [
             grad_qkv,
-            grad_outproj,
-            grad_up,
-            grad_down.reshape(model_width, ff_width),
             jnp.stack([gain_one, gain_two], axis=1),
             jnp.stack([bias_one, bias_two], axis=1),
             jnp.zeros((model_width, lane_pad), jnp.float32),
         ],
         axis=1,
     ).astype(jnp.bfloat16)
+    packed_grads = lax.dynamic_update_slice(early_grads, late_grads, (0, 0))
     device_count = model_width // shard_rows
+    row_major = Layout(major_to_minor=(0, 1, 2))
     scattered = lax.psum_scatter(
-        packed_grads.reshape(device_count, shard_rows, offsets[-1]),
+        with_layout_constraint(
+            packed_grads.reshape(device_count, shard_rows, offsets[-1]), row_major
+        ),
         ("seq", "fsdp"),
         scatter_dimension=0,
         tiled=False,
     )
-    owned = pieces(scattered.astype(jnp.float32))[:6]
-    owned[3] = owned[3].reshape(-1, model_width)
+    scattered = with_layout_constraint(scattered, Layout(major_to_minor=(0, 1)))
+    full_pieces = pieces(scattered.astype(jnp.float32))
+    owned = [
+        full_pieces[0],
+        full_pieces[4],
+        full_pieces[5],
+        full_pieces[6].reshape(-1, model_width),
+        full_pieces[1],
+        full_pieces[2],
+    ]
     depth_total = lax.psum(depth_terms, ("seq", "fsdp"))
     return (next_input, grad_input, grad_history, *owned, depth_total)
 

time: 647 us -> 652 us (level)
  local copies, waits for them, and re-layouts: 104 us -> 85.7 us
  waiting for transfers between devices: 369 us -> 387 us
  other arithmetic: 34.6 us -> 41.5 us
    concatenate x7 -> x3, local copies, waits for them, and re-layouts: 38.5 us -> 8.65 us  [the longest x1 6.81 us: local(): jnp.concatenate([grad_qkv, jnp.stack([gain_one, gain_two], axis=1), jnp.s...]
    all_gather x1 -> x2, waiting for transfers between devices: 70.4 us -> 89.4 us  [local(): kv_all = lax.all_gather(own_kv[micro], 'seq', axis=0, tiled=True)]
    slice x1 -> x8, local copies, waits for them, and re-layouts: 0.6 us -> 14.3 us  [the longest x4 9.87 us: local(): keys3 = kv_all[:, :model_width].reshape(slot_len, HEADS, HEAD)]
    concatenate x1 -> x5, other arithmetic: 3.32 us -> 14.6 us  [the longest x1 9.05 us: local(): jnp.concatenate([jnp.zeros((model_width, late_width), jnp.float32), grad_...]
    transpose x3 -> x0, local copies, waits for them, and re-layouts: 11.1 us -> none  [the longest x2 8.2 us: local(): jnp.swapaxes(kv_all[:, :, :model_width], 0, 1)]
    unnamed x6 -> x9, waiting for transfers between devices: 197 us -> 194 us
    unnamed x121 -> x170, local copies, waits for them, and re-layouts: 21.3 us -> 23.6 us
  transfers between devices with their start and end apart: 4 -> 6, of which waited for: 4 -> 6; matrix products, arithmetic and copies ran while one was open for 10% -> 16% of each run, Pallas kernels for 0% -> 0%
where the time goes in v5:
time: 652 us; the launch traced here: 642 us
  waiting for transfers between devices  387 us (59%)
  local copies, waits for them, and re-layouts  85.7 us (13%)
  matrix products  72 us (11%)
  other arithmetic  41.5 us (6%)
  blocking collectives  40.3 us (6%)
  between operations  16 us (2%)
    unnamed x9, waiting for transfers between devices  194 us
    all_gather x1, waiting for transfers between devices, local(): gathered = lax.all_gather(packed, ('seq', 'fsdp'), axis=0, tiled=True)  103 us
    all_gather x2, waiting for transfers between devices, local(): kv_all = lax.all_gather(own_kv[micro], 'seq', axis=0, tiled=True)  89.4 us
    psum x1, blocking collectives, local(): depth_total = lax.psum(depth_terms, ('seq', 'fsdp'))  40.3 us
    unnamed x170, local copies, waits for them, and re-layouts  23.6 us
  transfers between devices with their start and end apart: 6, of which 6 were waited for; matrix products, arithmetic and copies ran while one was open for 16% of the time, Pallas kernels for 0%

profile of v5, /device:TPU:0, one launch (start us, length us, event | category | flops | bytes accessed | tf_op | source)
XLA Modules:
  0.0 642.4 jit_solution(8200584143726461904)
XLA Ops:
  14.3 103.4 %all-gather.4.cloned.1.call-done = bf16[768,9344]{1,0:T(8,128)(2,1)} async-done(((bf16[24,9344]{1,0:T(8,128)(2,1)}), bf16[768,9344]{1,0:T(8,128)(2,1)}) %all-gather.4.cloned.1.call-update) | async-done | bytes 14352400 | tf_op jit(solution)/shard_map/all_gather | solution.py:231
  119.9 3.2 fusion.4
  133.8 4.9 slice.239
  138.7 8.5 %reshape.524 = bf16[3072,768]{1,0:T(8,128)(2,1)} reshape(bf16[768,3072]{1,0:T(8,128)(2,1)} %slice.239) | data formatting | bytes 9437184 | tf_op jit(solution)/shard_map/reshape | solution.py:233
  147.2 38.5 %all-gather.8.cloned.1.call-done = bf16[1024,1536]{1,0:T(8,128)(2,1)} async-done(((bf16[128,1536]{1,0:T(8,128)(2,1)}), bf16[1024,1536]{1,0:T(8,128)(2,1)}) %all-gather.8.cloned.1.call-update) | async-done | bytes 3145744 | tf_op jit(solution)/shard_map/all_gather | solution.py:264
  185.7 3.2 fusion.113
  196.3 50.9 %all-gather.6.cloned.1.call-done = bf16[1024,1536]{1,0:T(8,128)(2,1)} async-done(((bf16[128,1536]{1,0:T(8,128)(2,1)}), bf16[1024,1536]{1,0:T(8,128)(2,1)}) %all-gather.6.cloned.1.call-update) | async-done | bytes 3145744 | tf_op jit(solution)/shard_map/all_gather | solution.py:264
  247.2 3.2 fusion.112
  255.1 2.4 select_reduce_fusion.1
  261.2 2.5 fusion.118
  277.3 2.3 multiply_reduce_fusion.6
  284.7 4.7 convolution_convert_fusion.3
  289.6 2.6 multiply_convert_fusion
  296.5 4.7 copy.113
  301.2 2.7 convolution_convert_fusion.7
  306.8 5.9 multiply_convert_fusion.1
  317.7 4.7 copy.111
  323.9 3.6 convolution_convert_fusion.1
  327.5 8.9 %reshape.539 = bf16[768,3072]{1,0:T(8,128)(2,1)} reshape(bf16[3072,768]{1,0:T(8,128)(2,1)} %convolution_convert_fusion.1) | data formatting | bytes 9437184 | tf_op jit(solution)/shard_map/reshape | solution.py:353
  340.7 2.9 convolution_convert_fusion.2
  343.6 3.4 fusion.38
  348.3 9.0 %pad_maximum_fusion = bf16[768,9344]{1,0:T(8,128)(2,1)} fusion(bf16[768,3072]{1,0:T(8,128)(2,1)S(1)} %bitcast.171, bf16[768,3072]{1,0:T(8,128)(2,1)S(1)} %convolution_convert_fusion.2, bf16[768,768]{1,0:T(8,128)(2,1)S(1)} %copy.78, bf16[9344]{0:T(1024)(128)(2,1)S(1)} %pad.2.clone), kind=kLoop, calls=%fused_computation | loop fusion | flops 57409536 | bytes 24987904 | tf_op jit(solution)/shard_map/concatenate | solution.py:348
  357.3 16.7 %reduce-scatter.12.cloned.1.call-done = bf16[128,1536]{1,0:T(8,128)(2,1)} async-done(((bf16[1024,1536]{1,0:T(8,128)(2,1)}), bf16[128,1536]{1,0:T(8,128)(2,1)}) %reduce-scatter.12.cloned.1.call-update) | async-done | bytes 393232
  375.3 75.6 %reduce-scatter.10.cloned.1.call-done = bf16[128,1536]{1,0:T(8,128)(2,1)} async-done(((bf16[1024,1536]{1,0:T(8,128)(2,1)}), bf16[128,1536]{1,0:T(8,128)(2,1)}) %reduce-scatter.10.cloned.1.call-update) | async-done | bytes 393232
  453.2 3.0 convolution_convert_fusion
  456.2 3.3 fusion.107
  460.3 6.8 %concatenate.95 = bf16[768,2432]{1,0:T(8,128)(2,1)} concatenate(bf16[768,2304]{1,0:T(8,128)(2,1)} %convolution_convert_fusion, bf16[768,1]{1,0:T(8,128)(2,1)S(1)} %stack.12, bf16[768,1]{1,0:T(8,128)(2,1)S(1)} %add.216, bf16[768,1]{1,0:T(8,128)(2,1)S(1)} %stack.13, bf16[768,1]{1,0:T(8,128)(2,1)S(1)} %copy-done.45, bf16[768,124]{1,0:T(8,128)(2,1)S(1)} %broadcast_in_dim.135), dimensions={1} | concatenate | bytes 7471104 | tf_op jit(solution)/shard_map/concatenate | solution.py:371
  467.1 4.2 constant_dynamic-update-slice_fusion
  476.0 3.5 convolution_add_fusion.2
  479.5 3.4 convolution_add_fusion.3
  487.7 40.3 %psum.7 = f32[5]{0:T(128)} all-reduce(f32[5]{0:T(128)S(1)} %pad_maximum_fusion.12), channel_id=1, replica_groups=mesh['seq'=8,'fsdp'=4] {'seq','fsdp'}, use_global_device_ids=true, to_apply=%region_26.27 | all-reduce | flops 5 | bytes 40 | tf_op jit(solution)/shard_map/psum | solution.py:401
  529.1 100.7 %reduce-scatter.14.cloned.1.call-done = bf16[1,24,9344]{2,1,0:T(8,128)(2,1)} async-done(((bf16[32,24,9344]{2,1,0:T(8,128)(2,1)}), bf16[1,24,9344]{2,1,0:T(8,128)(2,1)}) %reduce-scatter.14.cloned.1.call-update) | async-done | bytes 448528
  (290 shorter events, 92.6 us)
Async XLA Ops:
  7.2 112.5 %copy-start.2 = (bf16[2,1,128,768]{3,2,1,0:T(8,128)(2,1)S(1)}, bf16[2,1,128,768]{3,2,1,0:T(8,128)(2,1)}, u32[]{:S(2)}) copy-start(bf16[2,1,128,768]{3,2,1,0:T(8,128)(2,1)} %param.11) | copy-start | bytes 1179652
  7.2 110.6 %all-gather.4.cloned.1.call-start = ((), (), s32[]{:S(2)}) async-start(), calls=%async_computation.3 | async-start | bytes 14800896 | tf_op jit(solution)/shard_map/all_gather | solution.py:231
  11.7 174.0 %all-gather.8.cloned.1.call-start = ((), (), s32[]{:S(2)}) async-start(), calls=%async_computation.5 | async-start | bytes 3538944 | tf_op jit(solution)/shard_map/all_gather | solution.py:264
  11.7 119.6 %copy-start.65 = (s32[128]{0:T(128)}, s32[128]{0:T(128)S(1)}, u32[]{:S(2)}) copy-start(s32[128]{0:T(128)S(1)} %get-tuple-element.131) | copy-start | bytes 1540
  124.9 128.9 %copy-start.10 = (bf16[256,12,32]{0,2,1:T(8,128)(2,1)}, bf16[256,12,32]{0,2,1:T(8,128)(2,1)S(1)}, u32[]{:S(2)}) copy-start(bf16[256,12,32]{0,2,1:T(8,128)(2,1)S(1)} %get-tuple-element.79) | copy-start | bytes 589828
  124.9 6.7 %copy-start.13 = (bf16[2,1,128,768]{3,2,1,0:T(8,128)(2,1)S(1)}, bf16[2,1,128,768]{3,2,1,0:T(8,128)(2,1)}, u32[]{:S(2)}) copy-start(bf16[2,1,128,768]{3,2,1,0:T(8,128)(2,1)} %param.13) | copy-start | bytes 1179652
  127.1 120.1 %all-gather.6.cloned.1.call-start = ((), (), s32[]{:S(2)}) async-start(), calls=%async_computation.4 | async-start | bytes 3538944 | tf_op jit(solution)/shard_map/all_gather | solution.py:264
  127.8 246.3 %reduce-scatter.12.cloned.1.call-start = ((), (), s32[]{:S(2)}) async-start(), calls=%async_computation.7 | async-start | bytes 3538944
  131.6 125.9 %copy-start.24 = (pred[128,1024]{1,0:T(8,128)(4,1)}, pred[128,1024]{1,0:T(8,128)(4,1)S(1)}, u32[]{:S(2)}) copy-start(pred[128,1024]{1,0:T(8,128)(4,1)S(1)} %get-tuple-element.107) | copy-start | bytes 393220
  131.6 132.3 %copy-start.26 = (pred[128,1024]{1,0:T(8,128)(4,1)}, pred[128,1024]{1,0:T(8,128)(4,1)S(1)}, u32[]{:S(2)}) copy-start(pred[128,1024]{1,0:T(8,128)(4,1)S(1)} %get-tuple-element.108) | copy-start | bytes 393220
  196.3 67.7 %copy-start.55 = (f32[12,128]{1,0:T(8,128)}, f32[12,128]{1,0:T(8,128)S(1)}, u32[]{:S(2)}) copy-start(f32[12,128]{1,0:T(8,128)S(1)} %log_add_fusion) | copy-start | bytes 18436
  253.8 12.5 %slice-start.10 = ((s8[14352384]{0:T(1024)(128)(4,1)}), s8[4194304]{0:T(1024)(128)(4,1)S(1)}, s32[]{:S(2)}) async-start(s8[14352384]{0:T(1024)(128)(4,1)} %bitcast.178), calls=%async_computation.19 | async-start | bytes 8388608
  255.1 8.9 %slice-start.4 = ((s8[6291456]{0:T(1024)(128)(4,1)}), s8[4194304]{0:T(1024)(128)(4,1)S(1)}, s32[]{:S(2)}) async-start(s8[6291456]{0:T(1024)(128)(4,1)} %bitcast.166), calls=%async_computation.13 | async-start | bytes 8388608
  255.1 11.2 %slice-start.11 = ((s8[14352384]{0:T(1024)(128)(4,1)}), s8[4194304]{0:T(1024)(128)(4,1)S(1)}, s32[]{:S(2)}) async-start(s8[14352384]{0:T(1024)(128)(4,1)} %bitcast.178), calls=%async_computation.20 | async-start | bytes 8388608
  258.3 5.7 slice-start.5
  258.3 5.7 copy-start.22
  258.3 8.0 %slice-start.12 = ((s8[14352384]{0:T(1024)(128)(4,1)}), s8[4194304]{0:T(1024)(128)(4,1)S(1)}, s32[]{:S(2)}) async-start(s8[14352384]{0:T(1024)(128)(4,1)} %bitcast.178), calls=%async_computation.21 | async-start | bytes 8388608
  280.0 9.5 %slice-start.6 = ((s8[6291456]{0:T(1024)(128)(4,1)}), s8[2097152]{0:T(1024)(128)(4,1)S(1)}, s32[]{:S(2)}) async-start(s8[6291456]{0:T(1024)(128)(4,1)} %bitcast.168), calls=%async_computation.15 | async-start | bytes 4194304
  284.7 4.8 copy-start.27
  301.1 149.8 %reduce-scatter.10.cloned.1.call-start = ((), (), s32[]{:S(2)}) async-start(), calls=%async_computation.6 | async-start | bytes 3538944
  301.2 12.2 %slice-start.2 = ((s8[6291456]{0:T(1024)(128)(4,1)}), s8[2097152]{0:T(1024)(128)(4,1)S(1)}, s32[]{:S(2)}) async-start(s8[6291456]{0:T(1024)(128)(4,1)} %bitcast.164), calls=%async_computation.11 | async-start | bytes 4194304
  306.8 5.9 copy-start.12
  306.8 6.6 %slice-start.3 = ((s8[6291456]{0:T(1024)(128)(4,1)}), s8[4194304]{0:T(1024)(128)(4,1)S(1)}, s32[]{:S(2)}) async-start(s8[6291456]{0:T(1024)(128)(4,1)} %bitcast.164), calls=%async_computation.12 | async-start | bytes 8388608
  322.4 307.4 %reduce-scatter.14.cloned.1.call-start = ((), (), s32[]{:S(2)}) async-start(), calls=%async_computation.8 | async-start | bytes 14800896
  327.5 8.9 %copy-start.35 = (bf16[128,12,64]{0,2,1:T(8,128)(2,1)S(1)}, bf16[128,12,64]{0,2,1:T(8,128)(2,1)}, u32[]{:S(2)}) copy-start(bf16[128,12,64]{0,2,1:T(8,128)(2,1)} %copy-done.34) | copy-start | bytes 589828
  327.5 8.9 %copy-start.41 = (bf16[128,12,64]{0,2,1:T(8,128)(2,1)S(1)}, bf16[128,12,64]{0,2,1:T(8,128)(2,1)}, u32[]{:S(2)}) copy-start(bf16[128,12,64]{0,2,1:T(8,128)(2,1)} %copy-done.40) | copy-start | bytes 589828
  327.5 8.9 %copy-start.42 = (bf16[128,768]{1,0:T(8,128)(2,1)S(1)}, bf16[128,768]{1,0:T(8,128)(2,1)}, u32[]{:S(2)}) copy-start(bf16[128,768]{1,0:T(8,128)(2,1)} %get-tuple-element.54) | copy-start | bytes 589828
  327.5 8.9 %copy-start.44 = (bf16[128,768]{1,0:T(8,128)(2,1)S(1)}, bf16[128,768]{1,0:T(8,128)(2,1)}, u32[]{:S(2)}) copy-start(bf16[128,768]{1,0:T(8,128)(2,1)} %copy-done.43) | copy-start | bytes 589828
  340.6 6.4 copy-start.9
  340.6 7.6 %slice-start.8 = ((s8[4718592]{0:T(1024)(128)(4,1)}), s8[4194304]{0:T(1024)(128)(4,1)S(1)}, s32[]{:S(2)}) async-start(s8[4718592]{0:T(1024)(128)(4,1)} %bitcast.170), calls=%async_computation.17 | async-start | bytes 8388608
  482.9 45.1 %copy-start.18 = (f32[128,768]{1,0:T(8,128)S(1)}, f32[128,768]{1,0:T(8,128)}, u32[]{:S(2)}) copy-start(f32[128,768]{1,0:T(8,128)} %get-tuple-element.55) | copy-start | bytes 1179652
  482.9 45.1 %copy-start.19 = (f32[128,768]{1,0:T(8,128)S(1)}, f32[128,768]{1,0:T(8,128)}, u32[]{:S(2)}) copy-start(f32[128,768]{1,0:T(8,128)} %get-tuple-element.85) | copy-start | bytes 1179652
  (55 other events, 153.7 us)
Sparse Core Ops, SparseCore 0:
  11.8 105.9 all-gather.3
  127.2 58.4 all-gather.7
  188.4 58.6 all-gather.5
  301.3 72.7 reduce-scatter.11
  377.5 73.3 reduce-scatter.9
  471.5 158.2 reduce-scatter.13

commit v6 on v4

--- a/solution.py
+++ b/solution.py
@@ -5,6 +5,7 @@
 import jax.numpy as jnp
 from jax import lax
 from jax.sharding import PartitionSpec as P
+from jax.experimental.layout import Layout, with_layout_constraint
 
 HEADS = 12
 HEAD = 64
@@ -206,10 +207,11 @@
     cosine_part, sine_part = rotary_tables(jnp.tile(positions, batches))
     gelu_tanh = partial(jax.nn.gelu, approximate=True)
     lane_pad = 128 - 4
-    widths = (3 * model_width, model_width, ff_width, ff_width, 2, 2, lane_pad)
+    widths = (3 * model_width, 2, 2, lane_pad, model_width, ff_width, ff_width)
     offsets = [0]
     for width in widths:
         offsets.append(offsets[-1] + width)
+    late_width = offsets[4]
 
     def pieces(packed_rows):
         return [packed_rows[:, offsets[i] : offsets[i + 1]] for i in range(len(widths))]
@@ -217,17 +219,17 @@
     packed = jnp.concatenate(
         [
             w_qkv,
+            ln_gains,
+            ln_biases,
+            jnp.zeros((shard_rows, lane_pad), w_qkv.dtype),
             w_out,
             w_up,
             w_down.reshape(shard_rows, ff_width),
-            ln_gains,
-            ln_biases,
-            jnp.zeros((shard_rows, lane_pad), w_qkv.dtype),
         ],
         axis=1,
     )
     gathered = lax.all_gather(packed, ("seq", "fsdp"), axis=0, tiled=True)
-    full_qkv, full_out, full_up, down_rows, gain_rows, bias_rows, _ = pieces(gathered)
+    full_qkv, gain_rows, bias_rows, _, full_out, full_up, down_rows = pieces(gathered)
     full_down = down_rows.reshape(ff_width, model_width)
     norm_gains = gain_rows.astype(jnp.float32)
     norm_biases = bias_rows.astype(jnp.float32)
@@ -244,12 +246,23 @@
     own_kv = jnp.concatenate([keys_own, values_own], axis=1).reshape(
         batches, row_count, 2 * model_width
     )
+    queries4 = queries.reshape(batches, row_count, HEADS, HEAD)
+    earlier = history[:, :, 0].reshape(4, all_rows, model_width).astype(jnp.float32)
+    usable = (positions[None, :] < slot_lengths[:, None]).reshape(all_rows, 1)
+    grad_next = jnp.where(
+        usable, cotangent[:, 0].reshape(all_rows, model_width).astype(jnp.float32), 0.0
+    )
+    history_part = jnp.einsum("j,jrd->rd", depth_weights[:4], earlier)
+    grad_history = (depth_weights[:4, None, None] * grad_next[None]).astype(jnp.bfloat16)
+    grad_history = grad_history.reshape(4, batches, 1, row_count, model_width)
+    out_grad = depth_weights[4] * grad_next
+    out_low = out_grad.astype(jnp.bfloat16)
+
     kv_all = lax.all_gather(jnp.swapaxes(own_kv, 0, 1), "seq", axis=0, tiled=True)
     keys4 = jnp.swapaxes(kv_all[:, :, :model_width], 0, 1).reshape(batches, slot_len, HEADS, HEAD)
     values4 = jnp.swapaxes(kv_all[:, :, model_width:], 0, 1).reshape(
         batches, slot_len, HEADS, HEAD
     )
-    queries4 = queries.reshape(batches, row_count, HEADS, HEAD)
     attended4, probabilities, probabilities_low = jax.vmap(
         slot_attention, in_axes=(0, 0, 0, None, 0)
     )(queries4, keys4, values4, positions, slot_lengths)
@@ -259,20 +272,6 @@
     hidden = jnp.dot(second_low, full_up, preferred_element_type=jnp.float32)
     hidden_low = gelu_tanh(hidden).astype(jnp.bfloat16)
     block_out = residual + jnp.dot(hidden_low, full_down, preferred_element_type=jnp.float32)
-    earlier = history[:, :, 0].reshape(4, all_rows, model_width).astype(jnp.float32)
-    usable = (positions[None, :] < slot_lengths[:, None]).reshape(all_rows, 1)
-    grad_next = jnp.where(
-        usable, cotangent[:, 0].reshape(all_rows, model_width).astype(jnp.float32), 0.0
-    )
-    combined = depth_weights[4] * block_out + jnp.einsum("j,jrd->rd", depth_weights[:4], earlier)
-    next_input = combined.astype(jnp.bfloat16).reshape(batches, 1, row_count, model_width)
-    grad_history = (depth_weights[:4, None, None] * grad_next[None]).astype(jnp.bfloat16)
-    grad_history = grad_history.reshape(4, batches, 1, row_count, model_width)
-    depth_terms = jnp.concatenate(
-        [jnp.einsum("jrd,rd->j", earlier, grad_next), jnp.sum(block_out * grad_next)[None]]
-    )
-    out_grad = depth_weights[4] * grad_next
-    out_low = out_grad.astype(jnp.bfloat16)
     hidden_grad = jnp.einsum("rd,fd->rf", out_low, full_down, preferred_element_type=jnp.float32)
     _, gelu_pullback = jax.vjp(gelu_tanh, hidden)
     up_low = gelu_pullback(hidden_grad)[0].astype(jnp.bfloat16)
@@ -305,14 +304,29 @@
     )
     key_value_all = jnp.swapaxes(key_value_all, 0, 1).reshape(all_rows, 2 * model_width)
     key_value_all = key_value_all.astype(jnp.float32)
+    query_grad = query_grad4.reshape(all_rows, model_width)
+    combined = depth_weights[4] * block_out + history_part
+    next_input = combined.astype(jnp.bfloat16).reshape(batches, 1, row_count, model_width)
+    depth_terms = jnp.concatenate(
+        [jnp.einsum("jrd,rd->j", earlier, grad_next), jnp.sum(block_out * grad_next)[None]]
+    )
     grad_down = jnp.einsum("rf,rd->fd", hidden_low, out_low, preferred_element_type=jnp.float32)
     grad_up = jnp.einsum("rd,rf->df", second_low, up_low, preferred_element_type=jnp.float32)
     grad_outproj = jnp.einsum(
         "rc,rd->cd", attended_low, branch_low, preferred_element_type=jnp.float32
     )
+    early_grads = jnp.concatenate(
+        [
+            jnp.zeros((model_width, late_width), jnp.float32),
+            grad_outproj,
+            grad_up,
+            grad_down.reshape(model_width, ff_width),
+        ],
+        axis=1,
+    ).astype(jnp.bfloat16)
     qkv_low = jnp.concatenate(
         [
-            rotate(query_grad4.reshape(all_rows, model_width), cosine_part, -sine_part),
+            rotate(query_grad, cosine_part, -sine_part),
             rotate(key_value_all[:, :model_width], cosine_part, -sine_part),
             key_value_all[:, model_width:],
         ],
@@ -324,27 +338,36 @@
     input_part, gain_one, bias_one = first_pullback(first_grad)
     grad_input = (residual_grad + input_part).astype(jnp.bfloat16)
     grad_input = grad_input.reshape(batches, 1, row_count, model_width)
-    packed_grads = jnp.concatenate(
+    late_grads = jnp.concatenate(
         [
             grad_qkv,
-            grad_outproj,
-            grad_up,
-            grad_down.reshape(model_width, ff_width),
             jnp.stack([gain_one, gain_two], axis=1),
             jnp.stack([bias_one, bias_two], axis=1),
             jnp.zeros((model_width, lane_pad), jnp.float32),
         ],
         axis=1,
     ).astype(jnp.bfloat16)
+    packed_grads = lax.dynamic_update_slice(early_grads, late_grads, (0, 0))
     device_count = model_width // shard_rows
+    row_major = Layout(major_to_minor=(0, 1, 2))
     scattered = lax.psum_scatter(
-        packed_grads.reshape(device_count, shard_rows, offsets[-1]),
+        with_layout_constraint(
+            packed_grads.reshape(device_count, shard_rows, offsets[-1]), row_major
+        ),
         ("seq", "fsdp"),
         scatter_dimension=0,
         tiled=False,
     )
-    owned = pieces(scattered.astype(jnp.float32))[:6]
-    owned[3] = owned[3].reshape(-1, model_width)
+    scattered = with_layout_constraint(scattered, Layout(major_to_minor=(0, 1)))
+    full_pieces = pieces(scattered.astype(jnp.float32))
+    owned = [
+        full_pieces[0],
+        full_pieces[4],
+        full_pieces[5],
+        full_pieces[6].reshape(-1, model_width),
+        full_pieces[1],
+        full_pieces[2],
+    ]
     depth_total = lax.psum(depth_terms, ("seq", "fsdp"))
     return (next_input, grad_input, grad_history, *owned, depth_total)
 

time: 647 us -> 638 us (0.986)
  local copies, waits for them, and re-layouts: 104 us -> 82.8 us
  other arithmetic: 34.6 us -> 44.1 us
  matrix products: 77.9 us -> 86.9 us
    unnamed x6 -> x5, waiting for transfers between devices: 197 us -> 113 us
    reduce_scatter x0 -> x1, waiting for transfers between devices: none -> 78.5 us  [local(): lax.psum_scatter(jnp.swapaxes(key_value_parts, 0, 1), 'seq', scatter_dime...]
    concatenate x7 -> x3, local copies, waits for them, and re-layouts: 38.5 us -> 9.03 us  [the longest x1 6.58 us: local(): jnp.concatenate([grad_qkv, jnp.stack([gain_one, gain_two], axis=1), jnp.s...]
    reshape x3 -> x4, local copies, waits for them, and re-layouts: 2.65 us -> 18.7 us  [the longest x1 8.57 us: local(): grad_down.reshape(model_width, ff_width)]
    unnamed x121 -> x113, local copies, waits for them, and re-layouts: 21.3 us -> 8.28 us
  transfers between devices with their start and end apart: 4 -> 4, of which waited for: 4 -> 4; matrix products, arithmetic and copies ran while one was open for 10% -> 12% of each run, Pallas kernels for 0% -> 0%
where the time goes in v6:
time: 638 us; the launch traced here: 632 us
  waiting for transfers between devices  364 us (57%)
  matrix products  86.9 us (14%)
  local copies, waits for them, and re-layouts  82.8 us (13%)
  other arithmetic  44.1 us (7%)
  blocking collectives  39.5 us (6%)
  between operations  14.8 us (2%)
    unnamed x5, waiting for transfers between devices  113 us
    all_gather x1, waiting for transfers between devices, local(): gathered = lax.all_gather(packed, ('seq', 'fsdp'), axis=0, tiled=True)  102 us
    reduce_scatter x1, waiting for transfers between devices, local(): lax.psum_scatter(jnp.swapaxes(key_value_parts, 0, 1), 'seq', scatter_dime...  78.5 us
    all_gather x1, waiting for transfers between devices, local(): lax.all_gather(jnp.swapaxes(own_kv, 0, 1), 'seq', axis=0, tiled=True)  70.2 us
    psum x1, blocking collectives, local(): depth_total = lax.psum(depth_terms, ('seq', 'fsdp'))  39.5 us
  transfers between devices with their start and end apart: 4, of which 4 were waited for; matrix products, arithmetic and copies ran while one was open for 12% of the time, Pallas kernels for 0%

profile of v6, /device:TPU:0, one launch (start us, length us, event | category | flops | bytes accessed | tf_op | source)
XLA Modules:
  0.0 632.1 jit_solution(10593594792310534995)
XLA Ops:
  15.5 102.3 %all-gather.3.cloned.1.call-done = bf16[768,9344]{1,0:T(8,128)(2,1)} async-done(((bf16[24,9344]{1,0:T(8,128)(2,1)}), bf16[768,9344]{1,0:T(8,128)(2,1)}) %all-gather.3.cloned.1.call-update) | async-done | bytes 14352400 | tf_op jit(solution)/shard_map/all_gather | solution.py:231
  119.9 3.2 fusion.14
  135.0 4.8 slice.157
  139.8 8.7 %reshape.393 = bf16[3072,768]{1,0:T(8,128)(2,1)} reshape(bf16[768,3072]{1,0:T(8,128)(2,1)} %slice.157) | data formatting | bytes 9437184 | tf_op jit(solution)/shard_map/reshape | solution.py:233
  148.5 5.5 fusion.59
  154.0 70.2 %all-gather.5.cloned.1.call-done = bf16[1024,2,1536]{2,0,1:T(8,128)(2,1)} async-done(((bf16[128,2,1536]{2,0,1:T(8,128)(2,1)}), bf16[1024,2,1536]{2,0,1:T(8,128)(2,1)}) %all-gather.5.cloned.1.call-update) | async-done | bytes 6291472 | tf_op jit(solution)/shard_map/all_gather | solution.py:261
  224.2 5.8 slice_bitcast_fusion
  230.0 3.2 copy.65
  233.2 3.6 select_reduce_fusion.1
  236.8 4.0 select_reduce_fusion
  242.0 4.7 copy.63
  246.6 9.1 %bitcast_convert_fusion = (bf16[2,128,12,64]{1,3,2,0:T(8,128)(2,1)S(1)}, f32[2,12,64,128]{3,2,1,0:T(8,128)}) fusion(bf16[2,1024,12,64]{1,3,2,0:T(8,128)(2,1)} %bitcast.151, f32[2,12,128,1024]{3,2,1,0:T(8,128)} %copy-done, f32[2,12,128]{2,1,0:T(8,128)} %log_add_fusion, pred[2,128,1024]{2,1,0:T(8,128)(4,1)} %broadcast_and_fusion), kind=kOutput, calls=%fused_computation.56 | convolution fusion | flops 415432704 | bytes 17182720 | tf_op jit(solution)/shard_map/vmap(hrk,khd->rhd)/dot_general | solution.py:164
  259.2 5.5 fusion.11
  264.8 6.3 multiply_reduce_fusion.2
  271.5 4.3 multiply_reduce_fusion.1
  284.4 9.5 %convolution_convert_fusion.3 = bf16[2,12,64,1024]{3,2,1,0:T(8,128)(2,1)} fusion(bf16[2,128,12,64]{1,0,3,2:T(2,128)(2,1)} %reshape.395, f32[2,12,128,1024]{3,2,1,0:T(8,128)} %copy-done, f32[2,12,128]{2,1,0:T(8,128)} %log_add_fusion, pred[2,128,1024]{2,1,0:T(8,128)(4,1)} %broadcast_and_fusion), kind=kOutput, calls=%fused_computation.33 | convolution fusion | flops 416808960 | bytes 16396288 | tf_op jit(solution)/shard_map/vmap(hrk,rhd->khd)/dot_general | solution.py:180
  294.0 7.8 %multiply_convert_fusion = bf16[2,12,128,1024]{3,2,1,0:T(8,128)(2,1)S(1)} fusion(f32[2,12,128,1024]{3,2,1,0:T(8,128)} %copy-done, f32[2,12,128]{2,1,0:T(8,128)S(1)} %fusion.21, f32[2,12,128]{2,1,0:T(8,128)S(1)} %copy-done.35, pred[2,128,1024]{2,1,0:T(8,128)(4,1)S(1)} %copy-done.11, bf16[2,1024,12,64]{1,3,2,0:T(8,128)(2,1)S(1)} %bitcast.152, ...), kind=kOutput, calls=%fused_computation.1 | convolution fusion | flops 421527552 | bytes 22700032 | tf_op jit(solution)/shard_map/vmap(rhd,khd->hrk)/dot_general | solution.py:171
  305.5 4.7 copy.73
  310.2 4.6 copy.74
  314.8 5.9 maximum_bitcast_fusion
  321.6 5.2 fusion.18
  328.6 5.1 convolution_convert_fusion.1
  333.7 8.6 %reshape.403 = bf16[768,3072]{1,0:T(8,128)(2,1)} reshape(bf16[3072,768]{1,0:T(8,128)(2,1)} %convolution_convert_fusion.1) | data formatting | bytes 9437184 | tf_op jit(solution)/shard_map/reshape | solution.py:323
  346.3 3.2 convolution_convert_fusion.2
  349.5 9.0 %pad_maximum_fusion = bf16[768,9344]{1,0:T(8,128)(2,1)} fusion(bf16[768,3072]{1,0:T(8,128)(2,1)S(1)} %bitcast.148, bf16[768,3072]{1,0:T(8,128)(2,1)S(1)} %convolution_convert_fusion.2, bf16[768,768]{1,0:T(8,128)(2,1)S(1)} %copy-done.7, bf16[9344]{0:T(1024)(128)(2,1)S(1)} %copy-done.30), kind=kLoop, calls=%fused_computation | loop fusion | flops 57409536 | bytes 24987904 | tf_op jit(solution)/shard_map/concatenate | solution.py:318
  358.5 78.5 %reduce-scatter.5.cloned.1.call-done = bf16[128,2,1536]{2,0,1:T(8,128)(2,1)} async-done(((bf16[1024,2,1536]{2,0,1:T(8,128)(2,1)}), bf16[128,2,1536]{2,0,1:T(8,128)(2,1)}) %reduce-scatter.5.cloned.1.call-update) | async-done | bytes 786448 | tf_op jit(solution)/shard_map/reduce_scatter | solution.py:302
  442.5 3.9 convolution_convert_fusion
  446.4 3.3 fusion.53
  450.6 6.6 %concatenate.50 = bf16[768,2432]{1,0:T(8,128)(2,1)} concatenate(bf16[768,2304]{1,0:T(8,128)(2,1)} %convolution_convert_fusion, bf16[768,1]{1,0:T(8,128)(2,1)S(1)} %stack.20, bf16[768,1]{1,0:T(8,128)(2,1)S(1)} %copy-done.24, bf16[768,1]{1,0:T(8,128)(2,1)S(1)} %stack.22, bf16[768,1]{1,0:T(8,128)(2,1)S(1)} %copy-done.25, bf16[768,124]{1,0:T(8,128)(2,1)S(1)} %broadcast_in_dim.104), dimensions={1} | concatenate | bytes 7471104 | tf_op jit(solution)/shard_map/concatenate | solution.py:341
  457.2 4.2 constant_dynamic-update-slice_fusion
  466.9 39.5 %psum.7 = f32[5]{0:T(128)} all-reduce(f32[5]{0:T(128)S(1)} %pad_maximum_fusion.8), channel_id=1, replica_groups=mesh['seq'=8,'fsdp'=4] {'seq','fsdp'}, use_global_device_ids=true, to_apply=%region_17.18 | all-reduce | flops 5 | bytes 40 | tf_op jit(solution)/shard_map/psum | solution.py:371
  507.5 112.6 %reduce-scatter.7.cloned.1.call-done = bf16[1,24,9344]{2,1,0:T(8,128)(2,1)} async-done(((bf16[32,24,9344]{2,1,0:T(8,128)(2,1)}), bf16[1,24,9344]{2,1,0:T(8,128)(2,1)}) %reduce-scatter.7.cloned.1.call-update) | async-done | bytes 448528
  (197 shorter events, 64.0 us)
Async XLA Ops:
  7.2 112.4 %copy-start.2 = (bf16[2,1,128,768]{3,2,1,0:T(8,128)(2,1)S(1)}, bf16[2,1,128,768]{3,2,1,0:T(8,128)(2,1)}, u32[]{:S(2)}) copy-start(bf16[2,1,128,768]{3,2,1,0:T(8,128)(2,1)} %param.11) | copy-start | bytes 1179652
  7.2 110.6 %all-gather.3.cloned.1.call-start = ((), (), s32[]{:S(2)}) async-start(), calls=%async_computation.2 | async-start | bytes 14800896 | tf_op jit(solution)/shard_map/all_gather | solution.py:231
  11.6 212.5 %all-gather.5.cloned.1.call-start = ((), (), s32[]{:S(2)}) async-start(), calls=%async_computation.3 | async-start | bytes 7077888 | tf_op jit(solution)/shard_map/all_gather | solution.py:261
  13.4 109.8 %copy-start.31 = (f32[256]{0:T(256)}, f32[256]{0:T(256)S(1)}, u32[]{:S(2)}) copy-start(f32[256]{0:T(256)S(1)} %get-tuple-element.84) | copy-start | bytes 3076
  14.6 108.5 %copy-start.38 = (f32[2,128]{1,0:T(2,128)}, f32[2,128]{1,0:T(2,128)S(1)}, u32[]{:S(2)}) copy-start(f32[2,128]{1,0:T(2,128)S(1)} %multiply_reduce_fusion.7) | copy-start | bytes 3076
  14.6 108.5 %copy-start.33 = (f32[256]{0:T(256)}, f32[256]{0:T(256)S(1)}, u32[]{:S(2)}) copy-start(f32[256]{0:T(256)S(1)} %bitcast_rsqrt_fusion) | copy-start | bytes 3076
  123.9 8.0 %copy-start.17 = (bf16[2,1,128,768]{3,2,1,0:T(8,128)(2,1)S(1)}, bf16[2,1,128,768]{3,2,1,0:T(8,128)(2,1)}, u32[]{:S(2)}) copy-start(bf16[2,1,128,768]{3,2,1,0:T(8,128)(2,1)} %param.13) | copy-start | bytes 1179652
  125.7 7.0 %copy-start.14 = (bf16[4,2,1,128,768]{4,3,2,1,0:T(8,128)(2,1)S(1)}, bf16[4,2,1,128,768]{4,3,2,1,0:T(8,128)(2,1)}, u32[]{:S(2)}) copy-start(bf16[4,2,1,128,768]{4,3,2,1,0:T(8,128)(2,1)} %param.12) | copy-start | bytes 4718596
  126.9 310.2 %reduce-scatter.5.cloned.1.call-start = ((), (), s32[]{:S(2)}) async-start(), calls=%async_computation.4 | async-start | bytes 7077888 | tf_op jit(solution)/shard_map/reduce_scatter | solution.py:302
  128.3 11.5 %copy-start.42 = (pred[2,128]{1,0:T(4,128)(4,1)}, pred[2,128]{1,0:T(4,128)(4,1)S(1)}, u32[]{:S(2)}) copy-start(pred[2,128]{1,0:T(4,128)(4,1)S(1)} %broadcast_compare_fusion) | copy-start | bytes 772
  257.0 14.5 %slice-start = ((s8[4718592]{0:T(1024)(128)(4,1)}), s8[4194304]{0:T(1024)(128)(4,1)S(1)}, s32[]{:S(2)}) async-start(s8[4718592]{0:T(1024)(128)(4,1)} %bitcast.145), calls=%async_computation.6 | async-start | bytes 8388608
  259.0 12.4 %copy-start.3 = (f32[256,768]{1,0:T(8,128)}, f32[256,768]{1,0:T(8,128)S(1)}, u32[]{:S(2)}) copy-start(f32[256,768]{1,0:T(8,128)S(1)} %get-tuple-element.91) | copy-start | bytes 2359300
  259.2 11.8 %copy-start.36 = (f32[256]{0:T(256)}, f32[256]{0:T(256)S(1)}, u32[]{:S(2)}) copy-start(f32[256]{0:T(256)S(1)} %fusion.41) | copy-start | bytes 3076
  259.2 12.2 %slice-start.1 = ((s8[4718592]{0:T(1024)(128)(4,1)}), s8[524288]{0:T(1024)(128)(4,1)S(1)}, s32[]{:S(2)}) async-start(s8[4718592]{0:T(1024)(128)(4,1)} %bitcast.145), calls=%async_computation.7 | async-start | bytes 1048576
  264.7 6.7 %copy-start.48 = (f32[256,3072]{1,0:T(8,128)}, f32[256,3072]{1,0:T(8,128)S(1)}, u32[]{:S(2)}) copy-start(f32[256,3072]{1,0:T(8,128)S(1)} %get-tuple-element.93) | copy-start | bytes 9437188
  264.7 6.7 %copy-start.18 = (bf16[2,1,128,768]{3,2,1,0:T(8,128)(2,1)S(1)}, bf16[2,1,128,768]{3,2,1,0:T(8,128)(2,1)}, u32[]{:S(2)}) copy-start(bf16[2,1,128,768]{3,2,1,0:T(8,128)(2,1)} %param.13) | copy-start | bytes 1179652
  264.7 6.7 %copy-start.46 = (pred[256]{0:T(512)(128)(4,1)S(1)}, pred[256]{0:T(512)(128)(4,1)}, u32[]{:S(2)}) copy-start(pred[256]{0:T(512)(128)(4,1)} %fusion.73) | copy-start | bytes 772
  264.8 6.7 %copy-start.47 = (f32[1,256,768]{2,0,1:T(1,128)S(1)}, f32[1,256,768]{2,0,1:T(1,128)}, u32[]{:S(2)}) copy-start(f32[1,256,768]{2,0,1:T(1,128)} %fusion.16) | copy-start | bytes 2359300
  284.3 9.6 %copy-start.23 = (f32[2,12,64,128]{3,2,1,0:T(8,128)S(1)}, f32[2,12,64,128]{3,2,1,0:T(8,128)}, u32[]{:S(2)}) copy-start(f32[2,12,64,128]{3,2,1,0:T(8,128)} %get-tuple-element.89) | copy-start | bytes 2359300
  284.3 9.7 %copy-start.8 = (bf16[2,1024,768]{1,2,0:T(8,128)(2,1)S(1)}, bf16[2,1024,768]{1,2,0:T(8,128)(2,1)}, u32[]{:S(2)}) copy-start(bf16[2,1024,768]{1,2,0:T(8,128)(2,1)} %copy.63) | copy-start | bytes 9437188
  284.3 9.7 %copy-start.11 = (pred[2,128,1024]{2,1,0:T(8,128)(4,1)S(1)}, pred[2,128,1024]{2,1,0:T(8,128)(4,1)}, u32[]{:S(2)}) copy-start(pred[2,128,1024]{2,1,0:T(8,128)(4,1)} %broadcast_and_fusion) | copy-start | bytes 786436
  284.3 9.7 %copy-start.20 = (bf16[2,128,12,64]{1,0,3,2:T(2,128)(2,1)S(1)}, bf16[2,128,12,64]{1,0,3,2:T(2,128)(2,1)}, u32[]{:S(2)}) copy-start(bf16[2,128,12,64]{1,0,3,2:T(2,128)(2,1)} %reshape.395) | copy-start | bytes 1179652
  284.3 9.7 %copy-start.35 = (f32[2,12,128]{2,1,0:T(8,128)S(1)}, f32[2,12,128]{2,1,0:T(8,128)}, u32[]{:S(2)}) copy-start(f32[2,12,128]{2,1,0:T(8,128)} %log_add_fusion) | copy-start | bytes 36868
  294.0 7.9 %copy-start.12 = (bf16[256,12,32]{0,2,1:T(8,128)(2,1)S(1)}, bf16[256,12,32]{0,2,1:T(8,128)(2,1)}, u32[]{:S(2)}) copy-start(bf16[256,12,32]{0,2,1:T(8,128)(2,1)} %get-tuple-element.67) | copy-start | bytes 589828
  294.0 7.9 %copy-start.13 = (bf16[256,12,32]{0,2,1:T(8,128)(2,1)S(1)}, bf16[256,12,32]{0,2,1:T(8,128)(2,1)}, u32[]{:S(2)}) copy-start(bf16[256,12,32]{0,2,1:T(8,128)(2,1)} %get-tuple-element.68) | copy-start | bytes 589828
  320.7 299.4 %reduce-scatter.7.cloned.1.call-start = ((), (), s32[]{:S(2)}) async-start(), calls=%async_computation.5 | async-start | bytes 14800896
  321.6 7.0 %copy-start.22 = (f32[256,768]{1,0:T(8,128)S(1)}, f32[256,768]{1,0:T(8,128)}, u32[]{:S(2)}) copy-start(f32[256,768]{1,0:T(8,128)} %get-tuple-element.76) | copy-start | bytes 2359300
  321.6 7.0 %copy-start.49 = (f32[256,3072]{1,0:T(8,128)S(1)}, f32[256,3072]{1,0:T(8,128)}, u32[]{:S(2)}) copy-start(f32[256,3072]{1,0:T(8,128)} %copy-done.48) | copy-start | bytes 9437188
  333.7 8.6 %copy-start.6 = (f32[256,768]{1,0:T(8,128)S(1)}, f32[256,768]{1,0:T(8,128)}, u32[]{:S(2)}) copy-start(f32[256,768]{1,0:T(8,128)} %copy-done.5) | copy-start | bytes 2359300
  333.7 8.6 %copy-start.16 = (bf16[2,128,12,64]{1,0,3,2:T(2,128)(2,1)S(1)}, bf16[2,128,12,64]{1,0,3,2:T(2,128)(2,1)}, u32[]{:S(2)}) copy-start(bf16[2,128,12,64]{1,0,3,2:T(2,128)(2,1)} %copy-done.15) | copy-start | bytes 1179652
  358.5 82.9 %copy-start.28 = (f32[256,32]{0,1:T(8,128)S(1)}, f32[256,32]{0,1:T(8,128)}, u32[]{:S(2)}) copy-start(f32[256,32]{0,1:T(8,128)} %get-tuple-element.83) | copy-start | bytes 98308
  358.5 82.9 %copy-start.29 = (f32[256,32]{0,1:T(8,128)S(1)}, f32[256,32]{0,1:T(8,128)}, u32[]{:S(2)}) copy-start(f32[256,32]{0,1:T(8,128)} %get-tuple-element.81) | copy-start | bytes 98308
  (26 other events, 90.0 us)
Sparse Core Ops, SparseCore 0:
  11.8 105.9 all-gather.2
  127.0 97.1 all-gather.4
  320.8 116.1 reduce-scatter.4
  461.5 158.5 reduce-scatter.6

commit v7 on v6

--- a/solution.py
+++ b/solution.py
@@ -6,6 +6,8 @@
 from jax import lax
 from jax.sharding import PartitionSpec as P
 from jax.experimental.layout import Layout, with_layout_constraint
+from jax.experimental import pallas as pl
+from jax.experimental.pallas import tpu as pltpu
 
 HEADS = 12
 HEAD = 64
@@ -181,6 +183,136 @@
         "hrk,rhd->khd", probabilities_low, grads3, preferred_element_type=jnp.float32
     )
     return query_grad, key_grad, value_grad
+
+
+def _pair_masks(scalars_ref, micro, row_count, key_count):
+    length = scalars_ref[micro]
+    first_row = scalars_ref[scalars_ref.shape[0] - 1]
+    query_pos = first_row + lax.broadcasted_iota(jnp.int32, (row_count, key_count), 0)
+    key_pos = lax.broadcasted_iota(jnp.int32, (row_count, key_count), 1)
+    return (key_pos <= query_pos) & (key_pos < length)
+
+
+def _forward_kernel(scalars_ref, q_ref, k_ref, v_ref, out_ref, lse_ref):
+    micro = pl.program_id(0)
+    row_count = q_ref.shape[0]
+    key_count = k_ref.shape[0]
+    allowed = _pair_masks(scalars_ref, micro, row_count, key_count)
+    for half in range(2):
+        lanes = slice(half * HEAD, (half + 1) * HEAD)
+        q_head = q_ref[:, lanes]
+        k_head = k_ref[:, lanes]
+        v_head = v_ref[:, lanes]
+        scores = lax.dot_general(
+            q_head, k_head, (((1,), (1,)), ((), ())), preferred_element_type=jnp.float32
+        ) * HEAD ** (-0.5)
+        masked = jnp.where(allowed, scores, masked_value)
+        top = jnp.max(masked, axis=1, keepdims=True)
+        kept = jnp.where(allowed, jnp.exp(masked - top), 0.0)
+        log_total = top + jnp.log(jnp.sum(kept, axis=1, keepdims=True))
+        probabilities = jnp.where(allowed, jnp.exp(scores - log_total), 0.0)
+        attended = jnp.dot(
+            probabilities.astype(jnp.bfloat16), v_head, preferred_element_type=jnp.float32
+        )
+        out_ref[:, lanes] = attended
+        lse_ref[:, lanes] = jnp.broadcast_to(log_total, (row_count, HEAD))
+
+
+def _backward_kernel(
+    scalars_ref, q_ref, k_ref, v_ref, do_ref, o_ref, lse_ref, dq_ref, kv_grad_ref
+):
+    micro = pl.program_id(0)
+    row_count = q_ref.shape[0]
+    key_count = k_ref.shape[0]
+    allowed = _pair_masks(scalars_ref, micro, row_count, key_count)
+    for half in range(2):
+        lanes = slice(half * HEAD, (half + 1) * HEAD)
+        q_head = q_ref[:, lanes]
+        k_head = k_ref[:, lanes]
+        v_head = v_ref[:, lanes]
+        grad_head = do_ref[:, lanes]
+        scores = lax.dot_general(
+            q_head, k_head, (((1,), (1,)), ((), ())), preferred_element_type=jnp.float32
+        ) * HEAD ** (-0.5)
+        log_total = lse_ref[:, half * HEAD : half * HEAD + 1]
+        probabilities = jnp.where(allowed, jnp.exp(scores - log_total), 0.0)
+        probabilities_low = probabilities.astype(jnp.bfloat16)
+        prob_grad = lax.dot_general(
+            grad_head, v_head, (((1,), (1,)), ((), ())), preferred_element_type=jnp.float32
+        )
+        row_delta = jnp.sum(
+            grad_head.astype(jnp.float32) * o_ref[:, lanes], axis=1, keepdims=True
+        )
+        score_low = (probabilities * (prob_grad - row_delta)).astype(jnp.bfloat16)
+        dq_ref[:, lanes] = jnp.dot(
+            score_low, k_head, preferred_element_type=jnp.float32
+        ) * HEAD ** (-0.5)
+        key_grad = lax.dot_general(
+            score_low, q_head, (((0,), (0,)), ((), ())), preferred_element_type=jnp.float32
+        ) * HEAD ** (-0.5)
+        value_grad = lax.dot_general(
+            probabilities_low, grad_head, (((0,), (0,)), ((), ())),
+            preferred_element_type=jnp.float32,
+        )
+        kv_grad_ref[:, lanes] = key_grad.astype(jnp.bfloat16)
+        kv_grad_ref[:, 2 * HEAD + half * HEAD : 2 * HEAD + (half + 1) * HEAD] = value_grad.astype(
+            jnp.bfloat16
+        )
+
+
+def attention_forward(scalars, queries, kv_flat, batches):
+    all_rows, model_width = queries.shape
+    row_count = all_rows // batches
+    key_count = kv_flat.shape[0]
+    pairs = model_width // (2 * HEAD)
+    micro_blocks = kv_flat.shape[1] // batches // (2 * HEAD)
+    row_spec = pl.BlockSpec((row_count, 2 * HEAD), lambda m, p, s: (m, p))
+    key_spec = pl.BlockSpec((key_count, 2 * HEAD), lambda m, p, s: (0, m * micro_blocks + p))
+    value_spec = pl.BlockSpec(
+        (key_count, 2 * HEAD), lambda m, p, s: (0, m * micro_blocks + pairs + p)
+    )
+    return pl.pallas_call(
+        _forward_kernel,
+        grid_spec=pltpu.PrefetchScalarGridSpec(
+            num_scalar_prefetch=1,
+            grid=(batches, pairs),
+            in_specs=[row_spec, key_spec, value_spec],
+            out_specs=[row_spec, row_spec],
+        ),
+        out_shape=[
+            jax.ShapeDtypeStruct((all_rows, model_width), jnp.float32),
+            jax.ShapeDtypeStruct((all_rows, model_width), jnp.float32),
+        ],
+        name="attention_forward",
+    )(scalars, queries, kv_flat, kv_flat)
+
+
+def attention_backward(scalars, queries, kv_flat, grads, attended, log_totals, batches):
+    all_rows, model_width = queries.shape
+    row_count = all_rows // batches
+    key_count = kv_flat.shape[0]
+    pairs = model_width // (2 * HEAD)
+    micro_blocks = kv_flat.shape[1] // batches // (2 * HEAD)
+    row_spec = pl.BlockSpec((row_count, 2 * HEAD), lambda m, p, s: (m, p))
+    key_spec = pl.BlockSpec((key_count, 2 * HEAD), lambda m, p, s: (0, m * micro_blocks + p))
+    value_spec = pl.BlockSpec(
+        (key_count, 2 * HEAD), lambda m, p, s: (0, m * micro_blocks + pairs + p)
+    )
+    grad_spec = pl.BlockSpec((key_count, 4 * HEAD), lambda m, p, s: (0, m * pairs + p))
+    return pl.pallas_call(
+        _backward_kernel,
+        grid_spec=pltpu.PrefetchScalarGridSpec(
+            num_scalar_prefetch=1,
+            grid=(batches, pairs),
+            in_specs=[row_spec, key_spec, value_spec, row_spec, row_spec, row_spec],
+            out_specs=[row_spec, grad_spec],
+        ),
+        out_shape=[
+            jax.ShapeDtypeStruct((all_rows, model_width), jnp.float32),
+            jax.ShapeDtypeStruct(kv_flat.shape, jnp.bfloat16),
+        ],
+        name="attention_backward",
+    )(scalars, queries, kv_flat, kv_flat, grads, attended, log_totals)
 
 
 def local(
@@ -246,7 +378,6 @@
     own_kv = jnp.concatenate([keys_own, values_own], axis=1).reshape(
         batches, row_count, 2 * model_width
     )
-    queries4 = queries.reshape(batches, row_count, HEADS, HEAD)
     earlier = history[:, :, 0].reshape(4, all_rows, model_width).astype(jnp.float32)
     usable = (positions[None, :] < slot_lengths[:, None]).reshape(all_rows, 1)
     grad_next = jnp.where(
@@ -259,14 +390,12 @@
     out_low = out_grad.astype(jnp.bfloat16)
 
     kv_all = lax.all_gather(jnp.swapaxes(own_kv, 0, 1), "seq", axis=0, tiled=True)
-    keys4 = jnp.swapaxes(kv_all[:, :, :model_width], 0, 1).reshape(batches, slot_len, HEADS, HEAD)
-    values4 = jnp.swapaxes(kv_all[:, :, model_width:], 0, 1).reshape(
-        batches, slot_len, HEADS, HEAD
-    )
-    attended4, probabilities, probabilities_low = jax.vmap(
-        slot_attention, in_axes=(0, 0, 0, None, 0)
-    )(queries4, keys4, values4, positions, slot_lengths)
-    attended_low = attended4.reshape(all_rows, model_width).astype(jnp.bfloat16)
+    kv_flat = kv_all.reshape(slot_len, batches * 2 * model_width)
+    scalars = jnp.concatenate(
+        [slot_lengths.astype(jnp.int32), (lax.axis_index("seq") * row_count)[None].astype(jnp.int32)]
+    )
+    attended_rows, log_totals = attention_forward(scalars, queries, kv_flat, batches)
+    attended_low = attended_rows.astype(jnp.bfloat16)
     residual = inputs + jnp.dot(attended_low, full_out, preferred_element_type=jnp.float32)
     second_low = layer_norm(residual, norm_gains[:, 1], norm_biases[:, 1]).astype(jnp.bfloat16)
     hidden = jnp.dot(second_low, full_up, preferred_element_type=jnp.float32)
@@ -283,28 +412,16 @@
     attended_grad = jnp.einsum(
         "rd,cd->rc", branch_low, full_out, preferred_element_type=jnp.float32
     ).astype(jnp.bfloat16)
-    query_grad4, key_grad4, value_grad4 = jax.vmap(slot_attention_grads)(
-        queries4,
-        keys4,
-        values4,
-        attended_grad.reshape(batches, row_count, HEADS, HEAD),
-        attended4,
-        probabilities,
-        probabilities_low,
-    )
-    key_value_parts = jnp.concatenate(
-        [
-            key_grad4.reshape(batches, slot_len, model_width),
-            value_grad4.reshape(batches, slot_len, model_width),
-        ],
-        axis=2,
-    ).astype(jnp.bfloat16)
-    key_value_all = lax.psum_scatter(
-        jnp.swapaxes(key_value_parts, 0, 1), "seq", scatter_dimension=0, tiled=True
-    )
-    key_value_all = jnp.swapaxes(key_value_all, 0, 1).reshape(all_rows, 2 * model_width)
-    key_value_all = key_value_all.astype(jnp.float32)
-    query_grad = query_grad4.reshape(all_rows, model_width)
+    query_grad, kv_grad_flat = attention_backward(
+        scalars, queries, kv_flat, attended_grad, attended_rows, log_totals, batches
+    )
+    kv_grad_own = lax.psum_scatter(kv_grad_flat, "seq", scatter_dimension=0, tiled=True)
+    pairs = model_width // (2 * HEAD)
+    kv_grad_own = kv_grad_own.reshape(row_count, batches, pairs, 2, 2 * HEAD)
+    kv_grad_own = jnp.transpose(kv_grad_own, (1, 0, 3, 2, 4)).reshape(
+        all_rows, 2 * model_width
+    )
+    key_value_all = kv_grad_own.astype(jnp.float32)
     combined = depth_weights[4] * block_out + history_part
     next_input = combined.astype(jnp.bfloat16).reshape(batches, 1, row_count, model_width)
     depth_terms = jnp.concatenate(

time: 638 us -> 603 us (0.945)
  Pallas kernels: 0 us -> 38.3 us
  matrix products: 86.9 us -> 49.1 us
  other arithmetic: 44.1 us -> 25.1 us
  local copies, waits for them, and re-layouts: 82.8 us -> 67.1 us
    dot_general x6 -> x0, matrix products: 38.4 us -> none  [the longest x1 9.5 us: slot_attention_grads(): jnp.einsum('hrk,rhd->khd', probabilities_low, grads3, preferred_element_t...]
    pallas_call x0 -> x2, Pallas kernels: none -> 38.3 us  [the longest x1 19.7 us: attention_backward(): pl.pallas_call(_backward_kernel, grid_spec=pltpu.PrefetchScalarGridSpec(n...]
    transpose x3 -> x0, local copies, waits for them, and re-layouts: 13.7 us -> none  [the longest x2 8.99 us: local(): jnp.swapaxes(kv_all[:, :, :model_width], 0, 1)]
    reshape x4 -> x1, local copies, waits for them, and re-layouts: 12.5 us -> 1.69 us  [local(): jnp.concatenate([keys_own, values_own], axis=1)]
where the time goes in v7:
time: 603 us; the launch traced here: 602 us
  waiting for transfers between devices  368 us (61%)
  local copies, waits for them, and re-layouts  67.1 us (11%)
  matrix products  49.1 us (8%)
  blocking collectives  39.5 us (7%)
  Pallas kernels  38.3 us (6%)
  other arithmetic  25.1 us (4%)
  between operations  14.4 us (2%)
    unnamed x5, waiting for transfers between devices  113 us
    all_gather x1, waiting for transfers between devices, local(): gathered = lax.all_gather(packed, ('seq', 'fsdp'), axis=0, tiled=True)  103 us
    reduce_scatter x1, waiting for transfers between devices, local(): lax.psum_scatter(kv_grad_flat, 'seq', scatter_dimension=0, tiled=True)  80 us
    all_gather x1, waiting for transfers between devices, local(): lax.all_gather(jnp.swapaxes(own_kv, 0, 1), 'seq', axis=0, tiled=True)  72.2 us
    psum x1, blocking collectives, local(): depth_total = lax.psum(depth_terms, ('seq', 'fsdp'))  39.5 us
    pallas_call x1, Pallas kernels, attention_backward(): pl.pallas_call(_backward_kernel, grid_spec=pltpu.PrefetchScalarGridSpec(n...  19.7 us
    pallas_call x1, Pallas kernels, attention_forward(): pl.pallas_call(_forward_kernel, grid_spec=pltpu.PrefetchScalarGridSpec(nu...  18.6 us
  transfers between devices with their start and end apart: 4, of which 4 were waited for; matrix products, arithmetic and copies ran while one was open for 12% of the time, Pallas kernels for 0%

profile of v7, /device:TPU:0, one launch (start us, length us, event | category | flops | bytes accessed | tf_op | source)
XLA Modules:
  0.0 602.0 jit_solution(9459596642919483588)
XLA Ops:
  9.8 1.8 concatenate.41
  14.4 103.4 %all-gather.3.cloned.1.call-done = bf16[768,9344]{1,0:T(8,128)(2,1)} async-done(((bf16[24,9344]{1,0:T(8,128)(2,1)}), bf16[768,9344]{1,0:T(8,128)(2,1)}) %all-gather.3.cloned.1.call-update) | async-done | bytes 14352400 | tf_op jit(solution)/shard_map/all_gather | solution.py:363
  119.9 3.2 fusion.13
  126.9 1.7 copy.83
  131.4 2.2 fusion.15
  134.5 5.2 slice.147
  139.7 8.5 %reshape.325 = bf16[3072,768]{1,0:T(8,128)(2,1)} reshape(bf16[768,3072]{1,0:T(8,128)(2,1)} %slice.147) | data formatting | bytes 9437184 | tf_op jit(solution)/shard_map/reshape | solution.py:365
  148.3 5.4 fusion.41
  153.7 72.2 %all-gather.5.cloned.1.call-done = bf16[1024,2,1536]{2,1,0:T(2,128)(2,1)} async-done(((bf16[128,2,1536]{2,1,0:T(2,128)(2,1)}), bf16[1024,2,1536]{2,1,0:T(2,128)(2,1)}) %all-gather.5.cloned.1.call-update) | async-done | bytes 6291472 | tf_op jit(solution)/shard_map/all_gather | solution.py:392
  225.9 7.0 %copy.75 = bf16[128,8,2,1536]{3,1,2,0:T(8,128)(2,1)} copy(bf16[128,8,2,1536]{3,2,1,0:T(2,128)(2,1)} %bitcast.103) | data formatting | bytes 12582912
  232.8 18.6 %attention_forward.1 = (f32[256,768]{1,0:T(8,128)}, f32[256,768]{1,0:T(8,128)}) custom-call(s32[3]{0:T(128)} %pad_add_fusion.scalars_ref, bf16[256,768]{1,0:T(8,128)(2,1)} %copy.54.q_ref, bf16[1024,3072]{1,0:T(8,128)(2,1)} %bitcast.93, bf16[1024,3072]{1,0:T(8,128)(2,1)} %bitcast.94), custom_call_target="tpu_custom_call" | custom-call | tf_op jit(solution)/shard_map/attention_forward/pallas_call | solution.py:274
  251.4 2.2 fusion.40
  253.9 5.1 fusion.10
  259.1 5.7 multiply_reduce_fusion.2
  265.3 4.2 multiply_reduce_fusion.1
  269.5 2.5 convolution_convert_fusion.4.do_ref
  272.0 19.7 %attention_backward.1 = (f32[256,768]{1,0:T(8,128)}, bf16[1024,3072]{1,0:T(8,128)(2,1)}) custom-call(s32[3]{0:T(128)} %pad_add_fusion.scalars_ref, bf16[256,768]{1,0:T(8,128)(2,1)} %copy.54.q_ref, bf16[1024,3072]{1,0:T(8,128)(2,1)} %bitcast.95, bf16[1024,3072]{1,0:T(8,128)(2,1)} %bitcast.96, bf16[256,768]{1,0:T(8,128)(2,1)} %convolution_convert_fusion.4.do_ref, ...), custom_call_target="tpu_custom_call" | custom-call | tf_op jit(solution)/shard_map/attention_backward/pallas_call | solution.py:302
  292.4 2.3 copy.56
  295.7 7.5 %convolution_convert_fusion.1 = bf16[3072,768]{1,0:T(8,128)(2,1)} fusion(f32[256,768]{1,0:T(8,128)S(1)} %copy-done.10, f32[]{:T(128)} %bitcast.2, f32[256,3072]{1,0:T(8,128)} %copy-done.30), kind=kOutput, calls=%fused_computation.2 | convolution fusion | flops 1217789952 | bytes 8650756 | tf_op jit(solution)/shard_map/rf,rd->fd/dot_general | solution.py:430
  303.2 8.6 %reshape.333 = bf16[768,3072]{1,0:T(8,128)(2,1)} reshape(bf16[3072,768]{1,0:T(8,128)(2,1)} %convolution_convert_fusion.1) | data formatting | bytes 9437184 | tf_op jit(solution)/shard_map/reshape | solution.py:440
  313.3 2.4 copy.58
  315.8 3.2 convolution_convert_fusion.2
  319.0 9.0 %pad_maximum_fusion = bf16[768,9344]{1,0:T(8,128)(2,1)} fusion(bf16[768,3072]{1,0:T(8,128)(2,1)S(1)} %bitcast.101, bf16[768,3072]{1,0:T(8,128)(2,1)S(1)} %convolution_convert_fusion.2, bf16[768,768]{1,0:T(8,128)(2,1)S(1)} %copy-done.2, bf16[9344]{0:T(1024)(128)(2,1)S(1)} %copy-done.15), kind=kLoop, calls=%fused_computation | loop fusion | flops 57409536 | bytes 24987904 | tf_op jit(solution)/shard_map/concatenate | solution.py:435
  328.0 80.0 %reduce-scatter.5.cloned.1.call-done = bf16[128,3072]{1,0:T(8,128)(2,1)} async-done(((bf16[1024,3072]{1,0:T(8,128)(2,1)}), bf16[128,3072]{1,0:T(8,128)(2,1)}) %reduce-scatter.5.cloned.1.call-update) | async-done | bytes 786448 | tf_op jit(solution)/shard_map/reduce_scatter | solution.py:418
  408.0 2.6 convert_element_type.137
  413.5 3.0 convolution_convert_fusion
  416.5 3.3 fusion.34
  420.6 6.6 %concatenate.49 = bf16[768,2432]{1,0:T(8,128)(2,1)} concatenate(bf16[768,2304]{1,0:T(8,128)(2,1)} %convolution_convert_fusion, bf16[768,1]{1,0:T(8,128)(2,1)S(1)} %stack.20, bf16[768,1]{1,0:T(8,128)(2,1)S(1)} %stack.21, bf16[768,1]{1,0:T(8,128)(2,1)S(1)} %stack.22, bf16[768,1]{1,0:T(8,128)(2,1)S(1)} %copy-done.12, bf16[768,124]{1,0:T(8,128)(2,1)S(1)} %broadcast_in_dim.75), dimensions={1} | concatenate | bytes 7471104 | tf_op jit(solution)/shard_map/concatenate | solution.py:458
  427.2 4.2 constant_dynamic-update-slice_fusion
  432.5 2.2 multiply_reduce_fusion
  437.0 39.5 %psum.7 = f32[5]{0:T(128)} all-reduce(f32[5]{0:T(128)S(1)} %pad_maximum_fusion.9), channel_id=1, replica_groups=mesh['seq'=8,'fsdp'=4] {'seq','fsdp'}, use_global_device_ids=true, to_apply=%region_15.16 | all-reduce | flops 5 | bytes 40 | tf_op jit(solution)/shard_map/psum | solution.py:488
  477.5 112.6 %reduce-scatter.7.cloned.1.call-done = bf16[1,24,9344]{2,1,0:T(8,128)(2,1)} async-done(((bf16[32,24,9344]{2,1,0:T(8,128)(2,1)}), bf16[1,24,9344]{2,1,0:T(8,128)(2,1)}) %reduce-scatter.7.cloned.1.call-update) | async-done | bytes 448528
  (146 shorter events, 31.9 us)
Async XLA Ops:
  7.2 112.5 %copy-start = (bf16[2,1,128,768]{3,2,1,0:T(8,128)(2,1)S(1)}, bf16[2,1,128,768]{3,2,1,0:T(8,128)(2,1)}, u32[]{:S(2)}) copy-start(bf16[2,1,128,768]{3,2,1,0:T(8,128)(2,1)} %param.11) | copy-start | bytes 1179652
  7.2 110.6 %all-gather.3.cloned.1.call-start = ((), (), s32[]{:S(2)}) async-start(), calls=%async_computation.2 | async-start | bytes 14800896 | tf_op jit(solution)/shard_map/all_gather | solution.py:363
  11.6 214.2 %all-gather.5.cloned.1.call-start = ((), (), s32[]{:S(2)}) async-start(), calls=%async_computation.3 | async-start | bytes 7077888 | tf_op jit(solution)/shard_map/all_gather | solution.py:392
  12.9 110.3 %copy-start.16 = (f32[256]{0:T(256)}, f32[256]{0:T(256)S(1)}, u32[]{:S(2)}) copy-start(f32[256]{0:T(256)S(1)} %get-tuple-element.90) | copy-start | bytes 3076
  14.1 109.1 %copy-start.21 = (f32[2,128]{1,0:T(2,128)}, f32[2,128]{1,0:T(2,128)S(1)}, u32[]{:S(2)}) copy-start(f32[2,128]{1,0:T(2,128)S(1)} %multiply_reduce_fusion.7) | copy-start | bytes 3076
  14.1 109.0 %copy-start.18 = (f32[256]{0:T(256)}, f32[256]{0:T(256)S(1)}, u32[]{:S(2)}) copy-start(f32[256]{0:T(256)S(1)} %bitcast_rsqrt_fusion) | copy-start | bytes 3076
  119.9 3.3 copy-start.13
  124.8 3.8 copy-start.25
  124.8 4.5 copy-start.27
  124.8 5.7 copy-start.6
  124.8 6.5 %copy-start.5 = (bf16[4,2,1,128,768]{4,3,2,1,0:T(8,128)(2,1)S(1)}, bf16[4,2,1,128,768]{4,3,2,1,0:T(8,128)(2,1)}, u32[]{:S(2)}) copy-start(bf16[4,2,1,128,768]{4,3,2,1,0:T(8,128)(2,1)} %param.12) | copy-start | bytes 4718596
  126.9 6.7 %copy-start.11 = (bf16[256,12,32]{0,2,1:T(8,128)(2,1)S(1)}, bf16[256,12,32]{0,2,1:T(8,128)(2,1)}, u32[]{:S(2)}) copy-start(bf16[256,12,32]{0,2,1:T(8,128)(2,1)} %get-tuple-element.86) | copy-start | bytes 589828
  128.6 279.5 %reduce-scatter.5.cloned.1.call-start = ((), (), s32[]{:S(2)}) async-start(), calls=%async_computation.4 | async-start | bytes 7077888 | tf_op jit(solution)/shard_map/reduce_scatter | solution.py:418
  130.0 9.8 %copy-start.23 = (pred[2,128]{1,0:T(4,128)(4,1)}, pred[2,128]{1,0:T(4,128)(4,1)S(1)}, u32[]{:S(2)}) copy-start(pred[2,128]{1,0:T(4,128)(4,1)S(1)} %broadcast_compare_fusion) | copy-start | bytes 772
  253.7 11.5 %slice-start = ((s8[4718592]{0:T(1024)(128)(4,1)}), s8[4194304]{0:T(1024)(128)(4,1)S(1)}, s32[]{:S(2)}) async-start(s8[4718592]{0:T(1024)(128)(4,1)} %bitcast.98), calls=%async_computation.6 | async-start | bytes 8388608
  253.9 10.9 %copy-start.20 = (f32[256]{0:T(256)}, f32[256]{0:T(256)S(1)}, u32[]{:S(2)}) copy-start(f32[256]{0:T(256)S(1)} %fusion.26) | copy-start | bytes 3076
  253.9 11.3 %slice-start.1 = ((s8[4718592]{0:T(1024)(128)(4,1)}), s8[524288]{0:T(1024)(128)(4,1)S(1)}, s32[]{:S(2)}) async-start(s8[4718592]{0:T(1024)(128)(4,1)} %bitcast.98), calls=%async_computation.7 | async-start | bytes 1048576
  259.1 5.7 copy-start.9
  259.1 6.1 %copy-start.30 = (f32[256,3072]{1,0:T(8,128)}, f32[256,3072]{1,0:T(8,128)S(1)}, u32[]{:S(2)}) copy-start(f32[256,3072]{1,0:T(8,128)S(1)} %get-tuple-element.95) | copy-start | bytes 9437188
  259.1 6.1 %copy-start.7 = (bf16[2,1,128,768]{3,2,1,0:T(8,128)(2,1)S(1)}, bf16[2,1,128,768]{3,2,1,0:T(8,128)(2,1)}, u32[]{:S(2)}) copy-start(bf16[2,1,128,768]{3,2,1,0:T(8,128)(2,1)} %param.13) | copy-start | bytes 1179652
  259.1 6.1 %copy-start.28 = (pred[256]{0:T(512)(128)(4,1)S(1)}, pred[256]{0:T(512)(128)(4,1)}, u32[]{:S(2)}) copy-start(pred[256]{0:T(512)(128)(4,1)} %fusion.49) | copy-start | bytes 772
  259.1 6.1 %copy-start.29 = (f32[1,256,768]{2,0,1:T(1,128)S(1)}, f32[1,256,768]{2,0,1:T(1,128)}, u32[]{:S(2)}) copy-start(f32[1,256,768]{2,0,1:T(1,128)} %fusion.15) | copy-start | bytes 2359300
  291.7 4.0 copy-start.10
  291.7 298.4 %reduce-scatter.7.cloned.1.call-start = ((), (), s32[]{:S(2)}) async-start(), calls=%async_computation.5 | async-start | bytes 14800896
  303.2 8.6 %copy-start.1 = (f32[256,768]{1,0:T(8,128)S(1)}, f32[256,768]{1,0:T(8,128)}, u32[]{:S(2)}) copy-start(f32[256,768]{1,0:T(8,128)} %get-tuple-element.14.o_ref) | copy-start | bytes 2359300
  313.3 5.7 slice-start.2
  315.8 3.2 slice-start.3
  315.8 3.2 copy-start.2
  315.8 3.2 copy-start.15
  416.4 3.3 copy-start.22
  416.4 3.3 copy-start.19
  416.4 4.1 copy-start.12
  (7 other events, 13.0 us)
Sparse Core Ops, SparseCore 0:
  11.8 105.9 all-gather.2
  128.7 97.1 all-gather.4
  291.8 116.1 reduce-scatter.4
  431.6 158.5 reduce-scatter.6

commit v8 on v7

--- a/solution.py
+++ b/solution.py
@@ -209,8 +209,9 @@
         masked = jnp.where(allowed, scores, masked_value)
         top = jnp.max(masked, axis=1, keepdims=True)
         kept = jnp.where(allowed, jnp.exp(masked - top), 0.0)
-        log_total = top + jnp.log(jnp.sum(kept, axis=1, keepdims=True))
-        probabilities = jnp.where(allowed, jnp.exp(scores - log_total), 0.0)
+        total = jnp.sum(kept, axis=1, keepdims=True)
+        log_total = top + jnp.log(total)
+        probabilities = kept * (1.0 / total)
         attended = jnp.dot(
             probabilities.astype(jnp.bfloat16), v_head, preferred_element_type=jnp.float32
         )
@@ -389,7 +390,12 @@
     out_grad = depth_weights[4] * grad_next
     out_low = out_grad.astype(jnp.bfloat16)
 
-    kv_all = lax.all_gather(jnp.swapaxes(own_kv, 0, 1), "seq", axis=0, tiled=True)
+    kv_all = lax.all_gather(
+        jnp.swapaxes(own_kv, 0, 1).reshape(row_count, batches * 2 * model_width),
+        "seq",
+        axis=0,
+        tiled=False,
+    )
     kv_flat = kv_all.reshape(slot_len, batches * 2 * model_width)
     scalars = jnp.concatenate(
         [slot_lengths.astype(jnp.int32), (lax.axis_index("seq") * row_count)[None].astype(jnp.int32)]

time: 603 us -> 597 us (0.990)
  local copies, waits for them, and re-layouts: 67.1 us -> 60.6 us
    unnamed x76 -> x73, local copies, waits for them, and re-layouts: 11.8 us -> 4.87 us
where the time goes in v8:
time: 597 us; the launch traced here: 595 us
  waiting for transfers between devices  367 us (61%)
  local copies, waits for them, and re-layouts  60.6 us (10%)
  matrix products  49.2 us (8%)
  blocking collectives  39.5 us (7%)
  Pallas kernels  37.7 us (6%)
  other arithmetic  26.3 us (4%)
  between operations  14.5 us (2%)
    unnamed x5, waiting for transfers between devices  113 us
    all_gather x1, waiting for transfers between devices, local(): gathered = lax.all_gather(packed, ('seq', 'fsdp'), axis=0, tiled=True)  103 us
    reduce_scatter x1, waiting for transfers between devices, local(): lax.psum_scatter(kv_grad_flat, 'seq', scatter_dimension=0, tiled=True)  80 us
    all_gather x1, waiting for transfers between devices, local(): lax.all_gather(jnp.swapaxes(own_kv, 0, 1).reshape(row_count, batches * 2...  71.1 us
    psum x1, blocking collectives, local(): depth_total = lax.psum(depth_terms, ('seq', 'fsdp'))  39.5 us
    pallas_call x1, Pallas kernels, attention_backward(): pl.pallas_call(_backward_kernel, grid_spec=pltpu.PrefetchScalarGridSpec(n...  19.6 us
    pallas_call x1, Pallas kernels, attention_forward(): pl.pallas_call(_forward_kernel, grid_spec=pltpu.PrefetchScalarGridSpec(nu...  18.1 us
  transfers between devices with their start and end apart: 4, of which 4 were waited for; matrix products, arithmetic and copies ran while one was open for 12% of the time, Pallas kernels for 0%

profile of v8, /device:TPU:0, one launch (start us, length us, event | category | flops | bytes accessed | tf_op | source)
XLA Modules:
  0.0 595.2 jit_solution(17186034924091159678)
XLA Ops:
  9.8 1.8 concatenate.41
  14.4 103.4 %all-gather.3.cloned.1.call-done = bf16[768,9344]{1,0:T(8,128)(2,1)} async-done(((bf16[24,9344]{1,0:T(8,128)(2,1)}), bf16[768,9344]{1,0:T(8,128)(2,1)}) %all-gather.3.cloned.1.call-update) | async-done | bytes 14352400 | tf_op jit(solution)/shard_map/all_gather | solution.py:364
  119.9 3.2 fusion.13
  132.3 2.2 fusion.15
  136.4 5.1 slice.147
  141.5 8.5 %reshape.325 = bf16[3072,768]{1,0:T(8,128)(2,1)} reshape(bf16[768,3072]{1,0:T(8,128)(2,1)} %slice.147) | data formatting | bytes 9437184 | tf_op jit(solution)/shard_map/reshape | solution.py:366
  150.0 5.5 fusion.41
  155.5 71.1 %all-gather.5.cloned.1.call-done = bf16[8,128,3072]{2,1,0:T(8,128)(2,1)} async-done(((bf16[1,128,3072]{2,1,0:T(8,128)(2,1)}), bf16[8,128,3072]{2,1,0:T(8,128)(2,1)}) %all-gather.5.cloned.1.call-update) | async-done | bytes 6291472 | tf_op jit(solution)/shard_map/all_gather | solution.py:393
  226.6 18.1 %attention_forward.1 = (f32[256,768]{1,0:T(8,128)}, f32[256,768]{1,0:T(8,128)}) custom-call(s32[3]{0:T(128)} %pad_add_fusion.scalars_ref, bf16[256,768]{1,0:T(8,128)(2,1)} %copy.54.q_ref, bf16[1024,3072]{1,0:T(8,128)(2,1)} %bitcast.91, bf16[1024,3072]{1,0:T(8,128)(2,1)} %bitcast.92), custom_call_target="tpu_custom_call" | custom-call | tf_op jit(solution)/shard_map/attention_forward/pallas_call | solution.py:275
  244.6 2.2 fusion.40
  247.2 5.1 fusion.10
  252.3 5.7 multiply_reduce_fusion.2
  258.5 4.3 multiply_reduce_fusion.1
  262.7 2.5 convolution_convert_fusion.4.do_ref
  265.2 19.6 %attention_backward.1 = (f32[256,768]{1,0:T(8,128)}, bf16[1024,3072]{1,0:T(8,128)(2,1)}) custom-call(s32[3]{0:T(128)} %pad_add_fusion.scalars_ref, bf16[256,768]{1,0:T(8,128)(2,1)} %copy.54.q_ref, bf16[1024,3072]{1,0:T(8,128)(2,1)} %bitcast.93, bf16[1024,3072]{1,0:T(8,128)(2,1)} %bitcast.94, bf16[256,768]{1,0:T(8,128)(2,1)} %convolution_convert_fusion.4.do_ref, ...), custom_call_target="tpu_custom_call" | custom-call | tf_op jit(solution)/shard_map/attention_backward/pallas_call | solution.py:303
  285.6 2.3 copy.56
  288.9 7.5 %convolution_convert_fusion.1 = bf16[3072,768]{1,0:T(8,128)(2,1)} fusion(f32[256,768]{1,0:T(8,128)S(1)} %copy-done.10, f32[]{:T(128)} %bitcast.2, f32[256,3072]{1,0:T(8,128)} %copy-done.29), kind=kOutput, calls=%fused_computation.2 | convolution fusion | flops 1217789952 | bytes 8650756 | tf_op jit(solution)/shard_map/rf,rd->fd/dot_general | solution.py:436
  296.4 8.6 %reshape.333 = bf16[768,3072]{1,0:T(8,128)(2,1)} reshape(bf16[3072,768]{1,0:T(8,128)(2,1)} %convolution_convert_fusion.1) | data formatting | bytes 9437184 | tf_op jit(solution)/shard_map/reshape | solution.py:446
  305.0 1.5 convolution_convert_fusion.3
  306.5 2.4 copy.58
  309.0 3.2 convolution_convert_fusion.2
  312.2 9.0 %pad_maximum_fusion = bf16[768,9344]{1,0:T(8,128)(2,1)} fusion(bf16[768,3072]{1,0:T(8,128)(2,1)S(1)} %bitcast.99, bf16[768,3072]{1,0:T(8,128)(2,1)S(1)} %convolution_convert_fusion.2, bf16[768,768]{1,0:T(8,128)(2,1)S(1)} %copy-done.2, bf16[9344]{0:T(1024)(128)(2,1)S(1)} %copy-done.14), kind=kLoop, calls=%fused_computation | loop fusion | flops 57409536 | bytes 24987904 | tf_op jit(solution)/shard_map/concatenate | solution.py:441
  321.2 80.0 %reduce-scatter.5.cloned.1.call-done = bf16[128,3072]{1,0:T(8,128)(2,1)} async-done(((bf16[1024,3072]{1,0:T(8,128)(2,1)}), bf16[128,3072]{1,0:T(8,128)(2,1)}) %reduce-scatter.5.cloned.1.call-update) | async-done | bytes 786448 | tf_op jit(solution)/shard_map/reduce_scatter | solution.py:424
  401.3 2.6 convert_element_type.137
  406.7 3.0 convolution_convert_fusion
  409.7 3.3 fusion.34
  413.8 6.6 %concatenate.49 = bf16[768,2432]{1,0:T(8,128)(2,1)} concatenate(bf16[768,2304]{1,0:T(8,128)(2,1)} %convolution_convert_fusion, bf16[768,1]{1,0:T(8,128)(2,1)S(1)} %stack.20, bf16[768,1]{1,0:T(8,128)(2,1)S(1)} %stack.21, bf16[768,1]{1,0:T(8,128)(2,1)S(1)} %stack.22, bf16[768,1]{1,0:T(8,128)(2,1)S(1)} %copy-done.11, bf16[768,124]{1,0:T(8,128)(2,1)S(1)} %broadcast_in_dim.75), dimensions={1} | concatenate | bytes 7471104 | tf_op jit(solution)/shard_map/concatenate | solution.py:464
  420.4 4.3 constant_dynamic-update-slice_fusion
  425.8 2.2 multiply_reduce_fusion
  428.7 1.5 multiply_convert_fusion
  430.3 39.5 %psum.7 = f32[5]{0:T(128)} all-reduce(f32[5]{0:T(128)S(1)} %pad_maximum_fusion.9), channel_id=1, replica_groups=mesh['seq'=8,'fsdp'=4] {'seq','fsdp'}, use_global_device_ids=true, to_apply=%region_15.16 | all-reduce | flops 5 | bytes 40 | tf_op jit(solution)/shard_map/psum | solution.py:494
  470.8 112.5 %reduce-scatter.7.cloned.1.call-done = bf16[1,24,9344]{2,1,0:T(8,128)(2,1)} async-done(((bf16[32,24,9344]{2,1,0:T(8,128)(2,1)}), bf16[1,24,9344]{2,1,0:T(8,128)(2,1)}) %reduce-scatter.7.cloned.1.call-update) | async-done | bytes 448528
  (144 shorter events, 32.4 us)
Async XLA Ops:
  7.2 112.5 %copy-start = (bf16[2,1,128,768]{3,2,1,0:T(8,128)(2,1)S(1)}, bf16[2,1,128,768]{3,2,1,0:T(8,128)(2,1)}, u32[]{:S(2)}) copy-start(bf16[2,1,128,768]{3,2,1,0:T(8,128)(2,1)} %param.11) | copy-start | bytes 1179652
  7.2 110.6 %all-gather.3.cloned.1.call-start = ((), (), s32[]{:S(2)}) async-start(), calls=%async_computation.2 | async-start | bytes 14800896 | tf_op jit(solution)/shard_map/all_gather | solution.py:364
  11.6 215.0 %all-gather.5.cloned.1.call-start = ((), (), s32[]{:S(2)}) async-start(), calls=%async_computation.3 | async-start | bytes 7077888 | tf_op jit(solution)/shard_map/all_gather | solution.py:393
  12.9 110.3 %copy-start.15 = (f32[256]{0:T(256)}, f32[256]{0:T(256)S(1)}, u32[]{:S(2)}) copy-start(f32[256]{0:T(256)S(1)} %get-tuple-element.90) | copy-start | bytes 3076
  14.1 109.1 %copy-start.20 = (f32[2,128]{1,0:T(2,128)}, f32[2,128]{1,0:T(2,128)S(1)}, u32[]{:S(2)}) copy-start(f32[2,128]{1,0:T(2,128)S(1)} %multiply_reduce_fusion.7) | copy-start | bytes 3076
  14.1 109.1 %copy-start.17 = (f32[256]{0:T(256)}, f32[256]{0:T(256)S(1)}, u32[]{:S(2)}) copy-start(f32[256]{0:T(256)S(1)} %bitcast_rsqrt_fusion) | copy-start | bytes 3076
  119.9 3.3 copy-start.12
  125.6 3.9 copy-start.24
  125.6 4.6 copy-start.26
  125.6 5.8 copy-start.6
  125.8 6.5 %copy-start.5 = (bf16[4,2,1,128,768]{4,3,2,1,0:T(8,128)(2,1)S(1)}, bf16[4,2,1,128,768]{4,3,2,1,0:T(8,128)(2,1)}, u32[]{:S(2)}) copy-start(bf16[4,2,1,128,768]{4,3,2,1,0:T(8,128)(2,1)} %param.12) | copy-start | bytes 4718596
  129.3 271.9 %reduce-scatter.5.cloned.1.call-start = ((), (), s32[]{:S(2)}) async-start(), calls=%async_computation.4 | async-start | bytes 7077888 | tf_op jit(solution)/shard_map/reduce_scatter | solution.py:424
  130.9 10.6 %copy-start.22 = (pred[2,128]{1,0:T(4,128)(4,1)}, pred[2,128]{1,0:T(4,128)(4,1)S(1)}, u32[]{:S(2)}) copy-start(pred[2,128]{1,0:T(4,128)(4,1)S(1)} %broadcast_compare_fusion) | copy-start | bytes 772
  246.9 11.5 %slice-start = ((s8[4718592]{0:T(1024)(128)(4,1)}), s8[4194304]{0:T(1024)(128)(4,1)S(1)}, s32[]{:S(2)}) async-start(s8[4718592]{0:T(1024)(128)(4,1)} %bitcast.96), calls=%async_computation.6 | async-start | bytes 8388608
  247.1 10.9 %copy-start.19 = (f32[256]{0:T(256)}, f32[256]{0:T(256)S(1)}, u32[]{:S(2)}) copy-start(f32[256]{0:T(256)S(1)} %fusion.26) | copy-start | bytes 3076
  247.1 11.3 %slice-start.1 = ((s8[4718592]{0:T(1024)(128)(4,1)}), s8[524288]{0:T(1024)(128)(4,1)S(1)}, s32[]{:S(2)}) async-start(s8[4718592]{0:T(1024)(128)(4,1)} %bitcast.96), calls=%async_computation.7 | async-start | bytes 1048576
  252.3 5.7 copy-start.9
  252.3 6.1 %copy-start.29 = (f32[256,3072]{1,0:T(8,128)}, f32[256,3072]{1,0:T(8,128)S(1)}, u32[]{:S(2)}) copy-start(f32[256,3072]{1,0:T(8,128)S(1)} %get-tuple-element.95) | copy-start | bytes 9437188
  252.3 6.1 %copy-start.7 = (bf16[2,1,128,768]{3,2,1,0:T(8,128)(2,1)S(1)}, bf16[2,1,128,768]{3,2,1,0:T(8,128)(2,1)}, u32[]{:S(2)}) copy-start(bf16[2,1,128,768]{3,2,1,0:T(8,128)(2,1)} %param.13) | copy-start | bytes 1179652
  252.3 6.1 %copy-start.27 = (pred[256]{0:T(512)(128)(4,1)S(1)}, pred[256]{0:T(512)(128)(4,1)}, u32[]{:S(2)}) copy-start(pred[256]{0:T(512)(128)(4,1)} %fusion.49) | copy-start | bytes 772
  252.3 6.1 %copy-start.28 = (f32[1,256,768]{2,0,1:T(1,128)S(1)}, f32[1,256,768]{2,0,1:T(1,128)}, u32[]{:S(2)}) copy-start(f32[1,256,768]{2,0,1:T(1,128)} %fusion.15) | copy-start | bytes 2359300
  284.9 4.0 copy-start.10
  284.9 298.4 %reduce-scatter.7.cloned.1.call-start = ((), (), s32[]{:S(2)}) async-start(), calls=%async_computation.5 | async-start | bytes 14800896
  296.4 8.6 %copy-start.1 = (f32[256,768]{1,0:T(8,128)S(1)}, f32[256,768]{1,0:T(8,128)}, u32[]{:S(2)}) copy-start(f32[256,768]{1,0:T(8,128)} %get-tuple-element.14.o_ref) | copy-start | bytes 2359300
  306.5 5.7 slice-start.2
  309.0 3.2 slice-start.3
  309.0 3.2 copy-start.2
  309.0 3.2 copy-start.14
  409.7 3.3 copy-start.21
  409.7 3.3 copy-start.18
  409.7 4.1 copy-start.11
  425.7 3.0 copy-start.25
  (6 other events, 10.0 us)
Sparse Core Ops, SparseCore 0:
  11.8 105.9 all-gather.2
  129.4 97.1 all-gather.4
  285.0 116.1 reduce-scatter.4
  424.9 158.4 reduce-scatter.6

commit v9 on v8

--- a/solution.py
+++ b/solution.py
@@ -185,11 +185,14 @@
     return query_grad, key_grad, value_grad
 
 
-def _pair_masks(scalars_ref, micro, row_count, key_count):
+ROW_CHUNK = 32
+
+
+def _chunk_mask(scalars_ref, micro, chunk, key_count):
     length = scalars_ref[micro]
-    first_row = scalars_ref[scalars_ref.shape[0] - 1]
-    query_pos = first_row + lax.broadcasted_iota(jnp.int32, (row_count, key_count), 0)
-    key_pos = lax.broadcasted_iota(jnp.int32, (row_count, key_count), 1)
+    first_row = scalars_ref[scalars_ref.shape[0] - 1] + chunk * ROW_CHUNK
+    query_pos = first_row + lax.broadcasted_iota(jnp.int32, (ROW_CHUNK, key_count), 0)
+    key_pos = lax.broadcasted_iota(jnp.int32, (ROW_CHUNK, key_count), 1)
     return (key_pos <= query_pos) & (key_pos < length)
 
 
@@ -197,68 +200,83 @@
     micro = pl.program_id(0)
     row_count = q_ref.shape[0]
     key_count = k_ref.shape[0]
-    allowed = _pair_masks(scalars_ref, micro, row_count, key_count)
-    for half in range(2):
-        lanes = slice(half * HEAD, (half + 1) * HEAD)
-        q_head = q_ref[:, lanes]
-        k_head = k_ref[:, lanes]
-        v_head = v_ref[:, lanes]
-        scores = lax.dot_general(
-            q_head, k_head, (((1,), (1,)), ((), ())), preferred_element_type=jnp.float32
-        ) * HEAD ** (-0.5)
-        masked = jnp.where(allowed, scores, masked_value)
-        top = jnp.max(masked, axis=1, keepdims=True)
-        kept = jnp.where(allowed, jnp.exp(masked - top), 0.0)
-        total = jnp.sum(kept, axis=1, keepdims=True)
-        log_total = top + jnp.log(total)
-        probabilities = kept * (1.0 / total)
-        attended = jnp.dot(
-            probabilities.astype(jnp.bfloat16), v_head, preferred_element_type=jnp.float32
-        )
-        out_ref[:, lanes] = attended
-        lse_ref[:, lanes] = jnp.broadcast_to(log_total, (row_count, HEAD))
+
+    def chunk_body(chunk, carry):
+        rows = pl.ds(pl.multiple_of(chunk * ROW_CHUNK, ROW_CHUNK), ROW_CHUNK)
+        allowed = _chunk_mask(scalars_ref, micro, chunk, key_count)
+        for half in range(2):
+            lanes = slice(half * HEAD, (half + 1) * HEAD)
+            scores = lax.dot_general(
+                q_ref[rows, lanes],
+                k_ref[:, lanes],
+                (((1,), (1,)), ((), ())),
+                preferred_element_type=jnp.float32,
+            ) * HEAD ** (-0.5)
+            masked = jnp.where(allowed, scores, masked_value)
+            top = jnp.max(masked, axis=1, keepdims=True)
+            kept = jnp.where(allowed, jnp.exp(masked - top), 0.0)
+            total = jnp.sum(kept, axis=1, keepdims=True)
+            log_total = top + jnp.log(total)
+            probabilities = kept * (1.0 / total)
+            out_ref[rows, lanes] = jnp.dot(
+                probabilities.astype(jnp.bfloat16), v_ref[:, lanes],
+                preferred_element_type=jnp.float32,
+            )
+            lse_ref[rows, lanes] = jnp.broadcast_to(log_total, (ROW_CHUNK, HEAD))
+        return carry
+
+    lax.fori_loop(0, row_count // ROW_CHUNK, chunk_body, 0)
 
 
 def _backward_kernel(
-    scalars_ref, q_ref, k_ref, v_ref, do_ref, o_ref, lse_ref, dq_ref, kv_grad_ref
+    scalars_ref, q_ref, k_ref, v_ref, do_ref, o_ref, lse_ref, dq_ref, kv_grad_ref, acc_ref
 ):
     micro = pl.program_id(0)
     row_count = q_ref.shape[0]
     key_count = k_ref.shape[0]
-    allowed = _pair_masks(scalars_ref, micro, row_count, key_count)
+    acc_ref[...] = jnp.zeros(acc_ref.shape, jnp.float32)
+
+    def chunk_body(chunk, carry):
+        rows = pl.ds(pl.multiple_of(chunk * ROW_CHUNK, ROW_CHUNK), ROW_CHUNK)
+        allowed = _chunk_mask(scalars_ref, micro, chunk, key_count)
+        for half in range(2):
+            lanes = slice(half * HEAD, (half + 1) * HEAD)
+            q_head = q_ref[rows, lanes]
+            grad_head = do_ref[rows, lanes]
+            scores = lax.dot_general(
+                q_head, k_ref[:, lanes], (((1,), (1,)), ((), ())),
+                preferred_element_type=jnp.float32,
+            ) * HEAD ** (-0.5)
+            log_total = lse_ref[rows, half * HEAD : half * HEAD + 1]
+            probabilities = jnp.where(allowed, jnp.exp(scores - log_total), 0.0)
+            prob_grad = lax.dot_general(
+                grad_head, v_ref[:, lanes], (((1,), (1,)), ((), ())),
+                preferred_element_type=jnp.float32,
+            )
+            row_delta = jnp.sum(
+                grad_head.astype(jnp.float32) * o_ref[rows, lanes], axis=1, keepdims=True
+            )
+            score_low = (probabilities * (prob_grad - row_delta)).astype(jnp.bfloat16)
+            dq_ref[rows, lanes] = jnp.dot(
+                score_low, k_ref[:, lanes], preferred_element_type=jnp.float32
+            ) * HEAD ** (-0.5)
+            acc_ref[0, half] += lax.dot_general(
+                score_low, q_head, (((0,), (0,)), ((), ())), preferred_element_type=jnp.float32
+            )
+            acc_ref[1, half] += lax.dot_general(
+                probabilities.astype(jnp.bfloat16), grad_head, (((0,), (0,)), ((), ())),
+                preferred_element_type=jnp.float32,
+            )
+        return carry
+
+    lax.fori_loop(0, row_count // ROW_CHUNK, chunk_body, 0)
     for half in range(2):
-        lanes = slice(half * HEAD, (half + 1) * HEAD)
-        q_head = q_ref[:, lanes]
-        k_head = k_ref[:, lanes]
-        v_head = v_ref[:, lanes]
-        grad_head = do_ref[:, lanes]
-        scores = lax.dot_general(
-            q_head, k_head, (((1,), (1,)), ((), ())), preferred_element_type=jnp.float32
-        ) * HEAD ** (-0.5)
-        log_total = lse_ref[:, half * HEAD : half * HEAD + 1]
-        probabilities = jnp.where(allowed, jnp.exp(scores - log_total), 0.0)
-        probabilities_low = probabilities.astype(jnp.bfloat16)
-        prob_grad = lax.dot_general(
-            grad_head, v_head, (((1,), (1,)), ((), ())), preferred_element_type=jnp.float32
-        )
-        row_delta = jnp.sum(
-            grad_head.astype(jnp.float32) * o_ref[:, lanes], axis=1, keepdims=True
-        )
-        score_low = (probabilities * (prob_grad - row_delta)).astype(jnp.bfloat16)
-        dq_ref[:, lanes] = jnp.dot(
-            score_low, k_head, preferred_element_type=jnp.float32
-        ) * HEAD ** (-0.5)
-        key_grad = lax.dot_general(
-            score_low, q_head, (((0,), (0,)), ((), ())), preferred_element_type=jnp.float32
-        ) * HEAD ** (-0.5)
-        value_grad = lax.dot_general(
-            probabilities_low, grad_head, (((0,), (0,)), ((), ())),
-            preferred_element_type=jnp.float32,
-        )
-        kv_grad_ref[:, lanes] = key_grad.astype(jnp.bfloat16)
-        kv_grad_ref[:, 2 * HEAD + half * HEAD : 2 * HEAD + (half + 1) * HEAD] = value_grad.astype(
-            jnp.bfloat16
-        )
+        kv_grad_ref[:, half * HEAD : (half + 1) * HEAD] = (
+            acc_ref[0, half] * HEAD ** (-0.5)
+        ).astype(jnp.bfloat16)
+        kv_grad_ref[:, 2 * HEAD + half * HEAD : 2 * HEAD + (half + 1) * HEAD] = acc_ref[
+            1, half
+        ].astype(jnp.bfloat16)
 
 
 def attention_forward(scalars, queries, kv_flat, batches):
@@ -307,6 +325,7 @@
             grid=(batches, pairs),
             in_specs=[row_spec, key_spec, value_spec, row_spec, row_spec, row_spec],
             out_specs=[row_spec, grad_spec],
+            scratch_shapes=[pltpu.VMEM((2, 2, key_count, HEAD), jnp.float32)],
         ),
         out_shape=[
             jax.ShapeDtypeStruct((all_rows, model_width), jnp.float32),

time: 597 us -> 671 us (1.12)
  Pallas kernels: 37.7 us -> 112 us
    pallas_call x1, Pallas kernels: 19.6 us -> 60.9 us  [attention_backward(): pl.pallas_call(_backward_kernel, grid_spec=pltpu.PrefetchScalarGridSpec(n...]
    pallas_call x1, Pallas kernels: 18.1 us -> 51.3 us  [attention_forward(): pl.pallas_call(_forward_kernel, grid_spec=pltpu.PrefetchScalarGridSpec(nu...]
  transfers between devices with their start and end apart: 4 -> 4, of which waited for: 4 -> 4; matrix products, arithmetic and copies ran while one was open for 12% -> 10% of each run, Pallas kernels for 0% -> 0%
where the time goes in v9:
time: 671 us; the launch traced here: 670 us
  waiting for transfers between devices  367 us (55%)
  Pallas kernels  112 us (17%)
  local copies, waits for them, and re-layouts  60.6 us (9%)
  matrix products  49.2 us (7%)
  blocking collectives  39.5 us (6%)
  other arithmetic  26.3 us (4%)
  between operations  14.5 us (2%)
    unnamed x5, waiting for transfers between devices  113 us
    all_gather x1, waiting for transfers between devices, local(): gathered = lax.all_gather(packed, ('seq', 'fsdp'), axis=0, tiled=True)  103 us
    reduce_scatter x1, waiting for transfers between devices, local(): lax.psum_scatter(kv_grad_flat, 'seq', scatter_dimension=0, tiled=True)  80 us
    all_gather x1, waiting for transfers between devices, local(): lax.all_gather(jnp.swapaxes(own_kv, 0, 1).reshape(row_count, batches * 2...  71.1 us
    pallas_call x1, Pallas kernels, attention_backward(): pl.pallas_call(_backward_kernel, grid_spec=pltpu.PrefetchScalarGridSpec(n...  60.9 us
    pallas_call x1, Pallas kernels, attention_forward(): pl.pallas_call(_forward_kernel, grid_spec=pltpu.PrefetchScalarGridSpec(nu...  51.3 us
    psum x1, blocking collectives, local(): depth_total = lax.psum(depth_terms, ('seq', 'fsdp'))  39.5 us
  transfers between devices with their start and end apart: 4, of which 4 were waited for; matrix products, arithmetic and copies ran while one was open for 10% of the time, Pallas kernels for 0%

profile of v9, /device:TPU:0, one launch (start us, length us, event | category | flops | bytes accessed | tf_op | source)
XLA Modules:
  0.0 669.7 jit_solution(6364660286701287106)
XLA Ops:
  9.8 1.8 concatenate.41
  14.4 103.4 %all-gather.3.cloned.1.call-done = bf16[768,9344]{1,0:T(8,128)(2,1)} async-done(((bf16[24,9344]{1,0:T(8,128)(2,1)}), bf16[768,9344]{1,0:T(8,128)(2,1)}) %all-gather.3.cloned.1.call-update) | async-done | bytes 14352400 | tf_op jit(solution)/shard_map/all_gather | solution.py:383
  119.9 3.2 fusion.13
  132.3 2.2 fusion.15
  136.4 5.1 slice.147
  141.5 8.5 %reshape.325 = bf16[3072,768]{1,0:T(8,128)(2,1)} reshape(bf16[768,3072]{1,0:T(8,128)(2,1)} %slice.147) | data formatting | bytes 9437184 | tf_op jit(solution)/shard_map/reshape | solution.py:385
  150.0 5.5 fusion.41
  155.5 71.1 %all-gather.5.cloned.1.call-done = bf16[8,128,3072]{2,1,0:T(8,128)(2,1)} async-done(((bf16[1,128,3072]{2,1,0:T(8,128)(2,1)}), bf16[8,128,3072]{2,1,0:T(8,128)(2,1)}) %all-gather.5.cloned.1.call-update) | async-done | bytes 6291472 | tf_op jit(solution)/shard_map/all_gather | solution.py:412
  226.6 51.3 %attention_forward.1 = (f32[256,768]{1,0:T(8,128)}, f32[256,768]{1,0:T(8,128)}) custom-call(s32[3]{0:T(128)} %pad_add_fusion.scalars_ref, bf16[256,768]{1,0:T(8,128)(2,1)} %copy.54.q_ref, bf16[1024,3072]{1,0:T(8,128)(2,1)} %bitcast.91, bf16[1024,3072]{1,0:T(8,128)(2,1)} %bitcast.92), custom_call_target="tpu_custom_call" | custom-call | tf_op jit(solution)/shard_map/attention_forward/pallas_call | solution.py:293
  277.9 2.2 fusion.40
  280.4 5.1 fusion.10
  285.6 5.7 multiply_reduce_fusion.2
  291.7 4.3 multiply_reduce_fusion.1
  296.0 2.5 convolution_convert_fusion.4.do_ref
  298.5 60.9 %attention_backward.1 = (f32[256,768]{1,0:T(8,128)}, bf16[1024,3072]{1,0:T(8,128)(2,1)}) custom-call(s32[3]{0:T(128)} %pad_add_fusion.scalars_ref, bf16[256,768]{1,0:T(8,128)(2,1)} %copy.54.q_ref, bf16[1024,3072]{1,0:T(8,128)(2,1)} %bitcast.93, bf16[1024,3072]{1,0:T(8,128)(2,1)} %bitcast.94, bf16[256,768]{1,0:T(8,128)(2,1)} %convolution_convert_fusion.4.do_ref, ...), custom_call_target="tpu_custom_call" | custom-call | tf_op jit(solution)/shard_map/attention_backward/pallas_call | solution.py:321
  360.1 2.3 copy.56
  363.4 7.5 %convolution_convert_fusion.1 = bf16[3072,768]{1,0:T(8,128)(2,1)} fusion(f32[256,768]{1,0:T(8,128)S(1)} %copy-done.10, f32[]{:T(128)} %bitcast.2, f32[256,3072]{1,0:T(8,128)} %copy-done.29), kind=kOutput, calls=%fused_computation.2 | convolution fusion | flops 1217789952 | bytes 8650756 | tf_op jit(solution)/shard_map/rf,rd->fd/dot_general | solution.py:455
  370.9 8.6 %reshape.333 = bf16[768,3072]{1,0:T(8,128)(2,1)} reshape(bf16[3072,768]{1,0:T(8,128)(2,1)} %convolution_convert_fusion.1) | data formatting | bytes 9437184 | tf_op jit(solution)/shard_map/reshape | solution.py:465
  379.5 1.5 convolution_convert_fusion.3
  381.0 2.4 copy.58
  383.5 3.2 convolution_convert_fusion.2
  386.7 9.0 %pad_maximum_fusion = bf16[768,9344]{1,0:T(8,128)(2,1)} fusion(bf16[768,3072]{1,0:T(8,128)(2,1)S(1)} %bitcast.99, bf16[768,3072]{1,0:T(8,128)(2,1)S(1)} %convolution_convert_fusion.2, bf16[768,768]{1,0:T(8,128)(2,1)S(1)} %copy-done.2, bf16[9344]{0:T(1024)(128)(2,1)S(1)} %copy-done.14), kind=kLoop, calls=%fused_computation | loop fusion | flops 57409536 | bytes 24987904 | tf_op jit(solution)/shard_map/concatenate | solution.py:460
  395.8 80.0 %reduce-scatter.5.cloned.1.call-done = bf16[128,3072]{1,0:T(8,128)(2,1)} async-done(((bf16[1024,3072]{1,0:T(8,128)(2,1)}), bf16[128,3072]{1,0:T(8,128)(2,1)}) %reduce-scatter.5.cloned.1.call-update) | async-done | bytes 786448 | tf_op jit(solution)/shard_map/reduce_scatter | solution.py:443
  475.8 2.6 convert_element_type.137
  481.2 3.0 convolution_convert_fusion
  484.2 3.3 fusion.34
  488.3 6.6 concatenate.49
  494.9 4.3 constant_dynamic-update-slice_fusion
  500.3 2.2 multiply_reduce_fusion
  503.2 1.5 multiply_convert_fusion
  504.8 39.5 %psum.7 = f32[5]{0:T(128)} all-reduce(f32[5]{0:T(128)S(1)} %pad_maximum_fusion.9), channel_id=1, replica_groups=mesh['seq'=8,'fsdp'=4] {'seq','fsdp'}, use_global_device_ids=true, to_apply=%region_15.16 | all-reduce | flops 5 | bytes 40 | tf_op jit(solution)/shard_map/psum | solution.py:513
  545.3 112.5 %reduce-scatter.7.cloned.1.call-done = bf16[1,24,9344]{2,1,0:T(8,128)(2,1)} async-done(((bf16[32,24,9344]{2,1,0:T(8,128)(2,1)}), bf16[1,24,9344]{2,1,0:T(8,128)(2,1)}) %reduce-scatter.7.cloned.1.call-update) | async-done | bytes 448528
  (144 shorter events, 32.4 us)
Async XLA Ops:
  7.2 112.5 %copy-start = (bf16[2,1,128,768]{3,2,1,0:T(8,128)(2,1)S(1)}, bf16[2,1,128,768]{3,2,1,0:T(8,128)(2,1)}, u32[]{:S(2)}) copy-start(bf16[2,1,128,768]{3,2,1,0:T(8,128)(2,1)} %param.11) | copy-start | bytes 1179652
  7.2 110.6 %all-gather.3.cloned.1.call-start = ((), (), s32[]{:S(2)}) async-start(), calls=%async_computation.2 | async-start | bytes 14800896 | tf_op jit(solution)/shard_map/all_gather | solution.py:383
  11.6 215.0 %all-gather.5.cloned.1.call-start = ((), (), s32[]{:S(2)}) async-start(), calls=%async_computation.3 | async-start | bytes 7077888 | tf_op jit(solution)/shard_map/all_gather | solution.py:412
  12.9 110.3 %copy-start.15 = (f32[256]{0:T(256)}, f32[256]{0:T(256)S(1)}, u32[]{:S(2)}) copy-start(f32[256]{0:T(256)S(1)} %get-tuple-element.90) | copy-start | bytes 3076
  14.1 109.1 %copy-start.20 = (f32[2,128]{1,0:T(2,128)}, f32[2,128]{1,0:T(2,128)S(1)}, u32[]{:S(2)}) copy-start(f32[2,128]{1,0:T(2,128)S(1)} %multiply_reduce_fusion.7) | copy-start | bytes 3076
  14.1 109.1 %copy-start.17 = (f32[256]{0:T(256)}, f32[256]{0:T(256)S(1)}, u32[]{:S(2)}) copy-start(f32[256]{0:T(256)S(1)} %bitcast_rsqrt_fusion) | copy-start | bytes 3076
  119.9 3.3 copy-start.12
  125.6 3.9 copy-start.24
  125.6 4.6 copy-start.26
  125.6 5.8 copy-start.6
  125.8 6.5 copy-start.5
  129.3 346.4 %reduce-scatter.5.cloned.1.call-start = ((), (), s32[]{:S(2)}) async-start(), calls=%async_computation.4 | async-start | bytes 7077888 | tf_op jit(solution)/shard_map/reduce_scatter | solution.py:443
  130.9 10.6 %copy-start.22 = (pred[2,128]{1,0:T(4,128)(4,1)}, pred[2,128]{1,0:T(4,128)(4,1)S(1)}, u32[]{:S(2)}) copy-start(pred[2,128]{1,0:T(4,128)(4,1)S(1)} %broadcast_compare_fusion) | copy-start | bytes 772
  280.1 11.5 %slice-start = ((s8[4718592]{0:T(1024)(128)(4,1)}), s8[4194304]{0:T(1024)(128)(4,1)S(1)}, s32[]{:S(2)}) async-start(s8[4718592]{0:T(1024)(128)(4,1)} %bitcast.96), calls=%async_computation.6 | async-start | bytes 8388608
  280.4 10.9 %copy-start.19 = (f32[256]{0:T(256)}, f32[256]{0:T(256)S(1)}, u32[]{:S(2)}) copy-start(f32[256]{0:T(256)S(1)} %fusion.26) | copy-start | bytes 3076
  280.4 11.3 %slice-start.1 = ((s8[4718592]{0:T(1024)(128)(4,1)}), s8[524288]{0:T(1024)(128)(4,1)S(1)}, s32[]{:S(2)}) async-start(s8[4718592]{0:T(1024)(128)(4,1)} %bitcast.96), calls=%async_computation.7 | async-start | bytes 1048576
  285.5 5.7 copy-start.9
  285.5 6.1 copy-start.29
  285.6 6.1 copy-start.7
  285.6 6.1 copy-start.27
  285.6 6.1 copy-start.28
  359.4 4.0 copy-start.10
  359.4 298.4 %reduce-scatter.7.cloned.1.call-start = ((), (), s32[]{:S(2)}) async-start(), calls=%async_computation.5 | async-start | bytes 14800896
  370.9 8.6 %copy-start.1 = (f32[256,768]{1,0:T(8,128)S(1)}, f32[256,768]{1,0:T(8,128)}, u32[]{:S(2)}) copy-start(f32[256,768]{1,0:T(8,128)} %get-tuple-element.14.o_ref) | copy-start | bytes 2359300
  381.0 5.7 slice-start.2
  383.5 3.2 slice-start.3
  383.5 3.2 copy-start.2
  383.5 3.2 copy-start.14
  484.1 3.3 copy-start.21
  484.1 3.3 copy-start.18
  484.2 4.1 copy-start.11
  500.2 3.0 copy-start.25
  (6 other events, 10.0 us)
Sparse Core Ops, SparseCore 0:
  11.8 105.9 all-gather.2
  129.4 97.1 all-gather.4
  359.5 116.1 reduce-scatter.4
  499.3 158.4 reduce-scatter.6

commit v10 on v8

--- a/solution.py
+++ b/solution.py
@@ -428,10 +428,11 @@
         all_rows, 2 * model_width
     )
     key_value_all = kv_grad_own.astype(jnp.float32)
-    combined = depth_weights[4] * block_out + history_part
+    block_side, _ = lax.optimization_barrier((block_out, kv_grad_flat))
+    combined = depth_weights[4] * block_side + history_part
     next_input = combined.astype(jnp.bfloat16).reshape(batches, 1, row_count, model_width)
     depth_terms = jnp.concatenate(
-        [jnp.einsum("jrd,rd->j", earlier, grad_next), jnp.sum(block_out * grad_next)[None]]
+        [jnp.einsum("jrd,rd->j", earlier, grad_next), jnp.sum(block_side * grad_next)[None]]
     )
     grad_down = jnp.einsum("rf,rd->fd", hidden_low, out_low, preferred_element_type=jnp.float32)
     grad_up = jnp.einsum("rd,rf->df", second_low, up_low, preferred_element_type=jnp.float32)
@@ -461,16 +462,16 @@
     input_part, gain_one, bias_one = first_pullback(first_grad)
     grad_input = (residual_grad + input_part).astype(jnp.bfloat16)
     grad_input = grad_input.reshape(batches, 1, row_count, model_width)
-    late_grads = jnp.concatenate(
+    norm_grads = jnp.concatenate(
         [
-            grad_qkv,
             jnp.stack([gain_one, gain_two], axis=1),
             jnp.stack([bias_one, bias_two], axis=1),
             jnp.zeros((model_width, lane_pad), jnp.float32),
         ],
         axis=1,
     ).astype(jnp.bfloat16)
-    packed_grads = lax.dynamic_update_slice(early_grads, late_grads, (0, 0))
+    packed_grads = lax.dynamic_update_slice(early_grads, grad_qkv.astype(jnp.bfloat16), (0, 0))
+    packed_grads = lax.dynamic_update_slice(packed_grads, norm_grads, (0, offsets[1]))
     device_count = model_width // shard_rows
     row_major = Layout(major_to_minor=(0, 1, 2))
     scattered = lax.psum_scatter(

time: 597 us -> 584 us (0.978)
  local copies, waits for them, and re-layouts: 60.6 us -> 49.8 us
  waiting for transfers between devices: 367 us -> 359 us
    reduce_scatter x1, waiting for transfers between devices: 80 us -> 67.9 us  [local(): lax.psum_scatter(kv_grad_flat, 'seq', scatter_dimension=0, tiled=True)]
    concatenate x1, local copies, waits for them, and re-layouts: 6.64 us -> 0.52 us  [local(): jnp.concatenate([jnp.stack([gain_one, gain_two], axis=1), jnp.stack([bias...]
  transfers between devices with their start and end apart: 4 -> 4, of which waited for: 4 -> 4; matrix products, arithmetic and copies ran while one was open for 12% -> 13% of each run, Pallas kernels for 0% -> 0%
where the time goes in v10:
time: 584 us; the launch traced here: 582 us
  waiting for transfers between devices  359 us (61%)
  matrix products  52.5 us (9%)
  local copies, waits for them, and re-layouts  49.8 us (9%)
  blocking collectives  39.5 us (7%)
  Pallas kernels  37.7 us (6%)
  other arithmetic  29.2 us (5%)
  between operations  14.4 us (2%)
    unnamed x5, waiting for transfers between devices  113 us
    all_gather x1, waiting for transfers between devices, local(): gathered = lax.all_gather(packed, ('seq', 'fsdp'), axis=0, tiled=True)  103 us
    all_gather x1, waiting for transfers between devices, local(): lax.all_gather(jnp.swapaxes(own_kv, 0, 1).reshape(row_count, batches * 2...  75.1 us
    reduce_scatter x1, waiting for transfers between devices, local(): lax.psum_scatter(kv_grad_flat, 'seq', scatter_dimension=0, tiled=True)  67.9 us
    psum x1, blocking collectives, local(): depth_total = lax.psum(depth_terms, ('seq', 'fsdp'))  39.5 us
    pallas_call x1, Pallas kernels, attention_backward(): pl.pallas_call(_backward_kernel, grid_spec=pltpu.PrefetchScalarGridSpec(n...  19.7 us
    pallas_call x1, Pallas kernels, attention_forward(): pl.pallas_call(_forward_kernel, grid_spec=pltpu.PrefetchScalarGridSpec(nu...  18.1 us
  transfers between devices with their start and end apart: 4, of which 4 were waited for; matrix products, arithmetic and copies ran while one was open for 13% of the time, Pallas kernels for 0%

profile of v10, /device:TPU:0, one launch (start us, length us, event | category | flops | bytes accessed | tf_op | source)
XLA Modules:
  0.0 582.3 jit_solution(2893615724462327672)
XLA Ops:
  9.8 1.8 concatenate.41
  15.0 102.8 %all-gather.3.cloned.1.call-done = bf16[768,9344]{1,0:T(8,128)(2,1)} async-done(((bf16[24,9344]{1,0:T(8,128)(2,1)}), bf16[768,9344]{1,0:T(8,128)(2,1)}) %all-gather.3.cloned.1.call-update) | async-done | bytes 14352400 | tf_op jit(solution)/shard_map/all_gather | solution.py:364
  119.9 3.2 fusion.14
  126.0 1.5 all_gather_reshape.3
  130.8 4.9 slice.147
  135.7 8.5 %reshape.325 = bf16[3072,768]{1,0:T(8,128)(2,1)} reshape(bf16[768,3072]{1,0:T(8,128)(2,1)} %slice.147) | data formatting | bytes 9437184 | tf_op jit(solution)/shard_map/reshape | solution.py:366
  144.2 5.5 fusion.42
  149.7 75.1 %all-gather.5.cloned.1.call-done = bf16[8,128,3072]{2,1,0:T(8,128)(2,1)} async-done(((bf16[1,128,3072]{2,1,0:T(8,128)(2,1)}), bf16[8,128,3072]{2,1,0:T(8,128)(2,1)}) %all-gather.5.cloned.1.call-update) | async-done | bytes 6291472 | tf_op jit(solution)/shard_map/all_gather | solution.py:393
  224.8 18.1 %attention_forward.1 = (f32[256,768]{1,0:T(8,128)}, f32[256,768]{1,0:T(8,128)}) custom-call(s32[3]{0:T(128)} %pad_add_fusion.scalars_ref, bf16[256,768]{1,0:T(8,128)(2,1)} %copy.54.q_ref, bf16[1024,3072]{1,0:T(8,128)(2,1)} %bitcast.91, bf16[1024,3072]{1,0:T(8,128)(2,1)} %bitcast.92), custom_call_target="tpu_custom_call" | custom-call | tf_op jit(solution)/shard_map/attention_forward/pallas_call | solution.py:275
  242.9 2.2 fusion.41
  245.4 7.3 %fusion.11 = (bf16[256,3072]{1,0:T(8,128)(2,1)S(1)}, f32[256,3072]{1,0:T(8,128)}) fusion(f32[256,3072]{1,0:T(8,128)S(1)} %copy-done.7, bf16[768,9344]{1,0:T(8,128)(2,1)} %all-gather.3.cloned.1.call-done, f32[256,768]{1,0:T(8,128)S(1)} %get-tuple-element.94, f32[768]{0:T(1024)S(1)} %get-tuple-element.59, f32[768]{0:T(1024)S(1)} %get-tuple-element.102, ...), kind=kOutput, calls=%fused_computation.17 | convolution fusion | flops 1224671232 | bytes 13377536 | tf_op jit(solution)/shard_map/dot_general | solution.py:407
  252.7 5.1 multiply_reduce_fusion.2
  258.9 2.5 convolution_convert_fusion.4.do_ref
  261.5 19.7 %attention_backward.1 = (f32[256,768]{1,0:T(8,128)}, bf16[1024,3072]{1,0:T(8,128)(2,1)}) custom-call(s32[3]{0:T(128)} %pad_add_fusion.scalars_ref, bf16[256,768]{1,0:T(8,128)(2,1)} %copy.54.q_ref, bf16[1024,3072]{1,0:T(8,128)(2,1)} %bitcast.93, bf16[1024,3072]{1,0:T(8,128)(2,1)} %bitcast.94, bf16[256,768]{1,0:T(8,128)(2,1)} %convolution_convert_fusion.4.do_ref, ...), custom_call_target="tpu_custom_call" | custom-call | tf_op jit(solution)/shard_map/attention_backward/pallas_call | solution.py:303
  282.0 3.6 fusion.16
  285.7 6.8 %convolution_add_fusion.1 = f32[256,768]{1,0:T(8,128)} fusion(f32[256,768]{1,0:T(8,128)S(1)} %get-tuple-element.94, bf16[3072,768]{1,0:T(8,128)(2,1)} %reshape.325, f32[256,3072]{1,0:T(8,128)} %get-tuple-element.96), kind=kOutput, calls=%fused_computation.29 | convolution fusion | flops 1215234048 | bytes 9437184 | tf_op jit(solution)/shard_map/dot_general | solution.py:409
  293.6 3.7 multiply_reduce_fusion.1
  298.2 5.1 convolution_convert_fusion.1
  303.3 8.6 %reshape.333 = bf16[768,3072]{1,0:T(8,128)(2,1)} reshape(bf16[3072,768]{1,0:T(8,128)(2,1)} %convolution_convert_fusion.1) | data formatting | bytes 9437184 | tf_op jit(solution)/shard_map/reshape | solution.py:447
  311.9 1.5 convolution_convert_fusion.3
  313.5 2.4 copy.58
  317.1 3.4 convolution_convert_fusion.2
  320.6 9.0 %pad_maximum_fusion = bf16[768,9344]{1,0:T(8,128)(2,1)} fusion(bf16[768,3072]{1,0:T(8,128)(2,1)S(1)} %bitcast.96, bf16[768,3072]{1,0:T(8,128)(2,1)S(1)} %convolution_convert_fusion.2, bf16[768,768]{1,0:T(8,128)(2,1)S(1)} %copy-done.3, bf16[9344]{0:T(1024)(128)(2,1)S(1)} %copy-done.14), kind=kLoop, calls=%fused_computation | loop fusion | flops 57409536 | bytes 24987904 | tf_op jit(solution)/shard_map/concatenate | solution.py:442
  329.6 67.9 %reduce-scatter.5.cloned.1.call-done = bf16[128,3072]{1,0:T(8,128)(2,1)} async-done(((bf16[1024,3072]{1,0:T(8,128)(2,1)}), bf16[128,3072]{1,0:T(8,128)(2,1)}) %reduce-scatter.5.cloned.1.call-update) | async-done | bytes 786448 | tf_op jit(solution)/shard_map/reduce_scatter | solution.py:424
  397.5 2.6 convert_element_type.140
  400.1 1.4 copy.57
  403.0 3.3 fusion.35
  406.3 2.9 fusion
  413.0 1.9 multiply_reduce_fusion
  415.6 1.5 multiply_convert_fusion
  417.2 39.5 %psum.7 = f32[5]{0:T(128)} all-reduce(f32[5]{0:T(128)S(1)} %pad_maximum_fusion.9), channel_id=1, replica_groups=mesh['seq'=8,'fsdp'=4] {'seq','fsdp'}, use_global_device_ids=true, to_apply=%region_15.16 | all-reduce | flops 5 | bytes 40 | tf_op jit(solution)/shard_map/psum | solution.py:495
  457.7 112.8 %reduce-scatter.7.cloned.1.call-done = bf16[1,24,9344]{2,1,0:T(8,128)(2,1)} async-done(((bf16[32,24,9344]{2,1,0:T(8,128)(2,1)}), bf16[1,24,9344]{2,1,0:T(8,128)(2,1)}) %reduce-scatter.7.cloned.1.call-update) | async-done | bytes 448528
  (139 shorter events, 31.8 us)
Async XLA Ops:
  7.2 112.5 %copy-start = (bf16[2,1,128,768]{3,2,1,0:T(8,128)(2,1)S(1)}, bf16[2,1,128,768]{3,2,1,0:T(8,128)(2,1)}, u32[]{:S(2)}) copy-start(bf16[2,1,128,768]{3,2,1,0:T(8,128)(2,1)} %param.11) | copy-start | bytes 1179652
  7.2 110.6 %all-gather.3.cloned.1.call-start = ((), (), s32[]{:S(2)}) async-start(), calls=%async_computation.2 | async-start | bytes 14800896 | tf_op jit(solution)/shard_map/all_gather | solution.py:364
  11.7 213.2 %all-gather.5.cloned.1.call-start = ((), (), s32[]{:S(2)}) async-start(), calls=%async_computation.3 | async-start | bytes 7077888 | tf_op jit(solution)/shard_map/all_gather | solution.py:393
  12.9 110.3 %copy-start.15 = (f32[256]{0:T(256)}, f32[256]{0:T(256)S(1)}, u32[]{:S(2)}) copy-start(f32[256]{0:T(256)S(1)} %get-tuple-element.91) | copy-start | bytes 3076
  14.2 109.0 %copy-start.17 = (f32[256]{0:T(256)}, f32[256]{0:T(256)S(1)}, u32[]{:S(2)}) copy-start(f32[256]{0:T(256)S(1)} %bitcast_rsqrt_fusion) | copy-start | bytes 3076
  119.9 3.3 copy-start.10
  125.0 2.8 copy-start.25
  125.0 3.4 copy-start.27
  125.0 4.1 copy-start.2
  127.5 270.0 %reduce-scatter.5.cloned.1.call-start = ((), (), s32[]{:S(2)}) async-start(), calls=%async_computation.4 | async-start | bytes 7077888 | tf_op jit(solution)/shard_map/reduce_scatter | solution.py:424
  129.0 6.7 %copy-start.23 = (pred[2,128]{1,0:T(4,128)(4,1)}, pred[2,128]{1,0:T(4,128)(4,1)S(1)}, u32[]{:S(2)}) copy-start(pred[2,128]{1,0:T(4,128)(4,1)S(1)} %broadcast_compare_fusion) | copy-start | bytes 772
  242.9 2.5 copy-start.7
  245.3 12.5 %copy-start.19 = (f32[256]{0:T(256)}, f32[256]{0:T(256)S(1)}, u32[]{:S(2)}) copy-start(f32[256]{0:T(256)S(1)} %fusion.27) | copy-start | bytes 3076
  252.7 5.1 copy-start.8
  281.2 289.4 %reduce-scatter.7.cloned.1.call-start = ((), (), s32[]{:S(2)}) async-start(), calls=%async_computation.5 | async-start | bytes 14800896
  285.7 6.8 %copy-start.9 = (f32[256,768]{1,0:T(8,128)S(1)}, f32[256,768]{1,0:T(8,128)}, u32[]{:S(2)}) copy-start(f32[256,768]{1,0:T(8,128)} %get-tuple-element.19) | copy-start | bytes 2359300
  293.6 4.7 copy-start.28
  303.3 8.6 %copy-start.1 = (f32[256,768]{1,0:T(8,128)S(1)}, f32[256,768]{1,0:T(8,128)}, u32[]{:S(2)}) copy-start(f32[256,768]{1,0:T(8,128)} %get-tuple-element.15.o_ref) | copy-start | bytes 2359300
  316.0 4.5 slice-start
  317.0 3.5 slice-start.1
  317.1 3.5 copy-start.3
  317.1 3.5 copy-start.14
  401.5 1.1 copy-start.6
  401.5 1.1 copy-start.12
  401.5 1.1 copy-start.13
  401.6 1.3 copy-start.16
  402.9 3.3 copy-start.21
  403.0 3.3 copy-start.11
  406.3 2.9 copy-start.18
  411.9 1.1 copy-start.5
  412.5 3.2 copy-start.26
  412.5 44.2 %copy-start.22 = (f32[256]{0:T(256)S(1)}, f32[256]{0:T(256)}, u32[]{:S(2)}) copy-start(f32[256]{0:T(256)} %get-tuple-element.53) | copy-start | bytes 3076
  (3 other events, 2.4 us)
Sparse Core Ops, SparseCore 0:
  11.8 105.9 all-gather.2
  127.7 97.1 all-gather.4
  281.3 116.1 reduce-scatter.4
  412.0 158.4 reduce-scatter.6

commit v11 on v10

--- a/solution.py
+++ b/solution.py
@@ -344,7 +344,6 @@
     offsets = [0]
     for width in widths:
         offsets.append(offsets[-1] + width)
-    late_width = offsets[4]
 
     def pieces(packed_rows):
         return [packed_rows[:, offsets[i] : offsets[i + 1]] for i in range(len(widths))]
@@ -441,7 +440,7 @@
     )
     early_grads = jnp.concatenate(
         [
-            jnp.zeros((model_width, late_width), jnp.float32),
+            jnp.zeros((model_width, 3 * model_width), jnp.float32),
             grad_outproj,
             grad_up,
             grad_down.reshape(model_width, ff_width),
@@ -462,37 +461,45 @@
     input_part, gain_one, bias_one = first_pullback(first_grad)
     grad_input = (residual_grad + input_part).astype(jnp.bfloat16)
     grad_input = grad_input.reshape(batches, 1, row_count, model_width)
-    norm_grads = jnp.concatenate(
-        [
-            jnp.stack([gain_one, gain_two], axis=1),
-            jnp.stack([bias_one, bias_two], axis=1),
-            jnp.zeros((model_width, lane_pad), jnp.float32),
-        ],
-        axis=1,
-    ).astype(jnp.bfloat16)
     packed_grads = lax.dynamic_update_slice(early_grads, grad_qkv.astype(jnp.bfloat16), (0, 0))
-    packed_grads = lax.dynamic_update_slice(packed_grads, norm_grads, (0, offsets[1]))
     device_count = model_width // shard_rows
     row_major = Layout(major_to_minor=(0, 1, 2))
+    grad_offsets = [0]
+    for width in (3 * model_width, model_width, ff_width, ff_width):
+        grad_offsets.append(grad_offsets[-1] + width)
     scattered = lax.psum_scatter(
         with_layout_constraint(
-            packed_grads.reshape(device_count, shard_rows, offsets[-1]), row_major
+            packed_grads.reshape(device_count, shard_rows, grad_offsets[-1]), row_major
         ),
         ("seq", "fsdp"),
         scatter_dimension=0,
         tiled=False,
     )
     scattered = with_layout_constraint(scattered, Layout(major_to_minor=(0, 1)))
-    full_pieces = pieces(scattered.astype(jnp.float32))
+    scattered = scattered.astype(jnp.float32)
+    full_pieces = [scattered[:, grad_offsets[i] : grad_offsets[i + 1]] for i in range(4)]
+    small_sums = lax.psum(
+        jnp.concatenate(
+            [
+                depth_terms,
+                jnp.stack([gain_one, gain_two, bias_one, bias_two], axis=1).reshape(-1),
+            ]
+        ),
+        ("seq", "fsdp"),
+    )
+    depth_total = small_sums[:5]
+    device_index = lax.axis_index("seq") * lax.axis_size("fsdp") + lax.axis_index("fsdp")
+    norm_owned = lax.dynamic_slice_in_dim(
+        small_sums[5:].reshape(model_width, 4), device_index * shard_rows, shard_rows, 0
+    )
     owned = [
         full_pieces[0],
-        full_pieces[4],
-        full_pieces[5],
-        full_pieces[6].reshape(-1, model_width),
         full_pieces[1],
         full_pieces[2],
+        full_pieces[3].reshape(-1, model_width),
+        norm_owned[:, :2],
+        norm_owned[:, 2:],
     ]
-    depth_total = lax.psum(depth_terms, ("seq", "fsdp"))
     return (next_input, grad_input, grad_history, *owned, depth_total)
 
 

time: 584 us -> 580 us (level)
    unnamed x5 -> x4, waiting for transfers between devices: 113 us -> 0.07 us
    reduce_scatter x0 -> x1, waiting for transfers between devices: none -> 111 us  [local(): lax.psum_scatter(with_layout_constraint(packed_grads.reshape(device_count...]
  transfers between devices with their start and end apart: 4 -> 4, of which waited for: 4 -> 4; matrix products, arithmetic and copies ran while one was open for 13% -> 14% of each run, Pallas kernels for 0% -> 0%
where the time goes in v11:
time: 580 us; the launch traced here: 579 us
  waiting for transfers between devices  360 us (62%)
  matrix products  52.1 us (9%)
  local copies, waits for them, and re-layouts  49.3 us (8%)
  blocking collectives  39.3 us (7%)
  Pallas kernels  37.7 us (7%)
  other arithmetic  26.4 us (5%)
  between operations  14.3 us (2%)
    reduce_scatter x1, waiting for transfers between devices, local(): lax.psum_scatter(with_layout_constraint(packed_grads.reshape(device_count...  111 us
    all_gather x1, waiting for transfers between devices, local(): gathered = lax.all_gather(packed, ('seq', 'fsdp'), axis=0, tiled=True)  103 us
    all_gather x1, waiting for transfers between devices, local(): lax.all_gather(jnp.swapaxes(own_kv, 0, 1).reshape(row_count, batches * 2...  75.1 us
    reduce_scatter x1, waiting for transfers between devices, local(): lax.psum_scatter(kv_grad_flat, 'seq', scatter_dimension=0, tiled=True)  69.9 us
    psum x1, blocking collectives, local(): lax.psum(jnp.concatenate([depth_terms, jnp.stack([gain_one, gain_two, bia...  39.3 us
    pallas_call x1, Pallas kernels, attention_backward(): pl.pallas_call(_backward_kernel, grid_spec=pltpu.PrefetchScalarGridSpec(n...  19.7 us
    pallas_call x1, Pallas kernels, attention_forward(): pl.pallas_call(_forward_kernel, grid_spec=pltpu.PrefetchScalarGridSpec(nu...  18.1 us
  transfers between devices with their start and end apart: 4, of which 4 were waited for; matrix products, arithmetic and copies ran while one was open for 14% of the time, Pallas kernels for 0%

profile of v11, /device:TPU:0, one launch (start us, length us, event | category | flops | bytes accessed | tf_op | source)
XLA Modules:
  0.0 579.2 jit_solution(11551924701487319775)
XLA Ops:
  9.8 1.8 concatenate.37
  12.9 1.2 multiply_reduce_fusion.7
  14.3 103.4 %all-gather.3.cloned.1.call-done = bf16[768,9344]{1,0:T(8,128)(2,1)} async-done(((bf16[24,9344]{1,0:T(8,128)(2,1)}), bf16[768,9344]{1,0:T(8,128)(2,1)}) %all-gather.3.cloned.1.call-update) | async-done | bytes 14352400 | tf_op jit(solution)/shard_map/all_gather | solution.py:363
  119.9 3.2 fusion.14
  127.0 1.5 all_gather_reshape.3
  131.8 4.9 slice.155
  136.7 8.5 %reshape.331 = bf16[3072,768]{1,0:T(8,128)(2,1)} reshape(bf16[768,3072]{1,0:T(8,128)(2,1)} %slice.155) | data formatting | bytes 9437184 | tf_op jit(solution)/shard_map/reshape | solution.py:365
  145.2 5.5 fusion.41
  150.7 75.1 %all-gather.5.cloned.1.call-done = bf16[8,128,3072]{2,1,0:T(8,128)(2,1)} async-done(((bf16[1,128,3072]{2,1,0:T(8,128)(2,1)}), bf16[8,128,3072]{2,1,0:T(8,128)(2,1)}) %all-gather.5.cloned.1.call-update) | async-done | bytes 6291472 | tf_op jit(solution)/shard_map/all_gather | solution.py:392
  225.7 18.1 %attention_forward.1 = (f32[256,768]{1,0:T(8,128)}, f32[256,768]{1,0:T(8,128)}) custom-call(s32[3]{0:T(128)} %pad_add_fusion.scalars_ref, bf16[256,768]{1,0:T(8,128)(2,1)} %copy.49.q_ref, bf16[1024,3072]{1,0:T(8,128)(2,1)} %bitcast.91, bf16[1024,3072]{1,0:T(8,128)(2,1)} %bitcast.92), custom_call_target="tpu_custom_call" | custom-call | tf_op jit(solution)/shard_map/attention_forward/pallas_call | solution.py:275
  243.8 2.2 fusion.40
  246.3 7.3 %fusion.11 = (bf16[256,3072]{1,0:T(8,128)(2,1)S(1)}, f32[256,3072]{1,0:T(8,128)}) fusion(f32[256,3072]{1,0:T(8,128)S(1)} %copy-done.8, bf16[768,9344]{1,0:T(8,128)(2,1)} %all-gather.3.cloned.1.call-done, f32[256,768]{1,0:T(8,128)S(1)} %get-tuple-element.93, f32[768]{0:T(1024)S(1)} %get-tuple-element.58, f32[768]{0:T(1024)S(1)} %get-tuple-element.102, ...), kind=kOutput, calls=%fused_computation.17 | convolution fusion | flops 1224671232 | bytes 13377536 | tf_op jit(solution)/shard_map/dot_general | solution.py:406
  253.6 4.5 multiply_reduce_fusion.1
  259.4 2.5 convolution_convert_fusion.4.do_ref
  261.9 19.7 %attention_backward.1 = (f32[256,768]{1,0:T(8,128)}, bf16[1024,3072]{1,0:T(8,128)(2,1)}) custom-call(s32[3]{0:T(128)} %pad_add_fusion.scalars_ref, bf16[256,768]{1,0:T(8,128)(2,1)} %copy.49.q_ref, bf16[1024,3072]{1,0:T(8,128)(2,1)} %bitcast.93, bf16[1024,3072]{1,0:T(8,128)(2,1)} %bitcast.94, bf16[256,768]{1,0:T(8,128)(2,1)} %convolution_convert_fusion.4.do_ref, ...), custom_call_target="tpu_custom_call" | custom-call | tf_op jit(solution)/shard_map/attention_backward/pallas_call | solution.py:303
  281.9 3.6 fusion.16
  285.5 6.7 %convolution_add_fusion.1 = f32[256,768]{1,0:T(8,128)} fusion(f32[256,768]{1,0:T(8,128)S(1)} %get-tuple-element.93, bf16[3072,768]{1,0:T(8,128)(2,1)} %reshape.331, f32[256,3072]{1,0:T(8,128)} %get-tuple-element.95), kind=kOutput, calls=%fused_computation.29 | convolution fusion | flops 1215234048 | bytes 9437184 | tf_op jit(solution)/shard_map/dot_general | solution.py:408
  293.4 3.9 multiply_reduce_fusion.3
  298.2 5.1 convolution_convert_fusion.1
  303.3 8.6 %reshape.339 = bf16[768,3072]{1,0:T(8,128)(2,1)} reshape(bf16[3072,768]{1,0:T(8,128)(2,1)} %convolution_convert_fusion.1) | data formatting | bytes 9437184 | tf_op jit(solution)/shard_map/reshape | solution.py:446
  311.8 1.5 convolution_convert_fusion.3
  313.4 2.4 copy.53
  315.8 3.2 convolution_convert_fusion.2
  319.1 8.9 %pad_maximum_fusion = bf16[768,9216]{1,0:T(8,128)(2,1)} fusion(bf16[768,3072]{1,0:T(8,128)(2,1)S(1)} %bitcast.97, bf16[768,3072]{1,0:T(8,128)(2,1)S(1)} %convolution_convert_fusion.2, bf16[768,768]{1,0:T(8,128)(2,1)S(1)} %copy-done.4, bf16[9216]{0:T(1024)(128)(2,1)S(1)} %pad.4.clone), kind=kLoop, calls=%fused_computation | loop fusion | flops 56623104 | bytes 24791040 | tf_op jit(solution)/shard_map/concatenate | solution.py:441
  328.0 69.9 %reduce-scatter.3.cloned.1.call-done = bf16[128,3072]{1,0:T(8,128)(2,1)} async-done(((bf16[1024,3072]{1,0:T(8,128)(2,1)}), bf16[128,3072]{1,0:T(8,128)(2,1)}) %reduce-scatter.3.cloned.1.call-update) | async-done | bytes 786448 | tf_op jit(solution)/shard_map/reduce_scatter | solution.py:423
  397.9 2.6 convert_element_type.139
  400.5 1.4 copy.52
  403.4 2.9 fusion
  407.5 1.5 multiply_convert_fusion
  409.7 3.6 multiply_reduce_fusion.4
  415.0 39.3 %psum.7 = f32[3077]{0:T(1024)S(1)} all-reduce(f32[3077]{0:T(1024)S(1)} %concatenate.45), channel_id=1, replica_groups=mesh['seq'=8,'fsdp'=4] {'seq','fsdp'}, use_global_device_ids=true, to_apply=%region_15.16 | all-reduce | flops 3077 | bytes 24616 | tf_op jit(solution)/shard_map/psum | solution.py:481
  457.7 111.1 %reduce-scatter.5.cloned.1.call-done = bf16[1,24,9216]{2,1,0:T(8,128)(2,1)} async-done(((bf16[32,24,9216]{2,1,0:T(8,128)(2,1)}), bf16[1,24,9216]{2,1,0:T(8,128)(2,1)}) %reduce-scatter.5.cloned.1.call-update) | async-done | bytes 442384 | tf_op jit(solution)/shard_map/reduce_scatter | solution.py:470
  (120 shorter events, 29.2 us)
Async XLA Ops:
  7.2 112.5 %copy-start = (bf16[2,1,128,768]{3,2,1,0:T(8,128)(2,1)S(1)}, bf16[2,1,128,768]{3,2,1,0:T(8,128)(2,1)}, u32[]{:S(2)}) copy-start(bf16[2,1,128,768]{3,2,1,0:T(8,128)(2,1)} %param.11) | copy-start | bytes 1179652
  7.2 110.6 %all-gather.3.cloned.1.call-start = ((), (), s32[]{:S(2)}) async-start(), calls=%async_computation.2 | async-start | bytes 14800896 | tf_op jit(solution)/shard_map/all_gather | solution.py:363
  11.7 214.1 %all-gather.5.cloned.1.call-start = ((), (), s32[]{:S(2)}) async-start(), calls=%async_computation.3 | async-start | bytes 7077888 | tf_op jit(solution)/shard_map/all_gather | solution.py:392
  119.9 3.3 copy-start.12
  124.9 3.8 copy-start.15
  124.9 4.4 copy-start.16
  124.9 5.1 copy-start.2
  128.5 269.5 %reduce-scatter.3.cloned.1.call-start = ((), (), s32[]{:S(2)}) async-start(), calls=%async_computation.4 | async-start | bytes 7077888 | tf_op jit(solution)/shard_map/reduce_scatter | solution.py:423
  243.8 2.5 copy-start.8
  253.6 4.5 copy-start.10
  281.6 287.2 %reduce-scatter.5.cloned.1.call-start = ((), (), s32[]{:S(2)}) async-start(), calls=%async_computation.5 | async-start | bytes 14598144 | tf_op jit(solution)/shard_map/reduce_scatter | solution.py:470
  285.5 6.7 %copy-start.11 = (f32[256,768]{1,0:T(8,128)S(1)}, f32[256,768]{1,0:T(8,128)}, u32[]{:S(2)}) copy-start(f32[256,768]{1,0:T(8,128)} %get-tuple-element.19) | copy-start | bytes 2359300
  293.4 4.7 copy-start.17
  297.3 0.9 copy-start.5
  303.3 8.6 %copy-start.1 = (f32[256,768]{1,0:T(8,128)S(1)}, f32[256,768]{1,0:T(8,128)}, u32[]{:S(2)}) copy-start(f32[256,768]{1,0:T(8,128)} %get-tuple-element.15.o_ref) | copy-start | bytes 2359300
  313.4 5.7 slice-start
  315.8 3.2 slice-start.1
  315.8 3.2 copy-start.4
  401.9 1.2 copy-start.7
  402.0 1.4 copy-start.13
  402.1 4.2 copy-start.14
  406.3 1.0 copy-start.3
  406.4 2.7 copy-start.6
  407.3 1.7 copy-start.9
Sparse Core Ops, SparseCore 0:
  11.8 105.9 all-gather.2
  128.6 97.1 all-gather.4
  281.7 116.1 reduce-scatter.2
  406.5 162.2 reduce-scatter.4

commit v12 on v11

--- a/solution.py
+++ b/solution.py
@@ -11,6 +11,7 @@
 
 HEADS = 12
 HEAD = 64
+STEP_HEADS = 4
 
 
 epsilon = 1e-05
@@ -198,7 +199,7 @@
     row_count = q_ref.shape[0]
     key_count = k_ref.shape[0]
     allowed = _pair_masks(scalars_ref, micro, row_count, key_count)
-    for half in range(2):
+    for half in range(STEP_HEADS):
         lanes = slice(half * HEAD, (half + 1) * HEAD)
         q_head = q_ref[:, lanes]
         k_head = k_ref[:, lanes]
@@ -226,7 +227,7 @@
     row_count = q_ref.shape[0]
     key_count = k_ref.shape[0]
     allowed = _pair_masks(scalars_ref, micro, row_count, key_count)
-    for half in range(2):
+    for half in range(STEP_HEADS):
         lanes = slice(half * HEAD, (half + 1) * HEAD)
         q_head = q_ref[:, lanes]
         k_head = k_ref[:, lanes]
@@ -256,7 +257,7 @@
             preferred_element_type=jnp.float32,
         )
         kv_grad_ref[:, lanes] = key_grad.astype(jnp.bfloat16)
-        kv_grad_ref[:, 2 * HEAD + half * HEAD : 2 * HEAD + (half + 1) * HEAD] = value_grad.astype(
+        kv_grad_ref[:, STEP_HEADS * HEAD + half * HEAD : STEP_HEADS * HEAD + (half + 1) * HEAD] = value_grad.astype(
             jnp.bfloat16
         )
 
@@ -265,12 +266,12 @@
     all_rows, model_width = queries.shape
     row_count = all_rows // batches
     key_count = kv_flat.shape[0]
-    pairs = model_width // (2 * HEAD)
-    micro_blocks = kv_flat.shape[1] // batches // (2 * HEAD)
-    row_spec = pl.BlockSpec((row_count, 2 * HEAD), lambda m, p, s: (m, p))
-    key_spec = pl.BlockSpec((key_count, 2 * HEAD), lambda m, p, s: (0, m * micro_blocks + p))
+    pairs = model_width // (STEP_HEADS * HEAD)
+    micro_blocks = kv_flat.shape[1] // batches // (STEP_HEADS * HEAD)
+    row_spec = pl.BlockSpec((row_count, STEP_HEADS * HEAD), lambda m, p, s: (m, p))
+    key_spec = pl.BlockSpec((key_count, STEP_HEADS * HEAD), lambda m, p, s: (0, m * micro_blocks + p))
     value_spec = pl.BlockSpec(
-        (key_count, 2 * HEAD), lambda m, p, s: (0, m * micro_blocks + pairs + p)
+        (key_count, STEP_HEADS * HEAD), lambda m, p, s: (0, m * micro_blocks + pairs + p)
     )
     return pl.pallas_call(
         _forward_kernel,
@@ -292,14 +293,14 @@
     all_rows, model_width = queries.shape
     row_count = all_rows // batches
     key_count = kv_flat.shape[0]
-    pairs = model_width // (2 * HEAD)
-    micro_blocks = kv_flat.shape[1] // batches // (2 * HEAD)
-    row_spec = pl.BlockSpec((row_count, 2 * HEAD), lambda m, p, s: (m, p))
-    key_spec = pl.BlockSpec((key_count, 2 * HEAD), lambda m, p, s: (0, m * micro_blocks + p))
+    pairs = model_width // (STEP_HEADS * HEAD)
+    micro_blocks = kv_flat.shape[1] // batches // (STEP_HEADS * HEAD)
+    row_spec = pl.BlockSpec((row_count, STEP_HEADS * HEAD), lambda m, p, s: (m, p))
+    key_spec = pl.BlockSpec((key_count, STEP_HEADS * HEAD), lambda m, p, s: (0, m * micro_blocks + p))
     value_spec = pl.BlockSpec(
-        (key_count, 2 * HEAD), lambda m, p, s: (0, m * micro_blocks + pairs + p)
-    )
-    grad_spec = pl.BlockSpec((key_count, 4 * HEAD), lambda m, p, s: (0, m * pairs + p))
+        (key_count, STEP_HEADS * HEAD), lambda m, p, s: (0, m * micro_blocks + pairs + p)
+    )
+    grad_spec = pl.BlockSpec((key_count, 2 * STEP_HEADS * HEAD), lambda m, p, s: (0, m * pairs + p))
     return pl.pallas_call(
         _backward_kernel,
         grid_spec=pltpu.PrefetchScalarGridSpec(
@@ -421,8 +422,8 @@
         scalars, queries, kv_flat, attended_grad, attended_rows, log_totals, batches
     )
     kv_grad_own = lax.psum_scatter(kv_grad_flat, "seq", scatter_dimension=0, tiled=True)
-    pairs = model_width // (2 * HEAD)
-    kv_grad_own = kv_grad_own.reshape(row_count, batches, pairs, 2, 2 * HEAD)
+    pairs = model_width // (STEP_HEADS * HEAD)
+    kv_grad_own = kv_grad_own.reshape(row_count, batches, pairs, 2, STEP_HEADS * HEAD)
     kv_grad_own = jnp.transpose(kv_grad_own, (1, 0, 3, 2, 4)).reshape(
         all_rows, 2 * model_width
     )

time: 580 us -> 583 us (level)
  no operation moved by 1% of the time
where the time goes in v12:
time: 583 us; the launch traced here: 577 us
  waiting for transfers between devices  359 us (62%)
  matrix products  52.1 us (9%)
  local copies, waits for them, and re-layouts  49.6 us (9%)
  blocking collectives  39.3 us (7%)
  Pallas kernels  35.8 us (6%)
  other arithmetic  26.4 us (5%)
  between operations  14.5 us (2%)
    reduce_scatter x1, waiting for transfers between devices, local(): lax.psum_scatter(with_layout_constraint(packed_grads.reshape(device_count...  111 us
    all_gather x1, waiting for transfers between devices, local(): gathered = lax.all_gather(packed, ('seq', 'fsdp'), axis=0, tiled=True)  103 us
    all_gather x1, waiting for transfers between devices, local(): lax.all_gather(jnp.swapaxes(own_kv, 0, 1).reshape(row_count, batches * 2...  74.7 us
    reduce_scatter x1, waiting for transfers between devices, local(): lax.psum_scatter(kv_grad_flat, 'seq', scatter_dimension=0, tiled=True)  70 us
    psum x1, blocking collectives, local(): lax.psum(jnp.concatenate([depth_terms, jnp.stack([gain_one, gain_two, bia...  39.3 us
    pallas_call x1, Pallas kernels, attention_backward(): pl.pallas_call(_backward_kernel, grid_spec=pltpu.PrefetchScalarGridSpec(n...  19.4 us
    pallas_call x1, Pallas kernels, attention_forward(): pl.pallas_call(_forward_kernel, grid_spec=pltpu.PrefetchScalarGridSpec(nu...  16.4 us
  transfers between devices with their start and end apart: 4, of which 4 were waited for; matrix products, arithmetic and copies ran while one was open for 14% of the time, Pallas kernels for 0%

profile of v12, /device:TPU:0, one launch (start us, length us, event | category | flops | bytes accessed | tf_op | source)
XLA Modules:
  0.0 577.2 jit_solution(17148170631234470015)
XLA Ops:
  9.8 1.8 concatenate.37
  12.9 1.2 multiply_reduce_fusion.7
  14.3 103.4 %all-gather.3.cloned.1.call-done = bf16[768,9344]{1,0:T(8,128)(2,1)} async-done(((bf16[24,9344]{1,0:T(8,128)(2,1)}), bf16[768,9344]{1,0:T(8,128)(2,1)}) %all-gather.3.cloned.1.call-update) | async-done | bytes 14352400 | tf_op jit(solution)/shard_map/all_gather | solution.py:364
  119.9 3.2 fusion.14
  127.0 1.5 all_gather_reshape.3
  132.1 5.0 slice.155
  137.1 8.5 %reshape.331 = bf16[3072,768]{1,0:T(8,128)(2,1)} reshape(bf16[768,3072]{1,0:T(8,128)(2,1)} %slice.155) | data formatting | bytes 9437184 | tf_op jit(solution)/shard_map/reshape | solution.py:366
  145.6 5.5 fusion.41
  151.0 74.7 %all-gather.5.cloned.1.call-done = bf16[8,128,3072]{2,1,0:T(8,128)(2,1)} async-done(((bf16[1,128,3072]{2,1,0:T(8,128)(2,1)}), bf16[8,128,3072]{2,1,0:T(8,128)(2,1)}) %all-gather.5.cloned.1.call-update) | async-done | bytes 6291472 | tf_op jit(solution)/shard_map/all_gather | solution.py:393
  225.7 16.4 %attention_forward.1 = (f32[256,768]{1,0:T(8,128)}, f32[256,768]{1,0:T(8,128)}) custom-call(s32[3]{0:T(128)} %pad_add_fusion.scalars_ref, bf16[256,768]{1,0:T(8,128)(2,1)} %copy.49.q_ref, bf16[1024,3072]{1,0:T(8,128)(2,1)} %bitcast.91, bf16[1024,3072]{1,0:T(8,128)(2,1)} %bitcast.92), custom_call_target="tpu_custom_call" | custom-call | tf_op jit(solution)/shard_map/attention_forward/pallas_call | solution.py:276
  242.1 2.2 fusion.40
  244.6 7.3 %fusion.11 = (bf16[256,3072]{1,0:T(8,128)(2,1)S(1)}, f32[256,3072]{1,0:T(8,128)}) fusion(f32[256,3072]{1,0:T(8,128)S(1)} %copy-done.8, bf16[768,9344]{1,0:T(8,128)(2,1)} %all-gather.3.cloned.1.call-done, f32[256,768]{1,0:T(8,128)S(1)} %get-tuple-element.93, f32[768]{0:T(1024)S(1)} %get-tuple-element.58, f32[768]{0:T(1024)S(1)} %get-tuple-element.102, ...), kind=kOutput, calls=%fused_computation.17 | convolution fusion | flops 1224671232 | bytes 13377536 | tf_op jit(solution)/shard_map/dot_general | solution.py:407
  251.9 4.5 multiply_reduce_fusion.1
  257.7 2.5 convolution_convert_fusion.4.do_ref
  260.2 19.4 %attention_backward.1 = (f32[256,768]{1,0:T(8,128)}, bf16[1024,3072]{1,0:T(8,128)(2,1)}) custom-call(s32[3]{0:T(128)} %pad_add_fusion.scalars_ref, bf16[256,768]{1,0:T(8,128)(2,1)} %copy.49.q_ref, bf16[1024,3072]{1,0:T(8,128)(2,1)} %bitcast.93, bf16[1024,3072]{1,0:T(8,128)(2,1)} %bitcast.94, bf16[256,768]{1,0:T(8,128)(2,1)} %convolution_convert_fusion.4.do_ref, ...), custom_call_target="tpu_custom_call" | custom-call | tf_op jit(solution)/shard_map/attention_backward/pallas_call | solution.py:304
  279.7 3.6 fusion.16
  283.3 6.7 %convolution_add_fusion.1 = f32[256,768]{1,0:T(8,128)} fusion(f32[256,768]{1,0:T(8,128)S(1)} %get-tuple-element.93, bf16[3072,768]{1,0:T(8,128)(2,1)} %reshape.331, f32[256,3072]{1,0:T(8,128)} %get-tuple-element.95), kind=kOutput, calls=%fused_computation.29 | convolution fusion | flops 1215234048 | bytes 9437184 | tf_op jit(solution)/shard_map/dot_general | solution.py:409
  291.3 3.9 multiply_reduce_fusion.3
  296.0 5.1 convolution_convert_fusion.1
  301.1 8.7 %reshape.339 = bf16[768,3072]{1,0:T(8,128)(2,1)} reshape(bf16[3072,768]{1,0:T(8,128)(2,1)} %convolution_convert_fusion.1) | data formatting | bytes 9437184 | tf_op jit(solution)/shard_map/reshape | solution.py:447
  309.9 1.5 convolution_convert_fusion.3
  311.4 2.4 copy.53
  313.8 3.2 convolution_convert_fusion.2
  317.1 8.9 %pad_maximum_fusion = bf16[768,9216]{1,0:T(8,128)(2,1)} fusion(bf16[768,3072]{1,0:T(8,128)(2,1)S(1)} %bitcast.97, bf16[768,3072]{1,0:T(8,128)(2,1)S(1)} %convolution_convert_fusion.2, bf16[768,768]{1,0:T(8,128)(2,1)S(1)} %copy-done.4, bf16[9216]{0:T(1024)(128)(2,1)S(1)} %pad.4.clone), kind=kLoop, calls=%fused_computation | loop fusion | flops 56623104 | bytes 24791040 | tf_op jit(solution)/shard_map/concatenate | solution.py:442
  326.0 70.0 %reduce-scatter.3.cloned.1.call-done = bf16[128,3072]{1,0:T(8,128)(2,1)} async-done(((bf16[1024,3072]{1,0:T(8,128)(2,1)}), bf16[128,3072]{1,0:T(8,128)(2,1)}) %reduce-scatter.3.cloned.1.call-update) | async-done | bytes 786448 | tf_op jit(solution)/shard_map/reduce_scatter | solution.py:424
  396.0 2.6 convert_element_type.139
  398.6 1.4 copy.52
  401.5 2.9 fusion
  405.6 1.5 multiply_convert_fusion
  407.7 3.6 multiply_reduce_fusion.4
  413.0 39.3 %psum.7 = f32[3077]{0:T(1024)S(1)} all-reduce(f32[3077]{0:T(1024)S(1)} %concatenate.45), channel_id=1, replica_groups=mesh['seq'=8,'fsdp'=4] {'seq','fsdp'}, use_global_device_ids=true, to_apply=%region_15.16 | all-reduce | flops 3077 | bytes 24616 | tf_op jit(solution)/shard_map/psum | solution.py:482
  455.8 110.7 %reduce-scatter.5.cloned.1.call-done = bf16[1,24,9216]{2,1,0:T(8,128)(2,1)} async-done(((bf16[32,24,9216]{2,1,0:T(8,128)(2,1)}), bf16[1,24,9216]{2,1,0:T(8,128)(2,1)}) %reduce-scatter.5.cloned.1.call-update) | async-done | bytes 442384 | tf_op jit(solution)/shard_map/reduce_scatter | solution.py:471
  (120 shorter events, 29.2 us)
Async XLA Ops:
  7.2 112.5 %copy-start = (bf16[2,1,128,768]{3,2,1,0:T(8,128)(2,1)S(1)}, bf16[2,1,128,768]{3,2,1,0:T(8,128)(2,1)}, u32[]{:S(2)}) copy-start(bf16[2,1,128,768]{3,2,1,0:T(8,128)(2,1)} %param.11) | copy-start | bytes 1179652
  7.2 110.6 %all-gather.3.cloned.1.call-start = ((), (), s32[]{:S(2)}) async-start(), calls=%async_computation.2 | async-start | bytes 14800896 | tf_op jit(solution)/shard_map/all_gather | solution.py:364
  11.7 214.1 %all-gather.5.cloned.1.call-start = ((), (), s32[]{:S(2)}) async-start(), calls=%async_computation.3 | async-start | bytes 7077888 | tf_op jit(solution)/shard_map/all_gather | solution.py:393
  119.9 3.3 copy-start.12
  124.9 4.1 copy-start.15
  124.9 4.7 copy-start.16
  124.9 5.4 copy-start.2
  128.5 267.5 %reduce-scatter.3.cloned.1.call-start = ((), (), s32[]{:S(2)}) async-start(), calls=%async_computation.4 | async-start | bytes 7077888 | tf_op jit(solution)/shard_map/reduce_scatter | solution.py:424
  242.1 2.5 copy-start.8
  251.9 4.5 copy-start.10
  279.6 286.8 %reduce-scatter.5.cloned.1.call-start = ((), (), s32[]{:S(2)}) async-start(), calls=%async_computation.5 | async-start | bytes 14598144 | tf_op jit(solution)/shard_map/reduce_scatter | solution.py:471
  283.3 6.7 %copy-start.11 = (f32[256,768]{1,0:T(8,128)S(1)}, f32[256,768]{1,0:T(8,128)}, u32[]{:S(2)}) copy-start(f32[256,768]{1,0:T(8,128)} %get-tuple-element.19) | copy-start | bytes 2359300
  291.3 4.8 copy-start.17
  295.1 0.9 copy-start.5
  301.1 8.7 %copy-start.1 = (f32[256,768]{1,0:T(8,128)S(1)}, f32[256,768]{1,0:T(8,128)}, u32[]{:S(2)}) copy-start(f32[256,768]{1,0:T(8,128)} %get-tuple-element.15.o_ref) | copy-start | bytes 2359300
  311.4 5.6 slice-start
  313.8 3.2 slice-start.1
  313.8 3.2 copy-start.4
  400.0 1.2 copy-start.7
  400.1 1.4 copy-start.13
  400.2 4.2 copy-start.14
  404.4 1.0 copy-start.3
  404.4 2.7 copy-start.6
  405.4 1.7 copy-start.9
Sparse Core Ops, SparseCore 0:
  11.8 105.9 all-gather.2
  128.6 97.1 all-gather.4
  279.8 116.1 reduce-scatter.2
  404.6 161.8 reduce-scatter.4

commit v13 on v12

--- a/solution.py
+++ b/solution.py
@@ -194,7 +194,7 @@
     return (key_pos <= query_pos) & (key_pos < length)
 
 
-def _forward_kernel(scalars_ref, q_ref, k_ref, v_ref, out_ref, lse_ref):
+def _forward_kernel(scalars_ref, q_ref, k_ref, v_ref, out_ref, prob_ref):
     micro = pl.program_id(0)
     row_count = q_ref.shape[0]
     key_count = k_ref.shape[0]
@@ -211,33 +211,24 @@
         top = jnp.max(masked, axis=1, keepdims=True)
         kept = jnp.where(allowed, jnp.exp(masked - top), 0.0)
         total = jnp.sum(kept, axis=1, keepdims=True)
-        log_total = top + jnp.log(total)
         probabilities = kept * (1.0 / total)
+        prob_ref[half] = probabilities
         attended = jnp.dot(
             probabilities.astype(jnp.bfloat16), v_head, preferred_element_type=jnp.float32
         )
         out_ref[:, lanes] = attended
-        lse_ref[:, lanes] = jnp.broadcast_to(log_total, (row_count, HEAD))
 
 
 def _backward_kernel(
-    scalars_ref, q_ref, k_ref, v_ref, do_ref, o_ref, lse_ref, dq_ref, kv_grad_ref
+    scalars_ref, q_ref, k_ref, v_ref, do_ref, o_ref, prob_ref, dq_ref, kv_grad_ref
 ):
-    micro = pl.program_id(0)
-    row_count = q_ref.shape[0]
-    key_count = k_ref.shape[0]
-    allowed = _pair_masks(scalars_ref, micro, row_count, key_count)
     for half in range(STEP_HEADS):
         lanes = slice(half * HEAD, (half + 1) * HEAD)
         q_head = q_ref[:, lanes]
         k_head = k_ref[:, lanes]
         v_head = v_ref[:, lanes]
         grad_head = do_ref[:, lanes]
-        scores = lax.dot_general(
-            q_head, k_head, (((1,), (1,)), ((), ())), preferred_element_type=jnp.float32
-        ) * HEAD ** (-0.5)
-        log_total = lse_ref[:, half * HEAD : half * HEAD + 1]
-        probabilities = jnp.where(allowed, jnp.exp(scores - log_total), 0.0)
+        probabilities = prob_ref[half]
         probabilities_low = probabilities.astype(jnp.bfloat16)
         prob_grad = lax.dot_general(
             grad_head, v_head, (((1,), (1,)), ((), ())), preferred_element_type=jnp.float32
@@ -273,23 +264,26 @@
     value_spec = pl.BlockSpec(
         (key_count, STEP_HEADS * HEAD), lambda m, p, s: (0, m * micro_blocks + pairs + p)
     )
+    prob_spec = pl.BlockSpec(
+        (STEP_HEADS, row_count, key_count), lambda m, p, s: (m * pairs + p, 0, 0)
+    )
     return pl.pallas_call(
         _forward_kernel,
         grid_spec=pltpu.PrefetchScalarGridSpec(
             num_scalar_prefetch=1,
             grid=(batches, pairs),
             in_specs=[row_spec, key_spec, value_spec],
-            out_specs=[row_spec, row_spec],
+            out_specs=[row_spec, prob_spec],
         ),
         out_shape=[
             jax.ShapeDtypeStruct((all_rows, model_width), jnp.float32),
-            jax.ShapeDtypeStruct((all_rows, model_width), jnp.float32),
+            jax.ShapeDtypeStruct((batches * HEADS, row_count, key_count), jnp.float32),
         ],
         name="attention_forward",
     )(scalars, queries, kv_flat, kv_flat)
 
 
-def attention_backward(scalars, queries, kv_flat, grads, attended, log_totals, batches):
+def attention_backward(scalars, queries, kv_flat, grads, attended, probabilities, batches):
     all_rows, model_width = queries.shape
     row_count = all_rows // batches
     key_count = kv_flat.shape[0]
@@ -301,12 +295,15 @@
         (key_count, STEP_HEADS * HEAD), lambda m, p, s: (0, m * micro_blocks + pairs + p)
     )
     grad_spec = pl.BlockSpec((key_count, 2 * STEP_HEADS * HEAD), lambda m, p, s: (0, m * pairs + p))
+    prob_spec = pl.BlockSpec(
+        (STEP_HEADS, row_count, key_count), lambda m, p, s: (m * pairs + p, 0, 0)
+    )
     return pl.pallas_call(
         _backward_kernel,
         grid_spec=pltpu.PrefetchScalarGridSpec(
             num_scalar_prefetch=1,
             grid=(batches, pairs),
-            in_specs=[row_spec, key_spec, value_spec, row_spec, row_spec, row_spec],
+            in_specs=[row_spec, key_spec, value_spec, row_spec, row_spec, prob_spec],
             out_specs=[row_spec, grad_spec],
         ),
         out_shape=[
@@ -314,7 +311,7 @@
             jax.ShapeDtypeStruct(kv_flat.shape, jnp.bfloat16),
         ],
         name="attention_backward",
-    )(scalars, queries, kv_flat, kv_flat, grads, attended, log_totals)
+    )(scalars, queries, kv_flat, kv_flat, grads, attended, probabilities)
 
 
 def local(
@@ -400,7 +397,7 @@
     scalars = jnp.concatenate(
         [slot_lengths.astype(jnp.int32), (lax.axis_index("seq") * row_count)[None].astype(jnp.int32)]
     )
-    attended_rows, log_totals = attention_forward(scalars, queries, kv_flat, batches)
+    attended_rows, probabilities = attention_forward(scalars, queries, kv_flat, batches)
     attended_low = attended_rows.astype(jnp.bfloat16)
     residual = inputs + jnp.dot(attended_low, full_out, preferred_element_type=jnp.float32)
     second_low = layer_norm(residual, norm_gains[:, 1], norm_biases[:, 1]).astype(jnp.bfloat16)
@@ -419,7 +416,7 @@
         "rd,cd->rc", branch_low, full_out, preferred_element_type=jnp.float32
     ).astype(jnp.bfloat16)
     query_grad, kv_grad_flat = attention_backward(
-        scalars, queries, kv_flat, attended_grad, attended_rows, log_totals, batches
+        scalars, queries, kv_flat, attended_grad, attended_rows, probabilities, batches
     )
     kv_grad_own = lax.psum_scatter(kv_grad_flat, "seq", scatter_dimension=0, tiled=True)
     pairs = model_width // (STEP_HEADS * HEAD)

time: 583 us -> 587 us (level)
  no operation moved by 1% of the time
where the time goes in v13:
time: 587 us; the launch traced here: 582 us
  waiting for transfers between devices  359 us (61%)
  matrix products  52 us (9%)
  local copies, waits for them, and re-layouts  49.4 us (8%)
  Pallas kernels  40.1 us (7%)
  blocking collectives  39.3 us (7%)
  other arithmetic  26.4 us (4%)
  between operations  14.7 us (3%)
    reduce_scatter x1, waiting for transfers between devices, local(): lax.psum_scatter(with_layout_constraint(packed_grads.reshape(device_count...  111 us
    all_gather x1, waiting for transfers between devices, local(): gathered = lax.all_gather(packed, ('seq', 'fsdp'), axis=0, tiled=True)  103 us
    all_gather x1, waiting for transfers between devices, local(): lax.all_gather(jnp.swapaxes(own_kv, 0, 1).reshape(row_count, batches * 2...  75.2 us
    reduce_scatter x1, waiting for transfers between devices, local(): lax.psum_scatter(kv_grad_flat, 'seq', scatter_dimension=0, tiled=True)  70 us
    psum x1, blocking collectives, local(): lax.psum(jnp.concatenate([depth_terms, jnp.stack([gain_one, gain_two, bia...  39.3 us
    pallas_call x1, Pallas kernels, attention_backward(): pl.pallas_call(_backward_kernel, grid_spec=pltpu.PrefetchScalarGridSpec(n...  23 us
    pallas_call x1, Pallas kernels, attention_forward(): pl.pallas_call(_forward_kernel, grid_spec=pltpu.PrefetchScalarGridSpec(nu...  17.1 us
  transfers between devices with their start and end apart: 4, of which 4 were waited for; matrix products, arithmetic and copies ran while one was open for 14% of the time, Pallas kernels for 0%

profile of v13, /device:TPU:0, one launch (start us, length us, event | category | flops | bytes accessed | tf_op | source)
XLA Modules:
  0.0 581.8 jit_solution(17077006807256037539)
XLA Ops:
  9.8 1.8 concatenate.37
  12.9 1.2 multiply_reduce_fusion.7
  14.3 103.4 %all-gather.3.cloned.1.call-done = bf16[768,9344]{1,0:T(8,128)(2,1)} async-done(((bf16[24,9344]{1,0:T(8,128)(2,1)}), bf16[768,9344]{1,0:T(8,128)(2,1)}) %all-gather.3.cloned.1.call-update) | async-done | bytes 14352400 | tf_op jit(solution)/shard_map/all_gather | solution.py:361
  119.9 3.2 fusion.14
  127.0 1.5 all_gather_reshape.3
  131.8 4.8 slice.155
  136.6 8.5 %reshape.331 = bf16[3072,768]{1,0:T(8,128)(2,1)} reshape(bf16[768,3072]{1,0:T(8,128)(2,1)} %slice.155) | data formatting | bytes 9437184 | tf_op jit(solution)/shard_map/reshape | solution.py:363
  145.1 5.5 fusion.41
  150.6 75.2 %all-gather.5.cloned.1.call-done = bf16[8,128,3072]{2,1,0:T(8,128)(2,1)} async-done(((bf16[1,128,3072]{2,1,0:T(8,128)(2,1)}), bf16[8,128,3072]{2,1,0:T(8,128)(2,1)}) %all-gather.5.cloned.1.call-update) | async-done | bytes 6291472 | tf_op jit(solution)/shard_map/all_gather | solution.py:390
  225.7 17.1 %attention_forward.1 = (f32[256,768]{1,0:T(8,128)}, f32[24,128,1024]{2,1,0:T(8,128)}) custom-call(s32[3]{0:T(128)} %pad_add_fusion.scalars_ref, bf16[256,768]{1,0:T(8,128)(2,1)} %copy.49.q_ref, bf16[1024,3072]{1,0:T(8,128)(2,1)} %bitcast.91, bf16[1024,3072]{1,0:T(8,128)(2,1)} %bitcast.92), custom_call_target="tpu_custom_call" | custom-call | tf_op jit(solution)/shard_map/attention_forward/pallas_call | solution.py:270
  242.8 2.2 fusion.40
  245.3 7.3 %fusion.11 = (bf16[256,3072]{1,0:T(8,128)(2,1)S(1)}, f32[256,3072]{1,0:T(8,128)}) fusion(f32[256,3072]{1,0:T(8,128)S(1)} %copy-done.8, bf16[768,9344]{1,0:T(8,128)(2,1)} %all-gather.3.cloned.1.call-done, f32[256,768]{1,0:T(8,128)S(1)} %get-tuple-element.93, f32[768]{0:T(1024)S(1)} %get-tuple-element.58, f32[768]{0:T(1024)S(1)} %get-tuple-element.102, ...), kind=kOutput, calls=%fused_computation.17 | convolution fusion | flops 1224671232 | bytes 13377536 | tf_op jit(solution)/shard_map/dot_general | solution.py:404
  252.6 4.5 multiply_reduce_fusion.1
  258.4 2.5 convolution_convert_fusion.4.do_ref
  260.9 23.0 %attention_backward.1 = (f32[256,768]{1,0:T(8,128)}, bf16[1024,3072]{1,0:T(8,128)(2,1)}) custom-call(s32[3]{0:T(128)} %pad_add_fusion.scalars_ref, bf16[256,768]{1,0:T(8,128)(2,1)} %copy.49.q_ref, bf16[1024,3072]{1,0:T(8,128)(2,1)} %bitcast.93, bf16[1024,3072]{1,0:T(8,128)(2,1)} %bitcast.94, bf16[256,768]{1,0:T(8,128)(2,1)} %convolution_convert_fusion.4.do_ref, ...), custom_call_target="tpu_custom_call" | custom-call | tf_op jit(solution)/shard_map/attention_backward/pallas_call | solution.py:301
  284.0 3.6 fusion.16
  287.6 6.7 %convolution_add_fusion.1 = f32[256,768]{1,0:T(8,128)} fusion(f32[256,768]{1,0:T(8,128)S(1)} %get-tuple-element.93, bf16[3072,768]{1,0:T(8,128)(2,1)} %reshape.331, f32[256,3072]{1,0:T(8,128)} %get-tuple-element.95), kind=kOutput, calls=%fused_computation.29 | convolution fusion | flops 1215234048 | bytes 9437184 | tf_op jit(solution)/shard_map/dot_general | solution.py:406
  295.5 3.9 multiply_reduce_fusion.3
  300.3 5.1 convolution_convert_fusion.1
  305.4 8.7 %reshape.339 = bf16[768,3072]{1,0:T(8,128)(2,1)} reshape(bf16[3072,768]{1,0:T(8,128)(2,1)} %convolution_convert_fusion.1) | data formatting | bytes 9437184 | tf_op jit(solution)/shard_map/reshape | solution.py:444
  314.1 1.5 convolution_convert_fusion.3
  315.7 2.4 copy.53
  318.1 3.2 convolution_convert_fusion.2
  321.3 8.9 %pad_maximum_fusion = bf16[768,9216]{1,0:T(8,128)(2,1)} fusion(bf16[768,3072]{1,0:T(8,128)(2,1)S(1)} %bitcast.97, bf16[768,3072]{1,0:T(8,128)(2,1)S(1)} %convolution_convert_fusion.2, bf16[768,768]{1,0:T(8,128)(2,1)S(1)} %copy-done.4, bf16[9216]{0:T(1024)(128)(2,1)S(1)} %pad.4.clone), kind=kLoop, calls=%fused_computation | loop fusion | flops 56623104 | bytes 24791040 | tf_op jit(solution)/shard_map/concatenate | solution.py:439
  330.3 70.0 %reduce-scatter.3.cloned.1.call-done = bf16[128,3072]{1,0:T(8,128)(2,1)} async-done(((bf16[1024,3072]{1,0:T(8,128)(2,1)}), bf16[128,3072]{1,0:T(8,128)(2,1)}) %reduce-scatter.3.cloned.1.call-update) | async-done | bytes 786448 | tf_op jit(solution)/shard_map/reduce_scatter | solution.py:421
  400.3 2.6 convert_element_type.139
  402.8 1.4 copy.52
  405.8 2.9 fusion
  409.8 1.5 multiply_convert_fusion
  412.0 3.6 multiply_reduce_fusion.4
  417.3 39.3 %psum.7 = f32[3077]{0:T(1024)S(1)} all-reduce(f32[3077]{0:T(1024)S(1)} %concatenate.45), channel_id=1, replica_groups=mesh['seq'=8,'fsdp'=4] {'seq','fsdp'}, use_global_device_ids=true, to_apply=%region_15.16 | all-reduce | flops 3077 | bytes 24616 | tf_op jit(solution)/shard_map/psum | solution.py:479
  460.0 110.8 %reduce-scatter.5.cloned.1.call-done = bf16[1,24,9216]{2,1,0:T(8,128)(2,1)} async-done(((bf16[32,24,9216]{2,1,0:T(8,128)(2,1)}), bf16[1,24,9216]{2,1,0:T(8,128)(2,1)}) %reduce-scatter.5.cloned.1.call-update) | async-done | bytes 442384 | tf_op jit(solution)/shard_map/reduce_scatter | solution.py:468
  (120 shorter events, 28.9 us)
Async XLA Ops:
  7.2 112.5 %copy-start = (bf16[2,1,128,768]{3,2,1,0:T(8,128)(2,1)S(1)}, bf16[2,1,128,768]{3,2,1,0:T(8,128)(2,1)}, u32[]{:S(2)}) copy-start(bf16[2,1,128,768]{3,2,1,0:T(8,128)(2,1)} %param.11) | copy-start | bytes 1179652
  7.2 110.6 %all-gather.3.cloned.1.call-start = ((), (), s32[]{:S(2)}) async-start(), calls=%async_computation.2 | async-start | bytes 14800896 | tf_op jit(solution)/shard_map/all_gather | solution.py:361
  11.7 214.1 %all-gather.5.cloned.1.call-start = ((), (), s32[]{:S(2)}) async-start(), calls=%async_computation.3 | async-start | bytes 7077888 | tf_op jit(solution)/shard_map/all_gather | solution.py:390
  119.9 3.3 copy-start.12
  124.9 3.8 copy-start.15
  124.9 4.4 copy-start.16
  124.9 5.1 copy-start.2
  128.5 271.8 %reduce-scatter.3.cloned.1.call-start = ((), (), s32[]{:S(2)}) async-start(), calls=%async_computation.4 | async-start | bytes 7077888 | tf_op jit(solution)/shard_map/reduce_scatter | solution.py:421
  242.8 2.5 copy-start.8
  252.6 4.5 copy-start.10
  283.9 286.9 %reduce-scatter.5.cloned.1.call-start = ((), (), s32[]{:S(2)}) async-start(), calls=%async_computation.5 | async-start | bytes 14598144 | tf_op jit(solution)/shard_map/reduce_scatter | solution.py:468
  287.6 6.7 %copy-start.11 = (f32[256,768]{1,0:T(8,128)S(1)}, f32[256,768]{1,0:T(8,128)}, u32[]{:S(2)}) copy-start(f32[256,768]{1,0:T(8,128)} %get-tuple-element.19) | copy-start | bytes 2359300
  295.5 4.8 copy-start.17
  299.4 0.9 copy-start.5
  305.4 8.7 %copy-start.1 = (f32[256,768]{1,0:T(8,128)S(1)}, f32[256,768]{1,0:T(8,128)}, u32[]{:S(2)}) copy-start(f32[256,768]{1,0:T(8,128)} %get-tuple-element.15.o_ref) | copy-start | bytes 2359300
  315.7 5.6 slice-start
  318.1 3.2 slice-start.1
  318.1 3.2 copy-start.4
  404.3 1.2 copy-start.7
  404.4 1.4 copy-start.13
  404.5 4.2 copy-start.14
  408.7 1.0 copy-start.3
  408.7 2.7 copy-start.6
  409.7 1.7 copy-start.9
Sparse Core Ops, SparseCore 0:
  11.8 105.9 all-gather.2
  128.6 97.1 all-gather.4
  284.1 116.1 reduce-scatter.2
  408.8 161.9 reduce-scatter.4

commit v14 on v11

--- a/solution.py
+++ b/solution.py
@@ -196,13 +196,15 @@
 def _forward_kernel(scalars_ref, q_ref, k_ref, v_ref, out_ref, lse_ref):
     micro = pl.program_id(0)
     row_count = q_ref.shape[0]
-    key_count = k_ref.shape[0]
+    key_count = k_ref.shape[0] * k_ref.shape[2]
     allowed = _pair_masks(scalars_ref, micro, row_count, key_count)
+    k_all = k_ref[...].reshape(key_count, k_ref.shape[3])
+    v_all = v_ref[...].reshape(key_count, v_ref.shape[3])
     for half in range(2):
         lanes = slice(half * HEAD, (half + 1) * HEAD)
         q_head = q_ref[:, lanes]
-        k_head = k_ref[:, lanes]
-        v_head = v_ref[:, lanes]
+        k_head = k_all[:, lanes]
+        v_head = v_all[:, lanes]
         scores = lax.dot_general(
             q_head, k_head, (((1,), (1,)), ((), ())), preferred_element_type=jnp.float32
         ) * HEAD ** (-0.5)
@@ -224,13 +226,15 @@
 ):
     micro = pl.program_id(0)
     row_count = q_ref.shape[0]
-    key_count = k_ref.shape[0]
+    key_count = k_ref.shape[0] * k_ref.shape[2]
     allowed = _pair_masks(scalars_ref, micro, row_count, key_count)
+    k_all = k_ref[...].reshape(key_count, k_ref.shape[3])
+    v_all = v_ref[...].reshape(key_count, v_ref.shape[3])
     for half in range(2):
         lanes = slice(half * HEAD, (half + 1) * HEAD)
         q_head = q_ref[:, lanes]
-        k_head = k_ref[:, lanes]
-        v_head = v_ref[:, lanes]
+        k_head = k_all[:, lanes]
+        v_head = v_all[:, lanes]
         grad_head = do_ref[:, lanes]
         scores = lax.dot_general(
             q_head, k_head, (((1,), (1,)), ((), ())), preferred_element_type=jnp.float32
@@ -264,13 +268,13 @@
 def attention_forward(scalars, queries, kv_flat, batches):
     all_rows, model_width = queries.shape
     row_count = all_rows // batches
-    key_count = kv_flat.shape[0]
+    devices = kv_flat.shape[0]
+    key_count = devices * row_count
     pairs = model_width // (2 * HEAD)
-    micro_blocks = kv_flat.shape[1] // batches // (2 * HEAD)
     row_spec = pl.BlockSpec((row_count, 2 * HEAD), lambda m, p, s: (m, p))
-    key_spec = pl.BlockSpec((key_count, 2 * HEAD), lambda m, p, s: (0, m * micro_blocks + p))
+    key_spec = pl.BlockSpec((devices, 1, row_count, 2 * HEAD), lambda m, p, s: (0, m, 0, p))
     value_spec = pl.BlockSpec(
-        (key_count, 2 * HEAD), lambda m, p, s: (0, m * micro_blocks + pairs + p)
+        (devices, 1, row_count, 2 * HEAD), lambda m, p, s: (0, m, 0, pairs + p)
     )
     return pl.pallas_call(
         _forward_kernel,
@@ -291,13 +295,13 @@
 def attention_backward(scalars, queries, kv_flat, grads, attended, log_totals, batches):
     all_rows, model_width = queries.shape
     row_count = all_rows // batches
-    key_count = kv_flat.shape[0]
+    devices = kv_flat.shape[0]
+    key_count = devices * row_count
     pairs = model_width // (2 * HEAD)
-    micro_blocks = kv_flat.shape[1] // batches // (2 * HEAD)
     row_spec = pl.BlockSpec((row_count, 2 * HEAD), lambda m, p, s: (m, p))
-    key_spec = pl.BlockSpec((key_count, 2 * HEAD), lambda m, p, s: (0, m * micro_blocks + p))
+    key_spec = pl.BlockSpec((devices, 1, row_count, 2 * HEAD), lambda m, p, s: (0, m, 0, p))
     value_spec = pl.BlockSpec(
-        (key_count, 2 * HEAD), lambda m, p, s: (0, m * micro_blocks + pairs + p)
+        (devices, 1, row_count, 2 * HEAD), lambda m, p, s: (0, m, 0, pairs + p)
     )
     grad_spec = pl.BlockSpec((key_count, 4 * HEAD), lambda m, p, s: (0, m * pairs + p))
     return pl.pallas_call(
@@ -310,7 +314,7 @@
         ),
         out_shape=[
             jax.ShapeDtypeStruct((all_rows, model_width), jnp.float32),
-            jax.ShapeDtypeStruct(kv_flat.shape, jnp.bfloat16),
+            jax.ShapeDtypeStruct((key_count, batches * 2 * model_width), jnp.bfloat16),
         ],
         name="attention_backward",
     )(scalars, queries, kv_flat, kv_flat, grads, attended, log_totals)
@@ -383,19 +387,18 @@
     grad_next = jnp.where(
         usable, cotangent[:, 0].reshape(all_rows, model_width).astype(jnp.float32), 0.0
     )
-    history_part = jnp.einsum("j,jrd->rd", depth_weights[:4], earlier)
+    history_part = (
+        depth_weights[0] * earlier[0]
+        + depth_weights[1] * earlier[1]
+        + depth_weights[2] * earlier[2]
+        + depth_weights[3] * earlier[3]
+    )
     grad_history = (depth_weights[:4, None, None] * grad_next[None]).astype(jnp.bfloat16)
     grad_history = grad_history.reshape(4, batches, 1, row_count, model_width)
     out_grad = depth_weights[4] * grad_next
     out_low = out_grad.astype(jnp.bfloat16)
 
-    kv_all = lax.all_gather(
-        jnp.swapaxes(own_kv, 0, 1).reshape(row_count, batches * 2 * model_width),
-        "seq",
-        axis=0,
-        tiled=False,
-    )
-    kv_flat = kv_all.reshape(slot_len, batches * 2 * model_width)
+    kv_flat = lax.all_gather(own_kv, "seq", axis=0, tiled=False)
     scalars = jnp.concatenate(
         [slot_lengths.astype(jnp.int32), (lax.axis_index("seq") * row_count)[None].astype(jnp.int32)]
     )
@@ -431,7 +434,7 @@
     combined = depth_weights[4] * block_side + history_part
     next_input = combined.astype(jnp.bfloat16).reshape(batches, 1, row_count, model_width)
     depth_terms = jnp.concatenate(
-        [jnp.einsum("jrd,rd->j", earlier, grad_next), jnp.sum(block_side * grad_next)[None]]
+        [jnp.sum(earlier * grad_next[None], axis=(1, 2)), jnp.sum(block_side * grad_next)[None]]
     )
     grad_down = jnp.einsum("rf,rd->fd", hidden_low, out_low, preferred_element_type=jnp.float32)
     grad_up = jnp.einsum("rd,rf->df", second_low, up_low, preferred_element_type=jnp.float32)

time: 580 us -> 613 us (1.057)
  waiting for transfers between devices: 360 us -> 385 us
  other arithmetic: 26.4 us -> 35.3 us
    reduce_scatter x1, waiting for transfers between devices: 69.9 us -> 93.1 us  [local(): lax.psum_scatter(kv_grad_flat, 'seq', scatter_dimension=0, tiled=True)]
  transfers between devices with their start and end apart: 4 -> 4, of which waited for: 4 -> 4; matrix products, arithmetic and copies ran while one was open for 14% -> 9% of each run, Pallas kernels for 0% -> 0%
where the time goes in v14:
time: 613 us; the launch traced here: 612 us
  waiting for transfers between devices  385 us (63%)
  local copies, waits for them, and re-layouts  49.7 us (8%)
  matrix products  48.4 us (8%)
  blocking collectives  39.6 us (6%)
  Pallas kernels  38.1 us (6%)
  other arithmetic  35.3 us (6%)
  between operations  14.5 us (2%)
    reduce_scatter x1, waiting for transfers between devices, local(): lax.psum_scatter(with_layout_constraint(packed_grads.reshape(device_count...  116 us
    all_gather x1, waiting for transfers between devices, local(): gathered = lax.all_gather(packed, ('seq', 'fsdp'), axis=0, tiled=True)  102 us
    reduce_scatter x1, waiting for transfers between devices, local(): lax.psum_scatter(kv_grad_flat, 'seq', scatter_dimension=0, tiled=True)  93.1 us
    all_gather x1, waiting for transfers between devices, local(): kv_flat = lax.all_gather(own_kv, 'seq', axis=0, tiled=False)  74.3 us
    psum x1, blocking collectives, local(): lax.psum(jnp.concatenate([depth_terms, jnp.stack([gain_one, gain_two, bia...  39.6 us
    pallas_call x1, Pallas kernels, attention_backward(): pl.pallas_call(_backward_kernel, grid_spec=pltpu.PrefetchScalarGridSpec(n...  20 us
    pallas_call x1, Pallas kernels, attention_forward(): pl.pallas_call(_forward_kernel, grid_spec=pltpu.PrefetchScalarGridSpec(nu...  18.1 us
  transfers between devices with their start and end apart: 4, of which 4 were waited for; matrix products, arithmetic and copies ran while one was open for 9% of the time, Pallas kernels for 0%

profile of v14, /device:TPU:0, one launch (start us, length us, event | category | flops | bytes accessed | tf_op | source)
XLA Modules:
  0.0 611.6 jit_solution(9948830330220140232)
XLA Ops:
  9.8 1.8 concatenate.37
  15.5 102.3 %all-gather.3.cloned.1.call-done = bf16[768,9344]{1,0:T(8,128)(2,1)} async-done(((bf16[24,9344]{1,0:T(8,128)(2,1)}), bf16[768,9344]{1,0:T(8,128)(2,1)}) %all-gather.3.cloned.1.call-update) | async-done | bytes 14352400 | tf_op jit(solution)/shard_map/all_gather | solution.py:367
  119.9 3.2 fusion.14
  130.2 5.0 slice.190
  135.2 8.5 %reshape.354 = bf16[3072,768]{1,0:T(8,128)(2,1)} reshape(bf16[768,3072]{1,0:T(8,128)(2,1)} %slice.190) | data formatting | bytes 9437184 | tf_op jit(solution)/shard_map/reshape | solution.py:369
  143.7 5.5 fusion.41
  149.2 74.3 %all-gather.5.cloned.1.call-done.k_ref.v_ref = bf16[8,2,128,1536]{3,2,1,0:T(8,128)(2,1)} async-done(((bf16[1,2,128,1536]{3,2,1,0:T(8,128)(2,1)}), bf16[8,2,128,1536]{3,2,1,0:T(8,128)(2,1)}) %all-gather.5.cloned.1.call-update) | async-done | bytes 6291472 | tf_op jit(solution)/shard_map/all_gather | solution.py:401
  223.5 18.1 %attention_forward.1 = (f32[256,768]{1,0:T(8,128)}, f32[256,768]{1,0:T(8,128)}) custom-call(s32[3]{0:T(128)} %pad_add_fusion.scalars_ref, bf16[256,768]{1,0:T(8,128)(2,1)} %copy.46.q_ref, bf16[8,2,128,1536]{3,2,1,0:T(8,128)(2,1)} %all-gather.5.cloned.1.call-done.k_ref.v_ref, bf16[8,2,128,1536]{3,2,1,0:T(8,128)(2,1)} %all-gather.5.cloned.1.call-done.k_ref.v_ref), custom_call_target="tpu_custom_call" | custom-call | tf_op jit(solution)/shard_map/attention_forward/pallas_call | solution.py:279
  241.6 2.2 fusion.40
  244.1 7.3 %fusion.11 = (bf16[256,3072]{1,0:T(8,128)(2,1)S(1)}, f32[256,3072]{1,0:T(8,128)}) fusion(f32[256,3072]{1,0:T(8,128)S(1)} %copy-done.7, bf16[768,9344]{1,0:T(8,128)(2,1)} %all-gather.3.cloned.1.call-done, f32[256,768]{1,0:T(8,128)S(1)} %get-tuple-element.101, f32[768]{0:T(1024)S(1)} %get-tuple-element.58, f32[768]{0:T(1024)S(1)} %get-tuple-element.110, ...), kind=kOutput, calls=%fused_computation.17 | convolution fusion | flops 1224671232 | bytes 13377536 | tf_op jit(solution)/shard_map/dot_general | solution.py:409
  251.3 5.1 multiply_reduce_fusion.1
  257.7 2.5 convolution_convert_fusion.4.do_ref
  260.2 20.0 %attention_backward.1 = (f32[256,768]{1,0:T(8,128)}, bf16[1024,3072]{1,0:T(8,128)(2,1)}) custom-call(s32[3]{0:T(128)} %pad_add_fusion.scalars_ref, bf16[256,768]{1,0:T(8,128)(2,1)} %copy.46.q_ref, bf16[8,2,128,1536]{3,2,1,0:T(8,128)(2,1)} %all-gather.5.cloned.1.call-done.k_ref.v_ref, bf16[8,2,128,1536]{3,2,1,0:T(8,128)(2,1)} %all-gather.5.cloned.1.call-done.k_ref.v_ref, ...), custom_call_target="tpu_custom_call" | custom-call | tf_op jit(solution)/shard_map/attention_backward/pallas_call | solution.py:307
  280.5 1.7 convert_element_type.142
  282.9 4.0 fusion.18
  286.8 5.3 convolution_add_fusion.1
  292.1 2.4 copy.48
  294.5 1.6 convolution_convert_fusion.3
  296.0 2.4 copy.50
  298.4 5.1 convolution_convert_fusion.2
  303.6 93.1 %reduce-scatter.3.cloned.1.call-done = bf16[128,3072]{1,0:T(8,128)(2,1)} async-done(((bf16[1024,3072]{1,0:T(8,128)(2,1)}), bf16[128,3072]{1,0:T(8,128)(2,1)}) %reduce-scatter.3.cloned.1.call-update) | async-done | bytes 786448 | tf_op jit(solution)/shard_map/reduce_scatter | solution.py:426
  396.6 2.6 convert_element_type.144
  399.2 2.9 copy.49
  404.2 3.4 multiply_reduce_fusion.4
  408.6 2.6 multiply_reduce_fusion.3
  411.3 4.4 convolution_convert_fusion.1
  415.7 8.6 %reshape.362 = bf16[768,3072]{1,0:T(8,128)(2,1)} reshape(bf16[3072,768]{1,0:T(8,128)(2,1)} %convolution_convert_fusion.1) | data formatting | bytes 9437184 | tf_op jit(solution)/shard_map/reshape | solution.py:449
  424.3 11.8 %pad_maximum_fusion = bf16[768,9216]{1,0:T(8,128)(2,1)} fusion(bf16[768,3072]{1,0:T(8,128)(2,1)} %reshape.362, bf16[768,3072]{1,0:T(8,128)(2,1)} %convolution_convert_fusion.2, bf16[768,768]{1,0:T(8,128)(2,1)S(1)} %copy-done.4, bf16[9216]{0:T(1024)(128)(2,1)S(1)} %copy-done.18), kind=kLoop, calls=%fused_computation | loop fusion | flops 56623104 | bytes 24791040 | tf_op jit(solution)/shard_map/concatenate | solution.py:444
  436.1 2.9 fusion
  440.4 1.8 multiply_reduce_fusion
  443.5 39.6 %psum.7 = f32[3077]{0:T(1024)S(1)} all-reduce(f32[3077]{0:T(1024)S(1)} %concatenate.45), channel_id=1, replica_groups=mesh['seq'=8,'fsdp'=4] {'seq','fsdp'}, use_global_device_ids=true, to_apply=%region_16.17 | all-reduce | flops 3077 | bytes 24616 | tf_op jit(solution)/shard_map/psum | solution.py:484
  485.4 115.8 %reduce-scatter.5.cloned.1.call-done = bf16[1,24,9216]{2,1,0:T(8,128)(2,1)} async-done(((bf16[32,24,9216]{2,1,0:T(8,128)(2,1)}), bf16[1,24,9216]{2,1,0:T(8,128)(2,1)}) %reduce-scatter.5.cloned.1.call-update) | async-done | bytes 442384 | tf_op jit(solution)/shard_map/reduce_scatter | solution.py:473
  (158 shorter events, 29.6 us)
Async XLA Ops:
  7.2 112.5 %copy-start = (bf16[2,1,128,768]{3,2,1,0:T(8,128)(2,1)S(1)}, bf16[2,1,128,768]{3,2,1,0:T(8,128)(2,1)}, u32[]{:S(2)}) copy-start(bf16[2,1,128,768]{3,2,1,0:T(8,128)(2,1)} %param.11) | copy-start | bytes 1179652
  7.2 110.6 %all-gather.3.cloned.1.call-start = ((), (), s32[]{:S(2)}) async-start(), calls=%async_computation.2 | async-start | bytes 14800896 | tf_op jit(solution)/shard_map/all_gather | solution.py:367
  11.7 211.8 %all-gather.5.cloned.1.call-start = ((), (), s32[]{:S(2)}) async-start(), calls=%async_computation.3 | async-start | bytes 7077888 | tf_op jit(solution)/shard_map/all_gather | solution.py:401
  13.4 109.8 %copy-start.21 = (f32[256]{0:T(256)}, f32[256]{0:T(256)S(1)}, u32[]{:S(2)}) copy-start(f32[256]{0:T(256)S(1)} %get-tuple-element.93) | copy-start | bytes 3076
  14.6 108.5 %copy-start.29 = (f32[2,128]{1,0:T(2,128)}, f32[2,128]{1,0:T(2,128)S(1)}, u32[]{:S(2)}) copy-start(f32[2,128]{1,0:T(2,128)S(1)} %multiply_reduce_fusion.7) | copy-start | bytes 3076
  14.7 108.5 %copy-start.23 = (f32[256]{0:T(256)}, f32[256]{0:T(256)S(1)}, u32[]{:S(2)}) copy-start(f32[256]{0:T(256)S(1)} %bitcast_rsqrt_fusion) | copy-start | bytes 3076
  119.9 3.3 copy-start.10
  123.9 4.5 copy-start.2
  126.2 270.4 %reduce-scatter.3.cloned.1.call-start = ((), (), s32[]{:S(2)}) async-start(), calls=%async_computation.4 | async-start | bytes 7077888 | tf_op jit(solution)/shard_map/reduce_scatter | solution.py:426
  244.0 12.4 %copy-start.26 = (f32[256]{0:T(256)}, f32[256]{0:T(256)S(1)}, u32[]{:S(2)}) copy-start(f32[256]{0:T(256)S(1)} %fusion.28) | copy-start | bytes 3076
  251.3 5.1 copy-start.8
  251.3 5.5 copy-start.35
  256.8 23.4 %copy-start.27 = (f32[256]{0:T(256)}, f32[256]{0:T(256)S(1)}, u32[]{:S(2)}) copy-start(f32[256]{0:T(256)S(1)} %negate_multiply_fusion.1) | copy-start | bytes 3076
  280.3 320.9 %reduce-scatter.5.cloned.1.call-start = ((), (), s32[]{:S(2)}) async-start(), calls=%async_computation.5 | async-start | bytes 14598144 | tf_op jit(solution)/shard_map/reduce_scatter | solution.py:473
  282.2 4.6 copy-start.39
  286.8 7.6 %copy-start.1 = (f32[256,768]{1,0:T(8,128)S(1)}, f32[256,768]{1,0:T(8,128)}, u32[]{:S(2)}) copy-start(f32[256,768]{1,0:T(8,128)} %get-tuple-element.15.o_ref) | copy-start | bytes 2359300
  399.2 4.4 copy-start.16
  399.2 4.4 copy-start.17
  403.5 4.0 copy-start.14
  403.9 3.6 copy-start.12
  404.1 3.4 copy-start.30
  404.1 3.4 copy-start.24
  404.1 4.5 copy-start.5
  404.1 4.5 copy-start.9
  404.1 4.5 copy-start.28
  404.1 4.5 copy-start.36
  407.6 3.7 copy-start.40
  415.7 8.6 %copy-start.4 = (bf16[768,768]{1,0:T(8,128)(2,1)S(1)}, bf16[768,768]{1,0:T(8,128)(2,1)}, u32[]{:S(2)}) copy-start(bf16[768,768]{1,0:T(8,128)(2,1)} %copy.50) | copy-start | bytes 3538948
  415.7 8.6 %copy-start.18 = (bf16[9216]{0:T(1024)(128)(2,1)S(1)}, bf16[9216]{0:T(1024)(128)(2,1)}, u32[]{:S(2)}) copy-start(bf16[9216]{0:T(1024)(128)(2,1)} %pad.4.clone) | copy-start | bytes 55300
  424.2 11.8 %copy-start.11 = (bf16[256,768]{1,0:T(8,128)(2,1)S(1)}, bf16[256,768]{1,0:T(8,128)(2,1)}, u32[]{:S(2)}) copy-start(bf16[256,768]{1,0:T(8,128)(2,1)} %copy-done.10) | copy-start | bytes 1179652
  424.3 11.8 %copy-start.13 = (bf16[256,12,64]{0,2,1:T(8,128)(2,1)S(1)}, bf16[256,12,64]{0,2,1:T(8,128)(2,1)}, u32[]{:S(2)}) copy-start(bf16[256,12,64]{0,2,1:T(8,128)(2,1)} %copy-done.12) | copy-start | bytes 1179652
  424.3 11.8 %copy-start.15 = (bf16[256,768]{0,1:T(8,128)(2,1)S(1)}, bf16[256,768]{0,1:T(8,128)(2,1)}, u32[]{:S(2)}) copy-start(bf16[256,768]{0,1:T(8,128)(2,1)} %copy-done.14) | copy-start | bytes 1179652
  (13 other events, 26.5 us)
Sparse Core Ops, SparseCore 0:
  11.8 105.9 all-gather.2
  126.3 97.1 all-gather.4
  280.4 116.2 reduce-scatter.2
  439.1 161.9 reduce-scatter.4

commit v15 on v14

--- a/solution.py
+++ b/solution.py
@@ -424,12 +424,6 @@
         scalars, queries, kv_flat, attended_grad, attended_rows, log_totals, batches
     )
     kv_grad_own = lax.psum_scatter(kv_grad_flat, "seq", scatter_dimension=0, tiled=True)
-    pairs = model_width // (2 * HEAD)
-    kv_grad_own = kv_grad_own.reshape(row_count, batches, pairs, 2, 2 * HEAD)
-    kv_grad_own = jnp.transpose(kv_grad_own, (1, 0, 3, 2, 4)).reshape(
-        all_rows, 2 * model_width
-    )
-    key_value_all = kv_grad_own.astype(jnp.float32)
     block_side, _ = lax.optimization_barrier((block_out, kv_grad_flat))
     combined = depth_weights[4] * block_side + history_part
     next_input = combined.astype(jnp.bfloat16).reshape(batches, 1, row_count, model_width)
@@ -450,6 +444,13 @@
         ],
         axis=1,
     ).astype(jnp.bfloat16)
+    kv_grad_own, early_grads = lax.optimization_barrier((kv_grad_own, early_grads))
+    pairs = model_width // (2 * HEAD)
+    kv_grad_own = kv_grad_own.reshape(row_count, batches, pairs, 2, 2 * HEAD)
+    kv_grad_own = jnp.transpose(kv_grad_own, (1, 0, 3, 2, 4)).reshape(
+        all_rows, 2 * model_width
+    )
+    key_value_all = kv_grad_own.astype(jnp.float32)
     qkv_low = jnp.concatenate(
         [
             rotate(query_grad, cosine_part, -sine_part),

time: 613 us -> 581 us (0.948)
  waiting for transfers between devices: 385 us -> 349 us
    reduce_scatter x1, waiting for transfers between devices: 116 us -> 89.5 us  [local(): lax.psum_scatter(with_layout_constraint(packed_grads.reshape(device_count...]
    reduce_scatter x1, waiting for transfers between devices: 93.1 us -> 82.1 us  [local(): lax.psum_scatter(kv_grad_flat, 'seq', scatter_dimension=0, tiled=True)]
  transfers between devices with their start and end apart: 4 -> 4, of which waited for: 4 -> 4; matrix products, arithmetic and copies ran while one was open for 9% -> 16% of each run, Pallas kernels for 0% -> 0%
where the time goes in v15:
time: 581 us; the launch traced here: 580 us
  waiting for transfers between devices  349 us (60%)
  local copies, waits for them, and re-layouts  50.7 us (9%)
  matrix products  46.2 us (8%)
  blocking collectives  40.8 us (7%)
  other arithmetic  40.3 us (7%)
  Pallas kernels  38 us (7%)
  between operations  14.5 us (2%)
    all_gather x1, waiting for transfers between devices, local(): gathered = lax.all_gather(packed, ('seq', 'fsdp'), axis=0, tiled=True)  102 us
    reduce_scatter x1, waiting for transfers between devices, local(): lax.psum_scatter(with_layout_constraint(packed_grads.reshape(device_count...  89.5 us
    reduce_scatter x1, waiting for transfers between devices, local(): lax.psum_scatter(kv_grad_flat, 'seq', scatter_dimension=0, tiled=True)  82.1 us
    all_gather x1, waiting for transfers between devices, local(): kv_flat = lax.all_gather(own_kv, 'seq', axis=0, tiled=False)  75 us
    psum x1, blocking collectives, local(): lax.psum(jnp.concatenate([depth_terms, jnp.stack([gain_one, gain_two, bia...  40.8 us
    pallas_call x1, Pallas kernels, attention_backward(): pl.pallas_call(_backward_kernel, grid_spec=pltpu.PrefetchScalarGridSpec(n...  19.9 us
    pallas_call x1, Pallas kernels, attention_forward(): pl.pallas_call(_forward_kernel, grid_spec=pltpu.PrefetchScalarGridSpec(nu...  18.1 us
  transfers between devices with their start and end apart: 4, of which 4 were waited for; matrix products, arithmetic and copies ran while one was open for 16% of the time, Pallas kernels for 0%

profile of v15, /device:TPU:0, one launch (start us, length us, event | category | flops | bytes accessed | tf_op | source)
XLA Modules:
  0.0 580.0 jit_solution(13244327525836592759)
XLA Ops:
  9.8 1.8 concatenate.37
  15.5 102.3 %all-gather.3.cloned.1.call-done = bf16[768,9344]{1,0:T(8,128)(2,1)} async-done(((bf16[24,9344]{1,0:T(8,128)(2,1)}), bf16[768,9344]{1,0:T(8,128)(2,1)}) %all-gather.3.cloned.1.call-update) | async-done | bytes 14352400 | tf_op jit(solution)/shard_map/all_gather | solution.py:367
  119.9 3.2 fusion.14
  129.6 4.9 slice.190
  134.5 8.5 %reshape.354 = bf16[3072,768]{1,0:T(8,128)(2,1)} reshape(bf16[768,3072]{1,0:T(8,128)(2,1)} %slice.190) | data formatting | bytes 9437184 | tf_op jit(solution)/shard_map/reshape | solution.py:369
  143.0 5.4 fusion.41
  148.4 75.0 %all-gather.5.cloned.1.call-done.k_ref.v_ref = bf16[8,2,128,1536]{3,2,1,0:T(8,128)(2,1)} async-done(((bf16[1,2,128,1536]{3,2,1,0:T(8,128)(2,1)}), bf16[8,2,128,1536]{3,2,1,0:T(8,128)(2,1)}) %all-gather.5.cloned.1.call-update) | async-done | bytes 6291472 | tf_op jit(solution)/shard_map/all_gather | solution.py:401
  223.4 18.1 %attention_forward.1 = (f32[256,768]{1,0:T(8,128)}, f32[256,768]{1,0:T(8,128)}) custom-call(s32[3]{0:T(128)} %pad_add_fusion.scalars_ref, bf16[256,768]{1,0:T(8,128)(2,1)} %copy.46.q_ref, bf16[8,2,128,1536]{3,2,1,0:T(8,128)(2,1)} %all-gather.5.cloned.1.call-done.k_ref.v_ref, bf16[8,2,128,1536]{3,2,1,0:T(8,128)(2,1)} %all-gather.5.cloned.1.call-done.k_ref.v_ref), custom_call_target="tpu_custom_call" | custom-call | tf_op jit(solution)/shard_map/attention_forward/pallas_call | solution.py:279
  241.5 2.2 fusion.40
  244.0 7.3 %fusion.11 = (bf16[256,3072]{1,0:T(8,128)(2,1)S(1)}, f32[256,3072]{1,0:T(8,128)}) fusion(f32[256,3072]{1,0:T(8,128)S(1)} %copy-done.7, bf16[768,9344]{1,0:T(8,128)(2,1)} %all-gather.3.cloned.1.call-done, f32[256,768]{1,0:T(8,128)S(1)} %get-tuple-element.106, f32[768]{0:T(1024)S(1)} %get-tuple-element.62, f32[768]{0:T(1024)S(1)} %get-tuple-element.115, ...), kind=kOutput, calls=%fused_computation.17 | convolution fusion | flops 1224671232 | bytes 13377536 | tf_op jit(solution)/shard_map/dot_general | solution.py:409
  251.3 5.1 multiply_reduce_fusion.1
  257.7 2.5 convolution_convert_fusion.4.do_ref
  260.2 19.9 %attention_backward.1 = (f32[256,768]{1,0:T(8,128)}, bf16[1024,3072]{1,0:T(8,128)(2,1)}) custom-call(s32[3]{0:T(128)} %pad_add_fusion.scalars_ref, bf16[256,768]{1,0:T(8,128)(2,1)} %copy.46.q_ref, bf16[8,2,128,1536]{3,2,1,0:T(8,128)(2,1)} %all-gather.5.cloned.1.call-done.k_ref.v_ref, bf16[8,2,128,1536]{3,2,1,0:T(8,128)(2,1)} %all-gather.5.cloned.1.call-done.k_ref.v_ref, ...), custom_call_target="tpu_custom_call" | custom-call | tf_op jit(solution)/shard_map/attention_backward/pallas_call | solution.py:307
  281.1 6.3 %convolution_convert_fusion.1 = bf16[3072,768]{1,0:T(8,128)(2,1)} fusion(bf16[256,768]{1,0:T(8,128)(2,1)S(1)} %get-tuple-element.87, f32[256,3072]{1,0:T(8,128)} %get-tuple-element.108), kind=kOutput, calls=%fused_computation.3 | convolution fusion | flops 1217396736 | bytes 8257536 | tf_op jit(solution)/shard_map/rf,rd->fd/dot_general | solution.py:433
  287.4 8.6 %reshape.358 = bf16[768,3072]{1,0:T(8,128)(2,1)} reshape(bf16[3072,768]{1,0:T(8,128)(2,1)} %convolution_convert_fusion.1) | data formatting | bytes 9437184 | tf_op jit(solution)/shard_map/reshape | solution.py:443
  296.0 1.5 convolution_convert_fusion.3
  297.5 2.4 copy.49
  299.9 2.4 copy.48
  302.3 3.2 convolution_convert_fusion.2
  305.5 8.9 %pad_maximum_fusion = bf16[768,9216]{1,0:T(8,128)(2,1)} fusion(bf16[768,3072]{1,0:T(8,128)(2,1)S(1)} %bitcast.99, bf16[768,3072]{1,0:T(8,128)(2,1)S(1)} %convolution_convert_fusion.2, bf16[768,768]{1,0:T(8,128)(2,1)S(1)} %copy-done.4, bf16[9216]{0:T(1024)(128)(2,1)S(1)} %copy-done.17), kind=kLoop, calls=%fused_computation | loop fusion | flops 56623104 | bytes 24791040 | tf_op jit(solution)/shard_map/concatenate | solution.py:438
  314.4 82.1 %reduce-scatter.3.cloned.1.call-done = bf16[128,3072]{1,0:T(8,128)(2,1)} async-done(((bf16[1024,3072]{1,0:T(8,128)(2,1)}), bf16[128,3072]{1,0:T(8,128)(2,1)}) %reduce-scatter.3.cloned.1.call-update) | async-done | bytes 786448 | tf_op jit(solution)/shard_map/reduce_scatter | solution.py:426
  396.5 2.6 convert_element_type.145
  399.1 2.9 copy.50
  404.4 3.0 fusion
  407.4 3.4 convert_element_type.142
  411.0 7.5 %fusion.18 = f32[1,2,1,128,768]{4,3,2,1,0:T(8,128)} fusion(f32[4,2,1,128,768]{4,3,2,1,0:T(8,128)} %convert_element_type.142, f32[]{:T(128)} %bitcast.18, f32[]{:T(128)} %bitcast.17, f32[]{:T(128)} %bitcast.16, f32[]{:T(128)} %bitcast.15), kind=kLoop, calls=%fused_computation.36 | loop fusion | flops 1376256 | bytes 3932176 | tf_op jit(solution)/shard_map/add | solution.py:391
  418.5 2.4 multiply_reduce_fusion
  420.9 2.9 convolution_add_fusion.1
  423.9 3.5 multiply_reduce_fusion.4
  431.5 3.9 multiply_reduce_fusion.3
  436.9 40.8 %psum.7 = f32[3077]{0:T(1024)S(1)} all-reduce(f32[3077]{0:T(1024)S(1)} %concatenate.45), channel_id=1, replica_groups=mesh['seq'=8,'fsdp'=4] {'seq','fsdp'}, use_global_device_ids=true, to_apply=%region_16.17 | all-reduce | flops 3077 | bytes 24616 | tf_op jit(solution)/shard_map/psum | solution.py:485
  480.0 89.5 %reduce-scatter.5.cloned.1.call-done = bf16[1,24,9216]{2,1,0:T(8,128)(2,1)} async-done(((bf16[32,24,9216]{2,1,0:T(8,128)(2,1)}), bf16[1,24,9216]{2,1,0:T(8,128)(2,1)}) %reduce-scatter.5.cloned.1.call-update) | async-done | bytes 442384 | tf_op jit(solution)/shard_map/reduce_scatter | solution.py:474
  (162 shorter events, 31.5 us)
Async XLA Ops:
  7.2 112.5 %copy-start = (bf16[2,1,128,768]{3,2,1,0:T(8,128)(2,1)S(1)}, bf16[2,1,128,768]{3,2,1,0:T(8,128)(2,1)}, u32[]{:S(2)}) copy-start(bf16[2,1,128,768]{3,2,1,0:T(8,128)(2,1)} %param.11) | copy-start | bytes 1179652
  7.2 110.6 %all-gather.3.cloned.1.call-start = ((), (), s32[]{:S(2)}) async-start(), calls=%async_computation.2 | async-start | bytes 14800896 | tf_op jit(solution)/shard_map/all_gather | solution.py:367
  11.7 211.8 %all-gather.5.cloned.1.call-start = ((), (), s32[]{:S(2)}) async-start(), calls=%async_computation.3 | async-start | bytes 7077888 | tf_op jit(solution)/shard_map/all_gather | solution.py:401
  13.4 106.5 %copy-start.21 = (f32[256]{0:T(256)}, f32[256]{0:T(256)S(1)}, u32[]{:S(2)}) copy-start(f32[256]{0:T(256)S(1)} %get-tuple-element.98) | copy-start | bytes 3076
  14.7 105.3 %copy-start.23 = (f32[256]{0:T(256)}, f32[256]{0:T(256)S(1)}, u32[]{:S(2)}) copy-start(f32[256]{0:T(256)S(1)} %bitcast_rsqrt_fusion) | copy-start | bytes 3076
  119.9 3.2 copy-start.9
  123.9 3.9 copy-start.2
  126.2 270.4 %reduce-scatter.3.cloned.1.call-start = ((), (), s32[]{:S(2)}) async-start(), calls=%async_computation.4 | async-start | bytes 7077888 | tf_op jit(solution)/shard_map/reduce_scatter | solution.py:426
  127.7 6.8 %copy-start.33 = (pred[2,128]{1,0:T(4,128)(4,1)}, pred[2,128]{1,0:T(4,128)(4,1)S(1)}, u32[]{:S(2)}) copy-start(pred[2,128]{1,0:T(4,128)(4,1)S(1)} %broadcast_compare_fusion) | copy-start | bytes 772
  127.8 129.0 %copy-start.32 = (pred[256]{0:T(512)(128)(4,1)}, pred[256]{0:T(512)(128)(4,1)S(1)}, u32[]{:S(2)}) copy-start(pred[256]{0:T(512)(128)(4,1)S(1)} %fusion.52) | copy-start | bytes 772
  244.0 12.4 %copy-start.25 = (f32[256]{0:T(256)}, f32[256]{0:T(256)S(1)}, u32[]{:S(2)}) copy-start(f32[256]{0:T(256)S(1)} %fusion.28) | copy-start | bytes 3076
  251.3 5.1 copy-start.8
  256.8 23.4 %copy-start.27 = (f32[256]{0:T(256)}, f32[256]{0:T(256)S(1)}, u32[]{:S(2)}) copy-start(f32[256]{0:T(256)S(1)} %negate_multiply_fusion.1) | copy-start | bytes 3076
  280.2 289.3 %reduce-scatter.5.cloned.1.call-start = ((), (), s32[]{:S(2)}) async-start(), calls=%async_computation.5 | async-start | bytes 14598144 | tf_op jit(solution)/shard_map/reduce_scatter | solution.py:474
  287.4 8.6 %copy-start.1 = (f32[256,768]{1,0:T(8,128)S(1)}, f32[256,768]{1,0:T(8,128)}, u32[]{:S(2)}) copy-start(f32[256,768]{1,0:T(8,128)} %get-tuple-element.17.o_ref) | copy-start | bytes 2359300
  297.5 4.7 copy-start.26
  299.9 5.6 slice-start.2
  302.3 3.2 copy-start.17
  399.1 4.4 copy-start.15
  399.1 4.4 copy-start.16
  403.4 4.0 copy-start.13
  403.8 3.5 copy-start.11
  407.4 3.5 copy-start.34
  407.4 13.5 %slice-start = ((s8[4718592]{0:T(1024)(128)(4,1)}), s8[524288]{0:T(1024)(128)(4,1)S(1)}, s32[]{:S(2)}) async-start(s8[4718592]{0:T(1024)(128)(4,1)} %bitcast.96), calls=%async_computation.6 | async-start | bytes 1048576
  410.8 7.6 %copy-start.20 = (f32[5]{0:T(128)S(1)}, f32[5]{0:T(128)}, u32[]{:S(2)}) copy-start(f32[5]{0:T(128)} %param.21) | copy-start | bytes 64
  410.8 7.6 %copy-start.3 = (bf16[4,2,1,128,768]{4,3,2,1,0:T(8,128)(2,1)S(1)}, bf16[4,2,1,128,768]{4,3,2,1,0:T(8,128)(2,1)}, u32[]{:S(2)}) copy-start(bf16[4,2,1,128,768]{4,3,2,1,0:T(8,128)(2,1)} %param.12) | copy-start | bytes 4718596
  411.0 9.9 %slice-start.1 = ((s8[4718592]{0:T(1024)(128)(4,1)}), s8[4194304]{0:T(1024)(128)(4,1)S(1)}, s32[]{:S(2)}) async-start(s8[4718592]{0:T(1024)(128)(4,1)} %bitcast.96), calls=%async_computation.7 | async-start | bytes 8388608
  411.0 9.9 %copy-start.37 = (f32[256,3072]{1,0:T(8,128)S(1)}, f32[256,3072]{1,0:T(8,128)}, u32[]{:S(2)}) copy-start(f32[256,3072]{1,0:T(8,128)} %get-tuple-element.108) | copy-start | bytes 9437188
  423.9 3.6 copy-start.29
  423.9 3.6 copy-start.24
  423.9 7.7 %copy-start.5 = (f32[1,2,1,128,768]{4,3,2,1,0:T(8,128)S(1)}, f32[1,2,1,128,768]{4,3,2,1,0:T(8,128)}, u32[]{:S(2)}) copy-start(f32[1,2,1,128,768]{4,3,2,1,0:T(8,128)} %fusion.18) | copy-start | bytes 2359300
  430.8 4.6 copy-start.18
  (14 other events, 34.2 us)
Sparse Core Ops, SparseCore 0:
  11.8 105.9 all-gather.2
  126.3 97.1 all-gather.4
  280.3 116.1 reduce-scatter.2
  407.5 161.9 reduce-scatter.4

commit v16 on v15

--- a/solution.py
+++ b/solution.py
@@ -424,7 +424,7 @@
         scalars, queries, kv_flat, attended_grad, attended_rows, log_totals, batches
     )
     kv_grad_own = lax.psum_scatter(kv_grad_flat, "seq", scatter_dimension=0, tiled=True)
-    block_side, _ = lax.optimization_barrier((block_out, kv_grad_flat))
+    block_side = block_out
     combined = depth_weights[4] * block_side + history_part
     next_input = combined.astype(jnp.bfloat16).reshape(batches, 1, row_count, model_width)
     depth_terms = jnp.concatenate(

time: 581 us -> 580 us (level)
  other arithmetic: 40.3 us -> 30.1 us
  waiting for transfers between devices: 349 us -> 357 us
  transfers between devices with their start and end apart: 4 -> 4, of which waited for: 4 -> 4; matrix products, arithmetic and copies ran while one was open for 16% -> 14% of each run, Pallas kernels for 0% -> 0%
where the time goes in v16:
time: 580 us; the launch traced here: 579 us
  waiting for transfers between devices  357 us (62%)
  matrix products  51.2 us (9%)
  local copies, waits for them, and re-layouts  47.5 us (8%)
  blocking collectives  40.1 us (7%)
  Pallas kernels  38.1 us (7%)
  other arithmetic  30.1 us (5%)
  between operations  14.4 us (2%)
    all_gather x1, waiting for transfers between devices, local(): gathered = lax.all_gather(packed, ('seq', 'fsdp'), axis=0, tiled=True)  103 us
    reduce_scatter x1, waiting for transfers between devices, local(): lax.psum_scatter(with_layout_constraint(packed_grads.reshape(device_count...  94.4 us
    reduce_scatter x1, waiting for transfers between devices, local(): lax.psum_scatter(kv_grad_flat, 'seq', scatter_dimension=0, tiled=True)  83.6 us
    all_gather x1, waiting for transfers between devices, local(): kv_flat = lax.all_gather(own_kv, 'seq', axis=0, tiled=False)  75.2 us
    psum x1, blocking collectives, local(): lax.psum(jnp.concatenate([depth_terms, jnp.stack([gain_one, gain_two, bia...  40.1 us
    pallas_call x1, Pallas kernels, attention_backward(): pl.pallas_call(_backward_kernel, grid_spec=pltpu.PrefetchScalarGridSpec(n...  20 us
    pallas_call x1, Pallas kernels, attention_forward(): pl.pallas_call(_forward_kernel, grid_spec=pltpu.PrefetchScalarGridSpec(nu...  18.1 us
  transfers between devices with their start and end apart: 4, of which 4 were waited for; matrix products, arithmetic and copies ran while one was open for 14% of the time, Pallas kernels for 0%

profile of v16, /device:TPU:0, one launch (start us, length us, event | category | flops | bytes accessed | tf_op | source)
XLA Modules:
  0.0 578.5 jit_solution(5823374415898465236)
XLA Ops:
  9.8 1.8 concatenate.37
  14.3 103.4 %all-gather.3.cloned.1.call-done = bf16[768,9344]{1,0:T(8,128)(2,1)} async-done(((bf16[24,9344]{1,0:T(8,128)(2,1)}), bf16[768,9344]{1,0:T(8,128)(2,1)}) %all-gather.3.cloned.1.call-update) | async-done | bytes 14352400 | tf_op jit(solution)/shard_map/all_gather | solution.py:367
  119.9 3.2 fusion.14
  125.1 1.9 pad_maximum_fusion.2
  130.4 4.8 slice.190
  135.2 8.5 %reshape.354 = bf16[3072,768]{1,0:T(8,128)(2,1)} reshape(bf16[768,3072]{1,0:T(8,128)(2,1)} %slice.190) | data formatting | bytes 9437184 | tf_op jit(solution)/shard_map/reshape | solution.py:369
  143.7 5.5 fusion.41
  149.2 75.2 %all-gather.5.cloned.1.call-done.k_ref.v_ref = bf16[8,2,128,1536]{3,2,1,0:T(8,128)(2,1)} async-done(((bf16[1,2,128,1536]{3,2,1,0:T(8,128)(2,1)}), bf16[8,2,128,1536]{3,2,1,0:T(8,128)(2,1)}) %all-gather.5.cloned.1.call-update) | async-done | bytes 6291472 | tf_op jit(solution)/shard_map/all_gather | solution.py:401
  224.3 18.1 %attention_forward.1 = (f32[256,768]{1,0:T(8,128)}, f32[256,768]{1,0:T(8,128)}) custom-call(s32[3]{0:T(128)} %pad_add_fusion.scalars_ref, bf16[256,768]{1,0:T(8,128)(2,1)} %copy.46.q_ref, bf16[8,2,128,1536]{3,2,1,0:T(8,128)(2,1)} %all-gather.5.cloned.1.call-done.k_ref.v_ref, bf16[8,2,128,1536]{3,2,1,0:T(8,128)(2,1)} %all-gather.5.cloned.1.call-done.k_ref.v_ref), custom_call_target="tpu_custom_call" | custom-call | tf_op jit(solution)/shard_map/attention_forward/pallas_call | solution.py:279
  242.4 2.2 fusion.40
  244.9 7.3 %fusion.11 = (bf16[256,3072]{1,0:T(8,128)(2,1)S(1)}, f32[256,3072]{1,0:T(8,128)}) fusion(f32[256,3072]{1,0:T(8,128)S(1)} %copy-done.8, bf16[768,9344]{1,0:T(8,128)(2,1)} %all-gather.3.cloned.1.call-done, f32[256,768]{1,0:T(8,128)S(1)} %get-tuple-element.104, f32[768]{0:T(1024)S(1)} %get-tuple-element.60, f32[768]{0:T(1024)S(1)} %get-tuple-element.113, ...), kind=kOutput, calls=%fused_computation.17 | convolution fusion | flops 1224671232 | bytes 13377536 | tf_op jit(solution)/shard_map/dot_general | solution.py:409
  252.2 4.5 multiply_reduce_fusion.1
  258.1 2.5 convolution_convert_fusion.4.do_ref
  260.6 20.0 %attention_backward.1 = (f32[256,768]{1,0:T(8,128)}, bf16[1024,3072]{1,0:T(8,128)(2,1)}) custom-call(s32[3]{0:T(128)} %pad_add_fusion.scalars_ref, bf16[256,768]{1,0:T(8,128)(2,1)} %copy.46.q_ref, bf16[8,2,128,1536]{3,2,1,0:T(8,128)(2,1)} %all-gather.5.cloned.1.call-done.k_ref.v_ref, bf16[8,2,128,1536]{3,2,1,0:T(8,128)(2,1)} %all-gather.5.cloned.1.call-done.k_ref.v_ref, ...), custom_call_target="tpu_custom_call" | custom-call | tf_op jit(solution)/shard_map/attention_backward/pallas_call | solution.py:307
  280.9 6.3 %convolution_convert_fusion.1 = bf16[3072,768]{1,0:T(8,128)(2,1)} fusion(bf16[256,768]{1,0:T(8,128)(2,1)S(1)} %get-tuple-element.85, f32[256,3072]{1,0:T(8,128)} %get-tuple-element.106), kind=kOutput, calls=%fused_computation.3 | convolution fusion | flops 1217396736 | bytes 8257536 | tf_op jit(solution)/shard_map/rf,rd->fd/dot_general | solution.py:433
  287.2 8.5 %reshape.358 = bf16[768,3072]{1,0:T(8,128)(2,1)} reshape(bf16[3072,768]{1,0:T(8,128)(2,1)} %convolution_convert_fusion.1) | data formatting | bytes 9437184 | tf_op jit(solution)/shard_map/reshape | solution.py:443
  295.7 1.5 convolution_convert_fusion.3
  297.3 1.6 copy.49
  298.8 2.4 copy.48
  301.2 3.1 convolution_convert_fusion.2
  304.4 8.9 %pad_maximum_fusion = bf16[768,9216]{1,0:T(8,128)(2,1)} fusion(bf16[768,3072]{1,0:T(8,128)(2,1)S(1)} %bitcast.97, bf16[768,3072]{1,0:T(8,128)(2,1)S(1)} %convolution_convert_fusion.2, bf16[768,768]{1,0:T(8,128)(2,1)S(1)} %copy.49, bf16[9216]{0:T(1024)(128)(2,1)S(1)} %pad.9.clone), kind=kLoop, calls=%fused_computation | loop fusion | flops 56623104 | bytes 24791040 | tf_op jit(solution)/shard_map/concatenate | solution.py:438
  313.3 83.6 %reduce-scatter.3.cloned.1.call-done = bf16[128,3072]{1,0:T(8,128)(2,1)} async-done(((bf16[1024,3072]{1,0:T(8,128)(2,1)}), bf16[128,3072]{1,0:T(8,128)(2,1)}) %reduce-scatter.3.cloned.1.call-update) | async-done | bytes 786448 | tf_op jit(solution)/shard_map/reduce_scatter | solution.py:426
  396.9 2.6 convert_element_type.145
  399.5 1.7 copy.50
  402.7 2.9 fusion
  407.0 2.0 convert_element_type.134
  409.2 5.9 %fusion.18 = f32[1,2,1,128,768]{4,3,2,1,0:T(8,128)} fusion(f32[4,2,1,128,768]{4,3,2,1,0:T(8,128)} %convert_element_type.134, f32[]{:T(128)} %bitcast.15, f32[]{:T(128)} %bitcast.14, f32[]{:T(128)} %bitcast.13, f32[]{:T(128)} %bitcast.12), kind=kLoop, calls=%fused_computation.36 | loop fusion | flops 1376256 | bytes 3932176 | tf_op jit(solution)/shard_map/add | solution.py:391
  415.1 1.9 multiply_reduce_fusion
  417.1 3.5 multiply_reduce_fusion.4
  422.0 8.5 %multiply_reduce_fusion.3 = (f32[]{:T(128)}, bf16[256,768]{1,0:T(8,128)(2,1)}, bf16[256,768]{1,0:T(8,128)(2,1)}) fusion(bf16[2,1,128,768]{3,2,1,0:T(8,128)(2,1)S(1)} %copy-done.4, pred[256]{0:T(512)(128)(4,1)S(1)} %fusion.52, f32[1,2,1,128,768]{4,3,2,1,0:T(8,128)} %fusion.18, f32[]{:T(128)} %bitcast, f32[256]{0:T(256)S(1)} %negate_multiply_fusion, ...), kind=kOutput, calls=%fused_computation.51 | convolution fusion | flops 1219166208 | bytes 12591368 | tf_op jit(solution)/shard_map/dot_general | solution.py:411
  431.2 40.1 %psum.7 = f32[3077]{0:T(1024)S(1)} all-reduce(f32[3077]{0:T(1024)S(1)} %concatenate.45), channel_id=1, replica_groups=mesh['seq'=8,'fsdp'=4] {'seq','fsdp'}, use_global_device_ids=true, to_apply=%region_16.17 | all-reduce | flops 3077 | bytes 24616 | tf_op jit(solution)/shard_map/psum | solution.py:485
  473.7 94.4 %reduce-scatter.5.cloned.1.call-done = bf16[1,24,9216]{2,1,0:T(8,128)(2,1)} async-done(((bf16[32,24,9216]{2,1,0:T(8,128)(2,1)}), bf16[1,24,9216]{2,1,0:T(8,128)(2,1)}) %reduce-scatter.5.cloned.1.call-update) | async-done | bytes 442384 | tf_op jit(solution)/shard_map/reduce_scatter | solution.py:474
  (122 shorter events, 25.7 us)
Async XLA Ops:
  7.2 112.5 %copy-start = (bf16[2,1,128,768]{3,2,1,0:T(8,128)(2,1)S(1)}, bf16[2,1,128,768]{3,2,1,0:T(8,128)(2,1)}, u32[]{:S(2)}) copy-start(bf16[2,1,128,768]{3,2,1,0:T(8,128)(2,1)} %param.11) | copy-start | bytes 1179652
  7.2 110.6 %all-gather.3.cloned.1.call-start = ((), (), s32[]{:S(2)}) async-start(), calls=%async_computation.2 | async-start | bytes 14800896 | tf_op jit(solution)/shard_map/all_gather | solution.py:367
  11.7 212.7 %all-gather.5.cloned.1.call-start = ((), (), s32[]{:S(2)}) async-start(), calls=%async_computation.3 | async-start | bytes 7077888 | tf_op jit(solution)/shard_map/all_gather | solution.py:401
  119.9 3.3 copy-start.11
  124.6 2.7 copy-start.20
  124.6 3.3 copy-start.19
  124.6 4.0 copy-start.3
  127.1 269.9 %reduce-scatter.3.cloned.1.call-start = ((), (), s32[]{:S(2)}) async-start(), calls=%async_computation.4 | async-start | bytes 7077888 | tf_op jit(solution)/shard_map/reduce_scatter | solution.py:426
  242.4 2.5 copy-start.8
  252.2 4.5 copy-start.9
  257.1 1.0 copy-start.5
  280.6 287.4 %reduce-scatter.5.cloned.1.call-start = ((), (), s32[]{:S(2)}) async-start(), calls=%async_computation.5 | async-start | bytes 14598144 | tf_op jit(solution)/shard_map/reduce_scatter | solution.py:474
  287.2 8.5 %copy-start.1 = (f32[256,768]{1,0:T(8,128)S(1)}, f32[256,768]{1,0:T(8,128)}, u32[]{:S(2)}) copy-start(f32[256,768]{1,0:T(8,128)} %get-tuple-element.16.o_ref) | copy-start | bytes 2359300
  298.8 5.5 slice-start
  301.2 3.2 slice-start.1
  401.2 1.2 copy-start.7
  401.3 1.4 copy-start.12
  401.4 4.3 copy-start.17
  402.6 3.0 copy-start.13
  402.7 2.9 copy-start.15
  405.6 1.4 copy-start.2
  407.0 2.0 copy-start.4
  409.2 7.8 %copy-start.14 = (bf16[256,12,64]{0,2,1:T(8,128)(2,1)S(1)}, bf16[256,12,64]{0,2,1:T(8,128)(2,1)}, u32[]{:S(2)}) copy-start(bf16[256,12,64]{0,2,1:T(8,128)(2,1)} %copy-done.13) | copy-start | bytes 1179652
  409.2 7.8 %copy-start.16 = (bf16[256,12,64]{0,2,1:T(8,128)(2,1)S(1)}, bf16[256,12,64]{0,2,1:T(8,128)(2,1)}, u32[]{:S(2)}) copy-start(bf16[256,12,64]{0,2,1:T(8,128)(2,1)} %copy-done.15) | copy-start | bytes 1179652
  409.2 7.8 %copy-start.18 = (bf16[256,768]{0,1:T(8,128)(2,1)S(1)}, bf16[256,768]{0,1:T(8,128)(2,1)}, u32[]{:S(2)}) copy-start(bf16[256,768]{0,1:T(8,128)(2,1)} %copy-done.17) | copy-start | bytes 1179652
  417.1 4.9 copy-start.6
  420.6 0.9 copy-start.10
Sparse Core Ops, SparseCore 0:
  11.8 105.9 all-gather.2
  127.2 97.1 all-gather.4
  280.7 116.1 reduce-scatter.2
  405.8 162.2 reduce-scatter.4

commit v17 on v16

--- a/solution.py
+++ b/solution.py
@@ -222,9 +222,10 @@
 
 
 def _backward_kernel(
-    scalars_ref, q_ref, k_ref, v_ref, do_ref, o_ref, lse_ref, dq_ref, kv_grad_ref
+    scalars_ref, q_ref, k_ref, v_ref, do_ref, o_ref, lse_ref, dq_ref, kv_grad_ref, pair_ref
 ):
     micro = pl.program_id(0)
+    pair = pl.program_id(1)
     row_count = q_ref.shape[0]
     key_count = k_ref.shape[0] * k_ref.shape[2]
     allowed = _pair_masks(scalars_ref, micro, row_count, key_count)
@@ -259,10 +260,12 @@
             probabilities_low, grad_head, (((0,), (0,)), ((), ())),
             preferred_element_type=jnp.float32,
         )
-        kv_grad_ref[:, lanes] = key_grad.astype(jnp.bfloat16)
-        kv_grad_ref[:, 2 * HEAD + half * HEAD : 2 * HEAD + (half + 1) * HEAD] = value_grad.astype(
-            jnp.bfloat16
-        )
+        pair_ref[0, :, lanes] = key_grad.astype(jnp.bfloat16)
+        pair_ref[1, :, lanes] = value_grad.astype(jnp.bfloat16)
+    half_width = kv_grad_ref.shape[1] // 2
+    first_col = pl.multiple_of(pair * 2 * HEAD, 2 * HEAD)
+    kv_grad_ref[:, pl.ds(first_col, 2 * HEAD)] = pair_ref[0]
+    kv_grad_ref[:, pl.ds(first_col + half_width, 2 * HEAD)] = pair_ref[1]
 
 
 def attention_forward(scalars, queries, kv_flat, batches):
@@ -303,7 +306,7 @@
     value_spec = pl.BlockSpec(
         (devices, 1, row_count, 2 * HEAD), lambda m, p, s: (0, m, 0, pairs + p)
     )
-    grad_spec = pl.BlockSpec((key_count, 4 * HEAD), lambda m, p, s: (0, m * pairs + p))
+    grad_spec = pl.BlockSpec((key_count, 2 * model_width), lambda m, p, s: (0, m))
     return pl.pallas_call(
         _backward_kernel,
         grid_spec=pltpu.PrefetchScalarGridSpec(
@@ -311,6 +314,7 @@
             grid=(batches, pairs),
             in_specs=[row_spec, key_spec, value_spec, row_spec, row_spec, row_spec],
             out_specs=[row_spec, grad_spec],
+            scratch_shapes=[pltpu.VMEM((2, key_count, 2 * HEAD), jnp.bfloat16)],
         ),
         out_shape=[
             jax.ShapeDtypeStruct((all_rows, model_width), jnp.float32),
@@ -445,11 +449,9 @@
         axis=1,
     ).astype(jnp.bfloat16)
     kv_grad_own, early_grads = lax.optimization_barrier((kv_grad_own, early_grads))
-    pairs = model_width // (2 * HEAD)
-    kv_grad_own = kv_grad_own.reshape(row_count, batches, pairs, 2, 2 * HEAD)
-    kv_grad_own = jnp.transpose(kv_grad_own, (1, 0, 3, 2, 4)).reshape(
-        all_rows, 2 * model_width
-    )
+    kv_grad_own = jnp.swapaxes(
+        kv_grad_own.reshape(row_count, batches, 2 * model_width), 0, 1
+    ).reshape(all_rows, 2 * model_width)
     key_value_all = kv_grad_own.astype(jnp.float32)
     qkv_low = jnp.concatenate(
         [

time: 580 us -> 581 us (level)
  no operation moved by 1% of the time
where the time goes in v17:
time: 581 us; the launch traced here: 580 us
  waiting for transfers between devices  356 us (61%)
  matrix products  51.3 us (9%)
  local copies, waits for them, and re-layouts  46.4 us (8%)
  Pallas kernels  40.2 us (7%)
  blocking collectives  40.1 us (7%)
  other arithmetic  31 us (5%)
  between operations  14.3 us (2%)
    all_gather x1, waiting for transfers between devices, local(): gathered = lax.all_gather(packed, ('seq', 'fsdp'), axis=0, tiled=True)  103 us
    reduce_scatter x1, waiting for transfers between devices, local(): lax.psum_scatter(with_layout_constraint(packed_grads.reshape(device_count...  94 us
    reduce_scatter x1, waiting for transfers between devices, local(): lax.psum_scatter(kv_grad_flat, 'seq', scatter_dimension=0, tiled=True)  83.8 us
    all_gather x1, waiting for transfers between devices, local(): kv_flat = lax.all_gather(own_kv, 'seq', axis=0, tiled=False)  75.2 us
    psum x1, blocking collectives, local(): lax.psum(jnp.concatenate([depth_terms, jnp.stack([gain_one, gain_two, bia...  40.1 us
    pallas_call x1, Pallas kernels, attention_backward(): pl.pallas_call(_backward_kernel, grid_spec=pltpu.PrefetchScalarGridSpec(n...  22.1 us
    pallas_call x1, Pallas kernels, attention_forward(): pl.pallas_call(_forward_kernel, grid_spec=pltpu.PrefetchScalarGridSpec(nu...  18.1 us
  transfers between devices with their start and end apart: 4, of which 4 were waited for; matrix products, arithmetic and copies ran while one was open for 14% of the time, Pallas kernels for 0%

profile of v17, /device:TPU:0, one launch (start us, length us, event | category | flops | bytes accessed | tf_op | source)
XLA Modules:
  0.0 580.0 jit_solution(10339798478541477412)
XLA Ops:
  9.8 1.8 concatenate.37
  14.3 103.4 %all-gather.3.cloned.1.call-done = bf16[768,9344]{1,0:T(8,128)(2,1)} async-done(((bf16[24,9344]{1,0:T(8,128)(2,1)}), bf16[768,9344]{1,0:T(8,128)(2,1)}) %all-gather.3.cloned.1.call-update) | async-done | bytes 14352400 | tf_op jit(solution)/shard_map/all_gather | solution.py:371
  119.9 3.2 fusion.14
  125.1 1.9 pad_maximum_fusion.2
  130.4 4.8 slice.190
  135.2 8.5 %reshape.354 = bf16[3072,768]{1,0:T(8,128)(2,1)} reshape(bf16[768,3072]{1,0:T(8,128)(2,1)} %slice.190) | data formatting | bytes 9437184 | tf_op jit(solution)/shard_map/reshape | solution.py:373
  143.7 5.5 fusion.40
  149.2 75.2 %all-gather.5.cloned.1.call-done.k_ref.v_ref = bf16[8,2,128,1536]{3,2,1,0:T(8,128)(2,1)} async-done(((bf16[1,2,128,1536]{3,2,1,0:T(8,128)(2,1)}), bf16[8,2,128,1536]{3,2,1,0:T(8,128)(2,1)}) %all-gather.5.cloned.1.call-update) | async-done | bytes 6291472 | tf_op jit(solution)/shard_map/all_gather | solution.py:405
  224.3 18.1 %attention_forward.1 = (f32[256,768]{1,0:T(8,128)}, f32[256,768]{1,0:T(8,128)}) custom-call(s32[3]{0:T(128)} %pad_add_fusion.scalars_ref, bf16[256,768]{1,0:T(8,128)(2,1)} %copy.48.q_ref, bf16[8,2,128,1536]{3,2,1,0:T(8,128)(2,1)} %all-gather.5.cloned.1.call-done.k_ref.v_ref, bf16[8,2,128,1536]{3,2,1,0:T(8,128)(2,1)} %all-gather.5.cloned.1.call-done.k_ref.v_ref), custom_call_target="tpu_custom_call" | custom-call | tf_op jit(solution)/shard_map/attention_forward/pallas_call | solution.py:282
  242.4 2.2 fusion.39
  244.9 7.3 %fusion.11 = (bf16[256,3072]{1,0:T(8,128)(2,1)S(1)}, f32[256,3072]{1,0:T(8,128)}) fusion(f32[256,3072]{1,0:T(8,128)S(1)} %copy-done.8, bf16[768,9344]{1,0:T(8,128)(2,1)} %all-gather.3.cloned.1.call-done, f32[256,768]{1,0:T(8,128)S(1)} %get-tuple-element.104, f32[768]{0:T(1024)S(1)} %get-tuple-element.60, f32[768]{0:T(1024)S(1)} %get-tuple-element.113, ...), kind=kOutput, calls=%fused_computation.17 | convolution fusion | flops 1224671232 | bytes 13377536 | tf_op jit(solution)/shard_map/dot_general | solution.py:413
  252.2 4.5 multiply_reduce_fusion.1
  258.1 2.5 convolution_convert_fusion.4.do_ref
  260.6 22.1 %attention_backward.1 = (f32[256,768]{1,0:T(8,128)}, bf16[1024,3072]{1,0:T(8,128)(2,1)}) custom-call(s32[3]{0:T(128)} %pad_add_fusion.scalars_ref, bf16[256,768]{1,0:T(8,128)(2,1)} %copy.48.q_ref, bf16[8,2,128,1536]{3,2,1,0:T(8,128)(2,1)} %all-gather.5.cloned.1.call-done.k_ref.v_ref, bf16[8,2,128,1536]{3,2,1,0:T(8,128)(2,1)} %all-gather.5.cloned.1.call-done.k_ref.v_ref, ...), custom_call_target="tpu_custom_call" | custom-call | tf_op jit(solution)/shard_map/attention_backward/pallas_call | solution.py:310
  282.7 6.3 %convolution_convert_fusion.1 = bf16[3072,768]{1,0:T(8,128)(2,1)} fusion(bf16[256,768]{1,0:T(8,128)(2,1)S(1)} %get-tuple-element.85, f32[256,3072]{1,0:T(8,128)} %get-tuple-element.106), kind=kOutput, calls=%fused_computation.3 | convolution fusion | flops 1217396736 | bytes 8257536 | tf_op jit(solution)/shard_map/rf,rd->fd/dot_general | solution.py:437
  289.1 8.5 %reshape.358 = bf16[768,3072]{1,0:T(8,128)(2,1)} reshape(bf16[3072,768]{1,0:T(8,128)(2,1)} %convolution_convert_fusion.1) | data formatting | bytes 9437184 | tf_op jit(solution)/shard_map/reshape | solution.py:447
  297.6 1.5 convolution_convert_fusion.3
  299.1 1.6 copy.51
  300.7 2.4 copy.50
  303.1 3.1 convolution_convert_fusion.2
  306.3 8.9 %pad_maximum_fusion = bf16[768,9216]{1,0:T(8,128)(2,1)} fusion(bf16[768,3072]{1,0:T(8,128)(2,1)S(1)} %bitcast.95, bf16[768,3072]{1,0:T(8,128)(2,1)S(1)} %convolution_convert_fusion.2, bf16[768,768]{1,0:T(8,128)(2,1)S(1)} %copy.51, bf16[9216]{0:T(1024)(128)(2,1)S(1)} %pad.9.clone), kind=kLoop, calls=%fused_computation | loop fusion | flops 56623104 | bytes 24791040 | tf_op jit(solution)/shard_map/concatenate | solution.py:442
  315.2 83.8 %reduce-scatter.3.cloned.1.call-done = bf16[128,3072]{1,0:T(8,128)(2,1)} async-done(((bf16[1024,3072]{1,0:T(8,128)(2,1)}), bf16[128,3072]{1,0:T(8,128)(2,1)}) %reduce-scatter.3.cloned.1.call-update) | async-done | bytes 786448 | tf_op jit(solution)/shard_map/reduce_scatter | solution.py:430
  402.1 1.4 copy.53
  404.5 2.9 fusion
  407.5 1.4 copy-done.2
  408.9 2.0 convert_element_type.134
  411.1 5.9 %fusion.18 = f32[1,2,1,128,768]{4,3,2,1,0:T(8,128)} fusion(f32[4,2,1,128,768]{4,3,2,1,0:T(8,128)} %convert_element_type.134, f32[]{:T(128)} %bitcast.15, f32[]{:T(128)} %bitcast.14, f32[]{:T(128)} %bitcast.13, f32[]{:T(128)} %bitcast.12), kind=kLoop, calls=%fused_computation.36 | loop fusion | flops 1376256 | bytes 3932176 | tf_op jit(solution)/shard_map/add | solution.py:395
  417.0 1.9 multiply_reduce_fusion
  418.9 3.5 multiply_reduce_fusion.4
  423.8 8.5 %multiply_reduce_fusion.3 = (f32[]{:T(128)}, bf16[256,768]{1,0:T(8,128)(2,1)}, bf16[256,768]{1,0:T(8,128)(2,1)}) fusion(bf16[2,1,128,768]{3,2,1,0:T(8,128)(2,1)S(1)} %copy-done.4, pred[256]{0:T(512)(128)(4,1)S(1)} %fusion.51, f32[1,2,1,128,768]{4,3,2,1,0:T(8,128)} %fusion.18, f32[]{:T(128)} %bitcast, f32[256]{0:T(256)S(1)} %negate_multiply_fusion, ...), kind=kOutput, calls=%fused_computation.51 | convolution fusion | flops 1219166208 | bytes 12591368 | tf_op jit(solution)/shard_map/dot_general | solution.py:415
  433.1 40.1 %psum.7 = f32[3077]{0:T(1024)S(1)} all-reduce(f32[3077]{0:T(1024)S(1)} %concatenate.45), channel_id=1, replica_groups=mesh['seq'=8,'fsdp'=4] {'seq','fsdp'}, use_global_device_ids=true, to_apply=%region_16.17 | all-reduce | flops 3077 | bytes 24616 | tf_op jit(solution)/shard_map/psum | solution.py:487
  475.5 94.0 %reduce-scatter.5.cloned.1.call-done = bf16[1,24,9216]{2,1,0:T(8,128)(2,1)} async-done(((bf16[32,24,9216]{2,1,0:T(8,128)(2,1)}), bf16[1,24,9216]{2,1,0:T(8,128)(2,1)}) %reduce-scatter.5.cloned.1.call-update) | async-done | bytes 442384 | tf_op jit(solution)/shard_map/reduce_scatter | solution.py:476
  (121 shorter events, 26.7 us)
Async XLA Ops:
  7.2 112.5 %copy-start = (bf16[2,1,128,768]{3,2,1,0:T(8,128)(2,1)S(1)}, bf16[2,1,128,768]{3,2,1,0:T(8,128)(2,1)}, u32[]{:S(2)}) copy-start(bf16[2,1,128,768]{3,2,1,0:T(8,128)(2,1)} %param.11) | copy-start | bytes 1179652
  7.2 110.6 %all-gather.3.cloned.1.call-start = ((), (), s32[]{:S(2)}) async-start(), calls=%async_computation.2 | async-start | bytes 14800896 | tf_op jit(solution)/shard_map/all_gather | solution.py:371
  11.7 212.7 %all-gather.5.cloned.1.call-start = ((), (), s32[]{:S(2)}) async-start(), calls=%async_computation.3 | async-start | bytes 7077888 | tf_op jit(solution)/shard_map/all_gather | solution.py:405
  119.9 3.3 copy-start.11
  124.6 2.7 copy-start.20
  124.6 3.3 copy-start.19
  124.6 4.0 copy-start.3
  127.1 272.0 %reduce-scatter.3.cloned.1.call-start = ((), (), s32[]{:S(2)}) async-start(), calls=%async_computation.4 | async-start | bytes 7077888 | tf_op jit(solution)/shard_map/reduce_scatter | solution.py:430
  242.4 2.5 copy-start.8
  252.2 4.5 copy-start.9
  257.1 1.0 copy-start.5
  282.7 286.8 %reduce-scatter.5.cloned.1.call-start = ((), (), s32[]{:S(2)}) async-start(), calls=%async_computation.5 | async-start | bytes 14598144 | tf_op jit(solution)/shard_map/reduce_scatter | solution.py:476
  289.1 8.5 %copy-start.1 = (f32[256,768]{1,0:T(8,128)S(1)}, f32[256,768]{1,0:T(8,128)}, u32[]{:S(2)}) copy-start(f32[256,768]{1,0:T(8,128)} %get-tuple-element.16.o_ref) | copy-start | bytes 2359300
  300.7 5.5 slice-start
  303.1 3.2 slice-start.1
  315.2 88.3 %copy-start.7 = (f32[256,768]{0,1:T(8,128)S(1)}, f32[256,768]{0,1:T(8,128)}, u32[]{:S(2)}) copy-start(f32[256,768]{0,1:T(8,128)} %copy.50) | copy-start | bytes 2359300
  402.1 1.8 copy-start.12
  403.5 1.0 copy-start.13
  403.8 3.6 copy-start.15
  403.9 3.6 copy-start.17
  407.5 1.4 copy-start.2
  408.9 2.0 copy-start.4
  411.0 7.8 %copy-start.14 = (bf16[256,768]{0,1:T(8,128)(2,1)S(1)}, bf16[256,768]{0,1:T(8,128)(2,1)}, u32[]{:S(2)}) copy-start(bf16[256,768]{0,1:T(8,128)(2,1)} %copy.60) | copy-start | bytes 1179652
  411.0 7.8 %copy-start.16 = (bf16[256,12,64]{0,2,1:T(8,128)(2,1)S(1)}, bf16[256,12,64]{0,2,1:T(8,128)(2,1)}, u32[]{:S(2)}) copy-start(bf16[256,12,64]{0,2,1:T(8,128)(2,1)} %copy-done.15) | copy-start | bytes 1179652
  411.1 7.8 %copy-start.18 = (bf16[256,12,64]{0,2,1:T(8,128)(2,1)S(1)}, bf16[256,12,64]{0,2,1:T(8,128)(2,1)}, u32[]{:S(2)}) copy-start(bf16[256,12,64]{0,2,1:T(8,128)(2,1)} %copy-done.17) | copy-start | bytes 1179652
  418.9 4.9 copy-start.6
  422.5 0.9 copy-start.10
Sparse Core Ops, SparseCore 0:
  11.8 105.9 all-gather.2
  127.2 97.1 all-gather.4
  282.8 116.1 reduce-scatter.2
  407.6 161.8 reduce-scatter.4

commit v18 on v17

--- a/solution.py
+++ b/solution.py
@@ -306,7 +306,7 @@
     value_spec = pl.BlockSpec(
         (devices, 1, row_count, 2 * HEAD), lambda m, p, s: (0, m, 0, pairs + p)
     )
-    grad_spec = pl.BlockSpec((key_count, 2 * model_width), lambda m, p, s: (0, m))
+    grad_spec = pl.BlockSpec((None, key_count, 2 * model_width), lambda m, p, s: (m, 0, 0))
     return pl.pallas_call(
         _backward_kernel,
         grid_spec=pltpu.PrefetchScalarGridSpec(
@@ -318,7 +318,7 @@
         ),
         out_shape=[
             jax.ShapeDtypeStruct((all_rows, model_width), jnp.float32),
-            jax.ShapeDtypeStruct((key_count, batches * 2 * model_width), jnp.bfloat16),
+            jax.ShapeDtypeStruct((batches, key_count, 2 * model_width), jnp.bfloat16),
         ],
         name="attention_backward",
     )(scalars, queries, kv_flat, kv_flat, grads, attended, log_totals)
@@ -427,7 +427,14 @@
     query_grad, kv_grad_flat = attention_backward(
         scalars, queries, kv_flat, attended_grad, attended_rows, log_totals, batches
     )
-    kv_grad_own = lax.psum_scatter(kv_grad_flat, "seq", scatter_dimension=0, tiled=True)
+    micro_major = Layout(major_to_minor=(1, 0, 2))
+    kv_grad_own = lax.psum_scatter(
+        with_layout_constraint(jnp.swapaxes(kv_grad_flat, 0, 1), micro_major),
+        "seq",
+        scatter_dimension=0,
+        tiled=True,
+    )
+    kv_grad_own = with_layout_constraint(kv_grad_own, micro_major)
     block_side = block_out
     combined = depth_weights[4] * block_side + history_part
     next_input = combined.astype(jnp.bfloat16).reshape(batches, 1, row_count, model_width)
@@ -449,9 +456,7 @@
         axis=1,
     ).astype(jnp.bfloat16)
     kv_grad_own, early_grads = lax.optimization_barrier((kv_grad_own, early_grads))
-    kv_grad_own = jnp.swapaxes(
-        kv_grad_own.reshape(row_count, batches, 2 * model_width), 0, 1
-    ).reshape(all_rows, 2 * model_width)
+    kv_grad_own = jnp.swapaxes(kv_grad_own, 0, 1).reshape(all_rows, 2 * model_width)
     key_value_all = kv_grad_own.astype(jnp.float32)
     qkv_low = jnp.concatenate(
         [

time: 581 us -> 579 us (level)
  no operation moved by 1% of the time
where the time goes in v18:
time: 579 us; the launch traced here: 578 us
  waiting for transfers between devices  356 us (61%)
  matrix products  51.2 us (9%)
  local copies, waits for them, and re-layouts  45.1 us (8%)
  Pallas kernels  40.1 us (7%)
  blocking collectives  40.1 us (7%)
  other arithmetic  30.1 us (5%)
  between operations  14.3 us (2%)
    all_gather x1, waiting for transfers between devices, local(): gathered = lax.all_gather(packed, ('seq', 'fsdp'), axis=0, tiled=True)  103 us
    reduce_scatter x1, waiting for transfers between devices, local(): lax.psum_scatter(with_layout_constraint(packed_grads.reshape(device_count...  94 us
    reduce_scatter x1, waiting for transfers between devices, local(): lax.psum_scatter(with_layout_constraint(jnp.swapaxes(kv_grad_flat, 0, 1),...  83.8 us
    all_gather x1, waiting for transfers between devices, local(): kv_flat = lax.all_gather(own_kv, 'seq', axis=0, tiled=False)  75.2 us
    psum x1, blocking collectives, local(): lax.psum(jnp.concatenate([depth_terms, jnp.stack([gain_one, gain_two, bia...  40.1 us
    pallas_call x1, Pallas kernels, attention_backward(): pl.pallas_call(_backward_kernel, grid_spec=pltpu.PrefetchScalarGridSpec(n...  22 us
    pallas_call x1, Pallas kernels, attention_forward(): pl.pallas_call(_forward_kernel, grid_spec=pltpu.PrefetchScalarGridSpec(nu...  18.1 us
  transfers between devices with their start and end apart: 4, of which 4 were waited for; matrix products, arithmetic and copies ran while one was open for 14% of the time, Pallas kernels for 0%

profile of v18, /device:TPU:0, one launch (start us, length us, event | category | flops | bytes accessed | tf_op | source)
XLA Modules:
  0.0 577.7 jit_solution(17174274356803305209)
XLA Ops:
  9.8 1.8 concatenate.37
  12.9 1.2 multiply_reduce_fusion.7
  14.3 103.4 %all-gather.3.cloned.1.call-done = bf16[768,9344]{1,0:T(8,128)(2,1)} async-done(((bf16[24,9344]{1,0:T(8,128)(2,1)}), bf16[768,9344]{1,0:T(8,128)(2,1)}) %all-gather.3.cloned.1.call-update) | async-done | bytes 14352400 | tf_op jit(solution)/shard_map/all_gather | solution.py:371
  119.9 3.2 fusion.14
  125.1 1.9 pad_maximum_fusion.2
  130.4 4.8 slice.190
  135.2 8.5 %reshape.351 = bf16[3072,768]{1,0:T(8,128)(2,1)} reshape(bf16[768,3072]{1,0:T(8,128)(2,1)} %slice.190) | data formatting | bytes 9437184 | tf_op jit(solution)/shard_map/reshape | solution.py:373
  143.7 5.5 fusion.41
  149.2 75.2 %all-gather.5.cloned.1.call-done.k_ref.v_ref = bf16[8,2,128,1536]{3,2,1,0:T(8,128)(2,1)} async-done(((bf16[1,2,128,1536]{3,2,1,0:T(8,128)(2,1)}), bf16[8,2,128,1536]{3,2,1,0:T(8,128)(2,1)}) %all-gather.5.cloned.1.call-update) | async-done | bytes 6291472 | tf_op jit(solution)/shard_map/all_gather | solution.py:405
  224.3 18.1 %attention_forward.1 = (f32[256,768]{1,0:T(8,128)}, f32[256,768]{1,0:T(8,128)}) custom-call(s32[3]{0:T(128)} %pad_add_fusion.scalars_ref, bf16[256,768]{1,0:T(8,128)(2,1)} %copy.47.q_ref, bf16[8,2,128,1536]{3,2,1,0:T(8,128)(2,1)} %all-gather.5.cloned.1.call-done.k_ref.v_ref, bf16[8,2,128,1536]{3,2,1,0:T(8,128)(2,1)} %all-gather.5.cloned.1.call-done.k_ref.v_ref), custom_call_target="tpu_custom_call" | custom-call | tf_op jit(solution)/shard_map/attention_forward/pallas_call | solution.py:282
  242.4 2.2 fusion.40
  244.9 7.3 %fusion.11 = (bf16[256,3072]{1,0:T(8,128)(2,1)S(1)}, f32[256,3072]{1,0:T(8,128)}) fusion(f32[256,3072]{1,0:T(8,128)S(1)} %copy-done.8, bf16[768,9344]{1,0:T(8,128)(2,1)} %all-gather.3.cloned.1.call-done, f32[256,768]{1,0:T(8,128)S(1)} %get-tuple-element.104, f32[768]{0:T(1024)S(1)} %get-tuple-element.60, f32[768]{0:T(1024)S(1)} %get-tuple-element.113, ...), kind=kOutput, calls=%fused_computation.17 | convolution fusion | flops 1224671232 | bytes 13377536 | tf_op jit(solution)/shard_map/dot_general | solution.py:413
  252.2 4.5 multiply_reduce_fusion.1
  258.1 2.5 convolution_convert_fusion.4.do_ref
  260.6 22.0 %attention_backward.1 = (f32[256,768]{1,0:T(8,128)}, bf16[2,1024,1536]{2,1,0:T(8,128)(2,1)}) custom-call(s32[3]{0:T(128)} %pad_add_fusion.scalars_ref, bf16[256,768]{1,0:T(8,128)(2,1)} %copy.47.q_ref, bf16[8,2,128,1536]{3,2,1,0:T(8,128)(2,1)} %all-gather.5.cloned.1.call-done.k_ref.v_ref, bf16[8,2,128,1536]{3,2,1,0:T(8,128)(2,1)} %all-gather.5.cloned.1.call-done.k_ref.v_ref, ...), custom_call_target="tpu_custom_call" | custom-call | tf_op jit(solution)/shard_map/attention_backward/pallas_call | solution.py:310
  282.7 6.3 %convolution_convert_fusion.1 = bf16[3072,768]{1,0:T(8,128)(2,1)} fusion(bf16[256,768]{1,0:T(8,128)(2,1)S(1)} %get-tuple-element.85, f32[256,3072]{1,0:T(8,128)} %get-tuple-element.106), kind=kOutput, calls=%fused_computation.3 | convolution fusion | flops 1217396736 | bytes 8257536 | tf_op jit(solution)/shard_map/rf,rd->fd/dot_general | solution.py:444
  289.0 8.5 %reshape.355 = bf16[768,3072]{1,0:T(8,128)(2,1)} reshape(bf16[3072,768]{1,0:T(8,128)(2,1)} %convolution_convert_fusion.1) | data formatting | bytes 9437184 | tf_op jit(solution)/shard_map/reshape | solution.py:454
  297.5 1.5 convolution_convert_fusion.3
  299.1 1.6 copy.50
  300.7 2.4 copy.49
  303.0 3.1 convolution_convert_fusion.2
  306.2 8.9 %pad_maximum_fusion = bf16[768,9216]{1,0:T(8,128)(2,1)} fusion(bf16[768,3072]{1,0:T(8,128)(2,1)S(1)} %bitcast.93, bf16[768,3072]{1,0:T(8,128)(2,1)S(1)} %convolution_convert_fusion.2, bf16[768,768]{1,0:T(8,128)(2,1)S(1)} %copy.50, bf16[9216]{0:T(1024)(128)(2,1)S(1)} %pad.9.clone), kind=kLoop, calls=%fused_computation | loop fusion | flops 56623104 | bytes 24791040 | tf_op jit(solution)/shard_map/concatenate | solution.py:449
  315.1 83.8 %reduce-scatter.3.cloned.1.call-done = bf16[128,2,1536]{2,0,1:T(8,128)(2,1)} async-done(((bf16[1024,2,1536]{2,0,1:T(8,128)(2,1)}), bf16[128,2,1536]{2,0,1:T(8,128)(2,1)}) %reduce-scatter.3.cloned.1.call-update) | async-done | bytes 786448 | tf_op jit(solution)/shard_map/reduce_scatter | solution.py:431
  402.2 2.9 fusion
  405.2 1.4 copy-done.2
  406.6 2.0 convert_element_type.131
  408.8 5.9 %fusion.18 = f32[1,2,1,128,768]{4,3,2,1,0:T(8,128)} fusion(f32[4,2,1,128,768]{4,3,2,1,0:T(8,128)} %convert_element_type.131, f32[]{:T(128)} %bitcast.15, f32[]{:T(128)} %bitcast.14, f32[]{:T(128)} %bitcast.13, f32[]{:T(128)} %bitcast.12), kind=kLoop, calls=%fused_computation.35 | loop fusion | flops 1376256 | bytes 3932176 | tf_op jit(solution)/shard_map/add | solution.py:395
  414.7 1.9 multiply_reduce_fusion
  416.6 3.5 multiply_reduce_fusion.4
  421.5 8.5 %multiply_reduce_fusion.3 = (f32[]{:T(128)}, bf16[256,768]{1,0:T(8,128)(2,1)}, bf16[256,768]{1,0:T(8,128)(2,1)}) fusion(bf16[2,1,128,768]{3,2,1,0:T(8,128)(2,1)S(1)} %copy-done.4, pred[256]{0:T(512)(128)(4,1)S(1)} %fusion.52, f32[1,2,1,128,768]{4,3,2,1,0:T(8,128)} %fusion.18, f32[]{:T(128)} %bitcast, f32[256]{0:T(256)S(1)} %negate_multiply_fusion, ...), kind=kOutput, calls=%fused_computation.50 | convolution fusion | flops 1219166208 | bytes 12591368 | tf_op jit(solution)/shard_map/dot_general | solution.py:415
  430.8 40.1 %psum.7 = f32[3077]{0:T(1024)S(1)} all-reduce(f32[3077]{0:T(1024)S(1)} %concatenate.45), channel_id=1, replica_groups=mesh['seq'=8,'fsdp'=4] {'seq','fsdp'}, use_global_device_ids=true, to_apply=%region_16.17 | all-reduce | flops 3077 | bytes 24616 | tf_op jit(solution)/shard_map/psum | solution.py:492
  473.2 94.0 %reduce-scatter.5.cloned.1.call-done = bf16[1,24,9216]{2,1,0:T(8,128)(2,1)} async-done(((bf16[32,24,9216]{2,1,0:T(8,128)(2,1)}), bf16[1,24,9216]{2,1,0:T(8,128)(2,1)}) %reduce-scatter.5.cloned.1.call-update) | async-done | bytes 442384 | tf_op jit(solution)/shard_map/reduce_scatter | solution.py:481
  (121 shorter events, 24.6 us)
Async XLA Ops:
  7.2 112.5 %copy-start = (bf16[2,1,128,768]{3,2,1,0:T(8,128)(2,1)S(1)}, bf16[2,1,128,768]{3,2,1,0:T(8,128)(2,1)}, u32[]{:S(2)}) copy-start(bf16[2,1,128,768]{3,2,1,0:T(8,128)(2,1)} %param.11) | copy-start | bytes 1179652
  7.2 110.6 %all-gather.3.cloned.1.call-start = ((), (), s32[]{:S(2)}) async-start(), calls=%async_computation.2 | async-start | bytes 14800896 | tf_op jit(solution)/shard_map/all_gather | solution.py:371
  11.7 212.7 %all-gather.5.cloned.1.call-start = ((), (), s32[]{:S(2)}) async-start(), calls=%async_computation.3 | async-start | bytes 7077888 | tf_op jit(solution)/shard_map/all_gather | solution.py:405
  119.9 3.3 copy-start.11
  124.6 2.7 copy-start.20
  124.6 3.3 copy-start.19
  124.6 4.0 copy-start.3
  127.1 271.9 %reduce-scatter.3.cloned.1.call-start = ((), (), s32[]{:S(2)}) async-start(), calls=%async_computation.4 | async-start | bytes 7077888 | tf_op jit(solution)/shard_map/reduce_scatter | solution.py:431
  242.4 2.5 copy-start.8
  252.2 4.5 copy-start.9
  257.1 1.0 copy-start.5
  282.6 284.6 %reduce-scatter.5.cloned.1.call-start = ((), (), s32[]{:S(2)}) async-start(), calls=%async_computation.5 | async-start | bytes 14598144 | tf_op jit(solution)/shard_map/reduce_scatter | solution.py:481
  289.0 8.5 %copy-start.1 = (f32[256,768]{1,0:T(8,128)S(1)}, f32[256,768]{1,0:T(8,128)}, u32[]{:S(2)}) copy-start(f32[256,768]{1,0:T(8,128)} %get-tuple-element.16.o_ref) | copy-start | bytes 2359300
  300.6 5.5 slice-start
  303.0 3.2 slice-start.1
  315.1 86.2 %copy-start.7 = (f32[256,768]{0,1:T(8,128)S(1)}, f32[256,768]{0,1:T(8,128)}, u32[]{:S(2)}) copy-start(f32[256,768]{0,1:T(8,128)} %copy.49) | copy-start | bytes 2359300
  401.0 1.0 copy-start.12
  401.2 1.0 copy-start.13
  401.6 3.6 copy-start.15
  401.6 3.5 copy-start.17
  405.2 1.4 copy-start.2
  406.6 2.0 copy-start.4
  408.7 7.8 %copy-start.14 = (bf16[256,768]{0,1:T(8,128)(2,1)S(1)}, bf16[256,768]{0,1:T(8,128)(2,1)}, u32[]{:S(2)}) copy-start(bf16[256,768]{0,1:T(8,128)(2,1)} %copy.59) | copy-start | bytes 1179652
  408.7 7.8 %copy-start.16 = (bf16[256,12,64]{0,2,1:T(8,128)(2,1)S(1)}, bf16[256,12,64]{0,2,1:T(8,128)(2,1)}, u32[]{:S(2)}) copy-start(bf16[256,12,64]{0,2,1:T(8,128)(2,1)} %copy-done.15) | copy-start | bytes 1179652
  408.7 7.8 %copy-start.18 = (bf16[256,12,64]{0,2,1:T(8,128)(2,1)S(1)}, bf16[256,12,64]{0,2,1:T(8,128)(2,1)}, u32[]{:S(2)}) copy-start(bf16[256,12,64]{0,2,1:T(8,128)(2,1)} %copy-done.17) | copy-start | bytes 1179652
  416.6 4.9 copy-start.6
  420.2 0.9 copy-start.10
Sparse Core Ops, SparseCore 0:
  11.8 105.9 all-gather.2
  127.2 97.1 all-gather.4
  282.7 116.1 reduce-scatter.2
  405.3 161.8 reduce-scatter.4

commit v19 on v18

--- a/solution.py
+++ b/solution.py
@@ -210,7 +210,7 @@
         ) * HEAD ** (-0.5)
         masked = jnp.where(allowed, scores, masked_value)
         top = jnp.max(masked, axis=1, keepdims=True)
-        kept = jnp.where(allowed, jnp.exp(masked - top), 0.0)
+        kept = jnp.exp(masked - top)
         total = jnp.sum(kept, axis=1, keepdims=True)
         log_total = top + jnp.log(total)
         probabilities = kept * (1.0 / total)

time: 579 us -> 579 us (level)
  no operation moved by 1% of the time
where the time goes in v19:
time: 579 us; the launch traced here: 577 us
  waiting for transfers between devices  356 us (61%)
  matrix products  51.3 us (9%)
  local copies, waits for them, and re-layouts  45.1 us (8%)
  blocking collectives  40.1 us (7%)
  Pallas kernels  39.7 us (7%)
  other arithmetic  30.1 us (5%)
  between operations  14.3 us (2%)
    all_gather x1, waiting for transfers between devices, local(): gathered = lax.all_gather(packed, ('seq', 'fsdp'), axis=0, tiled=True)  103 us
    reduce_scatter x1, waiting for transfers between devices, local(): lax.psum_scatter(with_layout_constraint(packed_grads.reshape(device_count...  94 us
    reduce_scatter x1, waiting for transfers between devices, local(): lax.psum_scatter(with_layout_constraint(jnp.swapaxes(kv_grad_flat, 0, 1),...  83.8 us
    all_gather x1, waiting for transfers between devices, local(): kv_flat = lax.all_gather(own_kv, 'seq', axis=0, tiled=False)  75.2 us
    psum x1, blocking collectives, local(): lax.psum(jnp.concatenate([depth_terms, jnp.stack([gain_one, gain_two, bia...  40.1 us
    pallas_call x1, Pallas kernels, attention_backward(): pl.pallas_call(_backward_kernel, grid_spec=pltpu.PrefetchScalarGridSpec(n...  22 us
    pallas_call x1, Pallas kernels, attention_forward(): pl.pallas_call(_forward_kernel, grid_spec=pltpu.PrefetchScalarGridSpec(nu...  17.7 us
  transfers between devices with their start and end apart: 4, of which 4 were waited for; matrix products, arithmetic and copies ran while one was open for 14% of the time, Pallas kernels for 0%

profile of v19, /device:TPU:0, one launch (start us, length us, event | category | flops | bytes accessed | tf_op | source)
XLA Modules:
  0.0 577.3 jit_solution(15474644413695326827)
XLA Ops:
  9.8 1.8 concatenate.37
  12.9 1.2 multiply_reduce_fusion.7
  14.3 103.4 %all-gather.3.cloned.1.call-done = bf16[768,9344]{1,0:T(8,128)(2,1)} async-done(((bf16[24,9344]{1,0:T(8,128)(2,1)}), bf16[768,9344]{1,0:T(8,128)(2,1)}) %all-gather.3.cloned.1.call-update) | async-done | bytes 14352400 | tf_op jit(solution)/shard_map/all_gather | solution.py:371
  119.9 3.2 fusion.14
  125.1 1.9 pad_maximum_fusion.2
  130.4 4.8 slice.190
  135.2 8.5 %reshape.351 = bf16[3072,768]{1,0:T(8,128)(2,1)} reshape(bf16[768,3072]{1,0:T(8,128)(2,1)} %slice.190) | data formatting | bytes 9437184 | tf_op jit(solution)/shard_map/reshape | solution.py:373
  143.7 5.5 fusion.41
  149.2 75.2 %all-gather.5.cloned.1.call-done.k_ref.v_ref = bf16[8,2,128,1536]{3,2,1,0:T(8,128)(2,1)} async-done(((bf16[1,2,128,1536]{3,2,1,0:T(8,128)(2,1)}), bf16[8,2,128,1536]{3,2,1,0:T(8,128)(2,1)}) %all-gather.5.cloned.1.call-update) | async-done | bytes 6291472 | tf_op jit(solution)/shard_map/all_gather | solution.py:405
  224.3 17.7 %attention_forward.1 = (f32[256,768]{1,0:T(8,128)}, f32[256,768]{1,0:T(8,128)}) custom-call(s32[3]{0:T(128)} %pad_add_fusion.scalars_ref, bf16[256,768]{1,0:T(8,128)(2,1)} %copy.47.q_ref, bf16[8,2,128,1536]{3,2,1,0:T(8,128)(2,1)} %all-gather.5.cloned.1.call-done.k_ref.v_ref, bf16[8,2,128,1536]{3,2,1,0:T(8,128)(2,1)} %all-gather.5.cloned.1.call-done.k_ref.v_ref), custom_call_target="tpu_custom_call" | custom-call | tf_op jit(solution)/shard_map/attention_forward/pallas_call | solution.py:282
  242.0 2.2 fusion.40
  244.5 7.3 %fusion.11 = (bf16[256,3072]{1,0:T(8,128)(2,1)S(1)}, f32[256,3072]{1,0:T(8,128)}) fusion(f32[256,3072]{1,0:T(8,128)S(1)} %copy-done.8, bf16[768,9344]{1,0:T(8,128)(2,1)} %all-gather.3.cloned.1.call-done, f32[256,768]{1,0:T(8,128)S(1)} %get-tuple-element.104, f32[768]{0:T(1024)S(1)} %get-tuple-element.60, f32[768]{0:T(1024)S(1)} %get-tuple-element.113, ...), kind=kOutput, calls=%fused_computation.17 | convolution fusion | flops 1224671232 | bytes 13377536 | tf_op jit(solution)/shard_map/dot_general | solution.py:413
  251.8 4.5 multiply_reduce_fusion.1
  257.7 2.5 convolution_convert_fusion.4.do_ref
  260.2 22.0 %attention_backward.1 = (f32[256,768]{1,0:T(8,128)}, bf16[2,1024,1536]{2,1,0:T(8,128)(2,1)}) custom-call(s32[3]{0:T(128)} %pad_add_fusion.scalars_ref, bf16[256,768]{1,0:T(8,128)(2,1)} %copy.47.q_ref, bf16[8,2,128,1536]{3,2,1,0:T(8,128)(2,1)} %all-gather.5.cloned.1.call-done.k_ref.v_ref, bf16[8,2,128,1536]{3,2,1,0:T(8,128)(2,1)} %all-gather.5.cloned.1.call-done.k_ref.v_ref, ...), custom_call_target="tpu_custom_call" | custom-call | tf_op jit(solution)/shard_map/attention_backward/pallas_call | solution.py:310
  282.3 6.3 %convolution_convert_fusion.1 = bf16[3072,768]{1,0:T(8,128)(2,1)} fusion(bf16[256,768]{1,0:T(8,128)(2,1)S(1)} %get-tuple-element.85, f32[256,3072]{1,0:T(8,128)} %get-tuple-element.106), kind=kOutput, calls=%fused_computation.3 | convolution fusion | flops 1217396736 | bytes 8257536 | tf_op jit(solution)/shard_map/rf,rd->fd/dot_general | solution.py:444
  288.6 8.5 %reshape.355 = bf16[768,3072]{1,0:T(8,128)(2,1)} reshape(bf16[3072,768]{1,0:T(8,128)(2,1)} %convolution_convert_fusion.1) | data formatting | bytes 9437184 | tf_op jit(solution)/shard_map/reshape | solution.py:454
  297.1 1.5 convolution_convert_fusion.3
  298.7 1.6 copy.50
  300.3 2.4 copy.49
  302.6 3.1 convolution_convert_fusion.2
  305.8 8.9 %pad_maximum_fusion = bf16[768,9216]{1,0:T(8,128)(2,1)} fusion(bf16[768,3072]{1,0:T(8,128)(2,1)S(1)} %bitcast.93, bf16[768,3072]{1,0:T(8,128)(2,1)S(1)} %convolution_convert_fusion.2, bf16[768,768]{1,0:T(8,128)(2,1)S(1)} %copy.50, bf16[9216]{0:T(1024)(128)(2,1)S(1)} %pad.9.clone), kind=kLoop, calls=%fused_computation | loop fusion | flops 56623104 | bytes 24791040 | tf_op jit(solution)/shard_map/concatenate | solution.py:449
  314.8 83.8 %reduce-scatter.3.cloned.1.call-done = bf16[128,2,1536]{2,0,1:T(8,128)(2,1)} async-done(((bf16[1024,2,1536]{2,0,1:T(8,128)(2,1)}), bf16[128,2,1536]{2,0,1:T(8,128)(2,1)}) %reduce-scatter.3.cloned.1.call-update) | async-done | bytes 786448 | tf_op jit(solution)/shard_map/reduce_scatter | solution.py:431
  401.8 2.9 fusion
  404.8 1.4 copy-done.2
  406.2 2.0 convert_element_type.131
  408.4 5.9 %fusion.18 = f32[1,2,1,128,768]{4,3,2,1,0:T(8,128)} fusion(f32[4,2,1,128,768]{4,3,2,1,0:T(8,128)} %convert_element_type.131, f32[]{:T(128)} %bitcast.15, f32[]{:T(128)} %bitcast.14, f32[]{:T(128)} %bitcast.13, f32[]{:T(128)} %bitcast.12), kind=kLoop, calls=%fused_computation.35 | loop fusion | flops 1376256 | bytes 3932176 | tf_op jit(solution)/shard_map/add | solution.py:395
  414.3 1.9 multiply_reduce_fusion
  416.2 3.5 multiply_reduce_fusion.4
  421.1 8.5 %multiply_reduce_fusion.3 = (f32[]{:T(128)}, bf16[256,768]{1,0:T(8,128)(2,1)}, bf16[256,768]{1,0:T(8,128)(2,1)}) fusion(bf16[2,1,128,768]{3,2,1,0:T(8,128)(2,1)S(1)} %copy-done.4, pred[256]{0:T(512)(128)(4,1)S(1)} %fusion.52, f32[1,2,1,128,768]{4,3,2,1,0:T(8,128)} %fusion.18, f32[]{:T(128)} %bitcast, f32[256]{0:T(256)S(1)} %negate_multiply_fusion, ...), kind=kOutput, calls=%fused_computation.50 | convolution fusion | flops 1219166208 | bytes 12591368 | tf_op jit(solution)/shard_map/dot_general | solution.py:415
  430.4 40.1 %psum.7 = f32[3077]{0:T(1024)S(1)} all-reduce(f32[3077]{0:T(1024)S(1)} %concatenate.45), channel_id=1, replica_groups=mesh['seq'=8,'fsdp'=4] {'seq','fsdp'}, use_global_device_ids=true, to_apply=%region_16.17 | all-reduce | flops 3077 | bytes 24616 | tf_op jit(solution)/shard_map/psum | solution.py:492
  472.8 94.0 %reduce-scatter.5.cloned.1.call-done = bf16[1,24,9216]{2,1,0:T(8,128)(2,1)} async-done(((bf16[32,24,9216]{2,1,0:T(8,128)(2,1)}), bf16[1,24,9216]{2,1,0:T(8,128)(2,1)}) %reduce-scatter.5.cloned.1.call-update) | async-done | bytes 442384 | tf_op jit(solution)/shard_map/reduce_scatter | solution.py:481
  (121 shorter events, 24.7 us)
Async XLA Ops:
  7.2 112.5 %copy-start = (bf16[2,1,128,768]{3,2,1,0:T(8,128)(2,1)S(1)}, bf16[2,1,128,768]{3,2,1,0:T(8,128)(2,1)}, u32[]{:S(2)}) copy-start(bf16[2,1,128,768]{3,2,1,0:T(8,128)(2,1)} %param.11) | copy-start | bytes 1179652
  7.2 110.6 %all-gather.3.cloned.1.call-start = ((), (), s32[]{:S(2)}) async-start(), calls=%async_computation.2 | async-start | bytes 14800896 | tf_op jit(solution)/shard_map/all_gather | solution.py:371
  11.7 212.7 %all-gather.5.cloned.1.call-start = ((), (), s32[]{:S(2)}) async-start(), calls=%async_computation.3 | async-start | bytes 7077888 | tf_op jit(solution)/shard_map/all_gather | solution.py:405
  119.9 3.3 copy-start.11
  124.6 2.7 copy-start.20
  124.6 3.3 copy-start.19
  124.6 4.0 copy-start.3
  127.1 271.5 %reduce-scatter.3.cloned.1.call-start = ((), (), s32[]{:S(2)}) async-start(), calls=%async_computation.4 | async-start | bytes 7077888 | tf_op jit(solution)/shard_map/reduce_scatter | solution.py:431
  242.0 2.5 copy-start.8
  251.8 4.5 copy-start.9
  256.7 1.0 copy-start.5
  282.2 284.6 %reduce-scatter.5.cloned.1.call-start = ((), (), s32[]{:S(2)}) async-start(), calls=%async_computation.5 | async-start | bytes 14598144 | tf_op jit(solution)/shard_map/reduce_scatter | solution.py:481
  288.6 8.5 %copy-start.1 = (f32[256,768]{1,0:T(8,128)S(1)}, f32[256,768]{1,0:T(8,128)}, u32[]{:S(2)}) copy-start(f32[256,768]{1,0:T(8,128)} %get-tuple-element.16.o_ref) | copy-start | bytes 2359300
  300.2 5.5 slice-start
  302.6 3.2 slice-start.1
  314.8 86.2 %copy-start.7 = (f32[256,768]{0,1:T(8,128)S(1)}, f32[256,768]{0,1:T(8,128)}, u32[]{:S(2)}) copy-start(f32[256,768]{0,1:T(8,128)} %copy.49) | copy-start | bytes 2359300
  400.6 1.0 copy-start.12
  400.8 1.0 copy-start.13
  401.2 3.6 copy-start.15
  401.2 3.5 copy-start.17
  404.8 1.4 copy-start.2
  406.2 2.0 copy-start.4
  408.3 7.8 %copy-start.14 = (bf16[256,768]{0,1:T(8,128)(2,1)S(1)}, bf16[256,768]{0,1:T(8,128)(2,1)}, u32[]{:S(2)}) copy-start(bf16[256,768]{0,1:T(8,128)(2,1)} %copy.59) | copy-start | bytes 1179652
  408.3 7.8 %copy-start.16 = (bf16[256,12,64]{0,2,1:T(8,128)(2,1)S(1)}, bf16[256,12,64]{0,2,1:T(8,128)(2,1)}, u32[]{:S(2)}) copy-start(bf16[256,12,64]{0,2,1:T(8,128)(2,1)} %copy-done.15) | copy-start | bytes 1179652
  408.4 7.8 %copy-start.18 = (bf16[256,12,64]{0,2,1:T(8,128)(2,1)S(1)}, bf16[256,12,64]{0,2,1:T(8,128)(2,1)}, u32[]{:S(2)}) copy-start(bf16[256,12,64]{0,2,1:T(8,128)(2,1)} %copy-done.17) | copy-start | bytes 1179652
  416.2 4.9 copy-start.6
  419.8 0.9 copy-start.10
Sparse Core Ops, SparseCore 0:
  11.8 105.9 all-gather.2
  127.2 97.1 all-gather.4
  282.3 116.1 reduce-scatter.2
  404.9 161.8 reduce-scatter.4

commit v20 on v18

--- a/solution.py
+++ b/solution.py
@@ -487,8 +487,9 @@
         tiled=False,
     )
     scattered = with_layout_constraint(scattered, Layout(major_to_minor=(0, 1)))
-    scattered = scattered.astype(jnp.float32)
-    full_pieces = [scattered[:, grad_offsets[i] : grad_offsets[i + 1]] for i in range(4)]
+    full_pieces = [
+        scattered[:, grad_offsets[i] : grad_offsets[i + 1]].astype(jnp.float32) for i in range(4)
+    ]
     small_sums = lax.psum(
         jnp.concatenate(
             [

time: 579 us -> 581 us (level)
  no operation moved by 1% of the time
where the time goes in v20:
time: 581 us; the launch traced here: 579 us
  waiting for transfers between devices  356 us (61%)
  matrix products  51.2 us (9%)
  local copies, waits for them, and re-layouts  43 us (7%)
  Pallas kernels  40.1 us (7%)
  blocking collectives  40.1 us (7%)
  other arithmetic  33.7 us (6%)
  between operations  14.3 us (2%)
    all_gather x1, waiting for transfers between devices, local(): gathered = lax.all_gather(packed, ('seq', 'fsdp'), axis=0, tiled=True)  103 us
    reduce_scatter x1, waiting for transfers between devices, local(): lax.psum_scatter(with_layout_constraint(packed_grads.reshape(device_count...  94 us
    reduce_scatter x1, waiting for transfers between devices, local(): lax.psum_scatter(with_layout_constraint(jnp.swapaxes(kv_grad_flat, 0, 1),...  83.8 us
    all_gather x1, waiting for transfers between devices, local(): kv_flat = lax.all_gather(own_kv, 'seq', axis=0, tiled=False)  75.2 us
    psum x1, blocking collectives, local(): lax.psum(jnp.concatenate([depth_terms, jnp.stack([gain_one, gain_two, bia...  40.1 us
    pallas_call x1, Pallas kernels, attention_backward(): pl.pallas_call(_backward_kernel, grid_spec=pltpu.PrefetchScalarGridSpec(n...  22 us
    pallas_call x1, Pallas kernels, attention_forward(): pl.pallas_call(_forward_kernel, grid_spec=pltpu.PrefetchScalarGridSpec(nu...  18.1 us
  transfers between devices with their start and end apart: 4, of which 4 were waited for; matrix products, arithmetic and copies ran while one was open for 14% of the time, Pallas kernels for 0%

profile of v20, /device:TPU:0, one launch (start us, length us, event | category | flops | bytes accessed | tf_op | source)
XLA Modules:
  0.0 579.3 jit_solution(17358293049683086763)
XLA Ops:
  9.8 1.8 concatenate.37
  14.3 103.4 %all-gather.3.cloned.1.call-done = bf16[768,9344]{1,0:T(8,128)(2,1)} async-done(((bf16[24,9344]{1,0:T(8,128)(2,1)}), bf16[768,9344]{1,0:T(8,128)(2,1)}) %all-gather.3.cloned.1.call-update) | async-done | bytes 14352400 | tf_op jit(solution)/shard_map/all_gather | solution.py:371
  119.9 3.2 fusion.14
  125.1 1.9 pad_maximum_fusion.2
  130.4 4.8 slice.190
  135.2 8.5 %reshape.354 = bf16[3072,768]{1,0:T(8,128)(2,1)} reshape(bf16[768,3072]{1,0:T(8,128)(2,1)} %slice.190) | data formatting | bytes 9437184 | tf_op jit(solution)/shard_map/reshape | solution.py:373
  143.7 5.5 fusion.40
  149.2 75.2 %all-gather.5.cloned.1.call-done.k_ref.v_ref = bf16[8,2,128,1536]{3,2,1,0:T(8,128)(2,1)} async-done(((bf16[1,2,128,1536]{3,2,1,0:T(8,128)(2,1)}), bf16[8,2,128,1536]{3,2,1,0:T(8,128)(2,1)}) %all-gather.5.cloned.1.call-update) | async-done | bytes 6291472 | tf_op jit(solution)/shard_map/all_gather | solution.py:405
  224.3 18.1 %attention_forward.1 = (f32[256,768]{1,0:T(8,128)}, f32[256,768]{1,0:T(8,128)}) custom-call(s32[3]{0:T(128)} %pad_add_fusion.scalars_ref, bf16[256,768]{1,0:T(8,128)(2,1)} %copy.47.q_ref, bf16[8,2,128,1536]{3,2,1,0:T(8,128)(2,1)} %all-gather.5.cloned.1.call-done.k_ref.v_ref, bf16[8,2,128,1536]{3,2,1,0:T(8,128)(2,1)} %all-gather.5.cloned.1.call-done.k_ref.v_ref), custom_call_target="tpu_custom_call" | custom-call | tf_op jit(solution)/shard_map/attention_forward/pallas_call | solution.py:282
  242.4 2.2 fusion.39
  244.9 7.3 %fusion.11 = (bf16[256,3072]{1,0:T(8,128)(2,1)S(1)}, f32[256,3072]{1,0:T(8,128)}) fusion(f32[256,3072]{1,0:T(8,128)S(1)} %copy-done.8, bf16[768,9344]{1,0:T(8,128)(2,1)} %all-gather.3.cloned.1.call-done, f32[256,768]{1,0:T(8,128)S(1)} %get-tuple-element.104, f32[768]{0:T(1024)S(1)} %get-tuple-element.60, f32[768]{0:T(1024)S(1)} %get-tuple-element.113, ...), kind=kOutput, calls=%fused_computation.17 | convolution fusion | flops 1224671232 | bytes 13377536 | tf_op jit(solution)/shard_map/dot_general | solution.py:413
  252.2 4.5 multiply_reduce_fusion.1
  258.1 2.5 convolution_convert_fusion.4.do_ref
  260.6 22.0 %attention_backward.1 = (f32[256,768]{1,0:T(8,128)}, bf16[2,1024,1536]{2,1,0:T(8,128)(2,1)}) custom-call(s32[3]{0:T(128)} %pad_add_fusion.scalars_ref, bf16[256,768]{1,0:T(8,128)(2,1)} %copy.47.q_ref, bf16[8,2,128,1536]{3,2,1,0:T(8,128)(2,1)} %all-gather.5.cloned.1.call-done.k_ref.v_ref, bf16[8,2,128,1536]{3,2,1,0:T(8,128)(2,1)} %all-gather.5.cloned.1.call-done.k_ref.v_ref, ...), custom_call_target="tpu_custom_call" | custom-call | tf_op jit(solution)/shard_map/attention_backward/pallas_call | solution.py:310
  282.7 6.3 %convolution_convert_fusion.1 = bf16[3072,768]{1,0:T(8,128)(2,1)} fusion(bf16[256,768]{1,0:T(8,128)(2,1)S(1)} %get-tuple-element.85, f32[256,3072]{1,0:T(8,128)} %get-tuple-element.106), kind=kOutput, calls=%fused_computation.3 | convolution fusion | flops 1217396736 | bytes 8257536 | tf_op jit(solution)/shard_map/rf,rd->fd/dot_general | solution.py:444
  289.0 8.5 %reshape.358 = bf16[768,3072]{1,0:T(8,128)(2,1)} reshape(bf16[3072,768]{1,0:T(8,128)(2,1)} %convolution_convert_fusion.1) | data formatting | bytes 9437184 | tf_op jit(solution)/shard_map/reshape | solution.py:454
  297.5 1.5 convolution_convert_fusion.3
  299.1 1.6 copy.50
  300.7 2.4 copy.49
  303.0 3.1 convolution_convert_fusion.2
  306.2 8.9 %pad_maximum_fusion = bf16[768,9216]{1,0:T(8,128)(2,1)} fusion(bf16[768,3072]{1,0:T(8,128)(2,1)S(1)} %bitcast.92, bf16[768,3072]{1,0:T(8,128)(2,1)S(1)} %convolution_convert_fusion.2, bf16[768,768]{1,0:T(8,128)(2,1)S(1)} %copy.50, bf16[9216]{0:T(1024)(128)(2,1)S(1)} %pad.9.clone), kind=kLoop, calls=%fused_computation | loop fusion | flops 56623104 | bytes 24791040 | tf_op jit(solution)/shard_map/concatenate | solution.py:449
  315.1 83.8 %reduce-scatter.3.cloned.1.call-done = bf16[128,2,1536]{2,0,1:T(8,128)(2,1)} async-done(((bf16[1024,2,1536]{2,0,1:T(8,128)(2,1)}), bf16[128,2,1536]{2,0,1:T(8,128)(2,1)}) %reduce-scatter.3.cloned.1.call-update) | async-done | bytes 786448 | tf_op jit(solution)/shard_map/reduce_scatter | solution.py:431
  402.2 2.9 fusion
  406.6 2.0 convert_element_type.138
  408.8 5.9 %fusion.18 = f32[1,2,1,128,768]{4,3,2,1,0:T(8,128)} fusion(f32[4,2,1,128,768]{4,3,2,1,0:T(8,128)} %convert_element_type.138, f32[]{:T(128)} %bitcast.15, f32[]{:T(128)} %bitcast.14, f32[]{:T(128)} %bitcast.13, f32[]{:T(128)} %bitcast.12), kind=kLoop, calls=%fused_computation.35 | loop fusion | flops 1376256 | bytes 3932176 | tf_op jit(solution)/shard_map/add | solution.py:395
  414.7 1.9 multiply_reduce_fusion
  416.6 3.5 multiply_reduce_fusion.4
  421.5 8.5 %multiply_reduce_fusion.3 = (f32[]{:T(128)}, bf16[256,768]{1,0:T(8,128)(2,1)}, bf16[256,768]{1,0:T(8,128)(2,1)}) fusion(bf16[2,1,128,768]{3,2,1,0:T(8,128)(2,1)S(1)} %copy-done.4, pred[256]{0:T(512)(128)(4,1)S(1)} %fusion.51, f32[1,2,1,128,768]{4,3,2,1,0:T(8,128)} %fusion.18, f32[]{:T(128)} %bitcast, f32[256]{0:T(256)S(1)} %negate_multiply_fusion, ...), kind=kOutput, calls=%fused_computation.50 | convolution fusion | flops 1219166208 | bytes 12591368 | tf_op jit(solution)/shard_map/dot_general | solution.py:415
  430.8 40.1 %psum.7 = f32[3077]{0:T(1024)S(1)} all-reduce(f32[3077]{0:T(1024)S(1)} %concatenate.45), channel_id=1, replica_groups=mesh['seq'=8,'fsdp'=4] {'seq','fsdp'}, use_global_device_ids=true, to_apply=%region_16.17 | all-reduce | flops 3077 | bytes 24616 | tf_op jit(solution)/shard_map/psum | solution.py:493
  473.2 94.0 %reduce-scatter.5.cloned.1.call-done = bf16[1,24,9216]{2,1,0:T(8,128)(2,1)} async-done(((bf16[32,24,9216]{2,1,0:T(8,128)(2,1)}), bf16[1,24,9216]{2,1,0:T(8,128)(2,1)}) %reduce-scatter.5.cloned.1.call-update) | async-done | bytes 442384 | tf_op jit(solution)/shard_map/reduce_scatter | solution.py:481
  567.2 1.6 slice_convert_fusion.5
  570.2 1.7 slice_convert_fusion.3
  (120 shorter events, 25.5 us)
Async XLA Ops:
  7.2 112.5 %copy-start = (bf16[2,1,128,768]{3,2,1,0:T(8,128)(2,1)S(1)}, bf16[2,1,128,768]{3,2,1,0:T(8,128)(2,1)}, u32[]{:S(2)}) copy-start(bf16[2,1,128,768]{3,2,1,0:T(8,128)(2,1)} %param.11) | copy-start | bytes 1179652
  7.2 110.6 %all-gather.3.cloned.1.call-start = ((), (), s32[]{:S(2)}) async-start(), calls=%async_computation.2 | async-start | bytes 14800896 | tf_op jit(solution)/shard_map/all_gather | solution.py:371
  11.7 212.7 %all-gather.5.cloned.1.call-start = ((), (), s32[]{:S(2)}) async-start(), calls=%async_computation.3 | async-start | bytes 7077888 | tf_op jit(solution)/shard_map/all_gather | solution.py:405
  119.9 3.3 copy-start.11
  124.6 2.7 copy-start.20
  124.6 3.3 copy-start.19
  124.6 4.0 copy-start.3
  127.1 271.9 %reduce-scatter.3.cloned.1.call-start = ((), (), s32[]{:S(2)}) async-start(), calls=%async_computation.4 | async-start | bytes 7077888 | tf_op jit(solution)/shard_map/reduce_scatter | solution.py:431
  242.4 2.5 copy-start.8
  252.2 4.5 copy-start.9
  257.1 1.0 copy-start.5
  282.6 284.6 %reduce-scatter.5.cloned.1.call-start = ((), (), s32[]{:S(2)}) async-start(), calls=%async_computation.5 | async-start | bytes 14598144 | tf_op jit(solution)/shard_map/reduce_scatter | solution.py:481
  289.0 8.5 %copy-start.1 = (f32[256,768]{1,0:T(8,128)S(1)}, f32[256,768]{1,0:T(8,128)}, u32[]{:S(2)}) copy-start(f32[256,768]{1,0:T(8,128)} %get-tuple-element.16.o_ref) | copy-start | bytes 2359300
  300.6 5.5 slice-start
  303.0 3.2 slice-start.1
  315.1 86.2 %copy-start.7 = (f32[256,768]{0,1:T(8,128)S(1)}, f32[256,768]{0,1:T(8,128)}, u32[]{:S(2)}) copy-start(f32[256,768]{0,1:T(8,128)} %copy.49) | copy-start | bytes 2359300
  401.0 1.0 copy-start.12
  401.2 1.0 copy-start.13
  401.6 3.6 copy-start.15
  401.6 3.5 copy-start.17
  405.2 1.4 copy-start.2
  406.6 2.0 copy-start.4
  408.7 7.8 %copy-start.14 = (bf16[256,768]{0,1:T(8,128)(2,1)S(1)}, bf16[256,768]{0,1:T(8,128)(2,1)}, u32[]{:S(2)}) copy-start(bf16[256,768]{0,1:T(8,128)(2,1)} %copy.59) | copy-start | bytes 1179652
  408.7 7.8 %copy-start.16 = (bf16[256,12,64]{0,2,1:T(8,128)(2,1)S(1)}, bf16[256,12,64]{0,2,1:T(8,128)(2,1)}, u32[]{:S(2)}) copy-start(bf16[256,12,64]{0,2,1:T(8,128)(2,1)} %copy-done.15) | copy-start | bytes 1179652
  408.7 7.8 %copy-start.18 = (bf16[256,12,64]{0,2,1:T(8,128)(2,1)S(1)}, bf16[256,12,64]{0,2,1:T(8,128)(2,1)}, u32[]{:S(2)}) copy-start(bf16[256,12,64]{0,2,1:T(8,128)(2,1)} %copy-done.17) | copy-start | bytes 1179652
  416.6 4.9 copy-start.6
  420.2 0.9 copy-start.10
Sparse Core Ops, SparseCore 0:
  11.8 105.9 all-gather.2
  127.2 97.1 all-gather.4
  282.7 116.1 reduce-scatter.2
  405.3 161.8 reduce-scatter.4
